TPU v7x, 128 devices: a whole 4x4x4 slice. The times are simulated.
128 devices in a mesh: seq: 16 (over x_hi, y, core), head: 8 (over x_lo, z).
Axes of the slice: x: 4 (x_hi: 2, x_lo: 2; x = x_hi * 2 + x_lo), y: 4, z: 4, core: 2. Of those that a mesh axis runs over, the one named last changes fastest.
Arguments:
- tokens: bfloat16 [4096, 2048], P('seq'), may hold values from -6 to 6
- norm_gain: float32 [2048], replicated, may hold values from 0.1 to 1.9
- w_query: bfloat16 [2048, 4096], P(None, 'head')
- w_key: bfloat16 [2048, 512], replicated
- w_value: bfloat16 [2048, 512], replicated, may hold values from -0.125 to 0.125
- query_gain: float32 [128], replicated, may hold values from 0.5 to 5.5
- key_gain: float32 [128], replicated, may hold values from 0.5 to 5.5
- w_out: bfloat16 [4096, 2048], P('head'), may hold values from -0.5 to 0.5
- post_gain: float32 [2048], replicated, may hold values from 0.1 to 1.9
- doc_lengths: int32 [6], replicated, may hold values from 1 to 2560, 4096 in all
- expert_ids: int32 [4096, 8], P(('seq', 'head')), may hold values from 0 to 127, all different within a row; in each aligned block of 32 rows (0 to 31, 32 to 63, ...) at most 4 rows name the same one
- route_weights: float32 [4096, 8], P(('seq', 'head')), may hold values from 0.15 to 1
- w_gate: bfloat16 [128, 2048, 768], P(('seq', 'head')), may hold values from -0.125 to 0.125
- w_up: bfloat16 [128, 2048, 768], P(('seq', 'head')), may hold values from -0.125 to 0.125
- w_down: bfloat16 [128, 768, 2048], P(('seq', 'head')), may hold values from -0.21875 to 0.21875
Outputs:
- layer_out: bfloat16 [4096, 2048], P(('seq', 'head'))
Inputs may be any that keep to these rules, and one draw needn't show every extreme that they name: `doc_lengths`: 6 document lengths that sum to 4096; the largest is exactly 2560. `expert_ids`: each row names 8 different experts. Among the 32 rows of one device no expert is named more than 4 times; in some devices' rows some expert is named exactly 4 times.
All inputs are finite; a program needn't handle non-finite values.
Results may differ from a plain program's by a relative error of at most 0.015.
The roundings to bfloat16 on the way count: a program that leaves them out, or rounds other values in their place, can miss the bound.
Values may be sent and summed in bfloat16 or wider, within the bound.
No kernel may reach another device: no remote copies, remote signals or barrier semaphores. Data moves between devices by JAX's collectives and lax.ppermute only.
A program may use at most 128 MiB of HBM per device.

v0:
```python
import math

import jax
import jax.numpy as jnp
from jax import lax
from jax.sharding import PartitionSpec as P

HEADS = 32
KV_HEADS = 4
TOP = 8


EPSILON = 1e-06
THETA = 1000000.0
FLOOR = -1e30


def rms_scale(values, gain):
    return values * lax.rsqrt(jnp.mean(values * values, axis=-1, keepdims=True) + EPSILON) * gain


def rotate(values, cosine, sine):
    half = values.shape[-1] // 2
    first = values[..., :half]
    second = values[..., half:]
    return jnp.concatenate(
        [first * cosine - second * sine, second * cosine + first * sine], axis=-1
    )


def doc_index(positions, ends):
    return jnp.sum((positions[:, None] >= ends[None, :]).astype(jnp.int32), axis=1)


def local(
    tokens,
    norm_gain,
    w_query,
    w_key,
    w_value,
    query_gain,
    key_gain,
    w_out,
    post_gain,
    doc_lengths,
    expert_ids,
    route_weights,
    w_gate,
    w_up,
    w_down,
):
    tok_dev, width = tokens.shape
    head_dim = query_gain.shape[0]
    per_dev = w_query.shape[1] // head_dim
    n_seq = lax.axis_size("seq")
    n_head = lax.axis_size("head")
    seq_index = lax.axis_index("seq")
    head_index = lax.axis_index("head")
    ndocs = doc_lengths.shape[0]
    ends = jnp.cumsum(doc_lengths)
    starts = ends - doc_lengths
    positions = seq_index * tok_dev + jnp.arange(tok_dev, dtype=jnp.int32)
    query_doc = doc_index(positions, ends)
    matches = query_doc[:, None] == jnp.arange(ndocs, dtype=jnp.int32)[None, :]
    own_start = jnp.sum(jnp.where(matches, starts[None, :], 0), axis=1)
    offset = (positions - own_start).astype(jnp.float32)
    half = head_dim // 2
    inverse = THETA ** (-2.0 * jnp.arange(half, dtype=jnp.float32) / head_dim)
    angles = offset[:, None] * inverse[None, :]
    cosine = jnp.cos(angles)
    sine = jnp.sin(angles)
    inputs = tokens.astype(jnp.float32)
    normed = rms_scale(inputs, norm_gain).astype(jnp.bfloat16)
    queries = jnp.dot(normed, w_query, preferred_element_type=jnp.float32).reshape(
        tok_dev, per_dev, head_dim
    )
    queries = rotate(rms_scale(queries, query_gain), cosine[:, None, :], sine[:, None, :]).astype(
        jnp.bfloat16
    )
    column = head_index * per_dev // (HEADS // KV_HEADS) * head_dim
    key_cols = lax.dynamic_slice_in_dim(w_key, column, head_dim, 1)
    value_cols = lax.dynamic_slice_in_dim(w_value, column, head_dim, 1)
    keys = rotate(
        rms_scale(jnp.dot(normed, key_cols, preferred_element_type=jnp.float32), key_gain),
        cosine,
        sine,
    ).astype(jnp.bfloat16)
    values = jnp.dot(normed, value_cols, preferred_element_type=jnp.float32).astype(jnp.bfloat16)
    stacked = jnp.stack([keys, values])
    scale = head_dim ** (-0.5)
    last_query = positions[-1]
    first_start = own_start[0]

    def attend(state, block, key_start):
        count = block.shape[1]
        key_pos = key_start + jnp.arange(count, dtype=jnp.int32)

        def update(carry):
            high, total, accum = carry
            key_doc = doc_index(key_pos, ends)
            allowed = (
                (key_doc[None, :] == query_doc[:, None])
                & (key_pos[None, :] <= positions[:, None])
                & (key_pos[None, :] >= 0)
            )
            scores = (
                jnp.einsum("qhd,kd->hqk", queries, block[0], preferred_element_type=jnp.float32)
                * scale
            )
            scores = jnp.where(allowed[None], scores, FLOOR)
            new_high = jnp.maximum(high, jnp.max(scores, axis=2))
            weights = jnp.where(allowed[None], jnp.exp(scores - new_high[:, :, None]), 0.0)
            factor = jnp.exp(high - new_high)
            total = total * factor + jnp.sum(weights, axis=2)
            accum = accum * jnp.transpose(factor)[:, :, None] + jnp.einsum(
                "hqk,kd->qhd",
                weights.astype(jnp.bfloat16),
                block[1],
                preferred_element_type=jnp.float32,
            )
            return (new_high, total, accum)

        needed = (key_start <= last_query) & (key_start + count - 1 >= first_start)
        return lax.cond(needed, update, lambda carry: carry, state)

    initial = (
        jnp.full((per_dev, tok_dev), FLOOR, jnp.float32),
        jnp.zeros((per_dev, tok_dev), jnp.float32),
        jnp.zeros((tok_dev, per_dev, head_dim), jnp.float32),
    )
    piece = lax.all_gather(stacked, "seq", axis=1, tiled=True)
    count = piece.shape[1]
    step = math.gcd(count, tok_dev * max(1, 512 // tok_dev))

    def inner(index, carry):
        block = lax.dynamic_slice_in_dim(piece, index * step, step, 1)
        return attend(carry, block, index * step)

    state = lax.fori_loop(0, count // step, inner, initial)
    high, total, accum = state
    attended = (
        (accum / jnp.transpose(total)[:, :, None])
        .astype(jnp.bfloat16)
        .reshape(tok_dev, per_dev * head_dim)
    )
    rows = tok_dev // n_head
    attn_rows = lax.psum_scatter(
        jnp.dot(attended, w_out, preferred_element_type=jnp.float32).astype(jnp.bfloat16),
        "head",
        scatter_dimension=0,
        tiled=True,
    ).astype(jnp.float32)
    resid = lax.dynamic_slice_in_dim(inputs, head_index * rows, rows, 0) + attn_rows
    routed = rms_scale(resid, post_gain).astype(jnp.bfloat16)
    experts = n_seq * n_head * w_gate.shape[0]
    capacity = 2 * TOP * rows // experts
    chosen = expert_ids.reshape(-1)
    hits = (chosen[:, None] == jnp.arange(experts, dtype=jnp.int32)[None, :]).astype(jnp.int32)
    rank = jnp.sum((jnp.cumsum(hits, axis=0) - hits) * hits, axis=1)
    target = chosen * capacity + rank
    outgoing = (
        jnp.zeros((experts * capacity, width), jnp.bfloat16)
        .at[target]
        .set(jnp.repeat(routed, TOP, axis=0))
    )
    outgoing = outgoing.reshape(experts, capacity, width)
    block = lax.all_to_all(outgoing, ("seq", "head"), split_axis=0, concat_axis=0, tiled=True)
    flat = block.reshape(-1, width)
    gate = jnp.dot(flat, w_gate[0], preferred_element_type=jnp.float32)
    up = jnp.dot(flat, w_up[0], preferred_element_type=jnp.float32)
    hidden = (jax.nn.silu(gate) * up).astype(jnp.bfloat16)
    returned = lax.all_to_all(
        jnp.dot(hidden, w_down[0], preferred_element_type=jnp.float32)
        .astype(jnp.bfloat16)
        .reshape(block.shape),
        ("seq", "head"),
        split_axis=0,
        concat_axis=0,
        tiled=True,
    )
    picked = returned.reshape(experts * capacity, width)[target].reshape(rows, TOP, width)
    combined = jnp.sum(picked.astype(jnp.float32) * route_weights[:, :, None], axis=1)
    return (resid + combined).astype(jnp.bfloat16)


def solution(mesh):
    placed = (
        P("seq", None),
        P(),
        P(None, "head"),
        P(),
        P(),
        P(),
        P(),
        P("head", None),
        P(),
        P(),
        P(("seq", "head"), None),
        P(("seq", "head"), None),
        P(("seq", "head"), None, None),
        P(("seq", "head"), None, None),
        P(("seq", "head"), None, None),
    )
    return jax.shard_map(
        local, mesh=mesh, in_specs=placed, out_specs=P(("seq", "head"), None), check_vma=False
    )
```

profile of v0, /device:TPU:0, one launch (start us, length us, event | category | flops | bytes accessed | tf_op | source)
XLA Modules:
  0.0 291.0 jit_solution(13176573164525477628)
XLA Ops:
  6.6 1.7 multiply_reduce_fusion
  8.3 2.0 multiply_reduce_fusion.3
  10.3 0.7 reduce-window.18
  11.0 0.7 bitcast_subtract_fusion.1
  11.7 0.7 convert_reduce_fusion.1
  12.4 0.1 select_reduce_fusion
  12.5 0.5 copy-done.3
  13.0 1.9 fusion.30
  15.0 0.1 multiply_multiply_fusion
  15.0 0.3 multiply_cosine_fusion
  15.4 0.7 pad_maximum_fusion.1
  16.0 0.0 all-gather.2.cloned.1.call-update
  16.1 0.0 reduce-scatter.2.cloned.1.call-start
  16.1 0.6 slice.35
  16.7 0.6 slice.34
  17.3 0.1 copy.68
  17.3 0.1 copy.69
  17.5 3.5 %fusion.51 = f32[256,512]{1,0:T(8,128)} fusion(bf16[2048,512]{1,0:T(8,128)(2,1)} %param.21, f32[2048]{0:T(1024)S(1)} %copy-done.9, f32[256]{0:T(256)S(1)} %add_rsqrt_fusion.2, bf16[256,2048]{1,0:T(8,128)(2,1)} %param.19), kind=kOutput, calls=%fused_computation.99 | convolution fusion | flops 538968064 | bytes 3679232 | tf_op jit(solution)/shard_map/dot_general | solution.py:74
  20.9 2.0 reshape.304
  23.0 1.4 multiply_reduce_fusion.1
  24.4 0.1 copy.66
  24.5 1.2 fusion.36
  25.7 0.3 subtract_convert_fusion
  26.0 0.1 pad_maximum_fusion
  26.1 39.4 %all-gather.2.cloned.1.call-done = bf16[2,4096,128]{1,2,0:T(8,128)(2,1)} async-done(((bf16[2,256,128]{1,2,0:T(8,128)(2,1)}), bf16[2,4096,128]{1,2,0:T(8,128)(2,1)}) %all-gather.2.cloned.1.call-update) | async-done | bytes 2097168 | tf_op jit(solution)/shard_map/all_gather | solution.py:131
  65.6 4.1 %copy.70 = bf16[2,4096,128]{2,1,0:T(8,128)(2,1)} copy(bf16[2,4096,128]{1,2,0:T(8,128)(2,1)} %all-gather.2.cloned.1.call-done) | data formatting | bytes 4194304
  69.7 0.8 broadcast_in_dim.60
  70.5 18.4 %while.22 = (s32[]{:T(128)}, f32[4,256]{1,0:T(4,128)S(1)}, f32[4,256]{1,0:T(4,128)S(1)}, f32[256,4,128]{2,0,1:T(8,128)}, s32[]{:T(128)}, /*index=5*/s32[]{:T(128...) while((s32[]{:T(128)}, f32[4,256]{1,0:T(4,128)S(1)}, ...), condition=%wide.region_12.13_spmd.clone, body=%wide.region_6.12_spmd.clone.sunk | while | flops 276050688 | bytes 16863676 | solution.py:139
  71.7 8.4 %conditional.3 = ((f32[4,256]{1,0:T(4,128)S(1)}, f32[4,256]{1,0:T(4,128)S(1)}, f32[256,4,128]{2,0,1:T(8,128)})) conditional(s32[]{:T(128)} %convert_element_type.143, (f32[4,256]{1,0:T(4,128)S(1)}, f32[4,256]{1,0:T(4,128)S(1)}, f32[256,4,128]{2,0,1:T(8,128)}) %tuple.83, (s32[]{:T(128)}, s32[512]{0:T(512)S(1)}, s32[6]{0:T(128)}, s32[256]{0:T(256)}, ...), branch_computations={%region_7.7_spmd, %region_8.11_spmd} | conditional | flops 276050688 | bytes 16860310 | solution.py:124
  71.7 0.7 convert_reduce_fusion
  72.5 0.9 and_and_fusion
  73.4 2.7 fusion.2
  76.1 3.5 %fusion.5 = f32[256,4,128]{2,0,1:T(8,128)} fusion(f32[512,256,4]{1,0,2:T(8,128)} %get-tuple-element.592, f32[4,256]{1,0:T(4,128)S(1)} %get-tuple-element.679, pred[256,512]{0,1:T(8,128)(4,1)S(1)} %and_and_fusion, f32[256,4,128]{2,0,1:T(8,128)} %get-tuple-element.459, f32[256,4]{0,1:T(4,128)S(1)} %get-tuple-element.587, ...), kind=kOutput, calls=%fused_computation.9 | convolution fusion | flops 137101312 | bytes 3416072 | tf_op jit(solution)/shard_map/while/body/eval_jaxpr/cond/branch_1_fun/hqk,kd->qhd/dot_general | solution.py:115
  79.6 0.5 fusion.4
  88.9 2.0 copy.71
  91.0 1.1 divide_convert_fusion
  92.1 3.3 %convolution_convert_fusion = bf16[256,2048]{1,0:T(8,128)(2,1)} fusion(bf16[256,512]{0,1:T(8,128)(2,1)S(1)} %bitcast.89, bf16[512,2048]{1,0:T(8,128)(2,1)} %param.26), kind=kOutput, calls=%fused_computation.37 | convolution fusion | flops 537395200 | bytes 3407872 | tf_op jit(solution)/shard_map/dot_general | solution.py:148
  95.4 0.0 reduce-scatter.2.cloned.1.call-update
  95.4 2.8 convert_element_type.85
  98.2 0.1 copy.73
  98.3 0.1 eq.64
  98.4 0.1 eq.60
  98.5 0.1 copy.75
  98.6 0.2 fusion.41
  98.9 0.1 copy.72
  99.0 0.1 mul.258
  99.1 0.2 fusion.43
  99.3 66.3 %reduce-scatter.2.cloned.1.call-done = bf16[32,2048]{1,0:T(8,128)(2,1)} async-done(((bf16[256,2048]{1,0:T(8,128)(2,1)}), bf16[32,2048]{1,0:T(8,128)(2,1)}) %reduce-scatter.2.cloned.1.call-update) | async-done | bytes 131088 | tf_op jit(solution)/shard_map/reduce_scatter | solution.py:147
  165.6 1.2 multiply_reduce_fusion.2
  166.8 1.1 multiply_convert_fusion.2
  167.9 3.7 %scatter_custom_fusion = bf16[512,2048]{1,0:T(8,128)(2,1)} fusion(s32[256]{0:T(256)S(1)} %bitcast.95, bf16[]{:T(256)} %constant.154.clone.1, bf16[32,2048]{1,0:T(8,128)(2,1)S(1)} %multiply_convert_fusion.2), kind=kCustom, calls=%fused_computation.45 | custom fusion | bytes 2228226 | tf_op jit(solution)/shard_map/scatter | solution.py:164
  171.6 4.1 %reshape.308 = bf16[128,4,2048]{2,1,0:T(4,128)(2,1)} reshape(bf16[512,2048]{1,0:T(8,128)(2,1)} %scatter_custom_fusion) | data formatting | bytes 4194304 | tf_op jit(solution)/shard_map/reshape | solution.py:166
  175.7 37.7 %all_to_all.10 = bf16[128,4,2048]{2,1,0:T(4,128)(2,1)} all-to-all(bf16[128,4,2048]{2,1,0:T(4,128)(2,1)} %reshape.308), channel_id=1, replica_groups=mesh['seq'=16,'head'=8] {'seq','head'}, dimensions={0} | all-to-all | bytes 4194304 | tf_op jit(solution)/shard_map/all_to_all | solution.py:167
  213.5 4.0 %reshape.309 = bf16[512,2048]{1,0:T(8,128)(2,1)} reshape(bf16[128,4,2048]{2,1,0:T(4,128)(2,1)} %all_to_all.10) | data formatting | bytes 4194304 | tf_op jit(solution)/shard_map/reshape | solution.py:168
  217.4 5.5 %fusion.22 = f32[512,768]{1,0:T(8,128)} fusion(bf16[512,2048]{1,0:T(8,128)(2,1)} %reshape.309, bf16[1,2048,768]{2,1,0:T(8,128)(2,1)} %param.31), kind=kOutput, calls=%fused_computation.34 | convolution fusion | flops 1610612736 | bytes 6815744 | tf_op jit(solution)/shard_map/dot_general | solution.py:169
  222.9 8.3 %fusion.24 = bf16[512,2048]{1,0:T(8,128)(2,1)} fusion(bf16[1,768,2048]{2,1,0:T(8,128)(2,1)S(1)} %copy-done, f32[512,768]{1,0:T(8,128)} %fusion.22, bf16[512,2048]{1,0:T(8,128)(2,1)} %reshape.309, bf16[1,2048,768]{2,1,0:T(8,128)(2,1)} %param.32), kind=kOutput, calls=%fused_computation.36 | convolution fusion | flops 3224633344 | bytes 12058624 | tf_op jit(solution)/shard_map/dot_general | solution.py:173
  231.2 4.1 %reshape.310 = bf16[128,4,2048]{2,1,0:T(4,128)(2,1)} reshape(bf16[512,2048]{1,0:T(8,128)(2,1)} %fusion.24) | data formatting | bytes 4194304 | tf_op jit(solution)/shard_map/reshape | solution.py:175
  235.3 5.9 %all-to-all-start.1 = ((bf16[128,4,2048]{2,1,0:T(4,128)(2,1)}), bf16[128,4,2048]{2,1,0:T(4,128)(2,1)}, u32[]{:S(2)}, u32[]{:S(2)}) async-start(bf16[128,4,2048]{2,1,0:T(4,128)(2,1)} %reshape.310), calls=%async_computation.2 | async-start | bytes 4194304 | tf_op jit(solution)/shard_map/all_to_all | solution.py:172
  241.2 0.1 copy.77
  241.3 29.7 %all-to-all-done.1 = bf16[128,4,2048]{2,1,0:T(4,128)(2,1)} async-done(((bf16[128,4,2048]{2,1,0:T(4,128)(2,1)}), bf16[128,4,2048]{2,1,0:T(4,128)(2,1)}, u32[]{:S(2)}, u32[]{:S(2)}) %all-to-all-start.1) | async-done | bytes 2097184 | tf_op jit(solution)/shard_map/all_to_all | solution.py:172
  271.0 4.0 %reshape.311 = bf16[512,2048]{1,0:T(8,128)(2,1)} reshape(bf16[128,4,2048]{2,1,0:T(4,128)(2,1)} %all-to-all-done.1) | data formatting | bytes 4194304 | tf_op jit(solution)/shard_map/reshape | solution.py:181
  275.0 5.2 %gather_fusion = bf16[256,2048]{1,0:T(8,128)(2,1)} fusion(bf16[512,2048]{1,0:T(8,128)(2,1)} %reshape.311, s32[1024]{0:T(1024)S(1)} %pad_clamp_fusion), kind=kCustom, calls=%fused_computation | custom fusion | bytes 2098176 | tf_op jit(solution)/shard_map/gather | solution.py:181
  280.2 2.2 fusion.27
  282.5 1.7 add_convert_fusion.1
  (68 shorter events, 0.4 us)
Async XLA Ops:
  6.5 216.4 %copy-start = (bf16[1,768,2048]{2,1,0:T(8,128)(2,1)S(1)}, bf16[1,768,2048]{2,1,0:T(8,128)(2,1)}, u32[]{:S(2)}) copy-start(bf16[1,768,2048]{2,1,0:T(8,128)(2,1)} %param.33) | copy-start | bytes 9437188
  6.5 6.5 %copy-start.9 = (f32[2048]{0:T(1024)S(1)}, f32[2048]{0:T(1024)}, u32[]{:S(2)}) copy-start(f32[2048]{0:T(1024)} %param.20) | copy-start | bytes 24580
  6.5 3.7 %copy-start.10 = (s32[6]{0:T(128)S(1)}, s32[6]{0:T(128)}, u32[]{:S(2)}) copy-start(s32[6]{0:T(128)} %param.28) | copy-start | bytes 76
  6.5 59.0 %all-gather.2.cloned.1.call-start = ((), (), s32[]{:S(2)}) async-start(), calls=%async_computation.3 | async-start | bytes 2228224 | tf_op jit(solution)/shard_map/all_gather | solution.py:131
  8.3 6.7 %copy-start.7 = (f32[128]{0:T(128)S(1)}, f32[128]{0:T(128)}, u32[]{:S(2)}) copy-start(f32[128]{0:T(128)} %param.25) | copy-start | bytes 1540
  12.4 0.6 copy-start.3
  16.1 149.5 %reduce-scatter.2.cloned.1.call-start = ((), (), s32[]{:S(2)}) async-start(), calls=%async_computation.4 | async-start | bytes 1179648 | tf_op jit(solution)/shard_map/reduce_scatter | solution.py:147
  17.4 7.0 %copy-start.8 = (f32[128]{0:T(128)S(1)}, f32[128]{0:T(128)}, u32[]{:S(2)}) copy-start(f32[128]{0:T(128)} %param.24) | copy-start | bytes 1540
  76.1 3.5 %copy-start.1 = (f32[512,256,4]{1,0,2:T(8,128)S(1)}, f32[512,256,4]{1,0,2:T(8,128)}, u32[]{:S(2)}) copy-start(f32[512,256,4]{1,0,2:T(8,128)} %get-tuple-element.592) | copy-start | bytes 6291460 | tf_op jit(solution)/shard_map/while/body/eval_jaxpr/cond
  95.4 2.9 copy-start.4
  95.4 71.4 %copy-start.5 = (f32[2048]{0:T(1024)S(1)}, f32[2048]{0:T(1024)}, u32[]{:S(2)}) copy-start(f32[2048]{0:T(1024)} %param.27) | copy-start | bytes 24580
  235.3 5.9 %copy-start.6 = (f32[32,8]{0,1:T(8,128)S(1)}, f32[32,8]{0,1:T(8,128)}, u32[]{:S(2)}) copy-start(f32[32,8]{0,1:T(8,128)} %param.30) | copy-start | bytes 3076
  235.3 35.7 %all-to-all-start.1 = ((bf16[128,4,2048]{2,1,0:T(4,128)(2,1)}), bf16[128,4,2048]{2,1,0:T(4,128)(2,1)}, u32[]{:S(2)}, u32[]{:S(2)}) async-start(bf16[128,4,2048]{2,1,0:T(4,128)(2,1)} %reshape.310), calls=%async_computation.2 | async-start | bytes 4194304 | tf_op jit(solution)/shard_map/all_to_all | solution.py:172
  275.0 7.5 %copy-start.2 = (bf16[32,2048]{1,0:T(8,128)(2,1)S(1)}, bf16[32,2048]{1,0:T(8,128)(2,1)}, u32[]{:S(2)}) copy-start(bf16[32,2048]{1,0:T(8,128)(2,1)} %reduce-scatter.2.cloned.1.call-done) | copy-start | bytes 393220
Sparse Core Ops, SparseCore 0:
  16.2 49.3 all-gather.1
  95.5 70.0 reduce-scatter.1
where the time goes:
time: 292 us; the launch traced here: 291 us
  waiting for transfers between devices  135 us (46%)
  blocking collectives  37.7 us (13%)
  local copies, waits for them, and re-layouts  36.7 us (13%)
  matrix products  30.5 us (10%)
  other arithmetic  20.8 us (7%)
  between operations  13.7 us (5%)
  loops' own time  10 us (3%)
  starting transfers between devices  5.95 us (2%)
    reduce_scatter x1, waiting for transfers between devices, local(): lax.psum_scatter(jnp.dot(attended, w_out, preferred_element_type=jnp.floa...  66.3 us
    all_gather x1, waiting for transfers between devices, local(): piece = lax.all_gather(stacked, 'seq', axis=1, tiled=True)  39.4 us
    all_to_all x1, blocking collectives, local(): lax.all_to_all(outgoing, ('seq', 'head'), split_axis=0, concat_axis=0, ti...  37.7 us
    all_to_all x1, waiting for transfers between devices, local(): lax.all_to_all(jnp.dot(hidden, w_down[0], preferred_element_type=jnp.floa...  29.7 us
    another operation x1, loops' own time, local(): state = lax.fori_loop(0, count // step, inner, initial)  9.87 us
    dot_general x1, matrix products, local(): jnp.dot(hidden, w_down[0], preferred_element_type=jnp.float32)  8.26 us
    all_to_all x1, starting transfers between devices, local(): lax.all_to_all(jnp.dot(hidden, w_down[0], preferred_element_type=jnp.floa...  5.91 us
  transfers between devices with their start and end apart: 3, of which 3 were waited for; matrix products, arithmetic and copies ran while one was open for 5% of the time, Pallas kernels for 0%

commit v1 on v0

--- a/solution.py
+++ b/solution.py
@@ -128,7 +128,8 @@
         jnp.zeros((per_dev, tok_dev), jnp.float32),
         jnp.zeros((tok_dev, per_dev, head_dim), jnp.float32),
     )
-    piece = lax.all_gather(stacked, "seq", axis=1, tiled=True)
+    spread = jnp.broadcast_to(stacked[:, None], (2, n_seq) + stacked.shape[1:])
+    piece = lax.all_to_all(spread, "seq", 1, 1, tiled=True).reshape(2, n_seq * tok_dev, head_dim)
     count = piece.shape[1]
     step = math.gcd(count, tok_dev * max(1, 512 // tok_dev))
 
@@ -144,12 +145,9 @@
         .reshape(tok_dev, per_dev * head_dim)
     )
     rows = tok_dev // n_head
-    attn_rows = lax.psum_scatter(
-        jnp.dot(attended, w_out, preferred_element_type=jnp.float32).astype(jnp.bfloat16),
-        "head",
-        scatter_dimension=0,
-        tiled=True,
-    ).astype(jnp.float32)
+    terms = jnp.dot(attended, w_out, preferred_element_type=jnp.float32).astype(jnp.bfloat16)
+    terms = lax.all_to_all(terms.reshape(n_head, rows, width), "head", 0, 0, tiled=True)
+    attn_rows = jnp.sum(terms.astype(jnp.float32), axis=0)
     resid = lax.dynamic_slice_in_dim(inputs, head_index * rows, rows, 0) + attn_rows
     routed = rms_scale(resid, post_gain).astype(jnp.bfloat16)
     experts = n_seq * n_head * w_gate.shape[0]
@@ -163,16 +161,13 @@
         .at[target]
         .set(jnp.repeat(routed, TOP, axis=0))
     )
-    outgoing = outgoing.reshape(experts, capacity, width)
-    block = lax.all_to_all(outgoing, ("seq", "head"), split_axis=0, concat_axis=0, tiled=True)
-    flat = block.reshape(-1, width)
+    flat = lax.all_to_all(outgoing, ("seq", "head"), split_axis=0, concat_axis=0, tiled=True)
     gate = jnp.dot(flat, w_gate[0], preferred_element_type=jnp.float32)
     up = jnp.dot(flat, w_up[0], preferred_element_type=jnp.float32)
     hidden = (jax.nn.silu(gate) * up).astype(jnp.bfloat16)
     returned = lax.all_to_all(
         jnp.dot(hidden, w_down[0], preferred_element_type=jnp.float32)
-        .astype(jnp.bfloat16)
-        .reshape(block.shape),
+        .astype(jnp.bfloat16),
         ("seq", "head"),
         split_axis=0,
         concat_axis=0,

time: 292 us -> 250 us (0.86)
  waiting for transfers between devices: 135 us -> 58.5 us
  blocking collectives: 37.7 us -> 68.9 us
  between operations: 13.7 us -> 0.34 us
  starting transfers between devices: 5.95 us -> 19.2 us
    reduce_scatter x1 -> x0, waiting for transfers between devices: 66.3 us -> none  [local(): lax.psum_scatter(jnp.dot(attended, w_out, preferred_element_type=jnp.floa...]
    all_gather x1 -> x0, waiting for transfers between devices: 39.4 us -> none  [local(): piece = lax.all_gather(stacked, 'seq', axis=1, tiled=True)]
    all_to_all x1, blocking collectives: 37.7 us -> 68.9 us  [local(): lax.all_to_all(outgoing, ('seq', 'head'), split_axis=0, concat_axis=0, ti...]
    all_to_all x0 -> x2, waiting for transfers between devices: none -> 28.8 us  [the longest x1 14.6 us: local(): lax.all_to_all(spread, 'seq', 1, 1, tiled=True)]
    all_to_all x0 -> x5, local copies, waits for them, and re-layouts: none -> 19.3 us  [the longest x2 8.08 us: local(): lax.all_to_all(jnp.dot(hidden, w_down[0], preferred_element_type=jnp.floa...]
    reshape x4 -> x0, local copies, waits for them, and re-layouts: 16.2 us -> none  [the longest x1 4.13 us: local(): returned = lax.all_to_all(jnp.dot(hidden, w_down[0], preferred_element_ty...]
    all_to_all x0 -> x2, starting transfers between devices: none -> 13.3 us  [the longest x1 7.19 us: local(): lax.all_to_all(spread, 'seq', 1, 1, tiled=True)]
    unnamed x24 -> x27, local copies, waits for them, and re-layouts: 4.77 us -> 0.66 us
  transfers between devices with their start and end apart: 3 -> 3, of which waited for: 3 -> 3; matrix products, arithmetic and copies ran while one was open for 5% -> 6% of each run, Pallas kernels for 0% -> 0%
where the time goes in v1:
time: 250 us; the launch traced here: 247 us
  blocking collectives  68.9 us (28%)
  waiting for transfers between devices  58.5 us (23%)
  local copies, waits for them, and re-layouts  38.2 us (15%)
  matrix products  30.6 us (12%)
  other arithmetic  20.1 us (8%)
  starting transfers between devices  19.2 us (8%)
  loops' own time  10.7 us (4%)
    all_to_all x1, blocking collectives, local(): lax.all_to_all(outgoing, ('seq', 'head'), split_axis=0, concat_axis=0, ti...  68.9 us
    all_to_all x1, waiting for transfers between devices, local(): lax.all_to_all(jnp.dot(hidden, w_down[0], preferred_element_type=jnp.floa...  29.7 us
    all_to_all x1, waiting for transfers between devices, local(): lax.all_to_all(spread, 'seq', 1, 1, tiled=True)  14.6 us
    all_to_all x1, waiting for transfers between devices, local(): lax.all_to_all(terms.reshape(n_head, rows, width), 'head', 0, 0, tiled=True)  14.2 us
    another operation x1, loops' own time, local(): state = lax.fori_loop(0, count // step, inner, initial)  10.5 us
    dot_general x1, matrix products, local(): jnp.dot(hidden, w_down[0], preferred_element_type=jnp.float32)  8.23 us
    all_to_all x2, local copies, waits for them, and re-layouts, local(): lax.all_to_all(jnp.dot(hidden, w_down[0], preferred_element_type=jnp.floa...  8.08 us
    all_to_all x2, local copies, waits for them, and re-layouts, local(): lax.all_to_all(outgoing, ('seq', 'head'), split_axis=0, concat_axis=0, ti...  8.07 us
  transfers between devices with their start and end apart: 3, of which 3 were waited for; matrix products, arithmetic and copies ran while one was open for 6% of the time, Pallas kernels for 0%

profile of v1, /device:TPU:0, one launch (start us, length us, event | category | flops | bytes accessed | tf_op | source)
XLA Modules:
  0.0 246.6 jit_solution(9416938864483729489)
XLA Ops:
  0.0 1.7 multiply_reduce_fusion
  1.7 2.0 multiply_reduce_fusion.3
  3.7 0.7 reduce-window.18
  4.5 0.7 bitcast_subtract_fusion.1
  5.1 0.7 convert_reduce_fusion.2
  5.9 0.1 select_reduce_fusion
  6.0 0.5 copy-done.3
  6.4 1.9 fusion.30
  8.4 0.1 multiply_multiply_fusion
  8.5 0.3 multiply_cosine_fusion
  8.8 0.1 copy.82
  8.9 1.8 broadcast_in_dim.65
  10.7 7.2 %all-to-all-start = ((bf16[2,16,256,128]{3,2,0,1:T(8,128)(2,1)}), bf16[2,16,256,128]{3,2,0,1:T(8,128)(2,1)}, u32[]{:S(2)}, u32[]{:S(2)}) async-start(bf16[2,16,256,128]{3,2,0,1:T(8,128)(2,1)} %broadcast_in_dim.65), calls=%async_computation | async-start | bytes 4194304 | tf_op jit(solution)/shard_map/all_to_all | solution.py:132
  17.9 0.5 slice.35
  18.5 0.6 slice.34
  19.1 2.8 %convert_element_type.85 = f32[256,2048]{1,0:T(8,128)} convert(bf16[256,2048]{1,0:T(8,128)(2,1)} %param.19) | non-fusion elementwise | flops 524288 | bytes 3145728 | tf_op jit(solution)/shard_map/convert_element_type | solution.py:72
  21.9 0.1 copy.90
  22.0 0.1 eq.64
  22.1 0.7 eq.60
  22.8 0.1 copy.86
  22.9 0.1 copy.87
  23.0 3.5 %fusion.51 = f32[256,512]{1,0:T(8,128)} fusion(bf16[2048,512]{1,0:T(8,128)(2,1)} %param.21, f32[2048]{0:T(1024)} %param.20, f32[256]{0:T(256)S(1)} %add_rsqrt_fusion.2, bf16[256,2048]{1,0:T(8,128)(2,1)} %param.19), kind=kOutput, calls=%fused_computation.100 | convolution fusion | flops 538968064 | bytes 3679232 | tf_op jit(solution)/shard_map/dot_general | solution.py:74
  26.5 2.0 reshape.304
  28.5 1.4 multiply_reduce_fusion.1
  30.0 0.1 copy.92
  30.2 1.2 fusion.36
  31.4 0.3 subtract_convert_fusion
  31.7 0.1 pad_maximum_fusion
  31.8 0.9 fusion.41
  32.7 14.6 %all-to-all-done = bf16[2,16,256,128]{3,2,0,1:T(8,128)(2,1)} async-done(((bf16[2,16,256,128]{3,2,0,1:T(8,128)(2,1)}), bf16[2,16,256,128]{3,2,0,1:T(8,128)(2,1)}, u32[]{:S(2)}, u32[]{:S(2)}) %all-to-all-start) | async-done | bytes 2097184 | tf_op jit(solution)/shard_map/all_to_all | solution.py:132
  47.3 3.1 %copy.83 = bf16[2,16,256,128]{3,2,1,0:T(8,128)(2,1)} copy(bf16[2,16,256,128]{3,2,0,1:T(8,128)(2,1)} %all-to-all-done) | data formatting | bytes 4194304 | tf_op jit(solution)/shard_map/all_to_all | solution.py:132
  50.4 0.8 broadcast_in_dim.62
  51.2 19.1 %while.22 = (s32[]{:T(128)}, f32[4,256]{1,0:T(4,128)S(1)}, f32[4,256]{1,0:T(4,128)S(1)}, f32[256,4,128]{2,0,1:T(8,128)}, s32[]{:T(128)}, /*index=5*/s32[]{:T(128...) while((s32[]{:T(128)}, f32[4,256]{1,0:T(4,128)S(1)}, ...), condition=%wide.region_12.13_spmd.clone, body=%wide.region_6.12_spmd.clone.sunk | while | flops 276050688 | bytes 16863676 | solution.py:140
  52.5 8.5 %conditional.3 = ((f32[4,256]{1,0:T(4,128)S(1)}, f32[4,256]{1,0:T(4,128)S(1)}, f32[256,4,128]{2,0,1:T(8,128)})) conditional(s32[]{:T(128)} %convert_element_type.137, (f32[4,256]{1,0:T(4,128)S(1)}, f32[4,256]{1,0:T(4,128)S(1)}, f32[256,4,128]{2,0,1:T(8,128)}) %tuple.79, (s32[]{:T(128)}, s32[512]{0:T(512)S(1)}, s32[6]{0:T(128)}, s32[256]{0:T(256)}, ...), branch_computations={%region_7.7_spmd, %region_8.11_spmd} | conditional | flops 276050688 | bytes 16860310 | solution.py:124
  52.5 0.7 convert_reduce_fusion
  53.3 0.9 and_and_fusion
  54.2 2.7 %fusion.2 = (f32[4,256]{1,0:T(4,128)S(1)}, f32[512,256,4]{1,0,2:T(8,128)}) fusion(pred[256,512]{0,1:T(8,128)(4,1)S(1)} %and_and_fusion, bf16[256,4,128]{2,0,1:T(8,128)(2,1)S(1)} %get-tuple-element.457, bf16[2,4096,128]{2,1,0:T(8,128)(2,1)} %get-tuple-element.456, s32[]{:T(128)S(6)} %select_n.41), kind=kOutput, calls=%fused_computation.5 | convolution fusion | flops 135789568 | bytes 2625540 | tf_op jit(solution)/shard_map/while/body/eval_jaxpr/cond/branch_1_fun/qhd,kd->hqk/dot_general | solution.py:107
  56.9 3.5 %fusion.5 = f32[256,4,128]{2,0,1:T(8,128)} fusion(f32[512,256,4]{1,0,2:T(8,128)} %get-tuple-element.539, f32[4,256]{1,0:T(4,128)S(1)} %get-tuple-element.626, pred[256,512]{0,1:T(8,128)(4,1)S(1)} %and_and_fusion, f32[256,4,128]{2,0,1:T(8,128)} %get-tuple-element.459, f32[256,4]{0,1:T(4,128)S(1)} %get-tuple-element.532, ...), kind=kOutput, calls=%fused_computation.9 | convolution fusion | flops 137101312 | bytes 3416072 | tf_op jit(solution)/shard_map/while/body/eval_jaxpr/cond/branch_1_fun/hqk,kd->qhd/dot_general | solution.py:115
  60.4 0.5 fusion.4
  70.4 2.0 copy.88
  72.4 1.1 divide_convert_fusion
  73.5 3.3 %convolution_convert_fusion = bf16[256,2048]{1,0:T(8,128)(2,1)} fusion(bf16[256,512]{0,1:T(8,128)(2,1)S(1)} %bitcast.93, bf16[512,2048]{1,0:T(8,128)(2,1)} %param.26), kind=kOutput, calls=%fused_computation.37 | convolution fusion | flops 537395200 | bytes 3407872 | tf_op jit(solution)/shard_map/dot_general | solution.py:148
  76.8 6.1 %all-to-all-start.1 = ((bf16[8,32,2048]{2,1,0:T(8,128)(2,1)}), bf16[8,32,2048]{2,1,0:T(8,128)(2,1)}, u32[]{:S(2)}, u32[]{:S(2)}) async-start(bf16[8,32,2048]{2,1,0:T(8,128)(2,1)} %bitcast.91), calls=%async_computation.1 | async-start | bytes 2097152 | tf_op jit(solution)/shard_map/all_to_all | solution.py:149
  83.1 0.1 copy.89
  83.2 0.1 mul.258
  83.3 0.2 fusion.43
  83.5 14.2 %all-to-all-done.1 = bf16[8,32,2048]{2,1,0:T(8,128)(2,1)} async-done(((bf16[8,32,2048]{2,1,0:T(8,128)(2,1)}), bf16[8,32,2048]{2,1,0:T(8,128)(2,1)}, u32[]{:S(2)}, u32[]{:S(2)}) %all-to-all-start.1) | async-done | bytes 1048608 | tf_op jit(solution)/shard_map/all_to_all | solution.py:149
  97.6 1.4 convert_reduce_fusion.1
  99.0 1.1 multiply_reduce_fusion.2
  100.1 0.1 multiply_convert_fusion.2
  100.2 3.7 %scatter_custom_fusion = bf16[512,2048]{1,0:T(8,128)(2,1)} fusion(s32[256]{0:T(256)S(1)} %bitcast.99, bf16[]{:T(256)} %constant.154.clone.1, bf16[32,2048]{1,0:T(8,128)(2,1)S(1)} %multiply_convert_fusion.2), kind=kCustom, calls=%fused_computation.46 | custom fusion | bytes 2228226 | tf_op jit(solution)/shard_map/scatter | solution.py:162
  103.9 4.1 %all_to_all.24 = bf16[128,4,2048]{2,1,0:T(4,128)(2,1)} reshape(bf16[512,2048]{1,0:T(8,128)(2,1)} %scatter_custom_fusion) | data formatting | bytes 4194304 | tf_op jit(solution)/shard_map/all_to_all | solution.py:164
  108.0 68.9 %all_to_all.34 = bf16[128,4,2048]{2,1,0:T(4,128)(2,1)} all-to-all(bf16[128,4,2048]{2,1,0:T(4,128)(2,1)} %all_to_all.24), channel_id=1, replica_groups=mesh['seq'=16,'head'=8] {'seq','head'}, dimensions={0} | all-to-all | bytes 4194304 | tf_op jit(solution)/shard_map/all_to_all | solution.py:164
  176.9 4.0 %all_to_all.26 = bf16[512,2048]{1,0:T(8,128)(2,1)} reshape(bf16[128,4,2048]{2,1,0:T(4,128)(2,1)} %all_to_all.34) | data formatting | bytes 4194304 | tf_op jit(solution)/shard_map/all_to_all | solution.py:164
  180.9 5.5 %fusion.22 = f32[512,768]{1,0:T(8,128)} fusion(bf16[512,2048]{1,0:T(8,128)(2,1)} %all_to_all.26, bf16[1,2048,768]{2,1,0:T(8,128)(2,1)} %param.31), kind=kOutput, calls=%fused_computation.34 | convolution fusion | flops 1610612736 | bytes 6815744 | tf_op jit(solution)/shard_map/dot_general | solution.py:165
  186.4 8.2 %fusion.24 = bf16[512,2048]{1,0:T(8,128)(2,1)} fusion(bf16[1,768,2048]{2,1,0:T(8,128)(2,1)S(1)} %copy-done, f32[512,768]{1,0:T(8,128)} %fusion.22, bf16[512,2048]{1,0:T(8,128)(2,1)} %all_to_all.26, bf16[1,2048,768]{2,1,0:T(8,128)(2,1)} %param.32), kind=kOutput, calls=%fused_computation.36 | convolution fusion | flops 3224633344 | bytes 12058624 | tf_op jit(solution)/shard_map/dot_general | solution.py:169
  194.6 4.1 %all_to_all.27 = bf16[128,4,2048]{2,1,0:T(4,128)(2,1)} reshape(bf16[512,2048]{1,0:T(8,128)(2,1)} %fusion.24) | data formatting | bytes 4194304 | tf_op jit(solution)/shard_map/all_to_all | solution.py:168
  198.7 5.9 %all-to-all-start.3 = ((bf16[128,4,2048]{2,1,0:T(4,128)(2,1)}), bf16[128,4,2048]{2,1,0:T(4,128)(2,1)}, u32[]{:S(2)}, u32[]{:S(2)}) async-start(bf16[128,4,2048]{2,1,0:T(4,128)(2,1)} %all_to_all.27), calls=%async_computation.3 | async-start | bytes 4194304 | tf_op jit(solution)/shard_map/all_to_all | solution.py:168
  204.7 0.1 copy.94
  204.7 29.7 %all-to-all-done.3 = bf16[128,4,2048]{2,1,0:T(4,128)(2,1)} async-done(((bf16[128,4,2048]{2,1,0:T(4,128)(2,1)}), bf16[128,4,2048]{2,1,0:T(4,128)(2,1)}, u32[]{:S(2)}, u32[]{:S(2)}) %all-to-all-start.3) | async-done | bytes 2097184 | tf_op jit(solution)/shard_map/all_to_all | solution.py:168
  234.5 4.0 %all_to_all.29 = bf16[512,2048]{1,0:T(8,128)(2,1)} reshape(bf16[128,4,2048]{2,1,0:T(4,128)(2,1)} %all-to-all-done.3) | data formatting | bytes 4194304 | tf_op jit(solution)/shard_map/all_to_all | solution.py:168
  238.4 5.2 %gather_fusion = bf16[256,2048]{1,0:T(8,128)(2,1)} fusion(bf16[512,2048]{1,0:T(8,128)(2,1)} %all_to_all.29, s32[1024]{0:T(1024)S(1)} %pad_clamp_fusion), kind=kCustom, calls=%fused_computation | custom fusion | bytes 2098176 | tf_op jit(solution)/shard_map/gather | solution.py:176
  243.7 2.2 fusion.27
  245.9 0.7 add_convert_fusion.1
  (73 shorter events, 0.5 us)
Async XLA Ops:
  0.0 186.4 %copy-start = (bf16[1,768,2048]{2,1,0:T(8,128)(2,1)S(1)}, bf16[1,768,2048]{2,1,0:T(8,128)(2,1)}, u32[]{:S(2)}) copy-start(bf16[1,768,2048]{2,1,0:T(8,128)(2,1)} %param.33) | copy-start | bytes 9437188
  0.0 6.4 %copy-start.11 = (f32[2048]{0:T(1024)S(1)}, f32[2048]{0:T(1024)}, u32[]{:S(2)}) copy-start(f32[2048]{0:T(1024)} %param.20) | copy-start | bytes 24580
  0.0 3.7 %copy-start.12 = (s32[6]{0:T(128)S(1)}, s32[6]{0:T(128)}, u32[]{:S(2)}) copy-start(s32[6]{0:T(128)} %param.28) | copy-start | bytes 76
  1.7 6.7 %copy-start.9 = (f32[128]{0:T(128)S(1)}, f32[128]{0:T(128)}, u32[]{:S(2)}) copy-start(f32[128]{0:T(128)} %param.25) | copy-start | bytes 1540
  5.9 0.5 copy-start.3
  10.7 36.6 %all-to-all-start = ((bf16[2,16,256,128]{3,2,0,1:T(8,128)(2,1)}), bf16[2,16,256,128]{3,2,0,1:T(8,128)(2,1)}, u32[]{:S(2)}, u32[]{:S(2)}) async-start(bf16[2,16,256,128]{3,2,0,1:T(8,128)(2,1)} %broadcast_in_dim.65), calls=%async_computation | async-start | bytes 4194304 | tf_op jit(solution)/shard_map/all_to_all | solution.py:132
  17.9 4.0 %copy-start.4 = (s32[32,8]{0,1:T(8,128)S(1)}, s32[32,8]{0,1:T(8,128)}, u32[]{:S(2)}) copy-start(s32[32,8]{0,1:T(8,128)} %param.29) | copy-start | bytes 3076
  23.0 7.2 %copy-start.10 = (f32[128]{0:T(128)S(1)}, f32[128]{0:T(128)}, u32[]{:S(2)}) copy-start(f32[128]{0:T(128)} %param.24) | copy-start | bytes 1540
  56.9 3.5 %copy-start.1 = (f32[512,256,4]{1,0,2:T(8,128)S(1)}, f32[512,256,4]{1,0,2:T(8,128)}, u32[]{:S(2)}) copy-start(f32[512,256,4]{1,0,2:T(8,128)} %get-tuple-element.539) | copy-start | bytes 6291460 | tf_op jit(solution)/shard_map/while/body/eval_jaxpr/cond
  73.5 9.5 %copy-start.2 = (s32[128,2,128]{0,1,2:T(2,128)S(1)}, s32[128,2,128]{0,1,2:T(2,128)}, u32[]{:S(2)}) copy-start(s32[128,2,128]{0,1,2:T(2,128)} %fusion.41) | copy-start | bytes 393220
  76.8 6.2 %copy-start.5 = (s32[32,8]{0,1:T(8,128)S(1)}, s32[32,8]{0,1:T(8,128)}, u32[]{:S(2)}) copy-start(s32[32,8]{0,1:T(8,128)} %param.29) | copy-start | bytes 3076
  76.8 6.4 %copy-start.7 = (s32[256]{0:T(256)S(1)}, s32[256]{0:T(256)}, u32[]{:S(2)}) copy-start(s32[256]{0:T(256)} %eq.60) | copy-start | bytes 3076
  76.8 23.3 %copy-start.6 = (f32[2048]{0:T(1024)S(1)}, f32[2048]{0:T(1024)}, u32[]{:S(2)}) copy-start(f32[2048]{0:T(1024)} %param.27) | copy-start | bytes 24580
  76.8 20.8 %all-to-all-start.1 = ((bf16[8,32,2048]{2,1,0:T(8,128)(2,1)}), bf16[8,32,2048]{2,1,0:T(8,128)(2,1)}, u32[]{:S(2)}, u32[]{:S(2)}) async-start(bf16[8,32,2048]{2,1,0:T(8,128)(2,1)} %bitcast.91), calls=%async_computation.1 | async-start | bytes 2097152 | tf_op jit(solution)/shard_map/all_to_all | solution.py:149
  198.7 5.9 %copy-start.8 = (f32[32,8]{0,1:T(8,128)S(1)}, f32[32,8]{0,1:T(8,128)}, u32[]{:S(2)}) copy-start(f32[32,8]{0,1:T(8,128)} %param.30) | copy-start | bytes 3076
  198.7 35.7 %all-to-all-start.3 = ((bf16[128,4,2048]{2,1,0:T(4,128)(2,1)}), bf16[128,4,2048]{2,1,0:T(4,128)(2,1)}, u32[]{:S(2)}, u32[]{:S(2)}) async-start(bf16[128,4,2048]{2,1,0:T(4,128)(2,1)} %all_to_all.27), calls=%async_computation.3 | async-start | bytes 4194304 | tf_op jit(solution)/shard_map/all_to_all | solution.py:168

commit v2 on v1

--- a/solution.py
+++ b/solution.py
@@ -1,8 +1,11 @@
+import functools
 import math
 
 import jax
 import jax.numpy as jnp
 from jax import lax
+from jax.experimental import pallas as pl
+from jax.experimental.pallas import tpu as pltpu
 from jax.sharding import PartitionSpec as P
 
 HEADS = 32
@@ -30,6 +33,55 @@
 
 def doc_index(positions, ends):
     return jnp.sum((positions[:, None] >= ends[None, :]).astype(jnp.int32), axis=1)
+
+
+def _attend_kernel(bounds_ref, q_ref, kv_ref, qpos_ref, qstart_ref, o_ref, *, block, scale):
+    q = q_ref[...]
+    qpos = qpos_ref[...]
+    qstart = qstart_ref[...]
+    rows, width = q.shape
+
+    def body(j, carry):
+        high, total, accum = carry
+        base = pl.multiple_of((bounds_ref[0] + j) * block, block)
+        keys = kv_ref[0, pl.ds(base, block), :]
+        values = kv_ref[1, pl.ds(base, block), :]
+        scores = lax.dot_general(q, keys, (((1,), (1,)), ((), ())), preferred_element_type=jnp.float32) * scale
+        key_pos = base + lax.broadcasted_iota(jnp.int32, (1, block), 1)
+        allowed = (key_pos >= qstart) & (key_pos <= qpos)
+        scores = jnp.where(allowed, scores, FLOOR)
+        new_high = jnp.maximum(high, jnp.max(scores, axis=1, keepdims=True))
+        weights = jnp.where(allowed, jnp.exp(scores - new_high), 0.0)
+        factor = jnp.exp(high - new_high)
+        total = total * factor + jnp.sum(weights, axis=1, keepdims=True)
+        accum = accum * factor + jnp.dot(weights.astype(jnp.bfloat16), values, preferred_element_type=jnp.float32)
+        return new_high, total, accum
+
+    initial = (
+        jnp.full((rows, 1), FLOOR, jnp.float32),
+        jnp.zeros((rows, 1), jnp.float32),
+        jnp.zeros((rows, width), jnp.float32),
+    )
+    high, total, accum = lax.fori_loop(0, bounds_ref[1], body, initial)
+    o_ref[...] = (accum / total).astype(o_ref.dtype)
+
+def attend(bounds, queries, kv, qpos, qstart, block):
+    tok, heads, dim = queries.shape
+    kernel = functools.partial(_attend_kernel, block=block, scale=dim ** (-0.5))
+    spec = pltpu.PrefetchScalarGridSpec(
+        num_scalar_prefetch=1,
+        grid=(heads,),
+        in_specs=[
+            pl.BlockSpec((tok, dim), lambda h, b: (0, h)),
+            pl.BlockSpec(kv.shape, lambda h, b: (0, 0, 0)),
+            pl.BlockSpec((tok, 1), lambda h, b: (0, 0)),
+            pl.BlockSpec((tok, 1), lambda h, b: (0, 0)),
+        ],
+        out_specs=pl.BlockSpec((tok, dim), lambda h, b: (0, h)),
+    )
+    return pl.pallas_call(
+        kernel, grid_spec=spec, out_shape=jax.ShapeDtypeStruct((tok, heads * dim), jnp.bfloat16),
+    )(bounds, queries.reshape(tok, heads * dim), kv, qpos, qstart)
 
 
 def local(
@@ -87,63 +139,12 @@
     ).astype(jnp.bfloat16)
     values = jnp.dot(normed, value_cols, preferred_element_type=jnp.float32).astype(jnp.bfloat16)
     stacked = jnp.stack([keys, values])
-    scale = head_dim ** (-0.5)
-    last_query = positions[-1]
-    first_start = own_start[0]
-
-    def attend(state, block, key_start):
-        count = block.shape[1]
-        key_pos = key_start + jnp.arange(count, dtype=jnp.int32)
-
-        def update(carry):
-            high, total, accum = carry
-            key_doc = doc_index(key_pos, ends)
-            allowed = (
-                (key_doc[None, :] == query_doc[:, None])
-                & (key_pos[None, :] <= positions[:, None])
-                & (key_pos[None, :] >= 0)
-            )
-            scores = (
-                jnp.einsum("qhd,kd->hqk", queries, block[0], preferred_element_type=jnp.float32)
-                * scale
-            )
-            scores = jnp.where(allowed[None], scores, FLOOR)
-            new_high = jnp.maximum(high, jnp.max(scores, axis=2))
-            weights = jnp.where(allowed[None], jnp.exp(scores - new_high[:, :, None]), 0.0)
-            factor = jnp.exp(high - new_high)
-            total = total * factor + jnp.sum(weights, axis=2)
-            accum = accum * jnp.transpose(factor)[:, :, None] + jnp.einsum(
-                "hqk,kd->qhd",
-                weights.astype(jnp.bfloat16),
-                block[1],
-                preferred_element_type=jnp.float32,
-            )
-            return (new_high, total, accum)
-
-        needed = (key_start <= last_query) & (key_start + count - 1 >= first_start)
-        return lax.cond(needed, update, lambda carry: carry, state)
-
-    initial = (
-        jnp.full((per_dev, tok_dev), FLOOR, jnp.float32),
-        jnp.zeros((per_dev, tok_dev), jnp.float32),
-        jnp.zeros((tok_dev, per_dev, head_dim), jnp.float32),
-    )
     spread = jnp.broadcast_to(stacked[:, None], (2, n_seq) + stacked.shape[1:])
     piece = lax.all_to_all(spread, "seq", 1, 1, tiled=True).reshape(2, n_seq * tok_dev, head_dim)
-    count = piece.shape[1]
-    step = math.gcd(count, tok_dev * max(1, 512 // tok_dev))
-
-    def inner(index, carry):
-        block = lax.dynamic_slice_in_dim(piece, index * step, step, 1)
-        return attend(carry, block, index * step)
-
-    state = lax.fori_loop(0, count // step, inner, initial)
-    high, total, accum = state
-    attended = (
-        (accum / jnp.transpose(total)[:, :, None])
-        .astype(jnp.bfloat16)
-        .reshape(tok_dev, per_dev * head_dim)
-    )
+    block = tok_dev
+    low = own_start[0] // block
+    bounds = jnp.stack([low, positions[-1] // block - low + 1]).astype(jnp.int32)
+    attended = attend(bounds, queries, piece, positions[:, None], own_start[:, None], block)
     rows = tok_dev // n_head
     terms = jnp.dot(attended, w_out, preferred_element_type=jnp.float32).astype(jnp.bfloat16)
     terms = lax.all_to_all(terms.reshape(n_head, rows, width), "head", 0, 0, tiled=True)

time: 250 us -> 215 us (0.86)
  blocking collectives: 68.9 us -> 53.7 us
  loops' own time: 10.7 us -> 0 us
  matrix products: 30.6 us -> 24.5 us
  Pallas kernels: 0 us -> 5.63 us
  waiting for transfers between devices: 58.5 us -> 52.9 us
  between operations: 0.34 us -> 5.32 us
  other arithmetic: 20.1 us -> 16.2 us
  local copies, waits for them, and re-layouts: 38.2 us -> 35.7 us
    all_to_all x1, blocking collectives: 68.9 us -> 53.7 us  [local(): lax.all_to_all(outgoing, ('seq', 'head'), split_axis=0, concat_axis=0, ti...]
    another operation x9 -> x0, loops' own time: 10.7 us -> none  [the longest x1 10.5 us: local(): state = lax.fori_loop(0, count // step, inner, initial)]
    all_to_all x1, waiting for transfers between devices: 14.6 us -> 7.41 us  [local(): lax.all_to_all(spread, 'seq', 1, 1, tiled=True)]
    dot_general x2 -> x0, matrix products: 6.19 us -> none  [the longest x1 3.48 us: update(): jnp.einsum('hqk,kd->qhd', weights.astype(jnp.bfloat16), block[1], preferr...]
    pallas_call x0 -> x1, Pallas kernels: none -> 5.63 us  [attend(): pl.pallas_call(kernel, grid_spec=spec, out_shape=jax.ShapeDtypeStruct((to...]
  transfers between devices with their start and end apart: 3 -> 3, of which waited for: 3 -> 3; matrix products, arithmetic and copies ran while one was open for 6% -> 8% of each run, Pallas kernels for 0% -> 0%
where the time goes in v2:
time: 215 us; the launch traced here: 213 us
  blocking collectives  53.7 us (25%)
  waiting for transfers between devices  52.9 us (25%)
  local copies, waits for them, and re-layouts  35.7 us (17%)
  matrix products  24.5 us (11%)
  starting transfers between devices  19.2 us (9%)
  other arithmetic  16.2 us (8%)
  Pallas kernels  5.63 us (3%)
  between operations  5.32 us (2%)
    all_to_all x1, blocking collectives, local(): lax.all_to_all(outgoing, ('seq', 'head'), split_axis=0, concat_axis=0, ti...  53.7 us
    all_to_all x1, waiting for transfers between devices, local(): lax.all_to_all(jnp.dot(hidden, w_down[0], preferred_element_type=jnp.floa...  29.7 us
    all_to_all x1, waiting for transfers between devices, local(): lax.all_to_all(terms.reshape(n_head, rows, width), 'head', 0, 0, tiled=True)  15.7 us
    dot_general x1, matrix products, local(): jnp.dot(hidden, w_down[0], preferred_element_type=jnp.float32)  8.23 us
    all_to_all x2, local copies, waits for them, and re-layouts, local(): lax.all_to_all(jnp.dot(hidden, w_down[0], preferred_element_type=jnp.floa...  8.08 us
    all_to_all x2, local copies, waits for them, and re-layouts, local(): lax.all_to_all(outgoing, ('seq', 'head'), split_axis=0, concat_axis=0, ti...  8.07 us
    all_to_all x1, waiting for transfers between devices, local(): lax.all_to_all(spread, 'seq', 1, 1, tiled=True)  7.41 us
    all_to_all x1, starting transfers between devices, local(): lax.all_to_all(spread, 'seq', 1, 1, tiled=True)  7.19 us
  transfers between devices with their start and end apart: 3, of which 3 were waited for; matrix products, arithmetic and copies ran while one was open for 8% of the time, Pallas kernels for 0%

profile of v2, /device:TPU:0, one launch (start us, length us, event | category | flops | bytes accessed | tf_op | source)
XLA Modules:
  0.0 213.2 jit_solution(6529242738332780672)
XLA Ops:
  0.0 0.0 copy-start
  0.0 1.7 multiply_reduce_fusion
  1.7 0.0 copy-start.4
  1.7 0.0 copy-start.5
  1.7 2.0 multiply_reduce_fusion.3
  3.7 0.0 copy-done.8
  3.7 0.2 reduce-window.18
  3.9 0.1 convert_reduce_fusion.1
  4.0 0.1 select_reduce_fusion
  4.1 1.9 fusion.12
  6.1 0.1 multiply_multiply_fusion.1
  6.2 0.3 fusion.27
  6.5 0.1 copy.74
  6.6 1.8 broadcast_in_dim.20
  8.4 7.2 %all-to-all-start = ((bf16[2,16,256,128]{3,2,0,1:T(8,128)(2,1)}), bf16[2,16,256,128]{3,2,0,1:T(8,128)(2,1)}, u32[]{:S(2)}, u32[]{:S(2)}) async-start(bf16[2,16,256,128]{3,2,0,1:T(8,128)(2,1)} %broadcast_in_dim.20), calls=%async_computation | async-start | bytes 4194304 | tf_op jit(solution)/shard_map/all_to_all | solution.py:143
  15.6 0.0 copy-start.1
  15.6 0.5 slice.24
  17.8 0.7 slice.25
  21.8 2.8 %convert_element_type.63 = f32[256,2048]{1,0:T(8,128)} convert(bf16[256,2048]{1,0:T(8,128)(2,1)} %param.15) | non-fusion elementwise | flops 524288 | bytes 3145728 | tf_op jit(solution)/shard_map/convert_element_type | solution.py:124
  24.7 0.1 copy.78
  24.7 0.1 eq.45
  24.8 0.1 eq.41
  24.9 0.1 copy.71
  25.0 0.1 copy.72
  25.1 0.0 copy-start.6
  25.1 3.5 %fusion.32 = f32[256,512]{1,0:T(8,128)} fusion(bf16[2048,512]{1,0:T(8,128)(2,1)} %param.17, f32[2048]{0:T(1024)} %param.16, f32[256]{0:T(256)} %copy-done.4, bf16[256,2048]{1,0:T(8,128)(2,1)} %param.15), kind=kOutput, calls=%fused_computation.73 | convolution fusion | flops 538968064 | bytes 3679232 | tf_op jit(solution)/shard_map/dot_general | solution.py:126
  28.6 2.0 reshape.230
  30.7 1.4 multiply_reduce_fusion.1
  32.1 0.0 copy-done.6
  32.1 1.4 multiply_multiply_fusion
  33.5 0.5 subtract_convert_fusion
  34.0 0.4 pad_maximum_fusion
  34.4 0.7 copy.87
  35.1 0.8 copy.76.qstart_ref
  35.9 0.1 copy.80
  36.0 0.7 pad_add_fusion.bounds_ref
  36.7 0.7 iota_add_fusion.qpos_ref
  37.4 0.2 fusion.22
  37.6 7.4 %all-to-all-done = bf16[2,16,256,128]{3,2,0,1:T(8,128)(2,1)} async-done(((bf16[2,16,256,128]{3,2,0,1:T(8,128)(2,1)}), bf16[2,16,256,128]{3,2,0,1:T(8,128)(2,1)}, u32[]{:S(2)}, u32[]{:S(2)}) %all-to-all-start) | async-done | bytes 2097184 | tf_op jit(solution)/shard_map/all_to_all | solution.py:143
  45.0 3.1 %copy.75 = bf16[2,16,256,128]{3,2,1,0:T(8,128)(2,1)} copy(bf16[2,16,256,128]{3,2,0,1:T(8,128)(2,1)} %all-to-all-done) | data formatting | bytes 4194304 | tf_op jit(solution)/shard_map/all_to_all | solution.py:143
  48.1 5.6 %shard_map.145 = bf16[256,512]{1,0:T(8,128)(2,1)} custom-call(s32[2]{0:T(128)} %pad_add_fusion.bounds_ref, bf16[256,512]{1,0:T(8,128)(2,1)} %bitcast.63, bf16[2,4096,128]{2,1,0:T(8,128)(2,1)} %bitcast.61, s32[256,1]{1,0:T(8,128)} %iota_add_fusion.qpos_ref, s32[256,1]{1,0:T(8,128)} %copy.76.qstart_ref), custom_call_target="tpu_custom_call" | custom-call | tf_op jit(solution)/shard_map/pallas_call | solution.py:82
  53.8 3.4 %convolution_convert_fusion = bf16[256,2048]{1,0:T(8,128)(2,1)} fusion(bf16[256,512]{1,0:T(8,128)(2,1)} %shard_map.145, bf16[512,2048]{1,0:T(8,128)(2,1)} %param.22), kind=kOutput, calls=%fused_computation.9 | convolution fusion | flops 537395200 | bytes 3407872 | tf_op jit(solution)/shard_map/dot_general | solution.py:149
  57.2 6.1 %all-to-all-start.1 = ((bf16[8,32,2048]{2,1,0:T(8,128)(2,1)}), bf16[8,32,2048]{2,1,0:T(8,128)(2,1)}, u32[]{:S(2)}, u32[]{:S(2)}) async-start(bf16[8,32,2048]{2,1,0:T(8,128)(2,1)} %bitcast.62), calls=%async_computation.1 | async-start | bytes 2097152 | tf_op jit(solution)/shard_map/all_to_all | solution.py:150
  63.4 0.1 copy.77
  63.5 0.1 mul.219
  63.6 0.2 fusion.24
  63.8 15.7 %all-to-all-done.1 = bf16[8,32,2048]{2,1,0:T(8,128)(2,1)} async-done(((bf16[8,32,2048]{2,1,0:T(8,128)(2,1)}), bf16[8,32,2048]{2,1,0:T(8,128)(2,1)}, u32[]{:S(2)}, u32[]{:S(2)}) %all-to-all-start.1) | async-done | bytes 1048608 | tf_op jit(solution)/shard_map/all_to_all | solution.py:150
  79.5 1.4 convert_reduce_fusion
  80.9 1.1 multiply_reduce_fusion.2
  82.0 0.1 multiply_convert_fusion.2
  82.1 3.7 %scatter_custom_fusion = bf16[512,2048]{1,0:T(8,128)(2,1)} fusion(s32[256]{0:T(256)S(1)} %bitcast.70, bf16[]{:T(256)} %constant.90.clone.1, bf16[32,2048]{1,0:T(8,128)(2,1)S(1)} %multiply_convert_fusion.2), kind=kCustom, calls=%fused_computation.18 | custom fusion | bytes 2228226 | tf_op jit(solution)/shard_map/scatter | solution.py:163
  85.8 4.1 %all_to_all.24 = bf16[128,4,2048]{2,1,0:T(4,128)(2,1)} reshape(bf16[512,2048]{1,0:T(8,128)(2,1)} %scatter_custom_fusion) | data formatting | bytes 4194304 | tf_op jit(solution)/shard_map/all_to_all | solution.py:165
  89.9 53.7 %all_to_all.34 = bf16[128,4,2048]{2,1,0:T(4,128)(2,1)} all-to-all(bf16[128,4,2048]{2,1,0:T(4,128)(2,1)} %all_to_all.24), channel_id=1, replica_groups=mesh['seq'=16,'head'=8] {'seq','head'}, dimensions={0} | all-to-all | bytes 4194304 | tf_op jit(solution)/shard_map/all_to_all | solution.py:165
  143.6 4.0 %all_to_all.26 = bf16[512,2048]{1,0:T(8,128)(2,1)} reshape(bf16[128,4,2048]{2,1,0:T(4,128)(2,1)} %all_to_all.34) | data formatting | bytes 4194304 | tf_op jit(solution)/shard_map/all_to_all | solution.py:165
  147.5 5.5 %fusion.4 = f32[512,768]{1,0:T(8,128)} fusion(bf16[512,2048]{1,0:T(8,128)(2,1)} %all_to_all.26, bf16[1,2048,768]{2,1,0:T(8,128)(2,1)} %param.27), kind=kOutput, calls=%fused_computation.6 | convolution fusion | flops 1610612736 | bytes 6815744 | tf_op jit(solution)/shard_map/dot_general | solution.py:166
  153.0 8.2 %fusion.6 = bf16[512,2048]{1,0:T(8,128)(2,1)} fusion(bf16[1,768,2048]{2,1,0:T(8,128)(2,1)S(1)} %copy-done, f32[512,768]{1,0:T(8,128)} %fusion.4, bf16[512,2048]{1,0:T(8,128)(2,1)} %all_to_all.26, bf16[1,2048,768]{2,1,0:T(8,128)(2,1)} %param.28), kind=kOutput, calls=%fused_computation.8 | convolution fusion | flops 3224633344 | bytes 12058624 | tf_op jit(solution)/shard_map/dot_general | solution.py:170
  161.2 4.1 %all_to_all.27 = bf16[128,4,2048]{2,1,0:T(4,128)(2,1)} reshape(bf16[512,2048]{1,0:T(8,128)(2,1)} %fusion.6) | data formatting | bytes 4194304 | tf_op jit(solution)/shard_map/all_to_all | solution.py:169
  165.3 5.9 %all-to-all-start.3 = ((bf16[128,4,2048]{2,1,0:T(4,128)(2,1)}), bf16[128,4,2048]{2,1,0:T(4,128)(2,1)}, u32[]{:S(2)}, u32[]{:S(2)}) async-start(bf16[128,4,2048]{2,1,0:T(4,128)(2,1)} %all_to_all.27), calls=%async_computation.3 | async-start | bytes 4194304 | tf_op jit(solution)/shard_map/all_to_all | solution.py:169
  171.3 0.1 copy.82
  171.3 29.7 %all-to-all-done.3 = bf16[128,4,2048]{2,1,0:T(4,128)(2,1)} async-done(((bf16[128,4,2048]{2,1,0:T(4,128)(2,1)}), bf16[128,4,2048]{2,1,0:T(4,128)(2,1)}, u32[]{:S(2)}, u32[]{:S(2)}) %all-to-all-start.3) | async-done | bytes 2097184 | tf_op jit(solution)/shard_map/all_to_all | solution.py:169
  201.1 4.0 %all_to_all.29 = bf16[512,2048]{1,0:T(8,128)(2,1)} reshape(bf16[128,4,2048]{2,1,0:T(4,128)(2,1)} %all-to-all-done.3) | data formatting | bytes 4194304 | tf_op jit(solution)/shard_map/all_to_all | solution.py:169
  205.0 5.2 %gather_fusion = bf16[256,2048]{1,0:T(8,128)(2,1)} fusion(bf16[512,2048]{1,0:T(8,128)(2,1)} %all_to_all.29, s32[1024]{0:T(1024)S(1)} %pad_clamp_fusion), kind=kCustom, calls=%fused_computation | custom fusion | bytes 2098176 | tf_op jit(solution)/shard_map/gather | solution.py:177
  210.3 2.2 %fusion.9 = f32[32,2048]{1,0:T(8,128)S(1)} fusion(bf16[256,2048]{1,0:T(8,128)(2,1)} %gather_fusion, f32[32,8]{1,0:T(8,128)S(1)} %copy.82), kind=kLoop, calls=%fused_computation.11 | loop fusion | flops 1507328 | bytes 1311744 | tf_op jit(solution)/shard_map/reduce_sum | solution.py:178
  212.5 0.7 add_convert_fusion.1
  (29 shorter events, 0.2 us)
Async XLA Ops:
  0.0 153.0 %copy-start = (bf16[1,768,2048]{2,1,0:T(8,128)(2,1)S(1)}, bf16[1,768,2048]{2,1,0:T(8,128)(2,1)}, u32[]{:S(2)}) copy-start(bf16[1,768,2048]{2,1,0:T(8,128)(2,1)} %param.29) | copy-start | bytes 9437188
  0.0 4.1 %copy-start.7 = (f32[2048]{0:T(1024)S(1)}, f32[2048]{0:T(1024)}, u32[]{:S(2)}) copy-start(f32[2048]{0:T(1024)} %param.16) | copy-start | bytes 24580
  0.0 3.7 %copy-start.8 = (s32[6]{0:T(128)S(1)}, s32[6]{0:T(128)}, u32[]{:S(2)}) copy-start(s32[6]{0:T(128)} %param.24) | copy-start | bytes 76
  1.7 4.4 %copy-start.4 = (f32[256]{0:T(256)}, f32[256]{0:T(256)S(1)}, u32[]{:S(2)}) copy-start(f32[256]{0:T(256)S(1)} %add_rsqrt_fusion.2) | copy-start | bytes 3076
  1.7 4.3 %copy-start.5 = (f32[128]{0:T(128)S(1)}, f32[128]{0:T(128)}, u32[]{:S(2)}) copy-start(f32[128]{0:T(128)} %param.21) | copy-start | bytes 1540
  8.4 36.5 %all-to-all-start = ((bf16[2,16,256,128]{3,2,0,1:T(8,128)(2,1)}), bf16[2,16,256,128]{3,2,0,1:T(8,128)(2,1)}, u32[]{:S(2)}, u32[]{:S(2)}) async-start(bf16[2,16,256,128]{3,2,0,1:T(8,128)(2,1)} %broadcast_in_dim.20), calls=%async_computation | async-start | bytes 4194304 | tf_op jit(solution)/shard_map/all_to_all | solution.py:143
  15.6 9.0 %copy-start.1 = (s32[32,8]{0,1:T(8,128)S(1)}, s32[32,8]{0,1:T(8,128)}, u32[]{:S(2)}) copy-start(s32[32,8]{0,1:T(8,128)} %param.25) | copy-start | bytes 3076
  25.1 7.0 %copy-start.6 = (f32[128]{0:T(128)S(1)}, f32[128]{0:T(128)}, u32[]{:S(2)}) copy-start(f32[128]{0:T(128)} %param.20) | copy-start | bytes 1540
  57.2 24.8 %copy-start.2 = (f32[2048]{0:T(1024)S(1)}, f32[2048]{0:T(1024)}, u32[]{:S(2)}) copy-start(f32[2048]{0:T(1024)} %param.23) | copy-start | bytes 24580
  57.2 22.3 %all-to-all-start.1 = ((bf16[8,32,2048]{2,1,0:T(8,128)(2,1)}), bf16[8,32,2048]{2,1,0:T(8,128)(2,1)}, u32[]{:S(2)}, u32[]{:S(2)}) async-start(bf16[8,32,2048]{2,1,0:T(8,128)(2,1)} %bitcast.62), calls=%async_computation.1 | async-start | bytes 2097152 | tf_op jit(solution)/shard_map/all_to_all | solution.py:150
  165.3 5.9 %copy-start.3 = (f32[32,8]{0,1:T(8,128)S(1)}, f32[32,8]{0,1:T(8,128)}, u32[]{:S(2)}) copy-start(f32[32,8]{0,1:T(8,128)} %param.26) | copy-start | bytes 3076
  165.3 35.7 %all-to-all-start.3 = ((bf16[128,4,2048]{2,1,0:T(4,128)(2,1)}), bf16[128,4,2048]{2,1,0:T(4,128)(2,1)}, u32[]{:S(2)}, u32[]{:S(2)}) async-start(bf16[128,4,2048]{2,1,0:T(4,128)(2,1)} %all_to_all.27), calls=%async_computation.3 | async-start | bytes 4194304 | tf_op jit(solution)/shard_map/all_to_all | solution.py:169

commit v3 on v2

--- a/solution.py
+++ b/solution.py
@@ -149,33 +149,39 @@
     terms = jnp.dot(attended, w_out, preferred_element_type=jnp.float32).astype(jnp.bfloat16)
     terms = lax.all_to_all(terms.reshape(n_head, rows, width), "head", 0, 0, tiled=True)
     attn_rows = jnp.sum(terms.astype(jnp.float32), axis=0)
-    resid = lax.dynamic_slice_in_dim(inputs, head_index * rows, rows, 0) + attn_rows
+    resid = lax.dynamic_slice_in_dim(tokens, head_index * rows, rows, 0).astype(jnp.float32) + attn_rows
     routed = rms_scale(resid, post_gain).astype(jnp.bfloat16)
     experts = n_seq * n_head * w_gate.shape[0]
     capacity = 2 * TOP * rows // experts
     chosen = expert_ids.reshape(-1)
     hits = (chosen[:, None] == jnp.arange(experts, dtype=jnp.int32)[None, :]).astype(jnp.int32)
     rank = jnp.sum((jnp.cumsum(hits, axis=0) - hits) * hits, axis=1)
-    target = chosen * capacity + rank
-    outgoing = (
-        jnp.zeros((experts * capacity, width), jnp.bfloat16)
-        .at[target]
-        .set(jnp.repeat(routed, TOP, axis=0))
-    )
-    flat = lax.all_to_all(outgoing, ("seq", "head"), split_axis=0, concat_axis=0, tiled=True)
+    slot = rank * experts + chosen
+    select = (slot[:, None] == jnp.arange(capacity * experts, dtype=jnp.int32)[None, :]).reshape(
+        rows, TOP, capacity * experts
+    )
+    sources = jnp.transpose(jnp.any(select, axis=1)).astype(jnp.bfloat16)
+    outgoing = jnp.dot(sources, routed, preferred_element_type=jnp.float32).astype(jnp.bfloat16)
+    outgoing = outgoing.reshape(capacity, experts, width)
+    block = lax.all_to_all(outgoing, ("seq", "head"), split_axis=1, concat_axis=1, tiled=True)
+    flat = block.reshape(-1, width)
     gate = jnp.dot(flat, w_gate[0], preferred_element_type=jnp.float32)
     up = jnp.dot(flat, w_up[0], preferred_element_type=jnp.float32)
     hidden = (jax.nn.silu(gate) * up).astype(jnp.bfloat16)
     returned = lax.all_to_all(
         jnp.dot(hidden, w_down[0], preferred_element_type=jnp.float32)
-        .astype(jnp.bfloat16),
+        .astype(jnp.bfloat16)
+        .reshape(block.shape),
         ("seq", "head"),
-        split_axis=0,
-        concat_axis=0,
+        split_axis=1,
+        concat_axis=1,
         tiled=True,
-    )
-    picked = returned.reshape(experts * capacity, width)[target].reshape(rows, TOP, width)
-    combined = jnp.sum(picked.astype(jnp.float32) * route_weights[:, :, None], axis=1)
+    ).reshape(-1, width)
+    mixing = jnp.sum(jnp.where(select, route_weights[:, :, None], 0.0), axis=1)
+    combined = jnp.dot(
+        mixing, returned.astype(jnp.float32), precision=lax.Precision.HIGHEST,
+        preferred_element_type=jnp.float32,
+    )
     return (resid + combined).astype(jnp.bfloat16)
 
 

time: 215 us -> 197 us (0.916)
  local copies, waits for them, and re-layouts: 35.7 us -> 22.9 us
  other arithmetic: 16.2 us -> 10.7 us
    all_to_all x2 -> x1, local copies, waits for them, and re-layouts: 8.07 us -> 1.15 us  [local(): lax.all_to_all(outgoing, ('seq', 'head'), split_axis=1, concat_axis=1, ti...]
    reshape x0 -> x2, local copies, waits for them, and re-layouts: none -> 6.13 us  [the longest x1 4.5 us: local(): returned = lax.all_to_all(jnp.dot(hidden, w_down[0], preferred_element_ty...]
    all_to_all x2 -> x1, local copies, waits for them, and re-layouts: 8.08 us -> 2.74 us  [local(): lax.all_to_all(jnp.dot(hidden, w_down[0], preferred_element_type=jnp.floa...]
    gather x1 -> x0, local copies, waits for them, and re-layouts: 5.21 us -> none  [local(): returned.reshape(experts * capacity, width)[target]]
    dot_general x0 -> x2, matrix products: none -> 4.36 us  [the longest x1 2.68 us: local(): jnp.dot(mixing, returned.astype(jnp.float32), precision=lax.Precision.HIG...]
    scatter x1 -> x0, local copies, waits for them, and re-layouts: 3.69 us -> none  [local(): outgoing = jnp.zeros((experts * capacity, width), jnp.bfloat16).at[target...]
    convert_element_type x3 -> x0, other arithmetic: 3.61 us -> none  [the longest x1 2.82 us: local(): inputs = tokens.astype(jnp.float32)]
    dot_general x1, matrix products: 5.48 us -> 2.98 us  [local(): gate = jnp.dot(flat, w_gate[0], preferred_element_type=jnp.float32)]
where the time goes in v3:
time: 197 us; the launch traced here: 196 us
  waiting for transfers between devices  54.3 us (28%)
  blocking collectives  51.6 us (26%)
  matrix products  26.4 us (13%)
  local copies, waits for them, and re-layouts  22.9 us (12%)
  starting transfers between devices  19.3 us (10%)
  other arithmetic  10.7 us (5%)
  Pallas kernels  5.62 us (3%)
  between operations  5.43 us (3%)
    all_to_all x1, blocking collectives, local(): lax.all_to_all(outgoing, ('seq', 'head'), split_axis=1, concat_axis=1, ti...  51.6 us
    all_to_all x1, waiting for transfers between devices, local(): lax.all_to_all(jnp.dot(hidden, w_down[0], preferred_element_type=jnp.floa...  29.5 us
    all_to_all x1, waiting for transfers between devices, local(): lax.all_to_all(terms.reshape(n_head, rows, width), 'head', 0, 0, tiled=True)  15.5 us
    all_to_all x1, waiting for transfers between devices, local(): lax.all_to_all(spread, 'seq', 1, 1, tiled=True)  9.2 us
    dot_general x1, matrix products, local(): jnp.dot(hidden, w_down[0], preferred_element_type=jnp.float32)  8.29 us
    all_to_all x1, starting transfers between devices, local(): lax.all_to_all(spread, 'seq', 1, 1, tiled=True)  7.31 us
    all_to_all x1, starting transfers between devices, local(): lax.all_to_all(terms.reshape(n_head, rows, width), 'head', 0, 0, tiled=True)  6.13 us
    all_to_all x1, starting transfers between devices, local(): lax.all_to_all(jnp.dot(hidden, w_down[0], preferred_element_type=jnp.floa...  5.91 us
  transfers between devices with their start and end apart: 3, of which 3 were waited for; matrix products, arithmetic and copies ran while one was open for 8% of the time, Pallas kernels for 0%

profile of v3, /device:TPU:0, one launch (start us, length us, event | category | flops | bytes accessed | tf_op | source)
XLA Modules:
  0.0 196.3 jit_solution(10200298767129621443)
XLA Ops:
  0.0 0.0 copy-start
  0.0 1.7 fusion.10
  1.7 0.0 copy-start.10
  1.7 2.0 %multiply_reduce_fusion.2 = (f32[256]{0:T(256)S(1)}, f32[256,128]{0,1:T(8,128)S(1)}) fusion(bf16[2048,512]{1,0:T(8,128)(2,1)} %param.18, s32[]{:T(128)S(6)} %select_n.31, bf16[256,2048]{1,0:T(8,128)(2,1)} %param.15, f32[2048]{0:T(1024)} %param.16, f32[256]{0:T(256)S(1)} %add_rsqrt_fusion.2), kind=kOutput, calls=%fused_computation.48 | convolution fusion | flops 136380160 | bytes 1714180 | tf_op jit(solution)/shard_map/dot_general | solution.py:136
  3.7 0.2 reduce-window.18
  3.9 0.1 convert_reduce_fusion.1
  4.0 0.1 select_reduce_fusion.1
  4.1 1.9 fusion.15
  6.1 0.0 copy-done.9
  6.1 0.0 copy-done.10
  6.1 0.1 multiply_multiply_fusion.1
  6.2 0.3 fusion.29
  6.5 0.1 copy.101
  6.6 1.8 broadcast_in_dim.24
  8.4 7.3 %all-to-all-start = ((bf16[2,16,256,128]{3,2,0,1:T(8,128)(2,1)}), bf16[2,16,256,128]{3,2,0,1:T(8,128)(2,1)}, u32[]{:S(2)}, u32[]{:S(2)}) async-start(bf16[2,16,256,128]{3,2,0,1:T(8,128)(2,1)} %broadcast_in_dim.24), calls=%async_computation | async-start | bytes 4194304 | tf_op jit(solution)/shard_map/all_to_all | solution.py:143
  15.7 0.5 slice.24
  18.1 0.6 slice.25
  21.9 0.1 copy.104
  22.0 0.7 eq.59
  22.7 0.7 eq.55
  23.3 0.1 copy.98
  23.4 0.1 copy.99
  23.5 0.0 copy-start.11
  23.5 3.5 %fusion.37 = f32[256,512]{1,0:T(8,128)} fusion(bf16[2048,512]{1,0:T(8,128)(2,1)} %param.17, bf16[256,2048]{1,0:T(8,128)(2,1)} %param.15, f32[2048]{0:T(1024)} %param.16, f32[256]{0:T(256)} %copy-done.9), kind=kOutput, calls=%fused_computation.74 | convolution fusion | flops 538968064 | bytes 3679232 | tf_op jit(solution)/shard_map/dot_general | solution.py:126
  27.0 2.0 %reshape.223 = f32[256,4,128]{2,1,0:T(4,128)} reshape(f32[256,512]{1,0:T(8,128)} %fusion.37) | data formatting | bytes 1048576 | tf_op jit(solution)/shard_map/reshape | solution.py:126
  29.1 1.4 multiply_reduce_fusion
  30.5 0.0 copy-start.6
  30.5 1.4 multiply_multiply_fusion
  31.9 0.5 subtract_convert_fusion
  32.4 0.4 pad_maximum_fusion
  32.8 0.7 copy.118
  33.5 0.8 copy.103.qstart_ref
  34.3 0.0 copy-done.6
  34.3 0.1 copy.106
  34.4 0.6 pad_add_fusion.bounds_ref
  35.0 0.7 iota_add_fusion.qpos_ref
  35.7 0.2 fusion.22
  35.9 9.2 %all-to-all-done = bf16[2,16,256,128]{3,2,0,1:T(8,128)(2,1)} async-done(((bf16[2,16,256,128]{3,2,0,1:T(8,128)(2,1)}), bf16[2,16,256,128]{3,2,0,1:T(8,128)(2,1)}, u32[]{:S(2)}, u32[]{:S(2)}) %all-to-all-start) | async-done | bytes 2097184 | tf_op jit(solution)/shard_map/all_to_all | solution.py:143
  45.1 3.1 %copy.102 = bf16[2,16,256,128]{3,2,1,0:T(8,128)(2,1)} copy(bf16[2,16,256,128]{3,2,0,1:T(8,128)(2,1)} %all-to-all-done) | data formatting | bytes 4194304 | tf_op jit(solution)/shard_map/all_to_all | solution.py:143
  48.2 5.6 %shard_map.145 = bf16[256,512]{1,0:T(8,128)(2,1)} custom-call(s32[2]{0:T(128)} %pad_add_fusion.bounds_ref, bf16[256,512]{1,0:T(8,128)(2,1)} %bitcast.67, bf16[2,4096,128]{2,1,0:T(8,128)(2,1)} %bitcast.60, s32[256,1]{1,0:T(8,128)} %iota_add_fusion.qpos_ref, s32[256,1]{1,0:T(8,128)} %copy.103.qstart_ref), custom_call_target="tpu_custom_call" | custom-call | tf_op jit(solution)/shard_map/pallas_call | solution.py:82
  53.8 3.4 %convolution_convert_fusion.1 = bf16[256,2048]{1,0:T(8,128)(2,1)} fusion(bf16[256,512]{1,0:T(8,128)(2,1)} %shard_map.145, bf16[512,2048]{1,0:T(8,128)(2,1)} %param.22), kind=kOutput, calls=%fused_computation.10 | convolution fusion | flops 537395200 | bytes 3407872 | tf_op jit(solution)/shard_map/dot_general | solution.py:149
  57.2 6.1 %all-to-all-start.1 = ((bf16[8,32,2048]{2,1,0:T(8,128)(2,1)}), bf16[8,32,2048]{2,1,0:T(8,128)(2,1)}, u32[]{:S(2)}, u32[]{:S(2)}) async-start(bf16[8,32,2048]{2,1,0:T(8,128)(2,1)} %bitcast.63), calls=%async_computation.1 | async-start | bytes 2097152 | tf_op jit(solution)/shard_map/all_to_all | solution.py:150
  63.4 0.0 copy-done.5
  63.5 0.2 fusion.24
  63.6 0.1 mul.209
  63.7 0.2 fusion.18
  64.0 15.5 %all-to-all-done.1 = bf16[8,32,2048]{2,1,0:T(8,128)(2,1)} async-done(((bf16[8,32,2048]{2,1,0:T(8,128)(2,1)}), bf16[8,32,2048]{2,1,0:T(8,128)(2,1)}, u32[]{:S(2)}, u32[]{:S(2)}) %all-to-all-start.1) | async-done | bytes 1048608 | tf_op jit(solution)/shard_map/all_to_all | solution.py:150
  79.5 1.4 convert_reduce_fusion
  80.9 1.1 multiply_reduce_fusion.1
  82.0 1.7 convolution_convert_fusion
  83.7 1.6 copy.110
  85.3 51.6 %all_to_all.20 = bf16[4,128,2048]{2,0,1:T(4,128)(2,1)S(1)} all-to-all(bf16[4,128,2048]{2,0,1:T(4,128)(2,1)S(1)} %copy.110), channel_id=1, replica_groups=mesh['seq'=16,'head'=8] {'seq','head'}, dimensions={1} | all-to-all | bytes 4194304 | tf_op jit(solution)/shard_map/all_to_all | solution.py:166
  136.9 1.2 copy.111
  138.0 1.3 copy-done.1
  139.3 0.0 copy-done.12
  139.3 3.0 %fusion.4 = f32[512,768]{1,0:T(8,128)} fusion(bf16[512,2048]{1,0:T(8,128)(2,1)S(1)} %bitcast.64, bf16[1,2048,768]{2,1,0:T(8,128)(2,1)S(1)} %copy-done.12), kind=kOutput, calls=%fused_computation.4 | convolution fusion | flops 1610612736 | bytes 6815744 | tf_op jit(solution)/shard_map/dot_general | solution.py:168
  142.3 8.3 %fusion.6 = bf16[512,2048]{1,0:T(8,128)(2,1)} fusion(bf16[1,768,2048]{2,1,0:T(8,128)(2,1)S(1)} %copy-done, f32[512,768]{1,0:T(8,128)} %fusion.4, bf16[512,2048]{1,0:T(8,128)(2,1)} %bitcast.65, bf16[1,2048,768]{2,1,0:T(8,128)(2,1)} %param.28), kind=kOutput, calls=%fused_computation.6 | convolution fusion | flops 3224633344 | bytes 12058624 | tf_op jit(solution)/shard_map/dot_general | solution.py:172
  150.6 4.5 %copy.112 = bf16[4,128,2048]{2,0,1:T(4,128)(2,1)} copy(bf16[4,128,2048]{2,1,0:T(8,128)(2,1)} %bitcast.66) | data formatting | bytes 4194304 | tf_op jit(solution)/shard_map/reshape | solution.py:174
  155.1 5.9 %all-to-all-start.3 = ((bf16[4,128,2048]{2,0,1:T(4,128)(2,1)}), bf16[4,128,2048]{2,0,1:T(4,128)(2,1)}, u32[]{:S(2)}, u32[]{:S(2)}) async-start(bf16[4,128,2048]{2,0,1:T(4,128)(2,1)} %copy.112), calls=%async_computation.3 | async-start | bytes 4194304 | tf_op jit(solution)/shard_map/all_to_all | solution.py:171
  161.0 0.1 copy.109
  161.1 0.2 select_reduce_fusion
  161.3 29.5 %all-to-all-done.3 = bf16[4,128,2048]{2,0,1:T(4,128)(2,1)} async-done(((bf16[4,128,2048]{2,0,1:T(4,128)(2,1)}), bf16[4,128,2048]{2,0,1:T(4,128)(2,1)}, u32[]{:S(2)}, u32[]{:S(2)}) %all-to-all-start.3) | async-done | bytes 2097184 | tf_op jit(solution)/shard_map/all_to_all | solution.py:171
  190.9 2.7 %copy.113 = bf16[4,128,2048]{2,1,0:T(8,128)(2,1)S(1)} copy(bf16[4,128,2048]{2,0,1:T(4,128)(2,1)} %all-to-all-done.3) | data formatting | bytes 4194304 | tf_op jit(solution)/shard_map/all_to_all | solution.py:171
  193.6 2.7 %fusion.9 = bf16[32,2048]{1,0:T(8,128)(2,1)} fusion(f32[32,512]{1,0:T(8,128)S(1)} %select_reduce_fusion, bf16[512,2048]{1,0:T(8,128)(2,1)S(1)} %bitcast.61, f32[32,2048]{1,0:T(8,128)S(1)} %convert_reduce_fusion, bf16[256,2048]{1,0:T(8,128)(2,1)} %param.15, s32[]{:T(128)S(6)} %select_n.26), kind=kOutput, calls=%fused_computation.12 | convolution fusion | flops 402915328 | bytes 2686980 | tf_op jit(solution)/shard_map/dot_general | solution.py:181
  (37 shorter events, 0.2 us)
Async XLA Ops:
  0.0 142.3 %copy-start = (bf16[1,768,2048]{2,1,0:T(8,128)(2,1)S(1)}, bf16[1,768,2048]{2,1,0:T(8,128)(2,1)}, u32[]{:S(2)}) copy-start(bf16[1,768,2048]{2,1,0:T(8,128)(2,1)} %param.29) | copy-start | bytes 9437188
  0.0 4.1 %copy-start.13 = (f32[2048]{0:T(1024)S(1)}, f32[2048]{0:T(1024)}, u32[]{:S(2)}) copy-start(f32[2048]{0:T(1024)} %param.16) | copy-start | bytes 24580
  0.0 3.7 %copy-start.14 = (s32[6]{0:T(128)S(1)}, s32[6]{0:T(128)}, u32[]{:S(2)}) copy-start(s32[6]{0:T(128)} %param.24) | copy-start | bytes 76
  1.7 4.4 %copy-start.9 = (f32[256]{0:T(256)}, f32[256]{0:T(256)S(1)}, u32[]{:S(2)}) copy-start(f32[256]{0:T(256)S(1)} %add_rsqrt_fusion.2) | copy-start | bytes 3076
  1.7 4.4 %copy-start.10 = (f32[128]{0:T(128)S(1)}, f32[128]{0:T(128)}, u32[]{:S(2)}) copy-start(f32[128]{0:T(128)} %param.21) | copy-start | bytes 1540
  4.1 11.6 %copy-start.2 = (s32[256]{0:T(256)}, s32[256]{0:T(256)S(1)}, u32[]{:S(2)}) copy-start(s32[256]{0:T(256)S(1)} %select_reduce_fusion.1) | copy-start | bytes 3076
  8.4 13.5 %copy-start.7 = (s32[32,8]{0,1:T(8,128)S(1)}, s32[32,8]{0,1:T(8,128)}, u32[]{:S(2)}) copy-start(s32[32,8]{0,1:T(8,128)} %param.25) | copy-start | bytes 3076
  8.4 36.7 %all-to-all-start = ((bf16[2,16,256,128]{3,2,0,1:T(8,128)(2,1)}), bf16[2,16,256,128]{3,2,0,1:T(8,128)(2,1)}, u32[]{:S(2)}, u32[]{:S(2)}) async-start(bf16[2,16,256,128]{3,2,0,1:T(8,128)(2,1)} %broadcast_in_dim.24), calls=%async_computation | async-start | bytes 4194304 | tf_op jit(solution)/shard_map/all_to_all | solution.py:143
  23.5 7.0 %copy-start.11 = (f32[128]{0:T(128)S(1)}, f32[128]{0:T(128)}, u32[]{:S(2)}) copy-start(f32[128]{0:T(128)} %param.20) | copy-start | bytes 1540
  30.5 3.0 %copy-start.3 = (s32[256]{0:T(256)S(1)}, s32[256]{0:T(256)}, u32[]{:S(2)}) copy-start(s32[256]{0:T(256)} %copy-done.2) | copy-start | bytes 3076
  30.5 3.8 %copy-start.6 = (s32[2,128]{1,0:T(2,128)S(1)}, s32[2,128]{1,0:T(2,128)}, u32[]{:S(2)}) copy-start(s32[2,128]{1,0:T(2,128)} %eq.59) | copy-start | bytes 3076
  57.2 6.2 %copy-start.5 = (s32[256]{0:T(256)S(1)}, s32[256]{0:T(256)}, u32[]{:S(2)}) copy-start(s32[256]{0:T(256)} %eq.55) | copy-start | bytes 3076
  57.2 24.8 %copy-start.4 = (f32[2048]{0:T(1024)S(1)}, f32[2048]{0:T(1024)}, u32[]{:S(2)}) copy-start(f32[2048]{0:T(1024)} %param.23) | copy-start | bytes 24580
  57.2 22.3 %all-to-all-start.1 = ((bf16[8,32,2048]{2,1,0:T(8,128)(2,1)}), bf16[8,32,2048]{2,1,0:T(8,128)(2,1)}, u32[]{:S(2)}, u32[]{:S(2)}) async-start(bf16[8,32,2048]{2,1,0:T(8,128)(2,1)} %bitcast.63), calls=%async_computation.1 | async-start | bytes 2097152 | tf_op jit(solution)/shard_map/all_to_all | solution.py:150
  136.9 2.5 %copy-start.12 = (bf16[1,2048,768]{2,1,0:T(8,128)(2,1)S(1)}, bf16[1,2048,768]{2,1,0:T(8,128)(2,1)}, u32[]{:S(2)}) copy-start(bf16[1,2048,768]{2,1,0:T(8,128)(2,1)} %param.27) | copy-start | bytes 9437188
  138.0 1.3 copy-start.1
  155.1 5.9 %copy-start.8 = (f32[32,8]{0,1:T(8,128)S(1)}, f32[32,8]{0,1:T(8,128)}, u32[]{:S(2)}) copy-start(f32[32,8]{0,1:T(8,128)} %param.26) | copy-start | bytes 3076
  155.1 35.7 %all-to-all-start.3 = ((bf16[4,128,2048]{2,0,1:T(4,128)(2,1)}), bf16[4,128,2048]{2,0,1:T(4,128)(2,1)}, u32[]{:S(2)}, u32[]{:S(2)}) async-start(bf16[4,128,2048]{2,0,1:T(4,128)(2,1)} %copy.112), calls=%async_computation.3 | async-start | bytes 4194304 | tf_op jit(solution)/shard_map/all_to_all | solution.py:171

commit v4 on v3

--- a/solution.py
+++ b/solution.py
@@ -163,20 +163,21 @@
     sources = jnp.transpose(jnp.any(select, axis=1)).astype(jnp.bfloat16)
     outgoing = jnp.dot(sources, routed, preferred_element_type=jnp.float32).astype(jnp.bfloat16)
     outgoing = outgoing.reshape(capacity, experts, width)
-    block = lax.all_to_all(outgoing, ("seq", "head"), split_axis=1, concat_axis=1, tiled=True)
-    flat = block.reshape(-1, width)
-    gate = jnp.dot(flat, w_gate[0], preferred_element_type=jnp.float32)
-    up = jnp.dot(flat, w_up[0], preferred_element_type=jnp.float32)
-    hidden = (jax.nn.silu(gate) * up).astype(jnp.bfloat16)
-    returned = lax.all_to_all(
-        jnp.dot(hidden, w_down[0], preferred_element_type=jnp.float32)
-        .astype(jnp.bfloat16)
-        .reshape(block.shape),
-        ("seq", "head"),
-        split_axis=1,
-        concat_axis=1,
-        tiled=True,
-    ).reshape(-1, width)
+    half = capacity // 2
+    results = []
+    for part in (outgoing[:half], outgoing[half:]):
+        block = lax.all_to_all(part, ("seq", "head"), split_axis=1, concat_axis=1, tiled=True)
+        flat = block.reshape(-1, width)
+        gate = jnp.dot(flat, w_gate[0], preferred_element_type=jnp.float32)
+        up = jnp.dot(flat, w_up[0], preferred_element_type=jnp.float32)
+        hidden = (jax.nn.silu(gate) * up).astype(jnp.bfloat16)
+        down = jnp.dot(hidden, w_down[0], preferred_element_type=jnp.float32).astype(jnp.bfloat16)
+        results.append(
+            lax.all_to_all(
+                down.reshape(block.shape), ("seq", "head"), split_axis=1, concat_axis=1, tiled=True
+            )
+        )
+    returned = jnp.concatenate(results, axis=0).reshape(-1, width)
     mixing = jnp.sum(jnp.where(select, route_weights[:, :, None], 0.0), axis=1)
     combined = jnp.dot(
         mixing, returned.astype(jnp.float32), precision=lax.Precision.HIGHEST,

time: 197 us -> 209 us (1.061)
  blocking collectives: 51.6 us -> 0 us
  starting transfers between devices: 19.3 us -> 53.9 us
  local copies, waits for them, and re-layouts: 22.9 us -> 34.1 us
  waiting for transfers between devices: 54.3 us -> 63.2 us
  matrix products: 26.4 us -> 33.6 us
    all_to_all x1 -> x0, blocking collectives: 51.6 us -> none  [local(): lax.all_to_all(outgoing, ('seq', 'head'), split_axis=1, concat_axis=1, ti...]
    all_to_all x1 -> x4, starting transfers between devices: 5.91 us -> 40.4 us  [the longest x2 27.2 us: local(): lax.all_to_all(part, ('seq', 'head'), split_axis=1, concat_axis=1, tiled=...]
    all_to_all x1 -> x4, waiting for transfers between devices: 29.5 us -> 38.4 us  [the longest x2 19.6 us: local(): lax.all_to_all(down.reshape(block.shape), ('seq', 'head'), split_axis=1,...]
    slice x0 -> x3, local copies, waits for them, and re-layouts: none -> 6.53 us  [the longest x1 3.29 us: local(): outgoing[half:]]
    dot_general x1 -> x2, matrix products: 2.98 us -> 7.49 us  [local(): gate = jnp.dot(flat, w_gate[0], preferred_element_type=jnp.float32)]
    all_to_all x2 -> x4, local copies, waits for them, and re-layouts: 3.9 us -> 7.37 us  [the longest x2 4.22 us: local(): lax.all_to_all(down.reshape(block.shape), ('seq', 'head'), split_axis=1,...]
    dot_general x1 -> x2, matrix products: 8.29 us -> 11 us  [local(): jnp.dot(hidden, w_down[0], preferred_element_type=jnp.float32)]
  transfers between devices with their start and end apart: 3 -> 6, of which waited for: 3 -> 6; matrix products, arithmetic and copies ran while one was open for 8% -> 24% of each run, Pallas kernels for 0% -> 0%
where the time goes in v4:
time: 209 us; the launch traced here: 207 us
  waiting for transfers between devices  63.2 us (30%)
  starting transfers between devices  53.9 us (26%)
  local copies, waits for them, and re-layouts  34.1 us (16%)
  matrix products  33.6 us (16%)
  other arithmetic  10.9 us (5%)
  Pallas kernels  5.62 us (3%)
  between operations  5.49 us (3%)
    all_to_all x2, starting transfers between devices, local(): lax.all_to_all(part, ('seq', 'head'), split_axis=1, concat_axis=1, tiled=...  27.2 us
    all_to_all x2, waiting for transfers between devices, local(): lax.all_to_all(down.reshape(block.shape), ('seq', 'head'), split_axis=1,...  19.6 us
    all_to_all x2, waiting for transfers between devices, local(): lax.all_to_all(part, ('seq', 'head'), split_axis=1, concat_axis=1, tiled=...  18.9 us
    all_to_all x1, waiting for transfers between devices, local(): lax.all_to_all(terms.reshape(n_head, rows, width), 'head', 0, 0, tiled=True)  15.5 us
    all_to_all x2, starting transfers between devices, local(): lax.all_to_all(down.reshape(block.shape), ('seq', 'head'), split_axis=1,...  13.2 us
    dot_general x2, matrix products, local(): jnp.dot(hidden, w_down[0], preferred_element_type=jnp.float32)  11 us
    all_to_all x1, waiting for transfers between devices, local(): lax.all_to_all(spread, 'seq', 1, 1, tiled=True)  9.2 us
    dot_general x2, matrix products, local(): gate = jnp.dot(flat, w_gate[0], preferred_element_type=jnp.float32)  7.49 us
  transfers between devices with their start and end apart: 6, of which 6 were waited for; matrix products, arithmetic and copies ran while one was open for 24% of the time, Pallas kernels for 0%

profile of v4, /device:TPU:0, one launch (start us, length us, event | category | flops | bytes accessed | tf_op | source)
XLA Modules:
  0.0 206.8 jit_solution(5364521425321947802)
XLA Ops:
  0.0 1.7 fusion.19
  1.7 2.0 multiply_reduce_fusion.2
  3.7 0.2 reduce-window.18
  4.0 0.1 select_reduce_fusion.1
  4.1 1.9 fusion.34
  6.2 0.3 fusion.52
  6.5 0.1 copy.115
  6.6 1.8 broadcast_in_dim.24
  8.4 7.3 %all-to-all-start = ((bf16[2,16,256,128]{3,2,0,1:T(8,128)(2,1)}), bf16[2,16,256,128]{3,2,0,1:T(8,128)(2,1)}, u32[]{:S(2)}, u32[]{:S(2)}) async-start(bf16[2,16,256,128]{3,2,0,1:T(8,128)(2,1)} %broadcast_in_dim.24), calls=%async_computation | async-start | bytes 4194304 | tf_op jit(solution)/shard_map/all_to_all | solution.py:143
  15.7 0.5 slice.36
  18.1 0.6 slice.37
  22.0 0.7 eq.59
  22.7 0.7 eq.55
  23.3 0.1 copy.112
  23.4 0.1 copy.113
  23.5 3.5 %fusion.61 = f32[256,512]{1,0:T(8,128)} fusion(bf16[2048,512]{1,0:T(8,128)(2,1)} %param.17, bf16[256,2048]{1,0:T(8,128)(2,1)} %param.15, f32[2048]{0:T(1024)} %param.16, f32[256]{0:T(256)} %copy-done.11), kind=kOutput, calls=%fused_computation.88 | convolution fusion | flops 538968064 | bytes 3679232 | tf_op jit(solution)/shard_map/dot_general | solution.py:126
  27.0 2.0 reshape.229
  29.1 1.4 multiply_reduce_fusion
  30.5 1.4 multiply_multiply_fusion
  31.9 0.5 subtract_convert_fusion
  32.4 0.4 pad_maximum_fusion.1
  32.8 0.7 copy.136
  33.5 0.8 copy.117.qstart_ref
  34.3 0.1 copy.120
  34.4 0.6 pad_add_fusion.bounds_ref
  35.0 0.7 iota_add_fusion.qpos_ref
  35.7 0.2 fusion.45
  35.9 9.2 %all-to-all-done = bf16[2,16,256,128]{3,2,0,1:T(8,128)(2,1)} async-done(((bf16[2,16,256,128]{3,2,0,1:T(8,128)(2,1)}), bf16[2,16,256,128]{3,2,0,1:T(8,128)(2,1)}, u32[]{:S(2)}, u32[]{:S(2)}) %all-to-all-start) | async-done | bytes 2097184 | tf_op jit(solution)/shard_map/all_to_all | solution.py:143
  45.1 3.1 %copy.116 = bf16[2,16,256,128]{3,2,1,0:T(8,128)(2,1)} copy(bf16[2,16,256,128]{3,2,0,1:T(8,128)(2,1)} %all-to-all-done) | data formatting | bytes 4194304 | tf_op jit(solution)/shard_map/all_to_all | solution.py:143
  48.2 5.6 %shard_map.145 = bf16[256,512]{1,0:T(8,128)(2,1)} custom-call(s32[2]{0:T(128)} %pad_add_fusion.bounds_ref, bf16[256,512]{1,0:T(8,128)(2,1)} %bitcast.86, bf16[2,4096,128]{2,1,0:T(8,128)(2,1)} %bitcast.81, s32[256,1]{1,0:T(8,128)} %iota_add_fusion.qpos_ref, s32[256,1]{1,0:T(8,128)} %copy.117.qstart_ref), custom_call_target="tpu_custom_call" | custom-call | tf_op jit(solution)/shard_map/pallas_call | solution.py:82
  53.8 3.4 %convolution_convert_fusion.1 = bf16[256,2048]{1,0:T(8,128)(2,1)} fusion(bf16[256,512]{1,0:T(8,128)(2,1)} %shard_map.145, bf16[512,2048]{1,0:T(8,128)(2,1)} %param.22), kind=kOutput, calls=%fused_computation.15 | convolution fusion | flops 537395200 | bytes 3407872 | tf_op jit(solution)/shard_map/dot_general | solution.py:149
  57.2 6.1 %all-to-all-start.1 = ((bf16[8,32,2048]{2,1,0:T(8,128)(2,1)}), bf16[8,32,2048]{2,1,0:T(8,128)(2,1)}, u32[]{:S(2)}, u32[]{:S(2)}) async-start(bf16[8,32,2048]{2,1,0:T(8,128)(2,1)} %bitcast.83), calls=%async_computation.1 | async-start | bytes 2097152 | tf_op jit(solution)/shard_map/all_to_all | solution.py:150
  63.5 0.2 fusion.47
  63.7 0.2 fusion.39
  64.0 15.5 %all-to-all-done.1 = bf16[8,32,2048]{2,1,0:T(8,128)(2,1)} async-done(((bf16[8,32,2048]{2,1,0:T(8,128)(2,1)}), bf16[8,32,2048]{2,1,0:T(8,128)(2,1)}, u32[]{:S(2)}, u32[]{:S(2)}) %all-to-all-start.1) | async-done | bytes 1048608 | tf_op jit(solution)/shard_map/all_to_all | solution.py:150
  79.5 1.4 convert_reduce_fusion
  80.9 1.1 multiply_reduce_fusion.1
  82.0 1.7 convolution_convert_fusion
  83.7 1.2 fusion.63
  84.8 2.1 copy.124
  86.9 21.3 %all-to-all-start.2 = ((bf16[2,128,2048]{2,0,1:T(2,128)(2,1)}), bf16[2,128,2048]{2,0,1:T(2,128)(2,1)}, u32[]{:S(2)}, u32[]{:S(2)}) async-start(bf16[2,128,2048]{2,0,1:T(2,128)(2,1)} %copy.124), calls=%async_computation.2 | async-start | bytes 2097152 | tf_op jit(solution)/shard_map/all_to_all | solution.py:169
  108.2 3.3 %copy.127 = bf16[2,128,2048]{2,0,1:T(2,128)(2,1)} copy(bf16[2,128,2048]{2,1,0:T(8,128)(2,1)} %bitcast.84) | data formatting | bytes 2097152 | tf_op jit(solution)/shard_map/slice | solution.py:168
  111.5 15.5 %all-to-all-done.2 = bf16[2,128,2048]{2,0,1:T(2,128)(2,1)} async-done(((bf16[2,128,2048]{2,0,1:T(2,128)(2,1)}), bf16[2,128,2048]{2,0,1:T(2,128)(2,1)}, u32[]{:S(2)}, u32[]{:S(2)}) %all-to-all-start.2) | async-done | bytes 1048608 | tf_op jit(solution)/shard_map/all_to_all | solution.py:169
  127.0 5.9 %all-to-all-start.4 = ((bf16[2,128,2048]{2,0,1:T(2,128)(2,1)}), bf16[2,128,2048]{2,0,1:T(2,128)(2,1)}, u32[]{:S(2)}, u32[]{:S(2)}) async-start(bf16[2,128,2048]{2,0,1:T(2,128)(2,1)} %copy.127), calls=%async_computation.4 | async-start | bytes 2097152 | tf_op jit(solution)/shard_map/all_to_all | solution.py:169
  132.9 1.6 copy.125
  134.5 1.0 copy-done.2
  135.5 3.7 %fusion.10 = f32[256,768]{1,0:T(8,128)} fusion(bf16[256,2048]{1,0:T(8,128)(2,1)S(1)} %bitcast.88, bf16[1,2048,768]{2,1,0:T(8,128)(2,1)} %param.27), kind=kOutput, calls=%fused_computation.10 | convolution fusion | flops 805306368 | bytes 4980736 | tf_op jit(solution)/shard_map/dot_general | solution.py:171
  139.3 5.5 %fusion.12 = bf16[256,2048]{1,0:T(8,128)(2,1)} fusion(bf16[1,768,2048]{2,1,0:T(8,128)(2,1)S(1)} %copy-done, bf16[256,2048]{1,0:T(8,128)(2,1)} %bitcast.89, bf16[1,2048,768]{2,1,0:T(8,128)(2,1)} %param.28, f32[256,768]{1,0:T(8,128)} %fusion.10), kind=kOutput, calls=%fused_computation.16 | convolution fusion | flops 1612316672 | bytes 9175040 | tf_op jit(solution)/shard_map/dot_general | solution.py:174
  144.8 3.3 %copy.126 = bf16[2,128,2048]{2,0,1:T(2,128)(2,1)} copy(bf16[2,128,2048]{2,1,0:T(8,128)(2,1)} %bitcast.90) | data formatting | bytes 2097152 | tf_op jit(solution)/shard_map/reshape | solution.py:177
  148.1 3.4 %all-to-all-done.4 = bf16[2,128,2048]{2,0,1:T(2,128)(2,1)} async-done(((bf16[2,128,2048]{2,0,1:T(2,128)(2,1)}), bf16[2,128,2048]{2,0,1:T(2,128)(2,1)}, u32[]{:S(2)}, u32[]{:S(2)}) %all-to-all-start.4) | async-done | bytes 1048608 | tf_op jit(solution)/shard_map/all_to_all | solution.py:169
  151.5 6.7 %all-to-all-start.3 = ((bf16[2,128,2048]{2,0,1:T(2,128)(2,1)}), bf16[2,128,2048]{2,0,1:T(2,128)(2,1)}, u32[]{:S(2)}, u32[]{:S(2)}) async-start(bf16[2,128,2048]{2,0,1:T(2,128)(2,1)} %copy.126), calls=%async_computation.3 | async-start | bytes 2097152 | tf_op jit(solution)/shard_map/all_to_all | solution.py:176
  158.2 1.6 copy.128
  159.7 1.0 copy-done.3
  160.7 3.7 %fusion.8 = f32[256,768]{1,0:T(8,128)} fusion(bf16[256,2048]{1,0:T(8,128)(2,1)S(1)} %bitcast.91, bf16[1,2048,768]{2,1,0:T(8,128)(2,1)} %param.27), kind=kOutput, calls=%fused_computation.8 | convolution fusion | flops 805306368 | bytes 4980736 | tf_op jit(solution)/shard_map/dot_general | solution.py:171
  164.5 5.5 %fusion.15 = bf16[256,2048]{1,0:T(8,128)(2,1)} fusion(bf16[1,768,2048]{2,1,0:T(8,128)(2,1)S(1)} %copy-done, bf16[256,2048]{1,0:T(8,128)(2,1)} %bitcast.92, bf16[1,2048,768]{2,1,0:T(8,128)(2,1)} %param.28, f32[256,768]{1,0:T(8,128)} %fusion.8), kind=kOutput, calls=%fused_computation.17 | convolution fusion | flops 1612316672 | bytes 9175040 | tf_op jit(solution)/shard_map/dot_general | solution.py:174
  170.0 3.3 %copy.129 = bf16[2,128,2048]{2,0,1:T(2,128)(2,1)} copy(bf16[2,128,2048]{2,1,0:T(8,128)(2,1)} %bitcast.93) | data formatting | bytes 2097152 | tf_op jit(solution)/shard_map/reshape | solution.py:177
  173.3 3.7 %all-to-all-done.3 = bf16[2,128,2048]{2,0,1:T(2,128)(2,1)} async-done(((bf16[2,128,2048]{2,0,1:T(2,128)(2,1)}), bf16[2,128,2048]{2,0,1:T(2,128)(2,1)}, u32[]{:S(2)}, u32[]{:S(2)}) %all-to-all-start.3) | async-done | bytes 1048608 | tf_op jit(solution)/shard_map/all_to_all | solution.py:176
  176.9 6.6 %all-to-all-start.5 = ((bf16[2,128,2048]{2,0,1:T(2,128)(2,1)}), bf16[2,128,2048]{2,0,1:T(2,128)(2,1)}, u32[]{:S(2)}, u32[]{:S(2)}) async-start(bf16[2,128,2048]{2,0,1:T(2,128)(2,1)} %copy.129), calls=%async_computation.5 | async-start | bytes 2097152 | tf_op jit(solution)/shard_map/all_to_all | solution.py:176
  183.6 0.2 select_reduce_fusion
  183.8 2.6 %copy.130 = bf16[2,128,2048]{2,1,0:T(8,128)(2,1)} copy(bf16[2,128,2048]{2,0,1:T(2,128)(2,1)} %all-to-all-done.3) | data formatting | bytes 2097152 | tf_op jit(solution)/shard_map/all_to_all | solution.py:176
  186.4 15.9 %all-to-all-done.5 = bf16[2,128,2048]{2,0,1:T(2,128)(2,1)} async-done(((bf16[2,128,2048]{2,0,1:T(2,128)(2,1)}), bf16[2,128,2048]{2,0,1:T(2,128)(2,1)}, u32[]{:S(2)}, u32[]{:S(2)}) %all-to-all-start.5) | async-done | bytes 1048608 | tf_op jit(solution)/shard_map/all_to_all | solution.py:176
  202.3 1.7 copy.131
  204.0 0.2 pad_maximum_fusion
  204.1 2.7 %fusion.18 = bf16[32,2048]{1,0:T(8,128)(2,1)} fusion(f32[32,512]{1,0:T(8,128)S(1)} %select_reduce_fusion, bf16[512,2048]{1,0:T(8,128)(2,1)S(1)} %bitcast.82, f32[32,2048]{1,0:T(8,128)S(1)} %convert_reduce_fusion, bf16[256,2048]{1,0:T(8,128)(2,1)} %param.15, s32[]{:T(128)S(6)} %select_n.26), kind=kOutput, calls=%fused_computation.19 | convolution fusion | flops 402915328 | bytes 2686980 | tf_op jit(solution)/shard_map/dot_general | solution.py:182
  (52 shorter events, 0.6 us)
Async XLA Ops:
  0.0 139.3 %copy-start = (bf16[1,768,2048]{2,1,0:T(8,128)(2,1)S(1)}, bf16[1,768,2048]{2,1,0:T(8,128)(2,1)}, u32[]{:S(2)}) copy-start(bf16[1,768,2048]{2,1,0:T(8,128)(2,1)} %param.29) | copy-start | bytes 9437188
  0.0 4.1 %copy-start.14 = (f32[2048]{0:T(1024)S(1)}, f32[2048]{0:T(1024)}, u32[]{:S(2)}) copy-start(f32[2048]{0:T(1024)} %param.16) | copy-start | bytes 24580
  0.0 3.7 %copy-start.15 = (s32[6]{0:T(128)S(1)}, s32[6]{0:T(128)}, u32[]{:S(2)}) copy-start(s32[6]{0:T(128)} %param.24) | copy-start | bytes 76
  1.7 4.4 %copy-start.11 = (f32[256]{0:T(256)}, f32[256]{0:T(256)S(1)}, u32[]{:S(2)}) copy-start(f32[256]{0:T(256)S(1)} %add_rsqrt_fusion.2) | copy-start | bytes 3076
  1.7 4.4 %copy-start.12 = (f32[128]{0:T(128)S(1)}, f32[128]{0:T(128)}, u32[]{:S(2)}) copy-start(f32[128]{0:T(128)} %param.21) | copy-start | bytes 1540
  4.1 11.6 %copy-start.4 = (s32[256]{0:T(256)}, s32[256]{0:T(256)S(1)}, u32[]{:S(2)}) copy-start(s32[256]{0:T(256)S(1)} %select_reduce_fusion.1) | copy-start | bytes 3076
  8.4 13.5 %copy-start.9 = (s32[32,8]{0,1:T(8,128)S(1)}, s32[32,8]{0,1:T(8,128)}, u32[]{:S(2)}) copy-start(s32[32,8]{0,1:T(8,128)} %param.25) | copy-start | bytes 3076
  8.4 36.7 %all-to-all-start = ((bf16[2,16,256,128]{3,2,0,1:T(8,128)(2,1)}), bf16[2,16,256,128]{3,2,0,1:T(8,128)(2,1)}, u32[]{:S(2)}, u32[]{:S(2)}) async-start(bf16[2,16,256,128]{3,2,0,1:T(8,128)(2,1)} %broadcast_in_dim.24), calls=%async_computation | async-start | bytes 4194304 | tf_op jit(solution)/shard_map/all_to_all | solution.py:143
  23.5 7.0 %copy-start.13 = (f32[128]{0:T(128)S(1)}, f32[128]{0:T(128)}, u32[]{:S(2)}) copy-start(f32[128]{0:T(128)} %param.20) | copy-start | bytes 1540
  30.5 3.0 %copy-start.5 = (s32[256]{0:T(256)S(1)}, s32[256]{0:T(256)}, u32[]{:S(2)}) copy-start(s32[256]{0:T(256)} %copy-done.4) | copy-start | bytes 3076
  30.5 3.8 %copy-start.8 = (s32[2,128]{1,0:T(2,128)S(1)}, s32[2,128]{1,0:T(2,128)}, u32[]{:S(2)}) copy-start(s32[2,128]{1,0:T(2,128)} %eq.59) | copy-start | bytes 3076
  57.2 6.2 %copy-start.7 = (s32[256]{0:T(256)S(1)}, s32[256]{0:T(256)}, u32[]{:S(2)}) copy-start(s32[256]{0:T(256)} %eq.55) | copy-start | bytes 3076
  57.2 24.8 %copy-start.6 = (f32[2048]{0:T(1024)S(1)}, f32[2048]{0:T(1024)}, u32[]{:S(2)}) copy-start(f32[2048]{0:T(1024)} %param.23) | copy-start | bytes 24580
  57.2 22.3 %all-to-all-start.1 = ((bf16[8,32,2048]{2,1,0:T(8,128)(2,1)}), bf16[8,32,2048]{2,1,0:T(8,128)(2,1)}, u32[]{:S(2)}, u32[]{:S(2)}) async-start(bf16[8,32,2048]{2,1,0:T(8,128)(2,1)} %bitcast.83), calls=%async_computation.1 | async-start | bytes 2097152 | tf_op jit(solution)/shard_map/all_to_all | solution.py:150
  86.9 40.0 %all-to-all-start.2 = ((bf16[2,128,2048]{2,0,1:T(2,128)(2,1)}), bf16[2,128,2048]{2,0,1:T(2,128)(2,1)}, u32[]{:S(2)}, u32[]{:S(2)}) async-start(bf16[2,128,2048]{2,0,1:T(2,128)(2,1)} %copy.124), calls=%async_computation.2 | async-start | bytes 2097152 | tf_op jit(solution)/shard_map/all_to_all | solution.py:169
  127.0 24.5 %all-to-all-start.4 = ((bf16[2,128,2048]{2,0,1:T(2,128)(2,1)}), bf16[2,128,2048]{2,0,1:T(2,128)(2,1)}, u32[]{:S(2)}, u32[]{:S(2)}) async-start(bf16[2,128,2048]{2,0,1:T(2,128)(2,1)} %copy.127), calls=%async_computation.4 | async-start | bytes 2097152 | tf_op jit(solution)/shard_map/all_to_all | solution.py:169
  134.5 1.0 copy-start.2
  151.5 25.4 %all-to-all-start.3 = ((bf16[2,128,2048]{2,0,1:T(2,128)(2,1)}), bf16[2,128,2048]{2,0,1:T(2,128)(2,1)}, u32[]{:S(2)}, u32[]{:S(2)}) async-start(bf16[2,128,2048]{2,0,1:T(2,128)(2,1)} %copy.126), calls=%async_computation.3 | async-start | bytes 2097152 | tf_op jit(solution)/shard_map/all_to_all | solution.py:176
  159.7 1.0 copy-start.3
  170.0 13.5 %copy-start.10 = (f32[32,8]{0,1:T(8,128)S(1)}, f32[32,8]{0,1:T(8,128)}, u32[]{:S(2)}) copy-start(f32[32,8]{0,1:T(8,128)} %param.26) | copy-start | bytes 3076
  176.9 25.3 %all-to-all-start.5 = ((bf16[2,128,2048]{2,0,1:T(2,128)(2,1)}), bf16[2,128,2048]{2,0,1:T(2,128)(2,1)}, u32[]{:S(2)}, u32[]{:S(2)}) async-start(bf16[2,128,2048]{2,0,1:T(2,128)(2,1)} %copy.129), calls=%async_computation.5 | async-start | bytes 2097152 | tf_op jit(solution)/shard_map/all_to_all | solution.py:176
  202.3 1.7 copy-start.1

commit v5 on v3

--- a/solution.py
+++ b/solution.py
@@ -35,53 +35,66 @@
     return jnp.sum((positions[:, None] >= ends[None, :]).astype(jnp.int32), axis=1)
 
 
-def _attend_kernel(bounds_ref, q_ref, kv_ref, qpos_ref, qstart_ref, o_ref, *, block, scale):
-    q = q_ref[...]
+def _attend_kernel(bounds_ref, q_ref, kv_ref, qpos_ref, qstart_ref, o_ref, *, dim):
+    heads = q_ref.shape[1] // dim
+    tok = q_ref.shape[0]
+    block = kv_ref.shape[2]
+    q = jnp.concatenate([q_ref[:, h * dim : (h + 1) * dim] for h in range(heads)], axis=0)
     qpos = qpos_ref[...]
     qstart = qstart_ref[...]
-    rows, width = q.shape
-
-    def body(j, carry):
+    scale = dim ** (-0.5)
+
+    def step(j, carry, masked):
         high, total, accum = carry
-        base = pl.multiple_of((bounds_ref[0] + j) * block, block)
-        keys = kv_ref[0, pl.ds(base, block), :]
-        values = kv_ref[1, pl.ds(base, block), :]
+        keys = kv_ref[j, 0]
+        values = kv_ref[j, 1]
         scores = lax.dot_general(q, keys, (((1,), (1,)), ((), ())), preferred_element_type=jnp.float32) * scale
-        key_pos = base + lax.broadcasted_iota(jnp.int32, (1, block), 1)
-        allowed = (key_pos >= qstart) & (key_pos <= qpos)
-        scores = jnp.where(allowed, scores, FLOOR)
+        if masked:
+            key_pos = j * block + lax.broadcasted_iota(jnp.int32, (1, block), 1)
+            allowed = (key_pos >= qstart) & (key_pos <= qpos)
+            scores = jnp.where(allowed, scores, FLOOR)
         new_high = jnp.maximum(high, jnp.max(scores, axis=1, keepdims=True))
-        weights = jnp.where(allowed, jnp.exp(scores - new_high), 0.0)
+        weights = jnp.exp(scores - new_high)
+        if masked:
+            weights = jnp.where(allowed, weights, 0.0)
         factor = jnp.exp(high - new_high)
         total = total * factor + jnp.sum(weights, axis=1, keepdims=True)
-        accum = accum * factor + jnp.dot(weights.astype(jnp.bfloat16), values, preferred_element_type=jnp.float32)
+        accum = accum * factor + jnp.dot(
+            weights.astype(jnp.bfloat16), values, preferred_element_type=jnp.float32
+        )
         return new_high, total, accum
 
-    initial = (
-        jnp.full((rows, 1), FLOOR, jnp.float32),
-        jnp.zeros((rows, 1), jnp.float32),
-        jnp.zeros((rows, width), jnp.float32),
-    )
-    high, total, accum = lax.fori_loop(0, bounds_ref[1], body, initial)
-    o_ref[...] = (accum / total).astype(o_ref.dtype)
-
-def attend(bounds, queries, kv, qpos, qstart, block):
+    carry = (
+        jnp.full((heads * tok, 1), FLOOR, jnp.float32),
+        jnp.zeros((heads * tok, 1), jnp.float32),
+        jnp.zeros((heads * tok, dim), jnp.float32),
+    )
+    carry = lax.fori_loop(bounds_ref[0], bounds_ref[1], lambda j, c: step(j, c, True), carry)
+    carry = lax.fori_loop(bounds_ref[1], bounds_ref[2], lambda j, c: step(j, c, False), carry)
+    carry = lax.fori_loop(bounds_ref[2], bounds_ref[3], lambda j, c: step(j, c, True), carry)
+    high, total, accum = carry
+    out = (accum / total).astype(o_ref.dtype)
+    for h in range(heads):
+        o_ref[:, h * dim : (h + 1) * dim] = out[h * tok : (h + 1) * tok]
+
+
+def attend(bounds, queries, kv, qpos, qstart):
     tok, heads, dim = queries.shape
-    kernel = functools.partial(_attend_kernel, block=block, scale=dim ** (-0.5))
+    kernel = functools.partial(_attend_kernel, dim=dim)
     spec = pltpu.PrefetchScalarGridSpec(
         num_scalar_prefetch=1,
-        grid=(heads,),
+        grid=(1,),
         in_specs=[
-            pl.BlockSpec((tok, dim), lambda h, b: (0, h)),
-            pl.BlockSpec(kv.shape, lambda h, b: (0, 0, 0)),
-            pl.BlockSpec((tok, 1), lambda h, b: (0, 0)),
-            pl.BlockSpec((tok, 1), lambda h, b: (0, 0)),
+            pl.BlockSpec((tok, heads * dim), lambda i, b: (0, 0)),
+            pl.BlockSpec(kv.shape, lambda i, b: (0, 0, 0, 0)),
+            pl.BlockSpec((heads * tok, 1), lambda i, b: (0, 0)),
+            pl.BlockSpec((heads * tok, 1), lambda i, b: (0, 0)),
         ],
-        out_specs=pl.BlockSpec((tok, dim), lambda h, b: (0, h)),
+        out_specs=pl.BlockSpec((tok, heads * dim), lambda i, b: (0, 0)),
     )
     return pl.pallas_call(
-        kernel, grid_spec=spec, out_shape=jax.ShapeDtypeStruct((tok, heads * dim), jnp.bfloat16),
-    )(bounds, queries.reshape(tok, heads * dim), kv, qpos, qstart)
+        kernel, grid_spec=spec, out_shape=jax.ShapeDtypeStruct((tok, heads * dim), jnp.bfloat16)
+    )(bounds, queries.reshape(tok, heads * dim), kv, jnp.tile(qpos, (heads, 1)), jnp.tile(qstart, (heads, 1)))
 
 
 def local(
@@ -139,12 +152,15 @@
     ).astype(jnp.bfloat16)
     values = jnp.dot(normed, value_cols, preferred_element_type=jnp.float32).astype(jnp.bfloat16)
     stacked = jnp.stack([keys, values])
-    spread = jnp.broadcast_to(stacked[:, None], (2, n_seq) + stacked.shape[1:])
-    piece = lax.all_to_all(spread, "seq", 1, 1, tiled=True).reshape(2, n_seq * tok_dev, head_dim)
+    spread = jnp.broadcast_to(stacked[None], (n_seq,) + stacked.shape)
+    piece = lax.all_to_all(spread, "seq", 0, 0, tiled=True)
     block = tok_dev
     low = own_start[0] // block
-    bounds = jnp.stack([low, positions[-1] // block - low + 1]).astype(jnp.int32)
-    attended = attend(bounds, queries, piece, positions[:, None], own_start[:, None], block)
+    high = positions[-1] // block + 1
+    inner_low = jnp.clip(-(-own_start[-1] // block), low, high)
+    inner_high = jnp.clip((positions[0] + 1) // block, inner_low, high)
+    bounds = jnp.stack([low, inner_low, inner_high, high]).astype(jnp.int32)
+    attended = attend(bounds, queries, piece, positions[:, None], own_start[:, None])
     rows = tok_dev // n_head
     terms = jnp.dot(attended, w_out, preferred_element_type=jnp.float32).astype(jnp.bfloat16)
     terms = lax.all_to_all(terms.reshape(n_head, rows, width), "head", 0, 0, tiled=True)

time: 197 us -> 185 us (0.939)
  blocking collectives: 51.6 us -> 43.9 us
  waiting for transfers between devices: 54.3 us -> 51.2 us
    all_to_all x1, blocking collectives: 51.6 us -> 43.9 us  [local(): lax.all_to_all(outgoing, ('seq', 'head'), split_axis=1, concat_axis=1, ti...]
    all_to_all x1 -> x0, local copies, waits for them, and re-layouts: 3.11 us -> none  [local(): lax.all_to_all(spread, 'seq', 1, 1, tiled=True)]
    all_to_all x1, waiting for transfers between devices: 9.2 us -> 6.61 us  [local(): piece = lax.all_to_all(spread, 'seq', 0, 0, tiled=True)]
    unnamed x34 -> x44, local copies, waits for them, and re-layouts: 2.23 us -> 4.36 us
  transfers between devices with their start and end apart: 3 -> 3, of which waited for: 3 -> 3; matrix products, arithmetic and copies ran while one was open for 8% -> 9% of each run, Pallas kernels for 0% -> 0%
where the time goes in v5:
time: 185 us
  waiting for transfers between devices  51.2 us (28%)
  blocking collectives  43.9 us (24%)
  matrix products  26.4 us (14%)
  local copies, waits for them, and re-layouts  21.2 us (11%)
  starting transfers between devices  19.4 us (10%)
  other arithmetic  10.1 us (5%)
  between operations  7.29 us (4%)
  Pallas kernels  5.37 us (3%)
    all_to_all x1, blocking collectives, local(): lax.all_to_all(outgoing, ('seq', 'head'), split_axis=1, concat_axis=1, ti...  43.9 us
    all_to_all x1, waiting for transfers between devices, local(): lax.all_to_all(jnp.dot(hidden, w_down[0], preferred_element_type=jnp.floa...  29.5 us
    all_to_all x1, waiting for transfers between devices, local(): lax.all_to_all(terms.reshape(n_head, rows, width), 'head', 0, 0, tiled=True)  15.1 us
    dot_general x1, matrix products, local(): jnp.dot(hidden, w_down[0], preferred_element_type=jnp.float32)  8.28 us
    all_to_all x1, starting transfers between devices, local(): piece = lax.all_to_all(spread, 'seq', 0, 0, tiled=True)  7.31 us
    all_to_all x1, waiting for transfers between devices, local(): piece = lax.all_to_all(spread, 'seq', 0, 0, tiled=True)  6.61 us
    all_to_all x1, starting transfers between devices, local(): lax.all_to_all(terms.reshape(n_head, rows, width), 'head', 0, 0, tiled=True)  6.13 us
    all_to_all x1, starting transfers between devices, local(): lax.all_to_all(jnp.dot(hidden, w_down[0], preferred_element_type=jnp.floa...  5.91 us
  transfers between devices with their start and end apart: 3, of which 3 were waited for; matrix products, arithmetic and copies ran while one was open for 9% of the time, Pallas kernels for 0%

profile of v5, /device:TPU:0, one launch (start us, length us, event | category | flops | bytes accessed | tf_op | source)
XLA Modules:
  0.0 184.8 jit_solution(4501492034972470190)
XLA Ops:
  0.0 1.7 fusion.10
  1.7 0.0 copy-start.12
  1.7 2.0 %multiply_reduce_fusion.2 = (f32[256]{0:T(256)S(1)}, f32[256,128]{0,1:T(8,128)S(1)}) fusion(bf16[2048,512]{1,0:T(8,128)(2,1)} %param.18, s32[]{:T(128)S(6)} %select_n.39, bf16[256,2048]{1,0:T(8,128)(2,1)} %param.15, f32[2048]{0:T(1024)} %param.16, f32[256]{0:T(256)S(1)} %add_rsqrt_fusion.2), kind=kOutput, calls=%fused_computation.47 | convolution fusion | flops 136380160 | bytes 1714180 | tf_op jit(solution)/shard_map/dot_general | solution.py:149
  3.8 0.2 reduce-window.18
  3.9 0.1 convert_reduce_fusion.1
  4.0 0.1 select_reduce_fusion.1
  4.1 0.0 copy-done.15
  4.1 1.9 %fusion.15 = bf16[1,256,128]{1,2,0:T(8,128)(2,1)S(1)} fusion(bf16[2048,512]{1,0:T(8,128)(2,1)} %param.19, s32[]{:T(128)S(6)} %select_n.39, bf16[256,2048]{1,0:T(8,128)(2,1)} %param.15, f32[2048]{0:T(1024)S(1)} %copy-done.15, f32[256]{0:T(256)S(1)} %add_rsqrt_fusion.2), kind=kOutput, calls=%fused_computation.19 | convolution fusion | flops 136347648 | bytes 1647620 | tf_op jit(solution)/shard_map/dot_general | solution.py:153
  6.1 0.1 multiply_multiply_fusion.1
  6.2 0.3 fusion.29
  6.5 0.1 copy.102
  6.7 1.8 broadcast_in_dim.24
  8.4 7.3 %all-to-all-start = ((bf16[16,2,256,128]{3,2,1,0:T(8,128)(2,1)}), bf16[16,2,256,128]{3,2,1,0:T(8,128)(2,1)}, u32[]{:S(2)}, u32[]{:S(2)}) async-start(bf16[16,2,256,128]{3,2,1,0:T(8,128)(2,1)} %broadcast_in_dim.24), calls=%async_computation | async-start | bytes 4194304 | tf_op jit(solution)/shard_map/all_to_all | solution.py:156
  15.8 0.6 fusion.40
  20.1 0.6 fusion.39
  23.9 0.0 copy-done.9
  23.9 0.1 copy.105
  23.9 0.7 eq.59
  24.6 0.7 eq.55
  25.3 0.1 copy.100
  25.4 0.1 copy.99
  25.5 0.0 copy-start.13
  25.5 3.5 %fusion.37 = f32[256,512]{1,0:T(8,128)} fusion(bf16[2048,512]{1,0:T(8,128)(2,1)} %param.17, bf16[256,2048]{1,0:T(8,128)(2,1)} %param.15, f32[2048]{0:T(1024)} %param.16, f32[256]{0:T(256)} %copy-done.11), kind=kOutput, calls=%fused_computation.75 | convolution fusion | flops 538968064 | bytes 3679232 | tf_op jit(solution)/shard_map/dot_general | solution.py:139
  29.0 2.0 %reshape.233 = f32[256,4,128]{2,1,0:T(4,128)} reshape(f32[256,512]{1,0:T(8,128)} %fusion.37) | data formatting | bytes 1048576 | tf_op jit(solution)/shard_map/reshape | solution.py:139
  31.0 1.4 multiply_reduce_fusion
  32.4 0.0 copy-done.13
  32.4 0.0 copy-start.3
  32.4 1.4 multiply_multiply_fusion
  33.8 0.0 copy-start.8
  33.8 0.5 subtract_convert_fusion
  34.4 0.4 pad_maximum_fusion
  34.7 0.7 copy.123
  35.5 0.0 copy-done.3
  35.5 1.0 copy.120
  36.5 1.1 copy.118
  37.6 0.1 copy.107
  37.7 0.6 pad_add_fusion.bounds_ref
  38.3 0.2 fusion.22
  38.5 6.6 %all-to-all-done.kv_ref = bf16[16,2,256,128]{3,2,1,0:T(8,128)(2,1)} async-done(((bf16[16,2,256,128]{3,2,1,0:T(8,128)(2,1)}), bf16[16,2,256,128]{3,2,1,0:T(8,128)(2,1)}, u32[]{:S(2)}, u32[]{:S(2)}) %all-to-all-start) | async-done | bytes 2097184 | tf_op jit(solution)/shard_map/all_to_all | solution.py:156
  45.1 5.4 %shard_map.145 = bf16[256,512]{1,0:T(8,128)(2,1)} custom-call(s32[4]{0:T(128)} %pad_add_fusion.bounds_ref, bf16[256,512]{1,0:T(8,128)(2,1)} %bitcast.81, bf16[16,2,256,128]{3,2,1,0:T(8,128)(2,1)} %all-to-all-done.kv_ref, s32[1024,1]{1,0:T(8,128)} %bitcast.79, s32[1024,1]{1,0:T(8,128)} %bitcast.78), custom_call_target="tpu_custom_call" | custom-call | tf_op jit(solution)/shard_map/pallas_call | solution.py:95
  50.5 3.4 %convolution_convert_fusion.1 = bf16[256,2048]{1,0:T(8,128)(2,1)} fusion(bf16[256,512]{1,0:T(8,128)(2,1)} %shard_map.145, bf16[512,2048]{1,0:T(8,128)(2,1)} %param.22), kind=kOutput, calls=%fused_computation.10 | convolution fusion | flops 537395200 | bytes 3407872 | tf_op jit(solution)/shard_map/dot_general | solution.py:165
  53.9 6.1 %all-to-all-start.1 = ((bf16[8,32,2048]{2,1,0:T(8,128)(2,1)}), bf16[8,32,2048]{2,1,0:T(8,128)(2,1)}, u32[]{:S(2)}, u32[]{:S(2)}) async-start(bf16[8,32,2048]{2,1,0:T(8,128)(2,1)} %bitcast.74), calls=%async_computation.1 | async-start | bytes 2097152 | tf_op jit(solution)/shard_map/all_to_all | solution.py:166
  60.1 0.2 fusion.24
  60.3 0.1 mul.209
  60.4 0.2 fusion.18
  60.6 15.1 %all-to-all-done.1 = bf16[8,32,2048]{2,1,0:T(8,128)(2,1)} async-done(((bf16[8,32,2048]{2,1,0:T(8,128)(2,1)}), bf16[8,32,2048]{2,1,0:T(8,128)(2,1)}, u32[]{:S(2)}, u32[]{:S(2)}) %all-to-all-start.1) | async-done | bytes 1048608 | tf_op jit(solution)/shard_map/all_to_all | solution.py:166
  75.7 1.4 convert_reduce_fusion
  77.1 1.1 multiply_reduce_fusion.1
  78.2 0.0 copy-done.6
  78.2 1.7 convolution_convert_fusion
  79.9 1.6 copy.111
  81.5 43.9 %all_to_all.20 = bf16[4,128,2048]{2,0,1:T(4,128)(2,1)S(1)} all-to-all(bf16[4,128,2048]{2,0,1:T(4,128)(2,1)S(1)} %copy.111), channel_id=1, replica_groups=mesh['seq'=16,'head'=8] {'seq','head'}, dimensions={1} | all-to-all | bytes 4194304 | tf_op jit(solution)/shard_map/all_to_all | solution.py:182
  125.4 1.2 copy.112
  126.6 0.0 copy-start.1
  126.6 1.3 copy-done.1
  127.9 3.0 %fusion.4 = f32[512,768]{1,0:T(8,128)} fusion(bf16[512,2048]{1,0:T(8,128)(2,1)S(1)} %bitcast.75, bf16[1,2048,768]{2,1,0:T(8,128)(2,1)S(1)} %copy-done.14), kind=kOutput, calls=%fused_computation.4 | convolution fusion | flops 1610612736 | bytes 6815744 | tf_op jit(solution)/shard_map/dot_general | solution.py:184
  130.8 8.3 %fusion.6 = bf16[512,2048]{1,0:T(8,128)(2,1)} fusion(bf16[1,768,2048]{2,1,0:T(8,128)(2,1)S(1)} %copy-done, f32[512,768]{1,0:T(8,128)} %fusion.4, bf16[512,2048]{1,0:T(8,128)(2,1)} %bitcast.76, bf16[1,2048,768]{2,1,0:T(8,128)(2,1)} %param.28), kind=kOutput, calls=%fused_computation.6 | convolution fusion | flops 3224633344 | bytes 12058624 | tf_op jit(solution)/shard_map/dot_general | solution.py:188
  139.1 4.5 %copy.113 = bf16[4,128,2048]{2,0,1:T(4,128)(2,1)} copy(bf16[4,128,2048]{2,1,0:T(8,128)(2,1)} %bitcast.77) | data formatting | bytes 4194304 | tf_op jit(solution)/shard_map/reshape | solution.py:190
  143.6 5.9 %all-to-all-start.3 = ((bf16[4,128,2048]{2,0,1:T(4,128)(2,1)}), bf16[4,128,2048]{2,0,1:T(4,128)(2,1)}, u32[]{:S(2)}, u32[]{:S(2)}) async-start(bf16[4,128,2048]{2,0,1:T(4,128)(2,1)} %copy.113), calls=%async_computation.3 | async-start | bytes 4194304 | tf_op jit(solution)/shard_map/all_to_all | solution.py:187
  149.6 0.1 copy.110
  149.6 0.2 select_reduce_fusion
  149.9 29.5 %all-to-all-done.3 = bf16[4,128,2048]{2,0,1:T(4,128)(2,1)} async-done(((bf16[4,128,2048]{2,0,1:T(4,128)(2,1)}), bf16[4,128,2048]{2,0,1:T(4,128)(2,1)}, u32[]{:S(2)}, u32[]{:S(2)}) %all-to-all-start.3) | async-done | bytes 2097184 | tf_op jit(solution)/shard_map/all_to_all | solution.py:187
  179.4 2.7 %copy.114 = bf16[4,128,2048]{2,1,0:T(8,128)(2,1)S(1)} copy(bf16[4,128,2048]{2,0,1:T(4,128)(2,1)} %all-to-all-done.3) | data formatting | bytes 4194304 | tf_op jit(solution)/shard_map/all_to_all | solution.py:187
  182.1 2.7 %fusion.9 = bf16[32,2048]{1,0:T(8,128)(2,1)} fusion(f32[32,512]{1,0:T(8,128)S(1)} %select_reduce_fusion, bf16[512,2048]{1,0:T(8,128)(2,1)S(1)} %bitcast.72, f32[32,2048]{1,0:T(8,128)S(1)} %convert_reduce_fusion, bf16[256,2048]{1,0:T(8,128)(2,1)} %param.15, s32[]{:T(128)S(6)} %select_n.32), kind=kOutput, calls=%fused_computation.12 | convolution fusion | flops 402915328 | bytes 2686980 | tf_op jit(solution)/shard_map/dot_general | solution.py:197
  (44 shorter events, 0.2 us)
Async XLA Ops:
  0.0 130.8 %copy-start = (bf16[1,768,2048]{2,1,0:T(8,128)(2,1)S(1)}, bf16[1,768,2048]{2,1,0:T(8,128)(2,1)}, u32[]{:S(2)}) copy-start(bf16[1,768,2048]{2,1,0:T(8,128)(2,1)} %param.29) | copy-start | bytes 9437188
  0.0 4.1 %copy-start.15 = (f32[2048]{0:T(1024)S(1)}, f32[2048]{0:T(1024)}, u32[]{:S(2)}) copy-start(f32[2048]{0:T(1024)} %param.16) | copy-start | bytes 24580
  0.0 3.7 %copy-start.16 = (s32[6]{0:T(128)S(1)}, s32[6]{0:T(128)}, u32[]{:S(2)}) copy-start(s32[6]{0:T(128)} %param.24) | copy-start | bytes 76
  1.7 4.4 %copy-start.11 = (f32[256]{0:T(256)}, f32[256]{0:T(256)S(1)}, u32[]{:S(2)}) copy-start(f32[256]{0:T(256)S(1)} %add_rsqrt_fusion.2) | copy-start | bytes 3076
  1.7 4.4 %copy-start.12 = (f32[128]{0:T(128)S(1)}, f32[128]{0:T(128)}, u32[]{:S(2)}) copy-start(f32[128]{0:T(128)} %param.21) | copy-start | bytes 1540
  3.7 16.4 %copy-start.4 = (s32[256]{0:T(256)}, s32[256]{0:T(256)S(1)}, u32[]{:S(2)}) copy-start(s32[256]{0:T(256)S(1)} %iota_add_fusion) | copy-start | bytes 3076
  4.1 11.6 %copy-start.2 = (s32[256]{0:T(256)}, s32[256]{0:T(256)S(1)}, u32[]{:S(2)}) copy-start(s32[256]{0:T(256)S(1)} %select_reduce_fusion.1) | copy-start | bytes 3076
  8.4 15.4 %copy-start.9 = (s32[32,8]{0,1:T(8,128)S(1)}, s32[32,8]{0,1:T(8,128)}, u32[]{:S(2)}) copy-start(s32[32,8]{0,1:T(8,128)} %param.25) | copy-start | bytes 3076
  8.4 36.7 %all-to-all-start = ((bf16[16,2,256,128]{3,2,1,0:T(8,128)(2,1)}), bf16[16,2,256,128]{3,2,1,0:T(8,128)(2,1)}, u32[]{:S(2)}, u32[]{:S(2)}) async-start(bf16[16,2,256,128]{3,2,1,0:T(8,128)(2,1)} %broadcast_in_dim.24), calls=%async_computation | async-start | bytes 4194304 | tf_op jit(solution)/shard_map/all_to_all | solution.py:156
  25.5 7.0 %copy-start.13 = (f32[128]{0:T(128)S(1)}, f32[128]{0:T(128)}, u32[]{:S(2)}) copy-start(f32[128]{0:T(128)} %param.20) | copy-start | bytes 1540
  32.4 3.0 %copy-start.3 = (s32[256]{0:T(256)S(1)}, s32[256]{0:T(256)}, u32[]{:S(2)}) copy-start(s32[256]{0:T(256)} %copy-done.2) | copy-start | bytes 3076
  33.8 2.7 %copy-start.5 = (s32[256]{0:T(256)S(1)}, s32[256]{0:T(256)}, u32[]{:S(2)}) copy-start(s32[256]{0:T(256)} %copy-done.4) | copy-start | bytes 3076
  33.8 3.8 %copy-start.8 = (s32[2,128]{1,0:T(2,128)S(1)}, s32[2,128]{1,0:T(2,128)}, u32[]{:S(2)}) copy-start(s32[2,128]{1,0:T(2,128)} %eq.59) | copy-start | bytes 3076
  53.9 6.2 %copy-start.7 = (s32[256]{0:T(256)S(1)}, s32[256]{0:T(256)}, u32[]{:S(2)}) copy-start(s32[256]{0:T(256)} %eq.55) | copy-start | bytes 3076
  53.9 24.3 %copy-start.6 = (f32[2048]{0:T(1024)S(1)}, f32[2048]{0:T(1024)}, u32[]{:S(2)}) copy-start(f32[2048]{0:T(1024)} %param.23) | copy-start | bytes 24580
  53.9 21.8 %all-to-all-start.1 = ((bf16[8,32,2048]{2,1,0:T(8,128)(2,1)}), bf16[8,32,2048]{2,1,0:T(8,128)(2,1)}, u32[]{:S(2)}, u32[]{:S(2)}) async-start(bf16[8,32,2048]{2,1,0:T(8,128)(2,1)} %bitcast.74), calls=%async_computation.1 | async-start | bytes 2097152 | tf_op jit(solution)/shard_map/all_to_all | solution.py:166
  125.4 2.5 %copy-start.14 = (bf16[1,2048,768]{2,1,0:T(8,128)(2,1)S(1)}, bf16[1,2048,768]{2,1,0:T(8,128)(2,1)}, u32[]{:S(2)}) copy-start(bf16[1,2048,768]{2,1,0:T(8,128)(2,1)} %param.27) | copy-start | bytes 9437188
  126.6 1.3 copy-start.1
  143.6 5.9 %copy-start.10 = (f32[32,8]{0,1:T(8,128)S(1)}, f32[32,8]{0,1:T(8,128)}, u32[]{:S(2)}) copy-start(f32[32,8]{0,1:T(8,128)} %param.26) | copy-start | bytes 3076
  143.6 35.7 %all-to-all-start.3 = ((bf16[4,128,2048]{2,0,1:T(4,128)(2,1)}), bf16[4,128,2048]{2,0,1:T(4,128)(2,1)}, u32[]{:S(2)}, u32[]{:S(2)}) async-start(bf16[4,128,2048]{2,0,1:T(4,128)(2,1)} %copy.113), calls=%async_computation.3 | async-start | bytes 4194304 | tf_op jit(solution)/shard_map/all_to_all | solution.py:187

commit v6 on v5

--- a/solution.py
+++ b/solution.py
@@ -172,30 +172,28 @@
     chosen = expert_ids.reshape(-1)
     hits = (chosen[:, None] == jnp.arange(experts, dtype=jnp.int32)[None, :]).astype(jnp.int32)
     rank = jnp.sum((jnp.cumsum(hits, axis=0) - hits) * hits, axis=1)
-    slot = rank * experts + chosen
-    select = (slot[:, None] == jnp.arange(capacity * experts, dtype=jnp.int32)[None, :]).reshape(
-        rows, TOP, capacity * experts
-    )
-    sources = jnp.transpose(jnp.any(select, axis=1)).astype(jnp.bfloat16)
-    outgoing = jnp.dot(sources, routed, preferred_element_type=jnp.float32).astype(jnp.bfloat16)
-    outgoing = outgoing.reshape(capacity, experts, width)
-    block = lax.all_to_all(outgoing, ("seq", "head"), split_axis=1, concat_axis=1, tiled=True)
-    flat = block.reshape(-1, width)
-    gate = jnp.dot(flat, w_gate[0], preferred_element_type=jnp.float32)
-    up = jnp.dot(flat, w_up[0], preferred_element_type=jnp.float32)
+    slot = chosen * capacity + rank
+    select = (slot[:, None] == jnp.arange(experts * capacity, dtype=jnp.int32)[None, :]).reshape(
+        rows, TOP, experts, capacity
+    )
+    sources = jnp.any(select, axis=1).astype(jnp.bfloat16)
+    outgoing = lax.dot_general(
+        sources, routed, (((0,), (0,)), ((), ())), preferred_element_type=jnp.float32
+    ).astype(jnp.bfloat16)
+    block = lax.all_to_all(outgoing, ("seq", "head"), split_axis=0, concat_axis=0, tiled=True)
+    gate = jnp.einsum("scd,df->scf", block, w_gate[0], preferred_element_type=jnp.float32)
+    up = jnp.einsum("scd,df->scf", block, w_up[0], preferred_element_type=jnp.float32)
     hidden = (jax.nn.silu(gate) * up).astype(jnp.bfloat16)
+    down = jnp.einsum("scf,fd->scd", hidden, w_down[0], preferred_element_type=jnp.float32)
     returned = lax.all_to_all(
-        jnp.dot(hidden, w_down[0], preferred_element_type=jnp.float32)
-        .astype(jnp.bfloat16)
-        .reshape(block.shape),
-        ("seq", "head"),
-        split_axis=1,
-        concat_axis=1,
-        tiled=True,
-    ).reshape(-1, width)
-    mixing = jnp.sum(jnp.where(select, route_weights[:, :, None], 0.0), axis=1)
-    combined = jnp.dot(
-        mixing, returned.astype(jnp.float32), precision=lax.Precision.HIGHEST,
+        down.astype(jnp.bfloat16), ("seq", "head"), split_axis=0, concat_axis=0, tiled=True
+    )
+    mixing = jnp.sum(jnp.where(select, route_weights[:, :, None, None], 0.0), axis=1)
+    combined = lax.dot_general(
+        mixing,
+        returned.astype(jnp.float32),
+        (((1, 2), (0, 1)), ((), ())),
+        precision=lax.Precision.HIGHEST,
         preferred_element_type=jnp.float32,
     )
     return (resid + combined).astype(jnp.bfloat16)

time: 185 us -> 188 us (1.016)
  matrix products: 26.4 us -> 32.4 us
  local copies, waits for them, and re-layouts: 21.2 us -> 16.1 us
    convert_element_type x0 -> x2, local copies, waits for them, and re-layouts: none -> 6.13 us  [the longest x1 4.5 us: local(): down.astype(jnp.bfloat16)]
    reshape x2 -> x0, local copies, waits for them, and re-layouts: 6.13 us -> none  [the longest x1 4.5 us: local(): returned = lax.all_to_all(jnp.dot(hidden, w_down[0], preferred_element_ty...]
    dot_general x4, matrix products: 15.6 us -> 21.6 us  [the longest x1 9.85 us: local(): jnp.einsum('scf,fd->scd', hidden, w_down[0], preferred_element_type=jnp.f...]
    all_to_all x2 -> x0, local copies, waits for them, and re-layouts: 3.9 us -> none  [the longest x1 2.74 us: local(): lax.all_to_all(jnp.dot(hidden, w_down[0], preferred_element_type=jnp.floa...]
    unnamed x44 -> x30, local copies, waits for them, and re-layouts: 4.36 us -> 4.34 us
  transfers between devices with their start and end apart: 3 -> 3, of which waited for: 3 -> 3; matrix products, arithmetic and copies ran while one was open for 9% -> 8% of each run, Pallas kernels for 0% -> 0%
where the time goes in v6:
time: 188 us; the launch traced here: 187 us
  waiting for transfers between devices  52.4 us (28%)
  blocking collectives  43.8 us (23%)
  matrix products  32.4 us (17%)
  starting transfers between devices  19.4 us (10%)
  local copies, waits for them, and re-layouts  16.1 us (9%)
  other arithmetic  10.1 us (5%)
  between operations  7.21 us (4%)
  Pallas kernels  5.37 us (3%)
    all_to_all x1, blocking collectives, local(): lax.all_to_all(outgoing, ('seq', 'head'), split_axis=0, concat_axis=0, ti...  43.8 us
    all_to_all x1, waiting for transfers between devices, local(): lax.all_to_all(down.astype(jnp.bfloat16), ('seq', 'head'), split_axis=0,...  29.3 us
    all_to_all x1, waiting for transfers between devices, local(): lax.all_to_all(terms.reshape(n_head, rows, width), 'head', 0, 0, tiled=True)  15.2 us
    dot_general x1, matrix products, local(): jnp.einsum('scf,fd->scd', hidden, w_down[0], preferred_element_type=jnp.f...  9.85 us
    all_to_all x1, waiting for transfers between devices, local(): piece = lax.all_to_all(spread, 'seq', 0, 0, tiled=True)  7.92 us
    all_to_all x1, starting transfers between devices, local(): piece = lax.all_to_all(spread, 'seq', 0, 0, tiled=True)  7.19 us
    all_to_all x1, starting transfers between devices, local(): lax.all_to_all(down.astype(jnp.bfloat16), ('seq', 'head'), split_axis=0,...  6.13 us
    all_to_all x1, starting transfers between devices, local(): lax.all_to_all(terms.reshape(n_head, rows, width), 'head', 0, 0, tiled=True)  6.12 us
  transfers between devices with their start and end apart: 3, of which 3 were waited for; matrix products, arithmetic and copies ran while one was open for 8% of the time, Pallas kernels for 0%

profile of v6, /device:TPU:0, one launch (start us, length us, event | category | flops | bytes accessed | tf_op | source)
XLA Modules:
  0.0 186.9 jit_solution(9927229524706781453)
XLA Ops:
  0.0 0.0 copy-start
  0.0 1.7 fusion.11
  1.7 0.0 copy-start.5
  1.7 2.0 %multiply_reduce_fusion.2 = (f32[256]{0:T(256)S(1)}, f32[256,128]{0,1:T(8,128)S(1)}) fusion(bf16[2048,512]{1,0:T(8,128)(2,1)} %param.18, s32[]{:T(128)S(6)} %select_n.39, bf16[256,2048]{1,0:T(8,128)(2,1)} %param.15, f32[2048]{0:T(1024)} %param.16, f32[256]{0:T(256)S(1)} %add_rsqrt_fusion.2), kind=kOutput, calls=%fused_computation.53 | convolution fusion | flops 136380160 | bytes 1714180 | tf_op jit(solution)/shard_map/dot_general | solution.py:149
  3.7 0.0 copy-done.9
  3.7 0.2 reduce-window.18
  3.9 0.1 convert_reduce_fusion.1
  4.0 0.1 select_reduce_fusion
  4.1 0.0 copy-done.8
  4.1 1.9 %fusion.21 = bf16[1,256,128]{1,2,0:T(8,128)(2,1)S(1)} fusion(bf16[2048,512]{1,0:T(8,128)(2,1)} %param.19, s32[]{:T(128)S(6)} %select_n.39, bf16[256,2048]{1,0:T(8,128)(2,1)} %param.15, f32[2048]{0:T(1024)S(1)} %copy-done.8, f32[256]{0:T(256)S(1)} %add_rsqrt_fusion.2), kind=kOutput, calls=%fused_computation.23 | convolution fusion | flops 136347648 | bytes 1647620 | tf_op jit(solution)/shard_map/dot_general | solution.py:153
  6.0 0.0 copy-done.5
  6.1 0.1 multiply_multiply_fusion.1
  6.1 0.3 fusion.42
  6.5 0.1 copy.95
  6.6 1.8 broadcast_in_dim.24
  8.4 7.2 %all-to-all-start = ((bf16[16,2,256,128]{3,2,1,0:T(8,128)(2,1)}), bf16[16,2,256,128]{3,2,1,0:T(8,128)(2,1)}, u32[]{:S(2)}, u32[]{:S(2)}) async-start(bf16[16,2,256,128]{3,2,1,0:T(8,128)(2,1)} %broadcast_in_dim.24), calls=%async_computation | async-start | bytes 4194304 | tf_op jit(solution)/shard_map/all_to_all | solution.py:156
  15.6 0.6 fusion.53
  19.9 0.6 fusion.52
  23.7 0.1 copy.92
  23.8 0.1 copy.93
  23.9 0.0 copy-start.6
  23.9 3.5 %fusion.50 = f32[256,512]{1,0:T(8,128)} fusion(bf16[2048,512]{1,0:T(8,128)(2,1)} %param.17, bf16[256,2048]{1,0:T(8,128)(2,1)} %param.15, f32[2048]{0:T(1024)} %param.16, f32[256]{0:T(256)S(1)} %add_rsqrt_fusion.2), kind=kOutput, calls=%fused_computation.84 | convolution fusion | flops 538968064 | bytes 3679232 | tf_op jit(solution)/shard_map/dot_general | solution.py:139
  27.4 2.0 %reshape.225 = f32[256,4,128]{2,1,0:T(4,128)} reshape(f32[256,512]{1,0:T(8,128)} %fusion.50) | data formatting | bytes 1048576 | tf_op jit(solution)/shard_map/reshape | solution.py:139
  29.4 1.4 multiply_reduce_fusion
  30.8 0.0 copy-done.6
  30.8 1.4 multiply_multiply_fusion
  32.2 0.0 copy-start.3
  32.2 0.5 subtract_convert_fusion
  32.7 0.4 pad_maximum_fusion
  33.1 0.7 copy.133
  33.9 1.1 copy.116
  34.9 1.0 copy.114
  36.0 0.0 copy-done.3
  36.0 0.1 copy.98
  36.0 0.1 eq.65
  36.1 0.1 copy.101
  36.2 0.6 pad_add_fusion.bounds_ref
  36.8 0.2 fusion.31
  37.0 7.9 %all-to-all-done.kv_ref = bf16[16,2,256,128]{3,2,1,0:T(8,128)(2,1)} async-done(((bf16[16,2,256,128]{3,2,1,0:T(8,128)(2,1)}), bf16[16,2,256,128]{3,2,1,0:T(8,128)(2,1)}, u32[]{:S(2)}, u32[]{:S(2)}) %all-to-all-start) | async-done | bytes 2097184 | tf_op jit(solution)/shard_map/all_to_all | solution.py:156
  44.9 5.4 %shard_map.145 = bf16[256,512]{1,0:T(8,128)(2,1)} custom-call(s32[4]{0:T(128)} %pad_add_fusion.bounds_ref, bf16[256,512]{1,0:T(8,128)(2,1)} %bitcast.79, bf16[16,2,256,128]{3,2,1,0:T(8,128)(2,1)} %all-to-all-done.kv_ref, s32[1024,1]{1,0:T(8,128)} %bitcast.77, s32[1024,1]{1,0:T(8,128)} %bitcast.76), custom_call_target="tpu_custom_call" | custom-call | tf_op jit(solution)/shard_map/pallas_call | solution.py:95
  50.3 3.4 %convolution_convert_fusion.1 = bf16[256,2048]{1,0:T(8,128)(2,1)} fusion(bf16[256,512]{1,0:T(8,128)(2,1)} %shard_map.145, bf16[512,2048]{1,0:T(8,128)(2,1)} %param.22), kind=kOutput, calls=%fused_computation.10 | convolution fusion | flops 537395200 | bytes 3407872 | tf_op jit(solution)/shard_map/dot_general | solution.py:165
  53.7 6.1 %all-to-all-start.1 = ((bf16[8,32,2048]{2,1,0:T(8,128)(2,1)}), bf16[8,32,2048]{2,1,0:T(8,128)(2,1)}, u32[]{:S(2)}, u32[]{:S(2)}) async-start(bf16[8,32,2048]{2,1,0:T(8,128)(2,1)} %bitcast.75), calls=%async_computation.1 | async-start | bytes 2097152 | tf_op jit(solution)/shard_map/all_to_all | solution.py:166
  59.8 0.1 eq.61
  60.0 0.2 fusion.35
  60.2 0.1 reduce_sum.90
  60.3 0.3 compare_reduce_fusion
  60.6 15.2 %all-to-all-done.1 = bf16[8,32,2048]{2,1,0:T(8,128)(2,1)} async-done(((bf16[8,32,2048]{2,1,0:T(8,128)(2,1)}), bf16[8,32,2048]{2,1,0:T(8,128)(2,1)}, u32[]{:S(2)}, u32[]{:S(2)}) %all-to-all-start.1) | async-done | bytes 1048608 | tf_op jit(solution)/shard_map/all_to_all | solution.py:166
  75.8 1.4 convert_reduce_fusion
  77.2 1.1 multiply_reduce_fusion.1
  78.3 1.7 convolution_convert_fusion
  80.0 1.6 copy.105
  81.6 0.0 copy-start.7
  81.6 43.8 %all_to_all.20 = bf16[128,4,2048]{2,1,0:T(4,128)(2,1)S(1)} all-to-all(bf16[128,4,2048]{2,1,0:T(4,128)(2,1)S(1)} %copy.105), channel_id=1, replica_groups=mesh['seq'=16,'head'=8] {'seq','head'}, dimensions={0} | all-to-all | bytes 4194304 | tf_op jit(solution)/shard_map/all_to_all | solution.py:183
  125.4 1.3 copy-done.1
  126.7 0.0 copy-done.7
  126.7 4.8 %fusion.4 = f32[128,4,768]{2,0,1:T(8,128)} fusion(bf16[1,2048,768]{2,1,0:T(8,128)(2,1)S(1)} %copy-done.7, bf16[128,4,2048]{2,1,0:T(4,128)(2,1)S(1)} %all_to_all.20), kind=kOutput, calls=%fused_computation.4 | convolution fusion | flops 1610612736 | bytes 6815744 | tf_op jit(solution)/shard_map/scd,df->scf/dot_general | solution.py:184
  131.5 0.0 copy-done
  131.5 9.9 %fusion.6 = bf16[128,4,2048]{2,0,1:T(8,128)(2,1)} fusion(bf16[1,768,2048]{2,1,0:T(8,128)(2,1)S(1)} %copy-done, f32[128,4,768]{2,0,1:T(8,128)} %fusion.4, bf16[1,2048,768]{2,1,0:T(8,128)(2,1)} %param.28, bf16[128,4,2048]{2,1,0:T(4,128)(2,1)} %copy-done.1), kind=kOutput, calls=%fused_computation.6 | convolution fusion | flops 3224633344 | bytes 12058624 | tf_op jit(solution)/shard_map/scf,fd->scd/dot_general | solution.py:187
  141.3 4.5 %copy.108 = bf16[128,4,2048]{2,1,0:T(4,128)(2,1)} copy(bf16[128,4,2048]{2,0,1:T(8,128)(2,1)} %fusion.6) | data formatting | bytes 4194304 | tf_op jit(solution)/shard_map/convert_element_type | solution.py:189
  145.8 6.1 %all-to-all-start.3 = ((bf16[128,4,2048]{2,1,0:T(4,128)(2,1)}), bf16[128,4,2048]{2,1,0:T(4,128)(2,1)}, u32[]{:S(2)}, u32[]{:S(2)}) async-start(bf16[128,4,2048]{2,1,0:T(4,128)(2,1)} %copy.108), calls=%async_computation.3 | async-start | bytes 4194304 | tf_op jit(solution)/shard_map/all_to_all | solution.py:188
  152.0 0.1 copy.103
  152.0 0.3 fusion.27
  152.3 29.3 %all-to-all-done.3 = bf16[128,4,2048]{2,1,0:T(4,128)(2,1)} async-done(((bf16[128,4,2048]{2,1,0:T(4,128)(2,1)}), bf16[128,4,2048]{2,1,0:T(4,128)(2,1)}, u32[]{:S(2)}, u32[]{:S(2)}) %all-to-all-start.3) | async-done | bytes 2097184 | tf_op jit(solution)/shard_map/all_to_all | solution.py:188
  181.6 5.3 %fusion.10 = bf16[32,2048]{1,0:T(8,128)(2,1)} fusion(bf16[128,4,2048]{2,1,0:T(4,128)(2,1)} %all-to-all-done.3, f32[32,2048]{1,0:T(8,128)S(1)} %convert_reduce_fusion, bf16[256,2048]{1,0:T(8,128)(2,1)} %param.15, s32[]{:T(128)S(6)} %select_n.32, f32[32,128,4]{1,2,0:T(4,128)S(1)} %fusion.27), kind=kOutput, calls=%fused_computation.13 | convolution fusion | flops 402915328 | bytes 2686980 | tf_op jit(solution)/shard_map/dot_general | solution.py:192
  (28 shorter events, 0.2 us)
Async XLA Ops:
  0.0 131.5 %copy-start = (bf16[1,768,2048]{2,1,0:T(8,128)(2,1)S(1)}, bf16[1,768,2048]{2,1,0:T(8,128)(2,1)}, u32[]{:S(2)}) copy-start(bf16[1,768,2048]{2,1,0:T(8,128)(2,1)} %param.29) | copy-start | bytes 9437188
  0.0 4.1 %copy-start.8 = (f32[2048]{0:T(1024)S(1)}, f32[2048]{0:T(1024)}, u32[]{:S(2)}) copy-start(f32[2048]{0:T(1024)} %param.16) | copy-start | bytes 24580
  0.0 3.7 %copy-start.9 = (s32[6]{0:T(128)S(1)}, s32[6]{0:T(128)}, u32[]{:S(2)}) copy-start(s32[6]{0:T(128)} %param.24) | copy-start | bytes 76
  1.7 4.3 %copy-start.5 = (f32[128]{0:T(128)S(1)}, f32[128]{0:T(128)}, u32[]{:S(2)}) copy-start(f32[128]{0:T(128)} %param.21) | copy-start | bytes 1540
  8.4 36.6 %all-to-all-start = ((bf16[16,2,256,128]{3,2,1,0:T(8,128)(2,1)}), bf16[16,2,256,128]{3,2,1,0:T(8,128)(2,1)}, u32[]{:S(2)}, u32[]{:S(2)}) async-start(bf16[16,2,256,128]{3,2,1,0:T(8,128)(2,1)} %broadcast_in_dim.24), calls=%async_computation | async-start | bytes 4194304 | tf_op jit(solution)/shard_map/all_to_all | solution.py:156
  23.9 7.0 %copy-start.6 = (f32[128]{0:T(128)S(1)}, f32[128]{0:T(128)}, u32[]{:S(2)}) copy-start(f32[128]{0:T(128)} %param.20) | copy-start | bytes 1540
  32.2 3.8 %copy-start.3 = (s32[32,8]{0,1:T(8,128)S(1)}, s32[32,8]{0,1:T(8,128)}, u32[]{:S(2)}) copy-start(s32[32,8]{0,1:T(8,128)} %param.25) | copy-start | bytes 3076
  53.7 24.6 %copy-start.2 = (f32[2048]{0:T(1024)S(1)}, f32[2048]{0:T(1024)}, u32[]{:S(2)}) copy-start(f32[2048]{0:T(1024)} %param.23) | copy-start | bytes 24580
  53.7 22.1 %all-to-all-start.1 = ((bf16[8,32,2048]{2,1,0:T(8,128)(2,1)}), bf16[8,32,2048]{2,1,0:T(8,128)(2,1)}, u32[]{:S(2)}, u32[]{:S(2)}) async-start(bf16[8,32,2048]{2,1,0:T(8,128)(2,1)} %bitcast.75), calls=%async_computation.1 | async-start | bytes 2097152 | tf_op jit(solution)/shard_map/all_to_all | solution.py:166
  81.6 45.1 %copy-start.7 = (bf16[1,2048,768]{2,1,0:T(8,128)(2,1)S(1)}, bf16[1,2048,768]{2,1,0:T(8,128)(2,1)}, u32[]{:S(2)}) copy-start(bf16[1,2048,768]{2,1,0:T(8,128)(2,1)} %param.27) | copy-start | bytes 9437188
  125.4 1.3 copy-start.1
  145.8 6.1 %copy-start.4 = (f32[32,8]{0,1:T(8,128)S(1)}, f32[32,8]{0,1:T(8,128)}, u32[]{:S(2)}) copy-start(f32[32,8]{0,1:T(8,128)} %param.26) | copy-start | bytes 3076
  145.8 35.7 %all-to-all-start.3 = ((bf16[128,4,2048]{2,1,0:T(4,128)(2,1)}), bf16[128,4,2048]{2,1,0:T(4,128)(2,1)}, u32[]{:S(2)}, u32[]{:S(2)}) async-start(bf16[128,4,2048]{2,1,0:T(4,128)(2,1)} %copy.108), calls=%async_computation.3 | async-start | bytes 4194304 | tf_op jit(solution)/shard_map/all_to_all | solution.py:188

commit v7 on v5

--- a/solution.py
+++ b/solution.py
@@ -35,10 +35,10 @@
     return jnp.sum((positions[:, None] >= ends[None, :]).astype(jnp.int32), axis=1)
 
 
-def _attend_kernel(bounds_ref, q_ref, kv_ref, qpos_ref, qstart_ref, o_ref, *, dim):
+def _attend_kernel(bounds_ref, q_ref, own_ref, other_ref, qpos_ref, qstart_ref, o_ref, *, dim):
     heads = q_ref.shape[1] // dim
     tok = q_ref.shape[0]
-    block = kv_ref.shape[2]
+    block = own_ref.shape[2]
     q = jnp.concatenate([q_ref[:, h * dim : (h + 1) * dim] for h in range(heads)], axis=0)
     qpos = qpos_ref[...]
     qstart = qstart_ref[...]
@@ -46,8 +46,9 @@
 
     def step(j, carry, masked):
         high, total, accum = carry
-        keys = kv_ref[j, 0]
-        values = kv_ref[j, 1]
+        mine = j % 2 == bounds_ref[4]
+        keys = jnp.where(mine, own_ref[j // 2, 0], other_ref[j // 2, 0])
+        values = jnp.where(mine, own_ref[j // 2, 1], other_ref[j // 2, 1])
         scores = lax.dot_general(q, keys, (((1,), (1,)), ((), ())), preferred_element_type=jnp.float32) * scale
         if masked:
             key_pos = j * block + lax.broadcasted_iota(jnp.int32, (1, block), 1)
@@ -78,7 +79,7 @@
         o_ref[:, h * dim : (h + 1) * dim] = out[h * tok : (h + 1) * tok]
 
 
-def attend(bounds, queries, kv, qpos, qstart):
+def attend(bounds, queries, own, other, qpos, qstart):
     tok, heads, dim = queries.shape
     kernel = functools.partial(_attend_kernel, dim=dim)
     spec = pltpu.PrefetchScalarGridSpec(
@@ -86,7 +87,8 @@
         grid=(1,),
         in_specs=[
             pl.BlockSpec((tok, heads * dim), lambda i, b: (0, 0)),
-            pl.BlockSpec(kv.shape, lambda i, b: (0, 0, 0, 0)),
+            pl.BlockSpec(own.shape, lambda i, b: (0, 0, 0, 0)),
+            pl.BlockSpec(other.shape, lambda i, b: (0, 0, 0, 0)),
             pl.BlockSpec((heads * tok, 1), lambda i, b: (0, 0)),
             pl.BlockSpec((heads * tok, 1), lambda i, b: (0, 0)),
         ],
@@ -94,7 +96,7 @@
     )
     return pl.pallas_call(
         kernel, grid_spec=spec, out_shape=jax.ShapeDtypeStruct((tok, heads * dim), jnp.bfloat16)
-    )(bounds, queries.reshape(tok, heads * dim), kv, jnp.tile(qpos, (heads, 1)), jnp.tile(qstart, (heads, 1)))
+    )(bounds, queries.reshape(tok, heads * dim), own, other, jnp.tile(qpos, (heads, 1)), jnp.tile(qstart, (heads, 1)))
 
 
 def local(
@@ -152,15 +154,18 @@
     ).astype(jnp.bfloat16)
     values = jnp.dot(normed, value_cols, preferred_element_type=jnp.float32).astype(jnp.bfloat16)
     stacked = jnp.stack([keys, values])
-    spread = jnp.broadcast_to(stacked[None], (n_seq,) + stacked.shape)
-    piece = lax.all_to_all(spread, "seq", 0, 0, tiled=True)
+    pairs = n_seq // 2
+    groups = [[2 * i + c for i in range(pairs)] for c in range(2)]
+    spread = jnp.broadcast_to(stacked[None], (pairs,) + stacked.shape)
+    same_core = lax.all_to_all(spread, "seq", 0, 0, tiled=True, axis_index_groups=groups)
+    other_core = lax.ppermute(same_core, "seq", [(i, i ^ 1) for i in range(n_seq)])
     block = tok_dev
     low = own_start[0] // block
     high = positions[-1] // block + 1
     inner_low = jnp.clip(-(-own_start[-1] // block), low, high)
     inner_high = jnp.clip((positions[0] + 1) // block, inner_low, high)
-    bounds = jnp.stack([low, inner_low, inner_high, high]).astype(jnp.int32)
-    attended = attend(bounds, queries, piece, positions[:, None], own_start[:, None])
+    bounds = jnp.stack([low, inner_low, inner_high, high, seq_index % 2]).astype(jnp.int32)
+    attended = attend(bounds, queries, same_core, other_core, positions[:, None], own_start[:, None])
     rows = tok_dev // n_head
     terms = jnp.dot(attended, w_out, preferred_element_type=jnp.float32).astype(jnp.bfloat16)
     terms = lax.all_to_all(terms.reshape(n_head, rows, width), "head", 0, 0, tiled=True)

time: 185 us -> 185 us (level)
  waiting for transfers between devices: 51.2 us -> 44.9 us
  blocking collectives: 43.9 us -> 48.2 us
    all_to_all x1, waiting for transfers between devices: 6.61 us -> 0.01 us  [local(): lax.all_to_all(spread, 'seq', 0, 0, tiled=True, axis_index_groups=groups)]
    all_to_all x1, blocking collectives: 43.9 us -> 48.2 us  [local(): lax.all_to_all(outgoing, ('seq', 'head'), split_axis=1, concat_axis=1, ti...]
    unnamed x44 -> x42, local copies, waits for them, and re-layouts: 4.36 us -> 5.05 us
  transfers between devices with their start and end apart: 3 -> 4, of which waited for: 3 -> 2; matrix products, arithmetic and copies ran while one was open for 9% -> 11% of each run, Pallas kernels for 0% -> 0%
where the time goes in v7:
time: 185 us; the launch traced here: 184 us
  blocking collectives  48.2 us (26%)
  waiting for transfers between devices  44.9 us (24%)
  matrix products  26.4 us (14%)
  local copies, waits for them, and re-layouts  22 us (12%)
  starting transfers between devices  18.5 us (10%)
  other arithmetic  11.5 us (6%)
  between operations  7.28 us (4%)
  Pallas kernels  5.37 us (3%)
    all_to_all x1, blocking collectives, local(): lax.all_to_all(outgoing, ('seq', 'head'), split_axis=1, concat_axis=1, ti...  48.2 us
    all_to_all x1, waiting for transfers between devices, local(): lax.all_to_all(jnp.dot(hidden, w_down[0], preferred_element_type=jnp.floa...  29.5 us
    all_to_all x1, waiting for transfers between devices, local(): lax.all_to_all(terms.reshape(n_head, rows, width), 'head', 0, 0, tiled=True)  15.3 us
    dot_general x1, matrix products, local(): jnp.dot(hidden, w_down[0], preferred_element_type=jnp.float32)  8.28 us
    all_to_all x1, starting transfers between devices, local(): lax.all_to_all(spread, 'seq', 0, 0, tiled=True, axis_index_groups=groups)  7.03 us
    all_to_all x1, starting transfers between devices, local(): lax.all_to_all(jnp.dot(hidden, w_down[0], preferred_element_type=jnp.floa...  5.91 us
    all_to_all x1, starting transfers between devices, local(): lax.all_to_all(terms.reshape(n_head, rows, width), 'head', 0, 0, tiled=True)  5.48 us
    pallas_call x1, Pallas kernels, attend(): pl.pallas_call(kernel, grid_spec=spec, out_shape=jax.ShapeDtypeStruct((to...  5.37 us
  transfers between devices with their start and end apart: 4, of which 2 were waited for; matrix products, arithmetic and copies ran while one was open for 11% of the time, Pallas kernels for 0%

profile of v7, /device:TPU:0, one launch (start us, length us, event | category | flops | bytes accessed | tf_op | source)
XLA Modules:
  0.0 184.2 jit_solution(2161375633483900019)
XLA Ops:
  0.0 0.0 copy-start
  0.0 1.7 fusion.10
  1.7 0.0 copy-start.10
  1.7 0.0 copy-start.11
  1.7 2.0 %multiply_reduce_fusion.2 = (f32[256]{0:T(256)S(1)}, f32[256,128]{0,1:T(8,128)S(1)}) fusion(bf16[2048,512]{1,0:T(8,128)(2,1)} %param.18, s32[]{:T(128)S(6)} %select_n.46, bf16[256,2048]{1,0:T(8,128)(2,1)} %param.15, f32[2048]{0:T(1024)} %param.16, f32[256]{0:T(256)S(1)} %add_rsqrt_fusion.2), kind=kOutput, calls=%fused_computation.47 | convolution fusion | flops 136380160 | bytes 1714180 | tf_op jit(solution)/shard_map/dot_general | solution.py:151
  3.8 0.2 reduce-window.18
  3.9 0.1 convert_reduce_fusion.1
  4.0 0.1 select_reduce_fusion.1
  4.1 0.0 copy-done.14
  4.1 1.9 %fusion.15 = bf16[1,256,128]{1,2,0:T(8,128)(2,1)S(1)} fusion(bf16[2048,512]{1,0:T(8,128)(2,1)} %param.19, s32[]{:T(128)S(6)} %select_n.46, bf16[256,2048]{1,0:T(8,128)(2,1)} %param.15, f32[2048]{0:T(1024)S(1)} %copy-done.14, f32[256]{0:T(256)S(1)} %add_rsqrt_fusion.2), kind=kOutput, calls=%fused_computation.19 | convolution fusion | flops 136347648 | bytes 1647620 | tf_op jit(solution)/shard_map/dot_general | solution.py:155
  6.1 0.1 multiply_multiply_fusion.1
  6.2 0.3 fusion.29
  6.5 0.1 copy.102
  6.7 1.2 broadcast_in_dim.24
  7.9 7.0 %all-to-all-start = ((bf16[8,2,256,128]{3,2,1,0:T(8,128)(2,1)}), bf16[8,2,256,128]{3,2,1,0:T(8,128)(2,1)}, u32[]{:S(2)}, u32[]{:S(2)}) async-start(bf16[8,2,256,128]{3,2,1,0:T(8,128)(2,1)} %broadcast_in_dim.24), calls=%async_computation | async-start | bytes 2097152 | tf_op jit(solution)/shard_map/all_to_all | solution.py:160
  14.9 0.0 copy-done.2
  14.9 0.6 fusion.40
  19.3 0.6 fusion.39
  23.0 0.8 copy.105
  23.8 0.7 eq.61
  24.4 0.7 eq.57
  25.1 0.1 copy.100
  25.2 0.1 copy.99
  25.3 0.0 copy-start.12
  25.3 3.5 %fusion.37 = f32[256,512]{1,0:T(8,128)} fusion(bf16[2048,512]{1,0:T(8,128)(2,1)} %param.17, bf16[256,2048]{1,0:T(8,128)(2,1)} %param.15, f32[2048]{0:T(1024)} %param.16, f32[256]{0:T(256)} %copy-done.10), kind=kOutput, calls=%fused_computation.74 | convolution fusion | flops 538968064 | bytes 3679232 | tf_op jit(solution)/shard_map/dot_general | solution.py:141
  28.8 2.0 %reshape.233 = f32[256,4,128]{2,1,0:T(4,128)} reshape(f32[256,512]{1,0:T(8,128)} %fusion.37) | data formatting | bytes 1048576 | tf_op jit(solution)/shard_map/reshape | solution.py:141
  30.8 1.4 multiply_reduce_fusion
  32.3 2.2 %multiply_multiply_fusion = f32[256,4,128]{2,1,0:T(4,128)} fusion(f32[256,4,128]{2,1,0:T(4,128)} %reshape.233, f32[128]{0:T(128)S(1)} %copy-done.12, f32[256,4]{1,0:T(8,128)S(1)} %add_rsqrt_fusion), kind=kLoop, calls=%fused_computation.28 | loop fusion | flops 262144 | bytes 1053184 | tf_op jit(solution)/shard_map/mul | solution.py:22
  34.5 0.0 all-to-all-done.own_ref
  34.5 0.1 collective-permute-start
  34.6 1.7 subtract_convert_fusion
  36.3 0.4 pad_maximum_fusion
  36.7 0.8 copy.123
  37.4 0.0 copy-done.3
  37.4 1.0 copy.120
  38.5 1.0 copy.118
  39.5 0.1 copy.107
  39.7 0.7 stack.30.bounds_ref
  40.3 0.2 fusion.22
  40.5 0.0 collective-permute-done.other_ref
  40.6 5.4 %shard_map.145 = bf16[256,512]{1,0:T(8,128)(2,1)} custom-call(s32[5]{0:T(128)} %stack.30.bounds_ref, bf16[256,512]{1,0:T(8,128)(2,1)} %bitcast.82, bf16[8,2,256,128]{3,2,1,0:T(8,128)(2,1)} %all-to-all-done.own_ref, bf16[8,2,256,128]{3,2,1,0:T(8,128)(2,1)} %collective-permute-done.other_ref, s32[1024,1]{1,0:T(8,128)} %bitcast.80, s32[1024,1]{1,0:T(8,128)} %bitcast.79), custom_call_target="tpu_custom_call" | custom-call | tf_op jit(solution)/shard_map/pallas_call | solution.py:97
  45.9 3.4 %convolution_convert_fusion.1 = bf16[256,2048]{1,0:T(8,128)(2,1)} fusion(bf16[256,512]{1,0:T(8,128)(2,1)} %shard_map.145, bf16[512,2048]{1,0:T(8,128)(2,1)} %param.22), kind=kOutput, calls=%fused_computation.10 | convolution fusion | flops 537395200 | bytes 3407872 | tf_op jit(solution)/shard_map/dot_general | solution.py:170
  49.3 5.5 %all-to-all-start.1 = ((bf16[8,32,2048]{2,1,0:T(8,128)(2,1)}), bf16[8,32,2048]{2,1,0:T(8,128)(2,1)}, u32[]{:S(2)}, u32[]{:S(2)}) async-start(bf16[8,32,2048]{2,1,0:T(8,128)(2,1)} %bitcast.75), calls=%async_computation.1 | async-start | bytes 2097152 | tf_op jit(solution)/shard_map/all_to_all | solution.py:171
  54.9 0.2 fusion.24
  55.1 0.1 mul.209
  55.2 0.2 fusion.18
  55.4 15.3 %all-to-all-done.1 = bf16[8,32,2048]{2,1,0:T(8,128)(2,1)} async-done(((bf16[8,32,2048]{2,1,0:T(8,128)(2,1)}), bf16[8,32,2048]{2,1,0:T(8,128)(2,1)}, u32[]{:S(2)}, u32[]{:S(2)}) %all-to-all-start.1) | async-done | bytes 1048608 | tf_op jit(solution)/shard_map/all_to_all | solution.py:171
  70.8 1.4 convert_reduce_fusion
  72.2 1.1 multiply_reduce_fusion.1
  73.3 1.7 convolution_convert_fusion
  74.9 1.6 copy.111
  76.6 48.2 %all_to_all.20 = bf16[4,128,2048]{2,0,1:T(4,128)(2,1)S(1)} all-to-all(bf16[4,128,2048]{2,0,1:T(4,128)(2,1)S(1)} %copy.111), channel_id=1, replica_groups=mesh['seq'=16,'head'=8] {'seq','head'}, dimensions={1} | all-to-all | bytes 4194304 | tf_op jit(solution)/shard_map/all_to_all | solution.py:187
  124.8 1.2 copy.112
  126.0 0.0 copy-start.1
  126.0 1.3 copy-done.1
  127.3 3.0 %fusion.4 = f32[512,768]{1,0:T(8,128)} fusion(bf16[512,2048]{1,0:T(8,128)(2,1)S(1)} %bitcast.76, bf16[1,2048,768]{2,1,0:T(8,128)(2,1)S(1)} %copy-done.13), kind=kOutput, calls=%fused_computation.4 | convolution fusion | flops 1610612736 | bytes 6815744 | tf_op jit(solution)/shard_map/dot_general | solution.py:189
  130.2 8.3 %fusion.6 = bf16[512,2048]{1,0:T(8,128)(2,1)} fusion(bf16[1,768,2048]{2,1,0:T(8,128)(2,1)S(1)} %copy-done, f32[512,768]{1,0:T(8,128)} %fusion.4, bf16[512,2048]{1,0:T(8,128)(2,1)} %bitcast.77, bf16[1,2048,768]{2,1,0:T(8,128)(2,1)} %param.28), kind=kOutput, calls=%fused_computation.6 | convolution fusion | flops 3224633344 | bytes 12058624 | tf_op jit(solution)/shard_map/dot_general | solution.py:193
  138.5 4.5 %copy.113 = bf16[4,128,2048]{2,0,1:T(4,128)(2,1)} copy(bf16[4,128,2048]{2,1,0:T(8,128)(2,1)} %bitcast.78) | data formatting | bytes 4194304 | tf_op jit(solution)/shard_map/reshape | solution.py:195
  143.0 5.9 %all-to-all-start.3 = ((bf16[4,128,2048]{2,0,1:T(4,128)(2,1)}), bf16[4,128,2048]{2,0,1:T(4,128)(2,1)}, u32[]{:S(2)}, u32[]{:S(2)}) async-start(bf16[4,128,2048]{2,0,1:T(4,128)(2,1)} %copy.113), calls=%async_computation.3 | async-start | bytes 4194304 | tf_op jit(solution)/shard_map/all_to_all | solution.py:192
  149.0 0.1 copy.110
  149.0 0.2 select_reduce_fusion
  149.3 29.5 %all-to-all-done.3 = bf16[4,128,2048]{2,0,1:T(4,128)(2,1)} async-done(((bf16[4,128,2048]{2,0,1:T(4,128)(2,1)}), bf16[4,128,2048]{2,0,1:T(4,128)(2,1)}, u32[]{:S(2)}, u32[]{:S(2)}) %all-to-all-start.3) | async-done | bytes 2097184 | tf_op jit(solution)/shard_map/all_to_all | solution.py:192
  178.8 2.7 %copy.114 = bf16[4,128,2048]{2,1,0:T(8,128)(2,1)S(1)} copy(bf16[4,128,2048]{2,0,1:T(4,128)(2,1)} %all-to-all-done.3) | data formatting | bytes 4194304 | tf_op jit(solution)/shard_map/all_to_all | solution.py:192
  181.5 2.7 %fusion.9 = bf16[32,2048]{1,0:T(8,128)(2,1)} fusion(f32[32,512]{1,0:T(8,128)S(1)} %select_reduce_fusion, bf16[512,2048]{1,0:T(8,128)(2,1)S(1)} %bitcast.73, f32[32,2048]{1,0:T(8,128)S(1)} %convert_reduce_fusion, bf16[256,2048]{1,0:T(8,128)(2,1)} %param.15, s32[]{:T(128)S(6)} %select_n.38), kind=kOutput, calls=%fused_computation.12 | convolution fusion | flops 402915328 | bytes 2686980 | tf_op jit(solution)/shard_map/dot_general | solution.py:202
  (44 shorter events, 0.2 us)
Async XLA Ops:
  0.0 130.2 %copy-start = (bf16[1,768,2048]{2,1,0:T(8,128)(2,1)S(1)}, bf16[1,768,2048]{2,1,0:T(8,128)(2,1)}, u32[]{:S(2)}) copy-start(bf16[1,768,2048]{2,1,0:T(8,128)(2,1)} %param.29) | copy-start | bytes 9437188
  0.0 4.1 %copy-start.14 = (f32[2048]{0:T(1024)S(1)}, f32[2048]{0:T(1024)}, u32[]{:S(2)}) copy-start(f32[2048]{0:T(1024)} %param.16) | copy-start | bytes 24580
  0.0 3.7 %copy-start.15 = (s32[6]{0:T(128)S(1)}, s32[6]{0:T(128)}, u32[]{:S(2)}) copy-start(s32[6]{0:T(128)} %param.24) | copy-start | bytes 76
  1.7 4.4 %copy-start.10 = (f32[256]{0:T(256)}, f32[256]{0:T(256)S(1)}, u32[]{:S(2)}) copy-start(f32[256]{0:T(256)S(1)} %add_rsqrt_fusion.2) | copy-start | bytes 3076
  1.7 4.4 %copy-start.11 = (f32[128]{0:T(128)S(1)}, f32[128]{0:T(128)}, u32[]{:S(2)}) copy-start(f32[128]{0:T(128)} %param.21) | copy-start | bytes 1540
  3.7 15.6 %copy-start.4 = (s32[256]{0:T(256)}, s32[256]{0:T(256)S(1)}, u32[]{:S(2)}) copy-start(s32[256]{0:T(256)S(1)} %iota_add_fusion) | copy-start | bytes 3076
  4.1 10.8 %copy-start.2 = (s32[256]{0:T(256)}, s32[256]{0:T(256)S(1)}, u32[]{:S(2)}) copy-start(s32[256]{0:T(256)S(1)} %select_reduce_fusion.1) | copy-start | bytes 3076
  7.9 26.6 %all-to-all-start = ((bf16[8,2,256,128]{3,2,1,0:T(8,128)(2,1)}), bf16[8,2,256,128]{3,2,1,0:T(8,128)(2,1)}, u32[]{:S(2)}, u32[]{:S(2)}) async-start(bf16[8,2,256,128]{3,2,1,0:T(8,128)(2,1)} %broadcast_in_dim.24), calls=%async_computation | async-start | bytes 2097152 | tf_op jit(solution)/shard_map/all_to_all | solution.py:160
  25.3 7.0 %copy-start.12 = (f32[128]{0:T(128)S(1)}, f32[128]{0:T(128)}, u32[]{:S(2)}) copy-start(f32[128]{0:T(128)} %param.20) | copy-start | bytes 1540
  32.3 5.1 %copy-start.3 = (s32[256]{0:T(256)S(1)}, s32[256]{0:T(256)}, u32[]{:S(2)}) copy-start(s32[256]{0:T(256)} %copy-done.2) | copy-start | bytes 3076
  34.5 4.0 %copy-start.5 = (s32[256]{0:T(256)S(1)}, s32[256]{0:T(256)}, u32[]{:S(2)}) copy-start(s32[256]{0:T(256)} %copy-done.4) | copy-start | bytes 3076
  34.5 5.0 %copy-start.8 = (s32[2,128]{1,0:T(2,128)S(1)}, s32[2,128]{1,0:T(2,128)}, u32[]{:S(2)}) copy-start(s32[2,128]{1,0:T(2,128)} %eq.61) | copy-start | bytes 3076
  34.5 6.0 %collective-permute-start = (bf16[8,2,256,128]{3,2,1,0:T(8,128)(2,1)}, bf16[8,2,256,128]{3,2,1,0:T(8,128)(2,1)}, u32[]{:S(2)}, u32[]{:S(2)}) collective-permute-start(bf16[8,2,256,128]{3,2,1,0:T(8,128)(2,1)} %all-to-all-done.own_ref), channel_id=1, source_target_pairs={{0,8},{8,0},{16,24},{24,16},{32,40},{40,32},{48,56},{56,48},{64,72... | collective-permute-start | bytes 3145736 | tf_op jit(solution)/shard_map/ppermute | solution.py:161
  49.3 5.6 %copy-start.7 = (s32[256]{0:T(256)S(1)}, s32[256]{0:T(256)}, u32[]{:S(2)}) copy-start(s32[256]{0:T(256)} %eq.57) | copy-start | bytes 3076
  49.3 23.9 %copy-start.6 = (f32[2048]{0:T(1024)S(1)}, f32[2048]{0:T(1024)}, u32[]{:S(2)}) copy-start(f32[2048]{0:T(1024)} %param.23) | copy-start | bytes 24580
  49.3 21.5 %all-to-all-start.1 = ((bf16[8,32,2048]{2,1,0:T(8,128)(2,1)}), bf16[8,32,2048]{2,1,0:T(8,128)(2,1)}, u32[]{:S(2)}, u32[]{:S(2)}) async-start(bf16[8,32,2048]{2,1,0:T(8,128)(2,1)} %bitcast.75), calls=%async_computation.1 | async-start | bytes 2097152 | tf_op jit(solution)/shard_map/all_to_all | solution.py:171
  124.8 2.5 %copy-start.13 = (bf16[1,2048,768]{2,1,0:T(8,128)(2,1)S(1)}, bf16[1,2048,768]{2,1,0:T(8,128)(2,1)}, u32[]{:S(2)}) copy-start(bf16[1,2048,768]{2,1,0:T(8,128)(2,1)} %param.27) | copy-start | bytes 9437188
  126.0 1.3 copy-start.1
  143.0 5.9 %copy-start.9 = (f32[32,8]{0,1:T(8,128)S(1)}, f32[32,8]{0,1:T(8,128)}, u32[]{:S(2)}) copy-start(f32[32,8]{0,1:T(8,128)} %param.26) | copy-start | bytes 3076
  143.0 35.7 %all-to-all-start.3 = ((bf16[4,128,2048]{2,0,1:T(4,128)(2,1)}), bf16[4,128,2048]{2,0,1:T(4,128)(2,1)}, u32[]{:S(2)}, u32[]{:S(2)}) async-start(bf16[4,128,2048]{2,0,1:T(4,128)(2,1)} %copy.113), calls=%async_computation.3 | async-start | bytes 4194304 | tf_op jit(solution)/shard_map/all_to_all | solution.py:192

commit v8 on v7

--- a/solution.py
+++ b/solution.py
@@ -158,6 +158,7 @@
     groups = [[2 * i + c for i in range(pairs)] for c in range(2)]
     spread = jnp.broadcast_to(stacked[None], (pairs,) + stacked.shape)
     same_core = lax.all_to_all(spread, "seq", 0, 0, tiled=True, axis_index_groups=groups)
+    queries, same_core = lax.optimization_barrier((queries, same_core))
     other_core = lax.ppermute(same_core, "seq", [(i, i ^ 1) for i in range(n_seq)])
     block = tok_dev
     low = own_start[0] // block

time: 185 us -> 188 us (1.016)
  waiting for transfers between devices: 44.9 us -> 50.4 us
  blocking collectives: 48.2 us -> 44.1 us
    all_to_all x1, waiting for transfers between devices: 0.01 us -> 5.62 us  [local(): lax.all_to_all(spread, 'seq', 0, 0, tiled=True, axis_index_groups=groups)]
    all_to_all x1, blocking collectives: 48.2 us -> 44.1 us  [local(): lax.all_to_all(outgoing, ('seq', 'head'), split_axis=1, concat_axis=1, ti...]
    unnamed x42 -> x36, local copies, waits for them, and re-layouts: 5.05 us -> 5.68 us
  transfers between devices with their start and end apart: 4 -> 4, of which waited for: 2 -> 3; matrix products, arithmetic and copies ran while one was open for 11% -> 11% of each run, Pallas kernels for 0% -> 0%
where the time goes in v8:
time: 188 us; the launch traced here: 187 us
  waiting for transfers between devices  50.4 us (27%)
  blocking collectives  44.1 us (23%)
  matrix products  26.5 us (14%)
  local copies, waits for them, and re-layouts  23.6 us (13%)
  starting transfers between devices  18.4 us (10%)
  other arithmetic  11 us (6%)
  between operations  7.23 us (4%)
  Pallas kernels  5.4 us (3%)
    all_to_all x1, blocking collectives, local(): lax.all_to_all(outgoing, ('seq', 'head'), split_axis=1, concat_axis=1, ti...  44.1 us
    all_to_all x1, waiting for transfers between devices, local(): lax.all_to_all(jnp.dot(hidden, w_down[0], preferred_element_type=jnp.floa...  29.5 us
    all_to_all x1, waiting for transfers between devices, local(): lax.all_to_all(terms.reshape(n_head, rows, width), 'head', 0, 0, tiled=True)  15.3 us
    dot_general x1, matrix products, local(): jnp.dot(hidden, w_down[0], preferred_element_type=jnp.float32)  8.29 us
    all_to_all x1, starting transfers between devices, local(): lax.all_to_all(spread, 'seq', 0, 0, tiled=True, axis_index_groups=groups)  7.03 us
    all_to_all x1, starting transfers between devices, local(): lax.all_to_all(jnp.dot(hidden, w_down[0], preferred_element_type=jnp.floa...  5.91 us
    unnamed x36, local copies, waits for them, and re-layouts  5.68 us
    all_to_all x1, waiting for transfers between devices, local(): lax.all_to_all(spread, 'seq', 0, 0, tiled=True, axis_index_groups=groups)  5.62 us
  transfers between devices with their start and end apart: 4, of which 3 were waited for; matrix products, arithmetic and copies ran while one was open for 11% of the time, Pallas kernels for 0%

profile of v8, /device:TPU:0, one launch (start us, length us, event | category | flops | bytes accessed | tf_op | source)
XLA Modules:
  0.0 186.7 jit_solution(10353722557107318356)
XLA Ops:
  0.0 1.7 fusion.10
  1.7 0.0 copy-start.8
  1.7 2.0 %multiply_reduce_fusion.2 = (f32[256]{0:T(256)S(1)}, f32[256,128]{0,1:T(8,128)S(1)}) fusion(bf16[2048,512]{1,0:T(8,128)(2,1)} %param.18, s32[]{:T(128)S(6)} %select_n.46, bf16[256,2048]{1,0:T(8,128)(2,1)} %param.15, f32[2048]{0:T(1024)} %param.16, f32[256]{0:T(256)S(1)} %add_rsqrt_fusion.2), kind=kOutput, calls=%fused_computation.47 | convolution fusion | flops 136380160 | bytes 1714180 | tf_op jit(solution)/shard_map/dot_general | solution.py:151
  3.7 0.2 reduce-window.18
  3.9 0.1 convert_reduce_fusion.1
  4.0 0.1 select_reduce_fusion.1
  4.1 0.0 copy-done.11
  4.1 1.9 %fusion.15 = bf16[1,256,128]{1,2,0:T(8,128)(2,1)S(1)} fusion(bf16[2048,512]{1,0:T(8,128)(2,1)} %param.19, s32[]{:T(128)S(6)} %select_n.46, bf16[256,2048]{1,0:T(8,128)(2,1)} %param.15, f32[2048]{0:T(1024)S(1)} %copy-done.11, f32[256]{0:T(256)S(1)} %add_rsqrt_fusion.2), kind=kOutput, calls=%fused_computation.19 | convolution fusion | flops 136347648 | bytes 1647620 | tf_op jit(solution)/shard_map/dot_general | solution.py:155
  6.1 0.0 copy-done.8
  6.1 0.1 multiply_multiply_fusion.1
  6.2 1.0 fusion.29
  7.1 0.1 copy.102
  7.3 1.2 broadcast_in_dim.24
  8.5 7.0 %all-to-all-start = ((bf16[8,2,256,128]{3,2,1,0:T(8,128)(2,1)}), bf16[8,2,256,128]{3,2,1,0:T(8,128)(2,1)}, u32[]{:S(2)}, u32[]{:S(2)}) async-start(bf16[8,2,256,128]{3,2,1,0:T(8,128)(2,1)} %broadcast_in_dim.24), calls=%async_computation | async-start | bytes 2097152 | tf_op jit(solution)/shard_map/all_to_all | solution.py:160
  15.6 3.5 %fusion.37 = f32[256,512]{1,0:T(8,128)} fusion(bf16[2048,512]{1,0:T(8,128)(2,1)} %param.17, bf16[256,2048]{1,0:T(8,128)(2,1)} %param.15, f32[2048]{0:T(1024)S(1)} %copy-done.11, f32[256]{0:T(256)S(1)} %add_rsqrt_fusion.2), kind=kOutput, calls=%fused_computation.74 | convolution fusion | flops 538968064 | bytes 3679232 | tf_op jit(solution)/shard_map/dot_general | solution.py:141
  19.1 2.0 %reshape.233 = f32[256,4,128]{2,1,0:T(4,128)} reshape(f32[256,512]{1,0:T(8,128)} %fusion.37) | data formatting | bytes 1048576 | tf_op jit(solution)/shard_map/reshape | solution.py:141
  21.1 1.4 multiply_reduce_fusion
  22.5 0.0 copy-done.2
  22.5 0.1 copy.100
  22.6 0.9 copy.99
  23.6 0.0 copy-start.6
  23.6 1.4 multiply_multiply_fusion
  25.0 0.5 subtract_convert_fusion
  25.5 0.4 pad_maximum_fusion
  25.9 5.6 %all-to-all-done.own_ref = bf16[8,2,256,128]{3,2,1,0:T(8,128)(2,1)} async-done(((bf16[8,2,256,128]{3,2,1,0:T(8,128)(2,1)}), bf16[8,2,256,128]{3,2,1,0:T(8,128)(2,1)}, u32[]{:S(2)}, u32[]{:S(2)}) %all-to-all-start) | async-done | bytes 1048608 | tf_op jit(solution)/shard_map/all_to_all | solution.py:160
  31.5 0.0 collective-permute-start
  31.5 0.6 fusion.40
  35.9 0.6 fusion.39
  39.6 0.1 copy.105
  39.7 0.1 eq.61
  39.8 0.7 eq.57
  40.5 0.7 broadcast_bitcast_fusion
  41.1 1.0 copy.120
  42.2 0.7 broadcast_bitcast_fusion.1
  42.9 1.0 copy.118
  43.9 0.7 copy.107
  44.6 0.7 stack.30.bounds_ref
  45.3 1.0 fusion.22
  46.4 0.7 copy.123
  47.1 0.0 collective-permute-done.other_ref
  47.1 5.4 %shard_map.145 = bf16[256,512]{1,0:T(8,128)(2,1)} custom-call(s32[5]{0:T(128)} %stack.30.bounds_ref, bf16[256,512]{1,0:T(8,128)(2,1)} %bitcast.82, bf16[8,2,256,128]{3,2,1,0:T(8,128)(2,1)} %all-to-all-done.own_ref, bf16[8,2,256,128]{3,2,1,0:T(8,128)(2,1)} %collective-permute-done.other_ref, s32[1024,1]{1,0:T(8,128)} %bitcast.80, s32[1024,1]{1,0:T(8,128)} %bitcast.79), custom_call_target="tpu_custom_call" | custom-call | tf_op jit(solution)/shard_map/pallas_call | solution.py:97
  52.5 3.4 %convolution_convert_fusion.1 = bf16[256,2048]{1,0:T(8,128)(2,1)} fusion(bf16[256,512]{1,0:T(8,128)(2,1)} %shard_map.145, bf16[512,2048]{1,0:T(8,128)(2,1)} %param.22), kind=kOutput, calls=%fused_computation.10 | convolution fusion | flops 537395200 | bytes 3407872 | tf_op jit(solution)/shard_map/dot_general | solution.py:171
  55.9 5.5 %all-to-all-start.1 = ((bf16[8,32,2048]{2,1,0:T(8,128)(2,1)}), bf16[8,32,2048]{2,1,0:T(8,128)(2,1)}, u32[]{:S(2)}, u32[]{:S(2)}) async-start(bf16[8,32,2048]{2,1,0:T(8,128)(2,1)} %bitcast.75), calls=%async_computation.1 | async-start | bytes 2097152 | tf_op jit(solution)/shard_map/all_to_all | solution.py:172
  61.5 0.2 fusion.24
  61.7 0.1 mul.209
  61.8 0.2 fusion.18
  62.0 15.3 %all-to-all-done.1 = bf16[8,32,2048]{2,1,0:T(8,128)(2,1)} async-done(((bf16[8,32,2048]{2,1,0:T(8,128)(2,1)}), bf16[8,32,2048]{2,1,0:T(8,128)(2,1)}, u32[]{:S(2)}, u32[]{:S(2)}) %all-to-all-start.1) | async-done | bytes 1048608 | tf_op jit(solution)/shard_map/all_to_all | solution.py:172
  77.3 1.4 convert_reduce_fusion
  78.7 1.1 multiply_reduce_fusion.1
  79.8 1.7 convolution_convert_fusion
  81.5 1.6 copy.111
  83.1 44.1 %all_to_all.20 = bf16[4,128,2048]{2,0,1:T(4,128)(2,1)S(1)} all-to-all(bf16[4,128,2048]{2,0,1:T(4,128)(2,1)S(1)} %copy.111), channel_id=1, replica_groups=mesh['seq'=16,'head'=8] {'seq','head'}, dimensions={1} | all-to-all | bytes 4194304 | tf_op jit(solution)/shard_map/all_to_all | solution.py:188
  127.3 1.2 copy.112
  128.4 0.0 copy-start.1
  128.4 1.3 copy-done.1
  129.7 3.0 %fusion.4 = f32[512,768]{1,0:T(8,128)} fusion(bf16[512,2048]{1,0:T(8,128)(2,1)S(1)} %bitcast.76, bf16[1,2048,768]{2,1,0:T(8,128)(2,1)S(1)} %copy-done.10), kind=kOutput, calls=%fused_computation.4 | convolution fusion | flops 1610612736 | bytes 6815744 | tf_op jit(solution)/shard_map/dot_general | solution.py:190
  132.7 8.3 %fusion.6 = bf16[512,2048]{1,0:T(8,128)(2,1)} fusion(bf16[1,768,2048]{2,1,0:T(8,128)(2,1)S(1)} %copy-done, f32[512,768]{1,0:T(8,128)} %fusion.4, bf16[512,2048]{1,0:T(8,128)(2,1)} %bitcast.77, bf16[1,2048,768]{2,1,0:T(8,128)(2,1)} %param.28), kind=kOutput, calls=%fused_computation.6 | convolution fusion | flops 3224633344 | bytes 12058624 | tf_op jit(solution)/shard_map/dot_general | solution.py:194
  141.0 4.5 %copy.113 = bf16[4,128,2048]{2,0,1:T(4,128)(2,1)} copy(bf16[4,128,2048]{2,1,0:T(8,128)(2,1)} %bitcast.78) | data formatting | bytes 4194304 | tf_op jit(solution)/shard_map/reshape | solution.py:196
  145.5 5.9 %all-to-all-start.3 = ((bf16[4,128,2048]{2,0,1:T(4,128)(2,1)}), bf16[4,128,2048]{2,0,1:T(4,128)(2,1)}, u32[]{:S(2)}, u32[]{:S(2)}) async-start(bf16[4,128,2048]{2,0,1:T(4,128)(2,1)} %copy.113), calls=%async_computation.3 | async-start | bytes 4194304 | tf_op jit(solution)/shard_map/all_to_all | solution.py:193
  151.4 0.1 copy.110
  151.5 0.2 select_reduce_fusion
  151.7 29.5 %all-to-all-done.3 = bf16[4,128,2048]{2,0,1:T(4,128)(2,1)} async-done(((bf16[4,128,2048]{2,0,1:T(4,128)(2,1)}), bf16[4,128,2048]{2,0,1:T(4,128)(2,1)}, u32[]{:S(2)}, u32[]{:S(2)}) %all-to-all-start.3) | async-done | bytes 2097184 | tf_op jit(solution)/shard_map/all_to_all | solution.py:193
  181.2 2.7 %copy.114 = bf16[4,128,2048]{2,1,0:T(8,128)(2,1)S(1)} copy(bf16[4,128,2048]{2,0,1:T(4,128)(2,1)} %all-to-all-done.3) | data formatting | bytes 4194304 | tf_op jit(solution)/shard_map/all_to_all | solution.py:193
  184.0 2.7 %fusion.9 = bf16[32,2048]{1,0:T(8,128)(2,1)} fusion(f32[32,512]{1,0:T(8,128)S(1)} %select_reduce_fusion, bf16[512,2048]{1,0:T(8,128)(2,1)S(1)} %bitcast.73, f32[32,2048]{1,0:T(8,128)S(1)} %convert_reduce_fusion, bf16[256,2048]{1,0:T(8,128)(2,1)} %param.15, s32[]{:T(128)S(6)} %select_n.38), kind=kOutput, calls=%fused_computation.12 | convolution fusion | flops 402915328 | bytes 2686980 | tf_op jit(solution)/shard_map/dot_general | solution.py:203
  (38 shorter events, 0.2 us)
Async XLA Ops:
  0.0 132.7 %copy-start = (bf16[1,768,2048]{2,1,0:T(8,128)(2,1)S(1)}, bf16[1,768,2048]{2,1,0:T(8,128)(2,1)}, u32[]{:S(2)}) copy-start(bf16[1,768,2048]{2,1,0:T(8,128)(2,1)} %param.29) | copy-start | bytes 9437188
  0.0 4.1 %copy-start.11 = (f32[2048]{0:T(1024)S(1)}, f32[2048]{0:T(1024)}, u32[]{:S(2)}) copy-start(f32[2048]{0:T(1024)} %param.16) | copy-start | bytes 24580
  0.0 3.7 %copy-start.12 = (s32[6]{0:T(128)S(1)}, s32[6]{0:T(128)}, u32[]{:S(2)}) copy-start(s32[6]{0:T(128)} %param.24) | copy-start | bytes 76
  1.7 4.3 %copy-start.8 = (f32[128]{0:T(128)S(1)}, f32[128]{0:T(128)}, u32[]{:S(2)}) copy-start(f32[128]{0:T(128)} %param.21) | copy-start | bytes 1540
  3.7 32.1 %copy-start.4 = (s32[256]{0:T(256)}, s32[256]{0:T(256)S(1)}, u32[]{:S(2)}) copy-start(s32[256]{0:T(256)S(1)} %iota_add_fusion) | copy-start | bytes 3076
  4.1 27.4 %copy-start.3 = (s32[256]{0:T(256)}, s32[256]{0:T(256)S(1)}, u32[]{:S(2)}) copy-start(s32[256]{0:T(256)S(1)} %select_reduce_fusion.1) | copy-start | bytes 3076
  8.5 23.0 %all-to-all-start = ((bf16[8,2,256,128]{3,2,1,0:T(8,128)(2,1)}), bf16[8,2,256,128]{3,2,1,0:T(8,128)(2,1)}, u32[]{:S(2)}, u32[]{:S(2)}) async-start(bf16[8,2,256,128]{3,2,1,0:T(8,128)(2,1)} %broadcast_in_dim.24), calls=%async_computation | async-start | bytes 2097152 | tf_op jit(solution)/shard_map/all_to_all | solution.py:160
  15.5 6.9 %copy-start.2 = (f32[256,64]{0,1:T(8,128)S(1)}, f32[256,64]{0,1:T(8,128)}, u32[]{:S(2)}) copy-start(f32[256,64]{0,1:T(8,128)} %get-tuple-element.13) | copy-start | bytes 196612
  19.1 4.5 %copy-start.9 = (f32[128]{0:T(128)S(1)}, f32[128]{0:T(128)}, u32[]{:S(2)}) copy-start(f32[128]{0:T(128)} %param.20) | copy-start | bytes 1540
  23.6 16.0 %copy-start.6 = (s32[32,8]{0,1:T(8,128)S(1)}, s32[32,8]{0,1:T(8,128)}, u32[]{:S(2)}) copy-start(s32[32,8]{0,1:T(8,128)} %param.25) | copy-start | bytes 3076
  31.5 15.6 %collective-permute-start = (bf16[8,2,256,128]{3,2,1,0:T(8,128)(2,1)}, bf16[8,2,256,128]{3,2,1,0:T(8,128)(2,1)}, u32[]{:S(2)}, u32[]{:S(2)}) collective-permute-start(bf16[8,2,256,128]{3,2,1,0:T(8,128)(2,1)} %all-to-all-done.own_ref), channel_id=1, source_target_pairs={{0,8},{8,0},{16,24},{24,16},{32,40},{40,32},{48,56},{56,48},{64,72... | collective-permute-start | bytes 3145736 | tf_op jit(solution)/shard_map/ppermute | solution.py:162
  55.9 5.6 %copy-start.5 = (s32[256]{0:T(256)S(1)}, s32[256]{0:T(256)}, u32[]{:S(2)}) copy-start(s32[256]{0:T(256)} %eq.57) | copy-start | bytes 3076
  55.9 21.4 %all-to-all-start.1 = ((bf16[8,32,2048]{2,1,0:T(8,128)(2,1)}), bf16[8,32,2048]{2,1,0:T(8,128)(2,1)}, u32[]{:S(2)}, u32[]{:S(2)}) async-start(bf16[8,32,2048]{2,1,0:T(8,128)(2,1)} %bitcast.75), calls=%async_computation.1 | async-start | bytes 2097152 | tf_op jit(solution)/shard_map/all_to_all | solution.py:172
  127.3 2.5 %copy-start.10 = (bf16[1,2048,768]{2,1,0:T(8,128)(2,1)S(1)}, bf16[1,2048,768]{2,1,0:T(8,128)(2,1)}, u32[]{:S(2)}) copy-start(bf16[1,2048,768]{2,1,0:T(8,128)(2,1)} %param.27) | copy-start | bytes 9437188
  128.4 1.3 copy-start.1
  145.5 5.9 %copy-start.7 = (f32[32,8]{0,1:T(8,128)S(1)}, f32[32,8]{0,1:T(8,128)}, u32[]{:S(2)}) copy-start(f32[32,8]{0,1:T(8,128)} %param.26) | copy-start | bytes 3076
  145.5 35.7 %all-to-all-start.3 = ((bf16[4,128,2048]{2,0,1:T(4,128)(2,1)}), bf16[4,128,2048]{2,0,1:T(4,128)(2,1)}, u32[]{:S(2)}, u32[]{:S(2)}) async-start(bf16[4,128,2048]{2,0,1:T(4,128)(2,1)} %copy.113), calls=%async_computation.3 | async-start | bytes 4194304 | tf_op jit(solution)/shard_map/all_to_all | solution.py:193

commit v9 on v7

--- a/solution.py
+++ b/solution.py
@@ -80,23 +80,24 @@
 
 
 def attend(bounds, queries, own, other, qpos, qstart):
-    tok, heads, dim = queries.shape
+    tok, width = queries.shape
+    dim = own.shape[-1]
     kernel = functools.partial(_attend_kernel, dim=dim)
     spec = pltpu.PrefetchScalarGridSpec(
         num_scalar_prefetch=1,
         grid=(1,),
         in_specs=[
-            pl.BlockSpec((tok, heads * dim), lambda i, b: (0, 0)),
+            pl.BlockSpec((tok, width), lambda i, b: (0, 0)),
             pl.BlockSpec(own.shape, lambda i, b: (0, 0, 0, 0)),
             pl.BlockSpec(other.shape, lambda i, b: (0, 0, 0, 0)),
-            pl.BlockSpec((heads * tok, 1), lambda i, b: (0, 0)),
-            pl.BlockSpec((heads * tok, 1), lambda i, b: (0, 0)),
+            pl.BlockSpec(qpos.shape, lambda i, b: (0, 0)),
+            pl.BlockSpec(qstart.shape, lambda i, b: (0, 0)),
         ],
-        out_specs=pl.BlockSpec((tok, heads * dim), lambda i, b: (0, 0)),
+        out_specs=pl.BlockSpec((tok, width), lambda i, b: (0, 0)),
     )
     return pl.pallas_call(
-        kernel, grid_spec=spec, out_shape=jax.ShapeDtypeStruct((tok, heads * dim), jnp.bfloat16)
-    )(bounds, queries.reshape(tok, heads * dim), own, other, jnp.tile(qpos, (heads, 1)), jnp.tile(qstart, (heads, 1)))
+        kernel, grid_spec=spec, out_shape=jax.ShapeDtypeStruct((tok, width), jnp.bfloat16)
+    )(bounds, queries, own, other, qpos, qstart)
 
 
 def local(
@@ -158,14 +159,22 @@
     groups = [[2 * i + c for i in range(pairs)] for c in range(2)]
     spread = jnp.broadcast_to(stacked[None], (pairs,) + stacked.shape)
     same_core = lax.all_to_all(spread, "seq", 0, 0, tiled=True, axis_index_groups=groups)
-    other_core = lax.ppermute(same_core, "seq", [(i, i ^ 1) for i in range(n_seq)])
     block = tok_dev
     low = own_start[0] // block
     high = positions[-1] // block + 1
     inner_low = jnp.clip(-(-own_start[-1] // block), low, high)
     inner_high = jnp.clip((positions[0] + 1) // block, inner_low, high)
     bounds = jnp.stack([low, inner_low, inner_high, high, seq_index % 2]).astype(jnp.int32)
-    attended = attend(bounds, queries, same_core, other_core, positions[:, None], own_start[:, None])
+    operands = (
+        bounds,
+        queries.reshape(tok_dev, per_dev * head_dim),
+        jnp.tile(positions[:, None], (per_dev, 1)),
+        jnp.tile(own_start[:, None], (per_dev, 1)),
+    )
+    operands, same_core = lax.optimization_barrier((operands, same_core))
+    other_core = lax.ppermute(same_core, "seq", [(i, i ^ 1) for i in range(n_seq)])
+    bounds, flat_queries, qpos, qstart = operands
+    attended = attend(bounds, flat_queries, same_core, other_core, qpos, qstart)
     rows = tok_dev // n_head
     terms = jnp.dot(attended, w_out, preferred_element_type=jnp.float32).astype(jnp.bfloat16)
     terms = lax.all_to_all(terms.reshape(n_head, rows, width), "head", 0, 0, tiled=True)

time: 185 us -> 182 us (0.984)
  local copies, waits for them, and re-layouts: 22 us -> 20.1 us
    unnamed x42 -> x28, local copies, waits for them, and re-layouts: 5.05 us -> 2.26 us
    optimization_barrier x0 -> x2, local copies, waits for them, and re-layouts: none -> 2.07 us  [local(): operands, same_core = lax.optimization_barrier((operands, same_core))]
  transfers between devices with their start and end apart: 4 -> 4, of which waited for: 2 -> 3; matrix products, arithmetic and copies ran while one was open for 11% -> 10% of each run, Pallas kernels for 0% -> 0%
where the time goes in v9:
time: 182 us; the launch traced here: 181 us
  blocking collectives  46.8 us (26%)
  waiting for transfers between devices  45.2 us (25%)
  matrix products  26.4 us (15%)
  local copies, waits for them, and re-layouts  20.1 us (11%)
  starting transfers between devices  18.4 us (10%)
  other arithmetic  11.5 us (6%)
  between operations  7.22 us (4%)
  Pallas kernels  5.37 us (3%)
    all_to_all x1, blocking collectives, local(): lax.all_to_all(outgoing, ('seq', 'head'), split_axis=1, concat_axis=1, ti...  46.8 us
    all_to_all x1, waiting for transfers between devices, local(): lax.all_to_all(jnp.dot(hidden, w_down[0], preferred_element_type=jnp.floa...  29.5 us
    all_to_all x1, waiting for transfers between devices, local(): lax.all_to_all(terms.reshape(n_head, rows, width), 'head', 0, 0, tiled=True)  15.4 us
    dot_general x1, matrix products, local(): jnp.dot(hidden, w_down[0], preferred_element_type=jnp.float32)  8.28 us
    all_to_all x1, starting transfers between devices, local(): lax.all_to_all(spread, 'seq', 0, 0, tiled=True, axis_index_groups=groups)  7.03 us
    all_to_all x1, starting transfers between devices, local(): lax.all_to_all(jnp.dot(hidden, w_down[0], preferred_element_type=jnp.floa...  5.91 us
    all_to_all x1, starting transfers between devices, local(): lax.all_to_all(terms.reshape(n_head, rows, width), 'head', 0, 0, tiled=True)  5.47 us
    pallas_call x1, Pallas kernels, attend(): pl.pallas_call(kernel, grid_spec=spec, out_shape=jax.ShapeDtypeStruct((to...  5.37 us
  transfers between devices with their start and end apart: 4, of which 3 were waited for; matrix products, arithmetic and copies ran while one was open for 10% of the time, Pallas kernels for 0%

profile of v9, /device:TPU:0, one launch (start us, length us, event | category | flops | bytes accessed | tf_op | source)
XLA Modules:
  0.0 181.1 jit_solution(2273012701427707901)
XLA Ops:
  0.0 0.0 copy-start
  0.0 1.7 fusion.10
  1.7 0.0 copy-start.5
  1.7 2.0 %multiply_reduce_fusion.2 = (f32[256]{0:T(256)S(1)}, f32[256,128]{0,1:T(8,128)S(1)}) fusion(bf16[2048,512]{1,0:T(8,128)(2,1)} %param.18, s32[]{:T(128)S(6)} %select_n.46, bf16[256,2048]{1,0:T(8,128)(2,1)} %param.15, f32[2048]{0:T(1024)} %param.16, f32[256]{0:T(256)S(1)} %add_rsqrt_fusion.2), kind=kOutput, calls=%fused_computation.47 | convolution fusion | flops 136380160 | bytes 1714180 | tf_op jit(solution)/shard_map/dot_general | solution.py:152
  3.7 0.0 copy-done.9
  3.7 0.2 reduce-window.18
  3.9 0.1 convert_reduce_fusion.1
  4.0 0.1 select_reduce_fusion.1
  4.1 0.0 copy-done.8
  4.1 1.9 %fusion.15 = bf16[1,256,128]{1,2,0:T(8,128)(2,1)S(1)} fusion(bf16[2048,512]{1,0:T(8,128)(2,1)} %param.19, s32[]{:T(128)S(6)} %select_n.46, bf16[256,2048]{1,0:T(8,128)(2,1)} %param.15, f32[2048]{0:T(1024)S(1)} %copy-done.8, f32[256]{0:T(256)S(1)} %add_rsqrt_fusion.2), kind=kOutput, calls=%fused_computation.19 | convolution fusion | flops 136347648 | bytes 1647620 | tf_op jit(solution)/shard_map/dot_general | solution.py:156
  6.1 0.1 multiply_multiply_fusion.1
  6.1 0.3 fusion.29
  6.5 0.1 copy.102
  6.6 1.2 broadcast_in_dim.24
  7.9 7.0 %all-to-all-start = ((bf16[8,2,256,128]{3,2,1,0:T(8,128)(2,1)}), bf16[8,2,256,128]{3,2,1,0:T(8,128)(2,1)}, u32[]{:S(2)}, u32[]{:S(2)}) async-start(bf16[8,2,256,128]{3,2,1,0:T(8,128)(2,1)} %broadcast_in_dim.24), calls=%async_computation | async-start | bytes 2097152 | tf_op jit(solution)/shard_map/all_to_all | solution.py:161
  14.9 0.6 fusion.40
  19.2 0.0 copy-start.6
  19.3 3.5 %fusion.37 = f32[256,512]{1,0:T(8,128)} fusion(bf16[2048,512]{1,0:T(8,128)(2,1)} %param.17, bf16[256,2048]{1,0:T(8,128)(2,1)} %param.15, f32[2048]{0:T(1024)} %param.16, f32[256]{0:T(256)S(1)} %add_rsqrt_fusion.2), kind=kOutput, calls=%fused_computation.74 | convolution fusion | flops 538968064 | bytes 3679232 | tf_op jit(solution)/shard_map/dot_general | solution.py:142
  22.8 2.0 %reshape.233 = f32[256,4,128]{2,1,0:T(4,128)} reshape(f32[256,512]{1,0:T(8,128)} %fusion.37) | data formatting | bytes 1048576 | tf_op jit(solution)/shard_map/reshape | solution.py:142
  24.8 1.4 multiply_reduce_fusion
  26.2 2.2 %multiply_multiply_fusion = f32[256,4,128]{2,1,0:T(4,128)} fusion(f32[256,4,128]{2,1,0:T(4,128)} %reshape.233, f32[128]{0:T(128)S(1)} %copy-done.6, f32[256,4]{1,0:T(8,128)S(1)} %add_rsqrt_fusion), kind=kLoop, calls=%fused_computation.28 | loop fusion | flops 262144 | bytes 1053184 | tf_op jit(solution)/shard_map/mul | solution.py:22
  28.4 0.6 fusion.39
  32.1 0.1 copy.100
  32.2 0.1 copy.99
  32.3 1.7 subtract_convert_fusion
  34.1 0.4 pad_maximum_fusion
  34.4 0.8 copy.121
  35.2 0.6 stack.30.bounds_ref
  35.8 0.0 all-to-all-done.own_ref
  35.8 0.0 collective-permute-start
  35.8 0.0 copy-done.3
  35.8 0.1 copy.105
  35.9 0.1 eq.61
  36.0 0.1 eq.57
  36.1 0.1 copy.107
  36.2 0.2 fusion.22
  36.4 1.0 copy.103.qpos_ref
  37.4 1.0 copy.104.qstart_ref
  38.5 0.3 collective-permute-done.other_ref
  38.8 5.4 %shard_map.145 = bf16[256,512]{1,0:T(8,128)(2,1)} custom-call(s32[5]{0:T(128)} %stack.30.bounds_ref, bf16[256,512]{1,0:T(8,128)(2,1)} %bitcast.80, bf16[8,2,256,128]{3,2,1,0:T(8,128)(2,1)} %all-to-all-done.own_ref, bf16[8,2,256,128]{3,2,1,0:T(8,128)(2,1)} %collective-permute-done.other_ref, s32[1024,1]{1,0:T(8,128)} %copy.103.qpos_ref, ...), custom_call_target="tpu_custom_call" | custom-call | tf_op jit(solution)/shard_map/pallas_call | solution.py:98
  44.2 3.4 %convolution_convert_fusion.1 = bf16[256,2048]{1,0:T(8,128)(2,1)} fusion(bf16[256,512]{1,0:T(8,128)(2,1)} %shard_map.145, bf16[512,2048]{1,0:T(8,128)(2,1)} %param.22), kind=kOutput, calls=%fused_computation.10 | convolution fusion | flops 537395200 | bytes 3407872 | tf_op jit(solution)/shard_map/dot_general | solution.py:179
  47.6 5.5 %all-to-all-start.1 = ((bf16[8,32,2048]{2,1,0:T(8,128)(2,1)}), bf16[8,32,2048]{2,1,0:T(8,128)(2,1)}, u32[]{:S(2)}, u32[]{:S(2)}) async-start(bf16[8,32,2048]{2,1,0:T(8,128)(2,1)} %bitcast.75), calls=%async_computation.1 | async-start | bytes 2097152 | tf_op jit(solution)/shard_map/all_to_all | solution.py:180
  53.2 0.2 fusion.24
  53.3 0.1 mul.209
  53.4 0.2 fusion.18
  53.7 15.4 %all-to-all-done.1 = bf16[8,32,2048]{2,1,0:T(8,128)(2,1)} async-done(((bf16[8,32,2048]{2,1,0:T(8,128)(2,1)}), bf16[8,32,2048]{2,1,0:T(8,128)(2,1)}, u32[]{:S(2)}, u32[]{:S(2)}) %all-to-all-start.1) | async-done | bytes 1048608 | tf_op jit(solution)/shard_map/all_to_all | solution.py:180
  69.0 1.4 convert_reduce_fusion
  70.4 1.1 multiply_reduce_fusion.1
  71.5 1.7 convolution_convert_fusion
  73.2 1.6 copy.111
  74.8 46.8 %all_to_all.20 = bf16[4,128,2048]{2,0,1:T(4,128)(2,1)S(1)} all-to-all(bf16[4,128,2048]{2,0,1:T(4,128)(2,1)S(1)} %copy.111), channel_id=1, replica_groups=mesh['seq'=16,'head'=8] {'seq','head'}, dimensions={1} | all-to-all | bytes 4194304 | tf_op jit(solution)/shard_map/all_to_all | solution.py:196
  121.7 1.2 copy.112
  122.8 1.3 copy-done.1
  124.1 3.0 %fusion.4 = f32[512,768]{1,0:T(8,128)} fusion(bf16[512,2048]{1,0:T(8,128)(2,1)S(1)} %bitcast.76, bf16[1,2048,768]{2,1,0:T(8,128)(2,1)S(1)} %copy-done.7), kind=kOutput, calls=%fused_computation.4 | convolution fusion | flops 1610612736 | bytes 6815744 | tf_op jit(solution)/shard_map/dot_general | solution.py:198
  127.1 0.0 copy-done
  127.1 8.3 %fusion.6 = bf16[512,2048]{1,0:T(8,128)(2,1)} fusion(bf16[1,768,2048]{2,1,0:T(8,128)(2,1)S(1)} %copy-done, f32[512,768]{1,0:T(8,128)} %fusion.4, bf16[512,2048]{1,0:T(8,128)(2,1)} %bitcast.77, bf16[1,2048,768]{2,1,0:T(8,128)(2,1)} %param.28), kind=kOutput, calls=%fused_computation.6 | convolution fusion | flops 3224633344 | bytes 12058624 | tf_op jit(solution)/shard_map/dot_general | solution.py:202
  135.4 4.5 %copy.113 = bf16[4,128,2048]{2,0,1:T(4,128)(2,1)} copy(bf16[4,128,2048]{2,1,0:T(8,128)(2,1)} %bitcast.78) | data formatting | bytes 4194304 | tf_op jit(solution)/shard_map/reshape | solution.py:204
  139.9 5.9 %all-to-all-start.3 = ((bf16[4,128,2048]{2,0,1:T(4,128)(2,1)}), bf16[4,128,2048]{2,0,1:T(4,128)(2,1)}, u32[]{:S(2)}, u32[]{:S(2)}) async-start(bf16[4,128,2048]{2,0,1:T(4,128)(2,1)} %copy.113), calls=%async_computation.3 | async-start | bytes 4194304 | tf_op jit(solution)/shard_map/all_to_all | solution.py:201
  145.8 0.0 copy-done.4
  145.8 0.1 copy.110
  145.9 0.2 select_reduce_fusion
  146.1 29.5 %all-to-all-done.3 = bf16[4,128,2048]{2,0,1:T(4,128)(2,1)} async-done(((bf16[4,128,2048]{2,0,1:T(4,128)(2,1)}), bf16[4,128,2048]{2,0,1:T(4,128)(2,1)}, u32[]{:S(2)}, u32[]{:S(2)}) %all-to-all-start.3) | async-done | bytes 2097184 | tf_op jit(solution)/shard_map/all_to_all | solution.py:201
  175.6 2.7 %copy.114 = bf16[4,128,2048]{2,1,0:T(8,128)(2,1)S(1)} copy(bf16[4,128,2048]{2,0,1:T(4,128)(2,1)} %all-to-all-done.3) | data formatting | bytes 4194304 | tf_op jit(solution)/shard_map/all_to_all | solution.py:201
  178.4 2.7 %fusion.9 = bf16[32,2048]{1,0:T(8,128)(2,1)} fusion(f32[32,512]{1,0:T(8,128)S(1)} %select_reduce_fusion, bf16[512,2048]{1,0:T(8,128)(2,1)S(1)} %bitcast.73, f32[32,2048]{1,0:T(8,128)S(1)} %convert_reduce_fusion, bf16[256,2048]{1,0:T(8,128)(2,1)} %param.15, s32[]{:T(128)S(6)} %select_n.38), kind=kOutput, calls=%fused_computation.12 | convolution fusion | flops 402915328 | bytes 2686980 | tf_op jit(solution)/shard_map/dot_general | solution.py:211
  (32 shorter events, 0.2 us)
Async XLA Ops:
  0.0 127.1 %copy-start = (bf16[1,768,2048]{2,1,0:T(8,128)(2,1)S(1)}, bf16[1,768,2048]{2,1,0:T(8,128)(2,1)}, u32[]{:S(2)}) copy-start(bf16[1,768,2048]{2,1,0:T(8,128)(2,1)} %param.29) | copy-start | bytes 9437188
  0.0 4.1 %copy-start.8 = (f32[2048]{0:T(1024)S(1)}, f32[2048]{0:T(1024)}, u32[]{:S(2)}) copy-start(f32[2048]{0:T(1024)} %param.16) | copy-start | bytes 24580
  0.0 3.7 %copy-start.9 = (s32[6]{0:T(128)S(1)}, s32[6]{0:T(128)}, u32[]{:S(2)}) copy-start(s32[6]{0:T(128)} %param.24) | copy-start | bytes 76
  1.7 4.3 %copy-start.5 = (f32[128]{0:T(128)S(1)}, f32[128]{0:T(128)}, u32[]{:S(2)}) copy-start(f32[128]{0:T(128)} %param.21) | copy-start | bytes 1540
  7.9 28.0 %all-to-all-start = ((bf16[8,2,256,128]{3,2,1,0:T(8,128)(2,1)}), bf16[8,2,256,128]{3,2,1,0:T(8,128)(2,1)}, u32[]{:S(2)}, u32[]{:S(2)}) async-start(bf16[8,2,256,128]{3,2,1,0:T(8,128)(2,1)} %broadcast_in_dim.24), calls=%async_computation | async-start | bytes 2097152 | tf_op jit(solution)/shard_map/all_to_all | solution.py:161
  19.2 7.0 %copy-start.6 = (f32[128]{0:T(128)S(1)}, f32[128]{0:T(128)}, u32[]{:S(2)}) copy-start(f32[128]{0:T(128)} %param.20) | copy-start | bytes 1540
  28.4 7.4 %copy-start.3 = (s32[32,8]{0,1:T(8,128)S(1)}, s32[32,8]{0,1:T(8,128)}, u32[]{:S(2)}) copy-start(s32[32,8]{0,1:T(8,128)} %param.25) | copy-start | bytes 3076
  35.8 3.0 %collective-permute-start = (bf16[8,2,256,128]{3,2,1,0:T(8,128)(2,1)}, bf16[8,2,256,128]{3,2,1,0:T(8,128)(2,1)}, u32[]{:S(2)}, u32[]{:S(2)}) collective-permute-start(bf16[8,2,256,128]{3,2,1,0:T(8,128)(2,1)} %all-to-all-done.own_ref), channel_id=1, source_target_pairs={{0,8},{8,0},{16,24},{24,16},{32,40},{40,32},{48,56},{56,48},{64,72... | collective-permute-start | bytes 3145736 | tf_op jit(solution)/shard_map/ppermute | solution.py:175
  47.6 23.9 %copy-start.2 = (f32[2048]{0:T(1024)S(1)}, f32[2048]{0:T(1024)}, u32[]{:S(2)}) copy-start(f32[2048]{0:T(1024)} %param.23) | copy-start | bytes 24580
  47.6 21.5 %all-to-all-start.1 = ((bf16[8,32,2048]{2,1,0:T(8,128)(2,1)}), bf16[8,32,2048]{2,1,0:T(8,128)(2,1)}, u32[]{:S(2)}, u32[]{:S(2)}) async-start(bf16[8,32,2048]{2,1,0:T(8,128)(2,1)} %bitcast.75), calls=%async_computation.1 | async-start | bytes 2097152 | tf_op jit(solution)/shard_map/all_to_all | solution.py:180
  121.7 2.5 %copy-start.7 = (bf16[1,2048,768]{2,1,0:T(8,128)(2,1)S(1)}, bf16[1,2048,768]{2,1,0:T(8,128)(2,1)}, u32[]{:S(2)}) copy-start(bf16[1,2048,768]{2,1,0:T(8,128)(2,1)} %param.27) | copy-start | bytes 9437188
  122.8 1.3 copy-start.1
  139.9 5.9 %copy-start.4 = (f32[32,8]{0,1:T(8,128)S(1)}, f32[32,8]{0,1:T(8,128)}, u32[]{:S(2)}) copy-start(f32[32,8]{0,1:T(8,128)} %param.26) | copy-start | bytes 3076
  139.9 35.7 %all-to-all-start.3 = ((bf16[4,128,2048]{2,0,1:T(4,128)(2,1)}), bf16[4,128,2048]{2,0,1:T(4,128)(2,1)}, u32[]{:S(2)}, u32[]{:S(2)}) async-start(bf16[4,128,2048]{2,0,1:T(4,128)(2,1)} %copy.113), calls=%async_computation.3 | async-start | bytes 4194304 | tf_op jit(solution)/shard_map/all_to_all | solution.py:201

commit v10 on v9

--- a/solution.py
+++ b/solution.py
@@ -35,11 +35,19 @@
     return jnp.sum((positions[:, None] >= ends[None, :]).astype(jnp.int32), axis=1)
 
 
-def _attend_kernel(bounds_ref, q_ref, own_ref, other_ref, qpos_ref, qstart_ref, o_ref, *, dim):
+def _attend_kernel(
+    bounds_ref, q_ref, cos_ref, sin_ref, gain_ref, own_ref, other_ref, qpos_ref, qstart_ref, o_ref, *, dim
+):
     heads = q_ref.shape[1] // dim
     tok = q_ref.shape[0]
     block = own_ref.shape[2]
-    q = jnp.concatenate([q_ref[:, h * dim : (h + 1) * dim] for h in range(heads)], axis=0)
+    parts = []
+    for h in range(heads):
+        part = q_ref[:, h * dim : (h + 1) * dim]
+        part = part * lax.rsqrt(jnp.mean(part * part, axis=1, keepdims=True) + EPSILON) * gain_ref[...]
+        part = part * cos_ref[...] + pltpu.roll(part, dim // 2, 1) * sin_ref[...]
+        parts.append(part.astype(jnp.bfloat16))
+    q = jnp.concatenate(parts, axis=0)
     qpos = qpos_ref[...]
     qstart = qstart_ref[...]
     scale = dim ** (-0.5)
@@ -79,7 +87,7 @@
         o_ref[:, h * dim : (h + 1) * dim] = out[h * tok : (h + 1) * tok]
 
 
-def attend(bounds, queries, own, other, qpos, qstart):
+def attend(bounds, queries, cosine, sine, gain, own, other, qpos, qstart):
     tok, width = queries.shape
     dim = own.shape[-1]
     kernel = functools.partial(_attend_kernel, dim=dim)
@@ -88,6 +96,9 @@
         grid=(1,),
         in_specs=[
             pl.BlockSpec((tok, width), lambda i, b: (0, 0)),
+            pl.BlockSpec(cosine.shape, lambda i, b: (0, 0)),
+            pl.BlockSpec(sine.shape, lambda i, b: (0, 0)),
+            pl.BlockSpec(gain.shape, lambda i, b: (0, 0)),
             pl.BlockSpec(own.shape, lambda i, b: (0, 0, 0, 0)),
             pl.BlockSpec(other.shape, lambda i, b: (0, 0, 0, 0)),
             pl.BlockSpec(qpos.shape, lambda i, b: (0, 0)),
@@ -97,7 +108,7 @@
     )
     return pl.pallas_call(
         kernel, grid_spec=spec, out_shape=jax.ShapeDtypeStruct((tok, width), jnp.bfloat16)
-    )(bounds, queries, own, other, qpos, qstart)
+    )(bounds, queries, cosine, sine, gain, own, other, qpos, qstart)
 
 
 def local(
@@ -139,12 +150,7 @@
     sine = jnp.sin(angles)
     inputs = tokens.astype(jnp.float32)
     normed = rms_scale(inputs, norm_gain).astype(jnp.bfloat16)
-    queries = jnp.dot(normed, w_query, preferred_element_type=jnp.float32).reshape(
-        tok_dev, per_dev, head_dim
-    )
-    queries = rotate(rms_scale(queries, query_gain), cosine[:, None, :], sine[:, None, :]).astype(
-        jnp.bfloat16
-    )
+    queries = jnp.dot(normed, w_query, preferred_element_type=jnp.float32)
     column = head_index * per_dev // (HEADS // KV_HEADS) * head_dim
     key_cols = lax.dynamic_slice_in_dim(w_key, column, head_dim, 1)
     value_cols = lax.dynamic_slice_in_dim(w_value, column, head_dim, 1)
@@ -167,14 +173,17 @@
     bounds = jnp.stack([low, inner_low, inner_high, high, seq_index % 2]).astype(jnp.int32)
     operands = (
         bounds,
-        queries.reshape(tok_dev, per_dev * head_dim),
+        queries,
+        jnp.concatenate([cosine, cosine], axis=-1),
+        jnp.concatenate([-sine, sine], axis=-1),
+        query_gain[None, :],
         jnp.tile(positions[:, None], (per_dev, 1)),
         jnp.tile(own_start[:, None], (per_dev, 1)),
     )
     operands, same_core = lax.optimization_barrier((operands, same_core))
     other_core = lax.ppermute(same_core, "seq", [(i, i ^ 1) for i in range(n_seq)])
-    bounds, flat_queries, qpos, qstart = operands
-    attended = attend(bounds, flat_queries, same_core, other_core, qpos, qstart)
+    bounds, queries, cosine2, sine2, gain, qpos, qstart = operands
+    attended = attend(bounds, queries, cosine2, sine2, gain, same_core, other_core, qpos, qstart)
     rows = tok_dev // n_head
     terms = jnp.dot(attended, w_out, preferred_element_type=jnp.float32).astype(jnp.bfloat16)
     terms = lax.all_to_all(terms.reshape(n_head, rows, width), "head", 0, 0, tiled=True)
@@ -197,6 +206,7 @@
     flat = block.reshape(-1, width)
     gate = jnp.dot(flat, w_gate[0], preferred_element_type=jnp.float32)
     up = jnp.dot(flat, w_up[0], preferred_element_type=jnp.float32)
+    gate, up = lax.optimization_barrier((gate, up))
     hidden = (jax.nn.silu(gate) * up).astype(jnp.bfloat16)
     returned = lax.all_to_all(
         jnp.dot(hidden, w_down[0], preferred_element_type=jnp.float32)

time: 182 us -> 167 us (0.918)
  matrix products: 26.4 us -> 20.5 us
  local copies, waits for them, and re-layouts: 20.1 us -> 15.1 us
  other arithmetic: 11.5 us -> 7.02 us
  waiting for transfers between devices: 45.2 us -> 48 us
  blocking collectives: 46.8 us -> 44.5 us
    dot_general x1, matrix products: 8.28 us -> 1.85 us  [local(): jnp.dot(hidden, w_down[0], preferred_element_type=jnp.float32)]
    all_to_all x1, waiting for transfers between devices: 0.01 us -> 2.81 us  [local(): lax.all_to_all(spread, 'seq', 0, 0, tiled=True, axis_index_groups=groups)]
    all_to_all x1, blocking collectives: 46.8 us -> 44.5 us  [local(): lax.all_to_all(outgoing, ('seq', 'head'), split_axis=1, concat_axis=1, ti...]
    mul x2 -> x1, other arithmetic: 2.27 us -> 0.1 us  [rms_scale(): values * lax.rsqrt(jnp.mean(values * values, axis=-1, keepdims=True) + EP...]
    reshape x1 -> x0, local copies, waits for them, and re-layouts: 2.02 us -> none  [local(): jnp.dot(normed, w_query, preferred_element_type=jnp.float32)]
    dot_general x1 -> x2, matrix products: 3.49 us -> 5.3 us  [the longest x1 3.5 us: local(): queries = jnp.dot(normed, w_query, preferred_element_type=jnp.float32)]
    reduce_sum x3 -> x2, other arithmetic: 4.1 us -> 2.71 us  [rms_scale(): jnp.mean(values * values, axis=-1, keepdims=True) + EPSILON]
  transfers between devices with their start and end apart: 4 -> 4, of which waited for: 3 -> 4; matrix products, arithmetic and copies ran while one was open for 10% -> 6% of each run, Pallas kernels for 0% -> 0%
where the time goes in v10:
time: 167 us
  waiting for transfers between devices  48 us (29%)
  blocking collectives  44.5 us (27%)
  matrix products  20.5 us (12%)
  starting transfers between devices  18.4 us (11%)
  local copies, waits for them, and re-layouts  15.1 us (9%)
  between operations  7.21 us (4%)
  other arithmetic  7.02 us (4%)
  Pallas kernels  6.15 us (4%)
    all_to_all x1, blocking collectives, local(): lax.all_to_all(outgoing, ('seq', 'head'), split_axis=1, concat_axis=1, ti...  44.5 us
    all_to_all x1, waiting for transfers between devices, local(): lax.all_to_all(jnp.dot(hidden, w_down[0], preferred_element_type=jnp.floa...  29.5 us
    all_to_all x1, waiting for transfers between devices, local(): lax.all_to_all(terms.reshape(n_head, rows, width), 'head', 0, 0, tiled=True)  15.4 us
    all_to_all x1, starting transfers between devices, local(): lax.all_to_all(spread, 'seq', 0, 0, tiled=True, axis_index_groups=groups)  7.03 us
    pallas_call x1, Pallas kernels, attend(): pl.pallas_call(kernel, grid_spec=spec, out_shape=jax.ShapeDtypeStruct((to...  6.15 us
    all_to_all x1, starting transfers between devices, local(): lax.all_to_all(jnp.dot(hidden, w_down[0], preferred_element_type=jnp.floa...  5.91 us
    all_to_all x1, starting transfers between devices, local(): lax.all_to_all(terms.reshape(n_head, rows, width), 'head', 0, 0, tiled=True)  5.47 us
    dot_general x1, matrix products, local(): queries = jnp.dot(normed, w_query, preferred_element_type=jnp.float32)  3.5 us
  transfers between devices with their start and end apart: 4, of which 4 were waited for; matrix products, arithmetic and copies ran while one was open for 6% of the time, Pallas kernels for 0%

profile of v10, /device:TPU:0, one launch (start us, length us, event | category | flops | bytes accessed | tf_op | source)
XLA Modules:
  0.0 166.9 jit_solution(15967319219714782089)
XLA Ops:
  0.0 0.0 copy-start
  0.0 0.0 copy-start.7
  0.0 0.0 copy-start.8
  0.0 1.7 fusion.10
  1.7 0.0 copy-start.4
  1.7 2.0 %multiply_reduce_fusion.1 = (f32[256]{0:T(256)S(1)}, f32[256,128]{0,1:T(8,128)S(1)}) fusion(bf16[2048,512]{1,0:T(8,128)(2,1)} %param.18, s32[]{:T(128)S(6)} %select_n.46, bf16[256,2048]{1,0:T(8,128)(2,1)} %param.15, f32[2048]{0:T(1024)} %param.16, f32[256]{0:T(256)S(1)} %add_rsqrt_fusion.1), kind=kOutput, calls=%fused_computation.52 | convolution fusion | flops 136380160 | bytes 1714180 | tf_op jit(solution)/shard_map/dot_general | solution.py:158
  3.7 0.1 copy.52
  3.8 0.0 copy-done.8
  3.8 0.2 reduce-window.18
  4.0 0.1 convert_reduce_fusion.1
  4.1 0.1 select_reduce_fusion.1
  4.2 0.0 copy-done.7
  4.2 1.9 %fusion.13 = bf16[1,256,128]{2,1,0:T(8,128)(2,1)S(1)} fusion(bf16[2048,512]{1,0:T(8,128)(2,1)} %param.19, s32[]{:T(128)S(6)} %select_n.46, bf16[256,2048]{1,0:T(8,128)(2,1)} %param.15, f32[2048]{0:T(1024)S(1)} %copy-done.7, f32[256]{0:T(256)S(1)} %add_rsqrt_fusion.1), kind=kOutput, calls=%fused_computation.19 | convolution fusion | flops 136347648 | bytes 1647620 | tf_op jit(solution)/shard_map/dot_general | solution.py:162
  6.1 0.0 copy-done.4
  6.1 0.1 multiply_multiply_fusion
  6.2 0.6 fusion.34
  6.8 0.1 pad_maximum_fusion.2
  6.9 1.2 broadcast_in_dim.27
  8.1 7.0 %all-to-all-start = ((bf16[8,2,256,128]{3,2,1,0:T(8,128)(2,1)}), bf16[8,2,256,128]{3,2,1,0:T(8,128)(2,1)}, u32[]{:S(2)}, u32[]{:S(2)}) async-start(bf16[8,2,256,128]{3,2,1,0:T(8,128)(2,1)} %broadcast_in_dim.27), calls=%async_computation | async-start | bytes 2097152 | tf_op jit(solution)/shard_map/all_to_all | solution.py:167
  15.1 0.6 fusion.44
  15.7 0.6 fusion.43
  23.3 0.7 stack.30.bounds_ref
  24.0 0.8 pad_maximum_fusion
  24.8 0.0 copy-start.2
  24.8 3.5 %fusion.41.q_ref = f32[256,512]{1,0:T(8,128)} fusion(bf16[2048,512]{1,0:T(8,128)(2,1)} %param.17, bf16[256,2048]{1,0:T(8,128)(2,1)} %param.15, f32[2048]{0:T(1024)} %param.16, f32[256]{0:T(256)S(1)} %add_rsqrt_fusion.1), kind=kOutput, calls=%fused_computation.75 | convolution fusion | flops 538968064 | bytes 3679232 | tf_op jit(solution)/shard_map/dot_general | solution.py:153
  28.3 2.8 %all-to-all-done.own_ref = bf16[8,2,256,128]{3,2,1,0:T(8,128)(2,1)} async-done(((bf16[8,2,256,128]{3,2,1,0:T(8,128)(2,1)}), bf16[8,2,256,128]{3,2,1,0:T(8,128)(2,1)}, u32[]{:S(2)}, u32[]{:S(2)}) %all-to-all-start) | async-done | bytes 1048608 | tf_op jit(solution)/shard_map/all_to_all | solution.py:167
  31.1 0.0 collective-permute-start
  31.1 0.0 copy-done.2
  31.1 0.1 copy.55
  31.2 0.1 eq.61
  31.3 0.1 eq.57
  31.4 0.1 copy.57
  31.5 0.2 fusion.26
  31.7 1.0 copy.53.qpos_ref
  32.7 1.0 copy.54.qstart_ref
  33.7 0.3 collective-permute-done.other_ref
  34.1 6.1 %shard_map.145 = bf16[256,512]{1,0:T(8,128)(2,1)} custom-call(s32[5]{0:T(128)} %stack.30.bounds_ref, f32[256,512]{1,0:T(8,128)} %fusion.41.q_ref, f32[256,128]{1,0:T(8,128)} %get-tuple-element.17.cos_ref, f32[256,128]{1,0:T(8,128)} %get-tuple-element.18.sin_ref, f32[1,128]{1,0:T(1,128)} %bitcast.77, bf16[8,2,256,128]{3,2,1,0:T(8,128)(2,1)} %all-to-all-done.own_ref, ...), custom_call_target="tpu_custom_call" | custom-call | tf_op jit(solution)/shard_map/pallas_call | solution.py:109
  40.2 3.4 %convolution_convert_fusion.1 = bf16[256,2048]{1,0:T(8,128)(2,1)} fusion(bf16[256,512]{1,0:T(8,128)(2,1)} %shard_map.145, bf16[512,2048]{1,0:T(8,128)(2,1)} %param.22), kind=kOutput, calls=%fused_computation.10 | convolution fusion | flops 537395200 | bytes 3407872 | tf_op jit(solution)/shard_map/dot_general | solution.py:188
  43.6 5.5 %all-to-all-start.1 = ((bf16[8,32,2048]{2,1,0:T(8,128)(2,1)}), bf16[8,32,2048]{2,1,0:T(8,128)(2,1)}, u32[]{:S(2)}, u32[]{:S(2)}) async-start(bf16[8,32,2048]{2,1,0:T(8,128)(2,1)} %bitcast.68), calls=%async_computation.1 | async-start | bytes 2097152 | tf_op jit(solution)/shard_map/all_to_all | solution.py:189
  49.2 0.2 fusion.28
  49.4 0.1 mul.144
  49.5 0.2 fusion.15
  49.7 15.4 %all-to-all-done.1 = bf16[8,32,2048]{2,1,0:T(8,128)(2,1)} async-done(((bf16[8,32,2048]{2,1,0:T(8,128)(2,1)}), bf16[8,32,2048]{2,1,0:T(8,128)(2,1)}, u32[]{:S(2)}, u32[]{:S(2)}) %all-to-all-start.1) | async-done | bytes 1048608 | tf_op jit(solution)/shard_map/all_to_all | solution.py:189
  65.1 1.4 convert_reduce_fusion
  66.5 1.1 multiply_reduce_fusion
  67.5 0.0 copy-done.1
  67.6 1.7 %convolution_convert_fusion = bf16[512,2048]{1,0:T(8,128)(2,1)S(1)} fusion(pred[32,512]{1,0:T(8,128)(4,1)S(1)} %fusion.15, f32[2048]{0:T(1024)S(1)} %copy-done.1, f32[32]{0:T(128)S(1)} %add_rsqrt_fusion.2, f32[32,2048]{1,0:T(8,128)S(1)} %convert_reduce_fusion, bf16[256,2048]{1,0:T(8,128)(2,1)} %param.15, s32[]{:T(128)S(6)} %select_n.38), kind=kOutput, calls=%fused_computation.7 | convolution fusion | flops 68485120 | bytes 2515076 | tf_op jit(solution)/shard_map/dot_general | solution.py:203
  69.2 1.6 copy.61
  70.9 44.5 %all_to_all.20 = bf16[4,128,2048]{2,0,1:T(4,128)(2,1)S(1)} all-to-all(bf16[4,128,2048]{2,0,1:T(4,128)(2,1)S(1)} %copy.61), channel_id=1, replica_groups=mesh['seq'=16,'head'=8] {'seq','head'}, dimensions={1} | all-to-all | bytes 4194304 | tf_op jit(solution)/shard_map/all_to_all | solution.py:205
  115.3 1.2 copy.62
  116.5 0.7 copy-done.5
  117.2 1.8 %fusion.2 = f32[512,768]{1,0:T(8,128)S(1)} fusion(bf16[512,2048]{1,0:T(8,128)(2,1)S(1)} %bitcast.69, bf16[1,2048,768]{2,1,0:T(8,128)(2,1)S(1)} %copy-done.5), kind=kOutput, calls=%fused_computation.2 | convolution fusion | flops 1610612736 | bytes 6815744 | tf_op jit(solution)/shard_map/dot_general | solution.py:208
  119.1 0.1 copy-done.6
  119.1 1.8 %fusion.4 = f32[512,768]{1,0:T(8,128)S(1)} fusion(bf16[512,2048]{1,0:T(8,128)(2,1)S(1)} %bitcast.70, bf16[1,2048,768]{2,1,0:T(8,128)(2,1)S(1)} %copy-done.6), kind=kOutput, calls=%fused_computation.4 | convolution fusion | flops 1610612736 | bytes 6815744 | tf_op jit(solution)/shard_map/dot_general | solution.py:207
  120.9 0.0 copy-done
  120.9 1.9 %fusion.6 = bf16[512,2048]{1,0:T(8,128)(2,1)S(1)} fusion(bf16[1,768,2048]{2,1,0:T(8,128)(2,1)S(1)} %copy-done, f32[512,768]{1,0:T(8,128)S(1)} %fusion.2, f32[512,768]{1,0:T(8,128)S(1)} %fusion.4), kind=kOutput, calls=%fused_computation.6 | convolution fusion | flops 1614020608 | bytes 8388608 | tf_op jit(solution)/shard_map/dot_general | solution.py:212
  122.8 2.9 %copy.63 = bf16[4,128,2048]{2,0,1:T(4,128)(2,1)} copy(bf16[4,128,2048]{2,1,0:T(8,128)(2,1)S(1)} %bitcast.71) | data formatting | bytes 4194304 | tf_op jit(solution)/shard_map/reshape | solution.py:214
  125.7 5.9 %all-to-all-start.3 = ((bf16[4,128,2048]{2,0,1:T(4,128)(2,1)}), bf16[4,128,2048]{2,0,1:T(4,128)(2,1)}, u32[]{:S(2)}, u32[]{:S(2)}) async-start(bf16[4,128,2048]{2,0,1:T(4,128)(2,1)} %copy.63), calls=%async_computation.3 | async-start | bytes 4194304 | tf_op jit(solution)/shard_map/all_to_all | solution.py:211
  131.6 0.0 copy-done.3
  131.7 0.1 copy.60
  131.7 0.2 select_reduce_fusion
  132.0 29.5 %all-to-all-done.3 = bf16[4,128,2048]{2,0,1:T(4,128)(2,1)} async-done(((bf16[4,128,2048]{2,0,1:T(4,128)(2,1)}), bf16[4,128,2048]{2,0,1:T(4,128)(2,1)}, u32[]{:S(2)}, u32[]{:S(2)}) %all-to-all-start.3) | async-done | bytes 2097184 | tf_op jit(solution)/shard_map/all_to_all | solution.py:211
  161.5 2.7 %copy.64 = bf16[4,128,2048]{2,1,0:T(8,128)(2,1)S(1)} copy(bf16[4,128,2048]{2,0,1:T(4,128)(2,1)} %all-to-all-done.3) | data formatting | bytes 4194304 | tf_op jit(solution)/shard_map/all_to_all | solution.py:211
  164.2 2.7 %fusion.9 = bf16[32,2048]{1,0:T(8,128)(2,1)} fusion(f32[32,512]{1,0:T(8,128)S(1)} %select_reduce_fusion, bf16[512,2048]{1,0:T(8,128)(2,1)S(1)} %bitcast.66, f32[32,2048]{1,0:T(8,128)S(1)} %convert_reduce_fusion, bf16[256,2048]{1,0:T(8,128)(2,1)} %param.15, s32[]{:T(128)S(6)} %select_n.38), kind=kOutput, calls=%fused_computation.12 | convolution fusion | flops 402915328 | bytes 2686980 | tf_op jit(solution)/shard_map/dot_general | solution.py:221
  (23 shorter events, 0.2 us)
Async XLA Ops:
  0.0 120.9 %copy-start = (bf16[1,768,2048]{2,1,0:T(8,128)(2,1)S(1)}, bf16[1,768,2048]{2,1,0:T(8,128)(2,1)}, u32[]{:S(2)}) copy-start(bf16[1,768,2048]{2,1,0:T(8,128)(2,1)} %param.29) | copy-start | bytes 9437188
  0.0 4.2 %copy-start.7 = (f32[2048]{0:T(1024)S(1)}, f32[2048]{0:T(1024)}, u32[]{:S(2)}) copy-start(f32[2048]{0:T(1024)} %param.16) | copy-start | bytes 24580
  0.0 3.8 %copy-start.8 = (s32[6]{0:T(128)S(1)}, s32[6]{0:T(128)}, u32[]{:S(2)}) copy-start(s32[6]{0:T(128)} %param.24) | copy-start | bytes 76
  1.7 4.4 %copy-start.4 = (f32[128]{0:T(128)S(1)}, f32[128]{0:T(128)}, u32[]{:S(2)}) copy-start(f32[128]{0:T(128)} %param.21) | copy-start | bytes 1540
  8.1 23.0 %all-to-all-start = ((bf16[8,2,256,128]{3,2,1,0:T(8,128)(2,1)}), bf16[8,2,256,128]{3,2,1,0:T(8,128)(2,1)}, u32[]{:S(2)}, u32[]{:S(2)}) async-start(bf16[8,2,256,128]{3,2,1,0:T(8,128)(2,1)} %broadcast_in_dim.27), calls=%async_computation | async-start | bytes 2097152 | tf_op jit(solution)/shard_map/all_to_all | solution.py:167
  24.8 6.3 %copy-start.2 = (s32[32,8]{0,1:T(8,128)S(1)}, s32[32,8]{0,1:T(8,128)}, u32[]{:S(2)}) copy-start(s32[32,8]{0,1:T(8,128)} %param.25) | copy-start | bytes 3076
  31.1 3.0 %collective-permute-start = (bf16[8,2,256,128]{3,2,1,0:T(8,128)(2,1)}, bf16[8,2,256,128]{3,2,1,0:T(8,128)(2,1)}, u32[]{:S(2)}, u32[]{:S(2)}) collective-permute-start(bf16[8,2,256,128]{3,2,1,0:T(8,128)(2,1)} %all-to-all-done.own_ref), channel_id=1, source_target_pairs={{0,8},{8,0},{16,24},{24,16},{32,40},{40,32},{48,56},{56,48},{64,72... | collective-permute-start | bytes 3145736 | tf_op jit(solution)/shard_map/ppermute | solution.py:184
  43.6 23.9 %copy-start.1 = (f32[2048]{0:T(1024)S(1)}, f32[2048]{0:T(1024)}, u32[]{:S(2)}) copy-start(f32[2048]{0:T(1024)} %param.23) | copy-start | bytes 24580
  43.6 21.5 %all-to-all-start.1 = ((bf16[8,32,2048]{2,1,0:T(8,128)(2,1)}), bf16[8,32,2048]{2,1,0:T(8,128)(2,1)}, u32[]{:S(2)}, u32[]{:S(2)}) async-start(bf16[8,32,2048]{2,1,0:T(8,128)(2,1)} %bitcast.68), calls=%async_computation.1 | async-start | bytes 2097152 | tf_op jit(solution)/shard_map/all_to_all | solution.py:189
  115.3 1.9 %copy-start.5 = (bf16[1,2048,768]{2,1,0:T(8,128)(2,1)S(1)}, bf16[1,2048,768]{2,1,0:T(8,128)(2,1)}, u32[]{:S(2)}) copy-start(bf16[1,2048,768]{2,1,0:T(8,128)(2,1)} %param.28) | copy-start | bytes 9437188
  117.2 1.9 %copy-start.6 = (bf16[1,2048,768]{2,1,0:T(8,128)(2,1)S(1)}, bf16[1,2048,768]{2,1,0:T(8,128)(2,1)}, u32[]{:S(2)}) copy-start(bf16[1,2048,768]{2,1,0:T(8,128)(2,1)} %param.27) | copy-start | bytes 9437188
  125.7 5.9 %copy-start.3 = (f32[32,8]{0,1:T(8,128)S(1)}, f32[32,8]{0,1:T(8,128)}, u32[]{:S(2)}) copy-start(f32[32,8]{0,1:T(8,128)} %param.26) | copy-start | bytes 3076
  125.7 35.7 %all-to-all-start.3 = ((bf16[4,128,2048]{2,0,1:T(4,128)(2,1)}), bf16[4,128,2048]{2,0,1:T(4,128)(2,1)}, u32[]{:S(2)}, u32[]{:S(2)}) async-start(bf16[4,128,2048]{2,0,1:T(4,128)(2,1)} %copy.63), calls=%async_computation.3 | async-start | bytes 4194304 | tf_op jit(solution)/shard_map/all_to_all | solution.py:211

commit v11 on v10

--- a/solution.py
+++ b/solution.py
@@ -36,7 +36,7 @@
 
 
 def _attend_kernel(
-    bounds_ref, q_ref, cos_ref, sin_ref, gain_ref, own_ref, other_ref, qpos_ref, qstart_ref, o_ref, *, dim
+    bounds_ref, q_ref, cos_ref, sin_ref, gain_ref, own_ref, other_ref, qpos_ref, qstart_ref, w_ref, o_ref, *, dim
 ):
     heads = q_ref.shape[1] // dim
     tok = q_ref.shape[0]
@@ -82,12 +82,16 @@
     carry = lax.fori_loop(bounds_ref[1], bounds_ref[2], lambda j, c: step(j, c, False), carry)
     carry = lax.fori_loop(bounds_ref[2], bounds_ref[3], lambda j, c: step(j, c, True), carry)
     high, total, accum = carry
-    out = (accum / total).astype(o_ref.dtype)
-    for h in range(heads):
-        o_ref[:, h * dim : (h + 1) * dim] = out[h * tok : (h + 1) * tok]
-
-
-def attend(bounds, queries, cosine, sine, gain, own, other, qpos, qstart):
+    out = (accum / total).astype(jnp.bfloat16)
+    terms = jnp.dot(out[:tok], w_ref[:dim, :], preferred_element_type=jnp.float32)
+    for h in range(1, heads):
+        terms = terms + jnp.dot(
+            out[h * tok : (h + 1) * tok], w_ref[h * dim : (h + 1) * dim, :], preferred_element_type=jnp.float32
+        )
+    o_ref[...] = terms.astype(o_ref.dtype)
+
+
+def attend(bounds, queries, cosine, sine, gain, own, other, qpos, qstart, w_out):
     tok, width = queries.shape
     dim = own.shape[-1]
     kernel = functools.partial(_attend_kernel, dim=dim)
@@ -103,12 +107,13 @@
             pl.BlockSpec(other.shape, lambda i, b: (0, 0, 0, 0)),
             pl.BlockSpec(qpos.shape, lambda i, b: (0, 0)),
             pl.BlockSpec(qstart.shape, lambda i, b: (0, 0)),
+            pl.BlockSpec(w_out.shape, lambda i, b: (0, 0)),
         ],
-        out_specs=pl.BlockSpec((tok, width), lambda i, b: (0, 0)),
+        out_specs=pl.BlockSpec((tok, w_out.shape[1]), lambda i, b: (0, 0)),
     )
     return pl.pallas_call(
-        kernel, grid_spec=spec, out_shape=jax.ShapeDtypeStruct((tok, width), jnp.bfloat16)
-    )(bounds, queries, cosine, sine, gain, own, other, qpos, qstart)
+        kernel, grid_spec=spec, out_shape=jax.ShapeDtypeStruct((tok, w_out.shape[1]), jnp.bfloat16)
+    )(bounds, queries, cosine, sine, gain, own, other, qpos, qstart, w_out)
 
 
 def local(
@@ -183,9 +188,8 @@
     operands, same_core = lax.optimization_barrier((operands, same_core))
     other_core = lax.ppermute(same_core, "seq", [(i, i ^ 1) for i in range(n_seq)])
     bounds, queries, cosine2, sine2, gain, qpos, qstart = operands
-    attended = attend(bounds, queries, cosine2, sine2, gain, same_core, other_core, qpos, qstart)
+    terms = attend(bounds, queries, cosine2, sine2, gain, same_core, other_core, qpos, qstart, w_out)
     rows = tok_dev // n_head
-    terms = jnp.dot(attended, w_out, preferred_element_type=jnp.float32).astype(jnp.bfloat16)
     terms = lax.all_to_all(terms.reshape(n_head, rows, width), "head", 0, 0, tiled=True)
     attn_rows = jnp.sum(terms.astype(jnp.float32), axis=0)
     resid = lax.dynamic_slice_in_dim(tokens, head_index * rows, rows, 0).astype(jnp.float32) + attn_rows

time: 167 us -> 167 us (level)
  matrix products: 20.5 us -> 17.1 us
  Pallas kernels: 6.15 us -> 8.34 us
    dot_general x1 -> x0, matrix products: 3.39 us -> none  [local(): jnp.dot(attended, w_out, preferred_element_type=jnp.float32)]
    pallas_call x1, Pallas kernels: 6.15 us -> 8.34 us  [attend(): pl.pallas_call(kernel, grid_spec=spec, out_shape=jax.ShapeDtypeStruct((to...]
where the time goes in v11:
time: 167 us; the launch traced here: 166 us
  waiting for transfers between devices  48 us (29%)
  blocking collectives  44.6 us (27%)
  starting transfers between devices  18.4 us (11%)
  matrix products  17.1 us (10%)
  local copies, waits for them, and re-layouts  15.1 us (9%)
  Pallas kernels  8.34 us (5%)
  between operations  7.21 us (4%)
  other arithmetic  7.03 us (4%)
    all_to_all x1, blocking collectives, local(): lax.all_to_all(outgoing, ('seq', 'head'), split_axis=1, concat_axis=1, ti...  44.6 us
    all_to_all x1, waiting for transfers between devices, local(): lax.all_to_all(jnp.dot(hidden, w_down[0], preferred_element_type=jnp.floa...  29.5 us
    all_to_all x1, waiting for transfers between devices, local(): lax.all_to_all(terms.reshape(n_head, rows, width), 'head', 0, 0, tiled=True)  15.4 us
    pallas_call x1, Pallas kernels, attend(): pl.pallas_call(kernel, grid_spec=spec, out_shape=jax.ShapeDtypeStruct((to...  8.34 us
    all_to_all x1, starting transfers between devices, local(): lax.all_to_all(spread, 'seq', 0, 0, tiled=True, axis_index_groups=groups)  7.03 us
    all_to_all x1, starting transfers between devices, local(): lax.all_to_all(jnp.dot(hidden, w_down[0], preferred_element_type=jnp.floa...  5.91 us
    all_to_all x1, starting transfers between devices, local(): lax.all_to_all(terms.reshape(n_head, rows, width), 'head', 0, 0, tiled=True)  5.47 us
    dot_general x1, matrix products, local(): queries = jnp.dot(normed, w_query, preferred_element_type=jnp.float32)  3.49 us
  transfers between devices with their start and end apart: 4, of which 4 were waited for; matrix products, arithmetic and copies ran while one was open for 6% of the time, Pallas kernels for 0%

profile of v11, /device:TPU:0, one launch (start us, length us, event | category | flops | bytes accessed | tf_op | source)
XLA Modules:
  0.0 165.8 jit_solution(3076970509139013224)
XLA Ops:
  0.0 0.0 copy-start
  0.0 0.0 copy-start.7
  0.0 0.0 copy-start.8
  0.0 1.7 %fusion.10 = f32[256]{0:T(256)S(1)} fusion(bf16[256,2048]{1,0:T(8,128)(2,1)} %param.15), kind=kLoop, calls=%fused_computation.12 | loop fusion | flops 1572608 | bytes 1049600 | tf_op jit(solution)/shard_map/reduce_sum | solution.py:22
  1.7 0.0 copy-start.4
  1.7 2.0 %multiply_reduce_fusion.1 = (f32[256]{0:T(256)S(1)}, f32[256,128]{0,1:T(8,128)S(1)}) fusion(bf16[2048,512]{1,0:T(8,128)(2,1)} %param.18, s32[]{:T(128)S(6)} %select_n.46, bf16[256,2048]{1,0:T(8,128)(2,1)} %param.15, f32[2048]{0:T(1024)} %param.16, f32[256]{0:T(256)S(1)} %add_rsqrt_fusion.1), kind=kOutput, calls=%fused_computation.51 | convolution fusion | flops 136380160 | bytes 1714180 | tf_op jit(solution)/shard_map/dot_general | solution.py:163
  3.7 0.1 copy.52
  3.8 0.0 copy-done.8
  3.8 0.2 reduce-window.18
  4.0 0.1 convert_reduce_fusion.1
  4.1 0.1 select_reduce_fusion.1
  4.2 0.0 copy-done.7
  4.2 1.9 %fusion.13 = bf16[1,256,128]{2,1,0:T(8,128)(2,1)S(1)} fusion(bf16[2048,512]{1,0:T(8,128)(2,1)} %param.19, s32[]{:T(128)S(6)} %select_n.46, bf16[256,2048]{1,0:T(8,128)(2,1)} %param.15, f32[2048]{0:T(1024)S(1)} %copy-done.7, f32[256]{0:T(256)S(1)} %add_rsqrt_fusion.1), kind=kOutput, calls=%fused_computation.18 | convolution fusion | flops 136347648 | bytes 1647620 | tf_op jit(solution)/shard_map/dot_general | solution.py:167
  6.1 0.0 copy-done.4
  6.1 0.1 multiply_multiply_fusion
  6.2 0.6 fusion.34
  6.8 0.1 pad_maximum_fusion.2
  6.9 1.2 broadcast_in_dim.27
  8.1 7.0 %all-to-all-start = ((bf16[8,2,256,128]{3,2,1,0:T(8,128)(2,1)}), bf16[8,2,256,128]{3,2,1,0:T(8,128)(2,1)}, u32[]{:S(2)}, u32[]{:S(2)}) async-start(bf16[8,2,256,128]{3,2,1,0:T(8,128)(2,1)} %broadcast_in_dim.27), calls=%async_computation | async-start | bytes 2097152 | tf_op jit(solution)/shard_map/all_to_all | solution.py:172
  15.1 0.6 fusion.44
  15.7 0.6 fusion.43
  23.3 0.7 stack.30.bounds_ref
  24.0 0.8 pad_maximum_fusion
  24.8 0.0 copy-start.2
  24.8 3.5 %fusion.41.q_ref = f32[256,512]{1,0:T(8,128)} fusion(bf16[2048,512]{1,0:T(8,128)(2,1)} %param.17, bf16[256,2048]{1,0:T(8,128)(2,1)} %param.15, f32[2048]{0:T(1024)} %param.16, f32[256]{0:T(256)S(1)} %add_rsqrt_fusion.1), kind=kOutput, calls=%fused_computation.74 | convolution fusion | flops 538968064 | bytes 3679232 | tf_op jit(solution)/shard_map/dot_general | solution.py:158
  28.3 2.8 %all-to-all-done.own_ref = bf16[8,2,256,128]{3,2,1,0:T(8,128)(2,1)} async-done(((bf16[8,2,256,128]{3,2,1,0:T(8,128)(2,1)}), bf16[8,2,256,128]{3,2,1,0:T(8,128)(2,1)}, u32[]{:S(2)}, u32[]{:S(2)}) %all-to-all-start) | async-done | bytes 1048608 | tf_op jit(solution)/shard_map/all_to_all | solution.py:172
  31.1 0.0 collective-permute-start
  31.1 0.0 copy-done.2
  31.1 0.1 copy.55
  31.2 0.1 eq.61
  31.3 0.1 eq.57
  31.4 0.1 copy.57
  31.5 0.2 fusion.26
  31.7 1.0 copy.53.qpos_ref
  32.7 1.0 copy.54.qstart_ref
  33.7 0.3 collective-permute-done.other_ref
  34.1 8.3 %shard_map.145 = bf16[256,2048]{1,0:T(8,128)(2,1)} custom-call(s32[5]{0:T(128)} %stack.30.bounds_ref, f32[256,512]{1,0:T(8,128)} %fusion.41.q_ref, f32[256,128]{1,0:T(8,128)} %get-tuple-element.17.cos_ref, f32[256,128]{1,0:T(8,128)} %get-tuple-element.18.sin_ref, f32[1,128]{1,0:T(1,128)} %bitcast.76, bf16[8,2,256,128]{3,2,1,0:T(8,128)(2,1)} %all-to-all-done.own_ref, ...), custom_call_target="tpu_custom_call" | custom-call | tf_op jit(solution)/shard_map/pallas_call | solution.py:114
  42.4 0.0 copy-start.1
  42.4 5.5 %all-to-all-start.1 = ((bf16[8,32,2048]{2,1,0:T(8,128)(2,1)}), bf16[8,32,2048]{2,1,0:T(8,128)(2,1)}, u32[]{:S(2)}, u32[]{:S(2)}) async-start(bf16[8,32,2048]{2,1,0:T(8,128)(2,1)} %bitcast.66), calls=%async_computation.1 | async-start | bytes 2097152 | tf_op jit(solution)/shard_map/all_to_all | solution.py:193
  48.0 0.2 fusion.28
  48.2 0.1 mul.144
  48.3 0.2 fusion.15
  48.5 15.4 %all-to-all-done.1 = bf16[8,32,2048]{2,1,0:T(8,128)(2,1)} async-done(((bf16[8,32,2048]{2,1,0:T(8,128)(2,1)}), bf16[8,32,2048]{2,1,0:T(8,128)(2,1)}, u32[]{:S(2)}, u32[]{:S(2)}) %all-to-all-start.1) | async-done | bytes 1048608 | tf_op jit(solution)/shard_map/all_to_all | solution.py:193
  63.9 1.4 convert_reduce_fusion
  65.3 1.1 multiply_reduce_fusion
  66.3 0.0 copy-done.1
  66.4 1.7 %convolution_convert_fusion = bf16[512,2048]{1,0:T(8,128)(2,1)S(1)} fusion(pred[32,512]{1,0:T(8,128)(4,1)S(1)} %fusion.15, f32[2048]{0:T(1024)S(1)} %copy-done.1, f32[32]{0:T(128)S(1)} %add_rsqrt_fusion.2, f32[32,2048]{1,0:T(8,128)S(1)} %convert_reduce_fusion, bf16[256,2048]{1,0:T(8,128)(2,1)} %param.15, s32[]{:T(128)S(6)} %select_n.38), kind=kOutput, calls=%fused_computation.7 | convolution fusion | flops 68485120 | bytes 2515076 | tf_op jit(solution)/shard_map/dot_general | solution.py:207
  68.0 1.6 copy.61
  69.7 44.6 %all_to_all.20 = bf16[4,128,2048]{2,0,1:T(4,128)(2,1)S(1)} all-to-all(bf16[4,128,2048]{2,0,1:T(4,128)(2,1)S(1)} %copy.61), channel_id=1, replica_groups=mesh['seq'=16,'head'=8] {'seq','head'}, dimensions={1} | all-to-all | bytes 4194304 | tf_op jit(solution)/shard_map/all_to_all | solution.py:209
  114.3 1.2 copy.62
  115.5 0.7 copy-done.5
  116.2 1.8 %fusion.2 = f32[512,768]{1,0:T(8,128)S(1)} fusion(bf16[512,2048]{1,0:T(8,128)(2,1)S(1)} %bitcast.67, bf16[1,2048,768]{2,1,0:T(8,128)(2,1)S(1)} %copy-done.5), kind=kOutput, calls=%fused_computation.2 | convolution fusion | flops 1610612736 | bytes 6815744 | tf_op jit(solution)/shard_map/dot_general | solution.py:212
  118.0 0.1 copy-done.6
  118.1 1.8 %fusion.4 = f32[512,768]{1,0:T(8,128)S(1)} fusion(bf16[512,2048]{1,0:T(8,128)(2,1)S(1)} %bitcast.68, bf16[1,2048,768]{2,1,0:T(8,128)(2,1)S(1)} %copy-done.6), kind=kOutput, calls=%fused_computation.4 | convolution fusion | flops 1610612736 | bytes 6815744 | tf_op jit(solution)/shard_map/dot_general | solution.py:211
  119.9 0.0 copy-done
  119.9 1.8 %fusion.6 = bf16[512,2048]{1,0:T(8,128)(2,1)S(1)} fusion(bf16[1,768,2048]{2,1,0:T(8,128)(2,1)S(1)} %copy-done, f32[512,768]{1,0:T(8,128)S(1)} %fusion.2, f32[512,768]{1,0:T(8,128)S(1)} %fusion.4), kind=kOutput, calls=%fused_computation.6 | convolution fusion | flops 1614020608 | bytes 8388608 | tf_op jit(solution)/shard_map/dot_general | solution.py:216
  121.8 2.9 %copy.63 = bf16[4,128,2048]{2,0,1:T(4,128)(2,1)} copy(bf16[4,128,2048]{2,1,0:T(8,128)(2,1)S(1)} %bitcast.69) | data formatting | bytes 4194304 | tf_op jit(solution)/shard_map/reshape | solution.py:218
  124.7 5.9 %all-to-all-start.3 = ((bf16[4,128,2048]{2,0,1:T(4,128)(2,1)}), bf16[4,128,2048]{2,0,1:T(4,128)(2,1)}, u32[]{:S(2)}, u32[]{:S(2)}) async-start(bf16[4,128,2048]{2,0,1:T(4,128)(2,1)} %copy.63), calls=%async_computation.3 | async-start | bytes 4194304 | tf_op jit(solution)/shard_map/all_to_all | solution.py:215
  130.6 0.0 copy-done.3
  130.6 0.1 copy.60
  130.7 0.2 select_reduce_fusion
  130.9 29.5 %all-to-all-done.3 = bf16[4,128,2048]{2,0,1:T(4,128)(2,1)} async-done(((bf16[4,128,2048]{2,0,1:T(4,128)(2,1)}), bf16[4,128,2048]{2,0,1:T(4,128)(2,1)}, u32[]{:S(2)}, u32[]{:S(2)}) %all-to-all-start.3) | async-done | bytes 2097184 | tf_op jit(solution)/shard_map/all_to_all | solution.py:215
  160.4 2.7 %copy.64 = bf16[4,128,2048]{2,1,0:T(8,128)(2,1)S(1)} copy(bf16[4,128,2048]{2,0,1:T(4,128)(2,1)} %all-to-all-done.3) | data formatting | bytes 4194304 | tf_op jit(solution)/shard_map/all_to_all | solution.py:215
  163.2 2.7 %fusion.9 = bf16[32,2048]{1,0:T(8,128)(2,1)} fusion(f32[32,512]{1,0:T(8,128)S(1)} %select_reduce_fusion, bf16[512,2048]{1,0:T(8,128)(2,1)S(1)} %bitcast.64, f32[32,2048]{1,0:T(8,128)S(1)} %convert_reduce_fusion, bf16[256,2048]{1,0:T(8,128)(2,1)} %param.15, s32[]{:T(128)S(6)} %select_n.38), kind=kOutput, calls=%fused_computation.11 | convolution fusion | flops 402915328 | bytes 2686980 | tf_op jit(solution)/shard_map/dot_general | solution.py:225
  (22 shorter events, 0.2 us)
Async XLA Ops:
  0.0 119.9 %copy-start = (bf16[1,768,2048]{2,1,0:T(8,128)(2,1)S(1)}, bf16[1,768,2048]{2,1,0:T(8,128)(2,1)}, u32[]{:S(2)}) copy-start(bf16[1,768,2048]{2,1,0:T(8,128)(2,1)} %param.29) | copy-start | bytes 9437188
  0.0 4.2 %copy-start.7 = (f32[2048]{0:T(1024)S(1)}, f32[2048]{0:T(1024)}, u32[]{:S(2)}) copy-start(f32[2048]{0:T(1024)} %param.16) | copy-start | bytes 24580
  0.0 3.8 %copy-start.8 = (s32[6]{0:T(128)S(1)}, s32[6]{0:T(128)}, u32[]{:S(2)}) copy-start(s32[6]{0:T(128)} %param.24) | copy-start | bytes 76
  1.7 4.4 %copy-start.4 = (f32[128]{0:T(128)S(1)}, f32[128]{0:T(128)}, u32[]{:S(2)}) copy-start(f32[128]{0:T(128)} %param.21) | copy-start | bytes 1540
  8.1 23.0 %all-to-all-start = ((bf16[8,2,256,128]{3,2,1,0:T(8,128)(2,1)}), bf16[8,2,256,128]{3,2,1,0:T(8,128)(2,1)}, u32[]{:S(2)}, u32[]{:S(2)}) async-start(bf16[8,2,256,128]{3,2,1,0:T(8,128)(2,1)} %broadcast_in_dim.27), calls=%async_computation | async-start | bytes 2097152 | tf_op jit(solution)/shard_map/all_to_all | solution.py:172
  24.8 6.3 %copy-start.2 = (s32[32,8]{0,1:T(8,128)S(1)}, s32[32,8]{0,1:T(8,128)}, u32[]{:S(2)}) copy-start(s32[32,8]{0,1:T(8,128)} %param.25) | copy-start | bytes 3076
  31.1 3.0 %collective-permute-start = (bf16[8,2,256,128]{3,2,1,0:T(8,128)(2,1)}, bf16[8,2,256,128]{3,2,1,0:T(8,128)(2,1)}, u32[]{:S(2)}, u32[]{:S(2)}) collective-permute-start(bf16[8,2,256,128]{3,2,1,0:T(8,128)(2,1)} %all-to-all-done.own_ref), channel_id=1, source_target_pairs={{0,8},{8,0},{16,24},{24,16},{32,40},{40,32},{48,56},{56,48},{64,72... | collective-permute-start | bytes 3145736 | tf_op jit(solution)/shard_map/ppermute | solution.py:189
  42.4 23.9 %copy-start.1 = (f32[2048]{0:T(1024)S(1)}, f32[2048]{0:T(1024)}, u32[]{:S(2)}) copy-start(f32[2048]{0:T(1024)} %param.23) | copy-start | bytes 24580
  42.4 21.4 %all-to-all-start.1 = ((bf16[8,32,2048]{2,1,0:T(8,128)(2,1)}), bf16[8,32,2048]{2,1,0:T(8,128)(2,1)}, u32[]{:S(2)}, u32[]{:S(2)}) async-start(bf16[8,32,2048]{2,1,0:T(8,128)(2,1)} %bitcast.66), calls=%async_computation.1 | async-start | bytes 2097152 | tf_op jit(solution)/shard_map/all_to_all | solution.py:193
  114.3 1.9 %copy-start.5 = (bf16[1,2048,768]{2,1,0:T(8,128)(2,1)S(1)}, bf16[1,2048,768]{2,1,0:T(8,128)(2,1)}, u32[]{:S(2)}) copy-start(bf16[1,2048,768]{2,1,0:T(8,128)(2,1)} %param.28) | copy-start | bytes 9437188
  116.2 1.9 %copy-start.6 = (bf16[1,2048,768]{2,1,0:T(8,128)(2,1)S(1)}, bf16[1,2048,768]{2,1,0:T(8,128)(2,1)}, u32[]{:S(2)}) copy-start(bf16[1,2048,768]{2,1,0:T(8,128)(2,1)} %param.27) | copy-start | bytes 9437188
  124.7 5.9 %copy-start.3 = (f32[32,8]{0,1:T(8,128)S(1)}, f32[32,8]{0,1:T(8,128)}, u32[]{:S(2)}) copy-start(f32[32,8]{0,1:T(8,128)} %param.26) | copy-start | bytes 3076
  124.7 35.7 %all-to-all-start.3 = ((bf16[4,128,2048]{2,0,1:T(4,128)(2,1)}), bf16[4,128,2048]{2,0,1:T(4,128)(2,1)}, u32[]{:S(2)}, u32[]{:S(2)}) async-start(bf16[4,128,2048]{2,0,1:T(4,128)(2,1)} %copy.63), calls=%async_computation.3 | async-start | bytes 4194304 | tf_op jit(solution)/shard_map/all_to_all | solution.py:215

commit v12 on v11

--- a/solution.py
+++ b/solution.py
@@ -40,7 +40,7 @@
 ):
     heads = q_ref.shape[1] // dim
     tok = q_ref.shape[0]
-    block = own_ref.shape[2]
+    block = 2 * own_ref.shape[2]
     parts = []
     for h in range(heads):
         part = q_ref[:, h * dim : (h + 1) * dim]
@@ -54,9 +54,15 @@
 
     def step(j, carry, masked):
         high, total, accum = carry
-        mine = j % 2 == bounds_ref[4]
-        keys = jnp.where(mine, own_ref[j // 2, 0], other_ref[j // 2, 0])
-        values = jnp.where(mine, own_ref[j // 2, 1], other_ref[j // 2, 1])
+        even = bounds_ref[4] == 0
+        keys = jnp.concatenate(
+            [jnp.where(even, own_ref[j, 0], other_ref[j, 0]), jnp.where(even, other_ref[j, 0], own_ref[j, 0])],
+            axis=0,
+        )
+        values = jnp.concatenate(
+            [jnp.where(even, own_ref[j, 1], other_ref[j, 1]), jnp.where(even, other_ref[j, 1], own_ref[j, 1])],
+            axis=0,
+        )
         scores = lax.dot_general(q, keys, (((1,), (1,)), ((), ())), preferred_element_type=jnp.float32) * scale
         if masked:
             key_pos = j * block + lax.broadcasted_iota(jnp.int32, (1, block), 1)
@@ -170,7 +176,7 @@
     groups = [[2 * i + c for i in range(pairs)] for c in range(2)]
     spread = jnp.broadcast_to(stacked[None], (pairs,) + stacked.shape)
     same_core = lax.all_to_all(spread, "seq", 0, 0, tiled=True, axis_index_groups=groups)
-    block = tok_dev
+    block = 2 * tok_dev
     low = own_start[0] // block
     high = positions[-1] // block + 1
     inner_low = jnp.clip(-(-own_start[-1] // block), low, high)

time: 167 us -> 165 us (0.988)
  no operation moved by 1% of the time
where the time goes in v12:
time: 165 us
  waiting for transfers between devices  47.6 us (29%)
  blocking collectives  44.2 us (27%)
  starting transfers between devices  18.4 us (11%)
  matrix products  17.1 us (10%)
  local copies, waits for them, and re-layouts  15.1 us (9%)
  Pallas kernels  8.82 us (5%)
  between operations  7.21 us (4%)
  other arithmetic  7.03 us (4%)
    all_to_all x1, blocking collectives, local(): lax.all_to_all(outgoing, ('seq', 'head'), split_axis=1, concat_axis=1, ti...  44.2 us
    all_to_all x1, waiting for transfers between devices, local(): lax.all_to_all(jnp.dot(hidden, w_down[0], preferred_element_type=jnp.floa...  29.5 us
    all_to_all x1, waiting for transfers between devices, local(): lax.all_to_all(terms.reshape(n_head, rows, width), 'head', 0, 0, tiled=True)  14.9 us
    pallas_call x1, Pallas kernels, attend(): pl.pallas_call(kernel, grid_spec=spec, out_shape=jax.ShapeDtypeStruct((to...  8.82 us
    all_to_all x1, starting transfers between devices, local(): lax.all_to_all(spread, 'seq', 0, 0, tiled=True, axis_index_groups=groups)  7.03 us
    all_to_all x1, starting transfers between devices, local(): lax.all_to_all(jnp.dot(hidden, w_down[0], preferred_element_type=jnp.floa...  5.91 us
    all_to_all x1, starting transfers between devices, local(): lax.all_to_all(terms.reshape(n_head, rows, width), 'head', 0, 0, tiled=True)  5.48 us
    dot_general x1, matrix products, local(): queries = jnp.dot(normed, w_query, preferred_element_type=jnp.float32)  3.49 us
  transfers between devices with their start and end apart: 4, of which 4 were waited for; matrix products, arithmetic and copies ran while one was open for 6% of the time, Pallas kernels for 0%

profile of v12, /device:TPU:0, one launch (start us, length us, event | category | flops | bytes accessed | tf_op | source)
XLA Modules:
  0.0 165.5 jit_solution(5358494042284572992)
XLA Ops:
  0.0 0.0 copy-start
  0.0 0.0 copy-start.7
  0.0 0.0 copy-start.8
  0.0 1.7 %fusion.10 = f32[256]{0:T(256)S(1)} fusion(bf16[256,2048]{1,0:T(8,128)(2,1)} %param.15), kind=kLoop, calls=%fused_computation.12 | loop fusion | flops 1572608 | bytes 1049600 | tf_op jit(solution)/shard_map/reduce_sum | solution.py:22
  1.7 0.0 copy-start.4
  1.7 2.0 %multiply_reduce_fusion.1 = (f32[256]{0:T(256)S(1)}, f32[256,128]{0,1:T(8,128)S(1)}) fusion(bf16[2048,512]{1,0:T(8,128)(2,1)} %param.18, s32[]{:T(128)S(6)} %select_n.46, bf16[256,2048]{1,0:T(8,128)(2,1)} %param.15, f32[2048]{0:T(1024)} %param.16, f32[256]{0:T(256)S(1)} %add_rsqrt_fusion.1), kind=kOutput, calls=%fused_computation.51 | convolution fusion | flops 136380160 | bytes 1714180 | tf_op jit(solution)/shard_map/dot_general | solution.py:169
  3.7 0.1 copy.52
  3.8 0.0 copy-done.8
  3.8 0.2 reduce-window.18
  4.0 0.1 convert_reduce_fusion.1
  4.1 0.1 select_reduce_fusion.1
  4.2 0.0 copy-done.7
  4.2 1.9 %fusion.13 = bf16[1,256,128]{2,1,0:T(8,128)(2,1)S(1)} fusion(bf16[2048,512]{1,0:T(8,128)(2,1)} %param.19, s32[]{:T(128)S(6)} %select_n.46, bf16[256,2048]{1,0:T(8,128)(2,1)} %param.15, f32[2048]{0:T(1024)S(1)} %copy-done.7, f32[256]{0:T(256)S(1)} %add_rsqrt_fusion.1), kind=kOutput, calls=%fused_computation.18 | convolution fusion | flops 136347648 | bytes 1647620 | tf_op jit(solution)/shard_map/dot_general | solution.py:173
  6.1 0.0 copy-done.4
  6.1 0.1 multiply_multiply_fusion
  6.2 0.6 fusion.34
  6.8 0.1 pad_maximum_fusion.2
  6.9 1.2 broadcast_in_dim.27
  8.1 7.0 %all-to-all-start = ((bf16[8,2,256,128]{3,2,1,0:T(8,128)(2,1)}), bf16[8,2,256,128]{3,2,1,0:T(8,128)(2,1)}, u32[]{:S(2)}, u32[]{:S(2)}) async-start(bf16[8,2,256,128]{3,2,1,0:T(8,128)(2,1)} %broadcast_in_dim.27), calls=%async_computation | async-start | bytes 2097152 | tf_op jit(solution)/shard_map/all_to_all | solution.py:178
  15.1 0.6 fusion.44
  15.7 0.6 fusion.43
  23.3 0.7 stack.30.bounds_ref
  24.0 0.8 pad_maximum_fusion
  24.8 0.0 copy-start.2
  24.8 3.5 %fusion.41.q_ref = f32[256,512]{1,0:T(8,128)} fusion(bf16[2048,512]{1,0:T(8,128)(2,1)} %param.17, bf16[256,2048]{1,0:T(8,128)(2,1)} %param.15, f32[2048]{0:T(1024)} %param.16, f32[256]{0:T(256)S(1)} %add_rsqrt_fusion.1), kind=kOutput, calls=%fused_computation.74 | convolution fusion | flops 538968064 | bytes 3679232 | tf_op jit(solution)/shard_map/dot_general | solution.py:164
  28.3 2.8 %all-to-all-done.own_ref = bf16[8,2,256,128]{3,2,1,0:T(8,128)(2,1)} async-done(((bf16[8,2,256,128]{3,2,1,0:T(8,128)(2,1)}), bf16[8,2,256,128]{3,2,1,0:T(8,128)(2,1)}, u32[]{:S(2)}, u32[]{:S(2)}) %all-to-all-start) | async-done | bytes 1048608 | tf_op jit(solution)/shard_map/all_to_all | solution.py:178
  31.1 0.0 collective-permute-start
  31.1 0.0 copy-done.2
  31.1 0.1 copy.55
  31.2 0.1 eq.61
  31.3 0.1 eq.57
  31.4 0.1 copy.57
  31.5 0.2 fusion.26
  31.7 1.0 copy.53.qpos_ref
  32.7 1.0 copy.54.qstart_ref
  33.7 0.3 collective-permute-done.other_ref
  34.1 8.8 %shard_map.145 = bf16[256,2048]{1,0:T(8,128)(2,1)} custom-call(s32[5]{0:T(128)} %stack.30.bounds_ref, f32[256,512]{1,0:T(8,128)} %fusion.41.q_ref, f32[256,128]{1,0:T(8,128)} %get-tuple-element.17.cos_ref, f32[256,128]{1,0:T(8,128)} %get-tuple-element.18.sin_ref, f32[1,128]{1,0:T(1,128)} %bitcast.76, bf16[8,2,256,128]{3,2,1,0:T(8,128)(2,1)} %all-to-all-done.own_ref, ...), custom_call_target="tpu_custom_call" | custom-call | tf_op jit(solution)/shard_map/pallas_call | solution.py:120
  42.9 0.0 copy-start.1
  42.9 5.5 %all-to-all-start.1 = ((bf16[8,32,2048]{2,1,0:T(8,128)(2,1)}), bf16[8,32,2048]{2,1,0:T(8,128)(2,1)}, u32[]{:S(2)}, u32[]{:S(2)}) async-start(bf16[8,32,2048]{2,1,0:T(8,128)(2,1)} %bitcast.66), calls=%async_computation.1 | async-start | bytes 2097152 | tf_op jit(solution)/shard_map/all_to_all | solution.py:199
  48.5 0.2 fusion.28
  48.7 0.1 mul.144
  48.8 0.2 fusion.15
  49.0 14.9 %all-to-all-done.1 = bf16[8,32,2048]{2,1,0:T(8,128)(2,1)} async-done(((bf16[8,32,2048]{2,1,0:T(8,128)(2,1)}), bf16[8,32,2048]{2,1,0:T(8,128)(2,1)}, u32[]{:S(2)}, u32[]{:S(2)}) %all-to-all-start.1) | async-done | bytes 1048608 | tf_op jit(solution)/shard_map/all_to_all | solution.py:199
  64.0 1.4 convert_reduce_fusion
  65.3 1.1 multiply_reduce_fusion
  66.4 0.0 copy-done.1
  66.4 1.7 %convolution_convert_fusion = bf16[512,2048]{1,0:T(8,128)(2,1)S(1)} fusion(pred[32,512]{1,0:T(8,128)(4,1)S(1)} %fusion.15, f32[2048]{0:T(1024)S(1)} %copy-done.1, f32[32]{0:T(128)S(1)} %add_rsqrt_fusion.2, f32[32,2048]{1,0:T(8,128)S(1)} %convert_reduce_fusion, bf16[256,2048]{1,0:T(8,128)(2,1)} %param.15, s32[]{:T(128)S(6)} %select_n.38), kind=kOutput, calls=%fused_computation.7 | convolution fusion | flops 68485120 | bytes 2515076 | tf_op jit(solution)/shard_map/dot_general | solution.py:213
  68.1 1.6 copy.61
  69.7 44.2 %all_to_all.20 = bf16[4,128,2048]{2,0,1:T(4,128)(2,1)S(1)} all-to-all(bf16[4,128,2048]{2,0,1:T(4,128)(2,1)S(1)} %copy.61), channel_id=1, replica_groups=mesh['seq'=16,'head'=8] {'seq','head'}, dimensions={1} | all-to-all | bytes 4194304 | tf_op jit(solution)/shard_map/all_to_all | solution.py:215
  113.9 1.2 copy.62
  115.1 0.7 copy-done.5
  115.8 1.8 %fusion.2 = f32[512,768]{1,0:T(8,128)S(1)} fusion(bf16[512,2048]{1,0:T(8,128)(2,1)S(1)} %bitcast.67, bf16[1,2048,768]{2,1,0:T(8,128)(2,1)S(1)} %copy-done.5), kind=kOutput, calls=%fused_computation.2 | convolution fusion | flops 1610612736 | bytes 6815744 | tf_op jit(solution)/shard_map/dot_general | solution.py:218
  117.6 0.1 copy-done.6
  117.7 1.8 %fusion.4 = f32[512,768]{1,0:T(8,128)S(1)} fusion(bf16[512,2048]{1,0:T(8,128)(2,1)S(1)} %bitcast.68, bf16[1,2048,768]{2,1,0:T(8,128)(2,1)S(1)} %copy-done.6), kind=kOutput, calls=%fused_computation.4 | convolution fusion | flops 1610612736 | bytes 6815744 | tf_op jit(solution)/shard_map/dot_general | solution.py:217
  119.5 0.0 copy-done
  119.5 1.9 %fusion.6 = bf16[512,2048]{1,0:T(8,128)(2,1)S(1)} fusion(bf16[1,768,2048]{2,1,0:T(8,128)(2,1)S(1)} %copy-done, f32[512,768]{1,0:T(8,128)S(1)} %fusion.2, f32[512,768]{1,0:T(8,128)S(1)} %fusion.4), kind=kOutput, calls=%fused_computation.6 | convolution fusion | flops 1614020608 | bytes 8388608 | tf_op jit(solution)/shard_map/dot_general | solution.py:222
  121.4 2.9 %copy.63 = bf16[4,128,2048]{2,0,1:T(4,128)(2,1)} copy(bf16[4,128,2048]{2,1,0:T(8,128)(2,1)S(1)} %bitcast.69) | data formatting | bytes 4194304 | tf_op jit(solution)/shard_map/reshape | solution.py:224
  124.3 5.9 %all-to-all-start.3 = ((bf16[4,128,2048]{2,0,1:T(4,128)(2,1)}), bf16[4,128,2048]{2,0,1:T(4,128)(2,1)}, u32[]{:S(2)}, u32[]{:S(2)}) async-start(bf16[4,128,2048]{2,0,1:T(4,128)(2,1)} %copy.63), calls=%async_computation.3 | async-start | bytes 4194304 | tf_op jit(solution)/shard_map/all_to_all | solution.py:221
  130.2 0.0 copy-done.3
  130.2 0.1 copy.60
  130.3 0.2 select_reduce_fusion
  130.6 29.5 %all-to-all-done.3 = bf16[4,128,2048]{2,0,1:T(4,128)(2,1)} async-done(((bf16[4,128,2048]{2,0,1:T(4,128)(2,1)}), bf16[4,128,2048]{2,0,1:T(4,128)(2,1)}, u32[]{:S(2)}, u32[]{:S(2)}) %all-to-all-start.3) | async-done | bytes 2097184 | tf_op jit(solution)/shard_map/all_to_all | solution.py:221
  160.1 2.7 %copy.64 = bf16[4,128,2048]{2,1,0:T(8,128)(2,1)S(1)} copy(bf16[4,128,2048]{2,0,1:T(4,128)(2,1)} %all-to-all-done.3) | data formatting | bytes 4194304 | tf_op jit(solution)/shard_map/all_to_all | solution.py:221
  162.8 2.7 %fusion.9 = bf16[32,2048]{1,0:T(8,128)(2,1)} fusion(f32[32,512]{1,0:T(8,128)S(1)} %select_reduce_fusion, bf16[512,2048]{1,0:T(8,128)(2,1)S(1)} %bitcast.64, f32[32,2048]{1,0:T(8,128)S(1)} %convert_reduce_fusion, bf16[256,2048]{1,0:T(8,128)(2,1)} %param.15, s32[]{:T(128)S(6)} %select_n.38), kind=kOutput, calls=%fused_computation.11 | convolution fusion | flops 402915328 | bytes 2686980 | tf_op jit(solution)/shard_map/dot_general | solution.py:231
  (22 shorter events, 0.2 us)
Async XLA Ops:
  0.0 119.5 %copy-start = (bf16[1,768,2048]{2,1,0:T(8,128)(2,1)S(1)}, bf16[1,768,2048]{2,1,0:T(8,128)(2,1)}, u32[]{:S(2)}) copy-start(bf16[1,768,2048]{2,1,0:T(8,128)(2,1)} %param.29) | copy-start | bytes 9437188
  0.0 4.2 %copy-start.7 = (f32[2048]{0:T(1024)S(1)}, f32[2048]{0:T(1024)}, u32[]{:S(2)}) copy-start(f32[2048]{0:T(1024)} %param.16) | copy-start | bytes 24580
  0.0 3.8 %copy-start.8 = (s32[6]{0:T(128)S(1)}, s32[6]{0:T(128)}, u32[]{:S(2)}) copy-start(s32[6]{0:T(128)} %param.24) | copy-start | bytes 76
  1.7 4.4 %copy-start.4 = (f32[128]{0:T(128)S(1)}, f32[128]{0:T(128)}, u32[]{:S(2)}) copy-start(f32[128]{0:T(128)} %param.21) | copy-start | bytes 1540
  8.1 23.0 %all-to-all-start = ((bf16[8,2,256,128]{3,2,1,0:T(8,128)(2,1)}), bf16[8,2,256,128]{3,2,1,0:T(8,128)(2,1)}, u32[]{:S(2)}, u32[]{:S(2)}) async-start(bf16[8,2,256,128]{3,2,1,0:T(8,128)(2,1)} %broadcast_in_dim.27), calls=%async_computation | async-start | bytes 2097152 | tf_op jit(solution)/shard_map/all_to_all | solution.py:178
  24.8 6.3 %copy-start.2 = (s32[32,8]{0,1:T(8,128)S(1)}, s32[32,8]{0,1:T(8,128)}, u32[]{:S(2)}) copy-start(s32[32,8]{0,1:T(8,128)} %param.25) | copy-start | bytes 3076
  31.1 3.0 %collective-permute-start = (bf16[8,2,256,128]{3,2,1,0:T(8,128)(2,1)}, bf16[8,2,256,128]{3,2,1,0:T(8,128)(2,1)}, u32[]{:S(2)}, u32[]{:S(2)}) collective-permute-start(bf16[8,2,256,128]{3,2,1,0:T(8,128)(2,1)} %all-to-all-done.own_ref), channel_id=1, source_target_pairs={{0,8},{8,0},{16,24},{24,16},{32,40},{40,32},{48,56},{56,48},{64,72... | collective-permute-start | bytes 3145736 | tf_op jit(solution)/shard_map/ppermute | solution.py:195
  42.9 23.5 %copy-start.1 = (f32[2048]{0:T(1024)S(1)}, f32[2048]{0:T(1024)}, u32[]{:S(2)}) copy-start(f32[2048]{0:T(1024)} %param.23) | copy-start | bytes 24580
  42.9 21.0 %all-to-all-start.1 = ((bf16[8,32,2048]{2,1,0:T(8,128)(2,1)}), bf16[8,32,2048]{2,1,0:T(8,128)(2,1)}, u32[]{:S(2)}, u32[]{:S(2)}) async-start(bf16[8,32,2048]{2,1,0:T(8,128)(2,1)} %bitcast.66), calls=%async_computation.1 | async-start | bytes 2097152 | tf_op jit(solution)/shard_map/all_to_all | solution.py:199
  113.9 1.9 %copy-start.5 = (bf16[1,2048,768]{2,1,0:T(8,128)(2,1)S(1)}, bf16[1,2048,768]{2,1,0:T(8,128)(2,1)}, u32[]{:S(2)}) copy-start(bf16[1,2048,768]{2,1,0:T(8,128)(2,1)} %param.28) | copy-start | bytes 9437188
  115.8 1.9 %copy-start.6 = (bf16[1,2048,768]{2,1,0:T(8,128)(2,1)S(1)}, bf16[1,2048,768]{2,1,0:T(8,128)(2,1)}, u32[]{:S(2)}) copy-start(bf16[1,2048,768]{2,1,0:T(8,128)(2,1)} %param.27) | copy-start | bytes 9437188
  124.3 5.9 %copy-start.3 = (f32[32,8]{0,1:T(8,128)S(1)}, f32[32,8]{0,1:T(8,128)}, u32[]{:S(2)}) copy-start(f32[32,8]{0,1:T(8,128)} %param.26) | copy-start | bytes 3076
  124.3 35.7 %all-to-all-start.3 = ((bf16[4,128,2048]{2,0,1:T(4,128)(2,1)}), bf16[4,128,2048]{2,0,1:T(4,128)(2,1)}, u32[]{:S(2)}, u32[]{:S(2)}) async-start(bf16[4,128,2048]{2,0,1:T(4,128)(2,1)} %copy.63), calls=%async_computation.3 | async-start | bytes 4194304 | tf_op jit(solution)/shard_map/all_to_all | solution.py:221

commit v13 on v12

--- a/solution.py
+++ b/solution.py
@@ -205,31 +205,29 @@
     chosen = expert_ids.reshape(-1)
     hits = (chosen[:, None] == jnp.arange(experts, dtype=jnp.int32)[None, :]).astype(jnp.int32)
     rank = jnp.sum((jnp.cumsum(hits, axis=0) - hits) * hits, axis=1)
-    slot = rank * experts + chosen
-    select = (slot[:, None] == jnp.arange(capacity * experts, dtype=jnp.int32)[None, :]).reshape(
-        rows, TOP, capacity * experts
-    )
-    sources = jnp.transpose(jnp.any(select, axis=1)).astype(jnp.bfloat16)
-    outgoing = jnp.dot(sources, routed, preferred_element_type=jnp.float32).astype(jnp.bfloat16)
-    outgoing = outgoing.reshape(capacity, experts, width)
-    block = lax.all_to_all(outgoing, ("seq", "head"), split_axis=1, concat_axis=1, tiled=True)
-    flat = block.reshape(-1, width)
-    gate = jnp.dot(flat, w_gate[0], preferred_element_type=jnp.float32)
-    up = jnp.dot(flat, w_up[0], preferred_element_type=jnp.float32)
+    slot = chosen * capacity + rank
+    select = (slot[:, None] == jnp.arange(experts * capacity, dtype=jnp.int32)[None, :]).reshape(
+        rows, TOP, experts, capacity
+    )
+    sources = jnp.any(select, axis=1).astype(jnp.bfloat16)
+    outgoing = lax.dot_general(
+        sources, routed, (((0,), (0,)), ((), ())), preferred_element_type=jnp.float32
+    ).astype(jnp.bfloat16)
+    block = lax.all_to_all(outgoing, ("seq", "head"), split_axis=0, concat_axis=0, tiled=True)
+    gate = jnp.einsum("scd,df->scf", block, w_gate[0], preferred_element_type=jnp.float32)
+    up = jnp.einsum("scd,df->scf", block, w_up[0], preferred_element_type=jnp.float32)
     gate, up = lax.optimization_barrier((gate, up))
     hidden = (jax.nn.silu(gate) * up).astype(jnp.bfloat16)
+    down = jnp.einsum("scf,fd->scd", hidden, w_down[0], preferred_element_type=jnp.float32)
     returned = lax.all_to_all(
-        jnp.dot(hidden, w_down[0], preferred_element_type=jnp.float32)
-        .astype(jnp.bfloat16)
-        .reshape(block.shape),
-        ("seq", "head"),
-        split_axis=1,
-        concat_axis=1,
-        tiled=True,
-    ).reshape(-1, width)
-    mixing = jnp.sum(jnp.where(select, route_weights[:, :, None], 0.0), axis=1)
-    combined = jnp.dot(
-        mixing, returned.astype(jnp.float32), precision=lax.Precision.HIGHEST,
+        down.astype(jnp.bfloat16), ("seq", "head"), split_axis=0, concat_axis=0, tiled=True
+    )
+    mixing = jnp.sum(jnp.where(select, route_weights[:, :, None, None], 0.0), axis=1)
+    combined = lax.dot_general(
+        mixing,
+        returned.astype(jnp.float32),
+        (((1, 2), (0, 1)), ((), ())),
+        precision=lax.Precision.HIGHEST,
         preferred_element_type=jnp.float32,
     )
     return (resid + combined).astype(jnp.bfloat16)

time: 165 us -> 167 us (1.012)
  matrix products: 17.1 us -> 23.4 us
  local copies, waits for them, and re-layouts: 15.1 us -> 10.4 us
    dot_general x5, matrix products: 9.83 us -> 16.1 us  [the longest x1 5.35 us: local(): lax.dot_general(mixing, returned.astype(jnp.float32), (((1, 2), (0, 1)),...]
    convert_element_type x0 -> x2, local copies, waits for them, and re-layouts: none -> 4.54 us  [the longest x1 2.91 us: local(): down.astype(jnp.bfloat16)]
    reshape x2 -> x0, local copies, waits for them, and re-layouts: 4.54 us -> none  [the longest x1 2.91 us: local(): returned = lax.all_to_all(jnp.dot(hidden, w_down[0], preferred_element_ty...]
    all_to_all x2 -> x0, local copies, waits for them, and re-layouts: 3.9 us -> none  [the longest x1 2.74 us: local(): lax.all_to_all(jnp.dot(hidden, w_down[0], preferred_element_type=jnp.floa...]
where the time goes in v13:
time: 167 us; the launch traced here: 166 us
  waiting for transfers between devices  47.3 us (28%)
  blocking collectives  43.6 us (26%)
  matrix products  23.4 us (14%)
  starting transfers between devices  18.6 us (11%)
  local copies, waits for them, and re-layouts  10.4 us (6%)
  Pallas kernels  8.82 us (5%)
  between operations  7.19 us (4%)
  other arithmetic  7.12 us (4%)
    all_to_all x1, blocking collectives, local(): lax.all_to_all(outgoing, ('seq', 'head'), split_axis=0, concat_axis=0, ti...  43.6 us
    all_to_all x1, waiting for transfers between devices, local(): lax.all_to_all(down.astype(jnp.bfloat16), ('seq', 'head'), split_axis=0,...  29.3 us
    all_to_all x1, waiting for transfers between devices, local(): lax.all_to_all(terms.reshape(n_head, rows, width), 'head', 0, 0, tiled=True)  14.8 us
    pallas_call x1, Pallas kernels, attend(): pl.pallas_call(kernel, grid_spec=spec, out_shape=jax.ShapeDtypeStruct((to...  8.82 us
    all_to_all x1, starting transfers between devices, local(): lax.all_to_all(spread, 'seq', 0, 0, tiled=True, axis_index_groups=groups)  7.03 us
    all_to_all x1, starting transfers between devices, local(): lax.all_to_all(down.astype(jnp.bfloat16), ('seq', 'head'), split_axis=0,...  6.13 us
    all_to_all x1, starting transfers between devices, local(): lax.all_to_all(terms.reshape(n_head, rows, width), 'head', 0, 0, tiled=True)  5.48 us
    dot_general x1, matrix products, local(): lax.dot_general(mixing, returned.astype(jnp.float32), (((1, 2), (0, 1)),...  5.35 us
  transfers between devices with their start and end apart: 4, of which 4 were waited for; matrix products, arithmetic and copies ran while one was open for 6% of the time, Pallas kernels for 0%

profile of v13, /device:TPU:0, one launch (start us, length us, event | category | flops | bytes accessed | tf_op | source)
XLA Modules:
  0.0 166.4 jit_solution(7821441411344294822)
XLA Ops:
  0.0 0.0 copy-start
  0.0 0.0 copy-start.7
  0.0 0.0 copy-start.8
  0.0 1.7 fusion.11
  1.7 0.0 copy-start.4
  1.7 2.0 %multiply_reduce_fusion.1 = (f32[256]{0:T(256)S(1)}, f32[256,128]{0,1:T(8,128)S(1)}) fusion(bf16[2048,512]{1,0:T(8,128)(2,1)} %param.18, s32[]{:T(128)S(6)} %select_n.46, bf16[256,2048]{1,0:T(8,128)(2,1)} %param.15, f32[2048]{0:T(1024)} %param.16, f32[256]{0:T(256)S(1)} %add_rsqrt_fusion.1), kind=kOutput, calls=%fused_computation.56 | convolution fusion | flops 136380160 | bytes 1714180 | tf_op jit(solution)/shard_map/dot_general | solution.py:169
  3.7 0.1 copy.42
  3.8 0.0 copy-done.8
  3.8 0.2 reduce-window.18
  4.0 0.1 convert_reduce_fusion.1
  4.1 0.1 select_reduce_fusion
  4.2 0.0 copy-done.7
  4.2 1.9 %fusion.17 = bf16[1,256,128]{2,1,0:T(8,128)(2,1)S(1)} fusion(bf16[2048,512]{1,0:T(8,128)(2,1)} %param.19, s32[]{:T(128)S(6)} %select_n.46, bf16[256,2048]{1,0:T(8,128)(2,1)} %param.15, f32[2048]{0:T(1024)S(1)} %copy-done.7, f32[256]{0:T(256)S(1)} %add_rsqrt_fusion.1), kind=kOutput, calls=%fused_computation.22 | convolution fusion | flops 136347648 | bytes 1647620 | tf_op jit(solution)/shard_map/dot_general | solution.py:173
  6.1 0.0 copy-done.4
  6.1 0.1 multiply_multiply_fusion
  6.2 0.6 fusion.41
  6.8 0.1 pad_maximum_fusion.2
  6.9 1.2 broadcast_in_dim.27
  8.1 7.0 %all-to-all-start = ((bf16[8,2,256,128]{3,2,1,0:T(8,128)(2,1)}), bf16[8,2,256,128]{3,2,1,0:T(8,128)(2,1)}, u32[]{:S(2)}, u32[]{:S(2)}) async-start(bf16[8,2,256,128]{3,2,1,0:T(8,128)(2,1)} %broadcast_in_dim.27), calls=%async_computation | async-start | bytes 2097152 | tf_op jit(solution)/shard_map/all_to_all | solution.py:178
  15.1 0.6 fusion.51
  15.7 0.6 fusion.52
  23.3 0.7 stack.30.bounds_ref
  23.9 0.8 pad_maximum_fusion
  24.8 0.0 copy-start.2
  24.8 3.5 %fusion.49.q_ref = f32[256,512]{1,0:T(8,128)} fusion(bf16[2048,512]{1,0:T(8,128)(2,1)} %param.17, bf16[256,2048]{1,0:T(8,128)(2,1)} %param.15, f32[2048]{0:T(1024)} %param.16, f32[256]{0:T(256)S(1)} %add_rsqrt_fusion.1), kind=kOutput, calls=%fused_computation.82 | convolution fusion | flops 538968064 | bytes 3679232 | tf_op jit(solution)/shard_map/dot_general | solution.py:164
  28.3 2.8 %all-to-all-done.own_ref = bf16[8,2,256,128]{3,2,1,0:T(8,128)(2,1)} async-done(((bf16[8,2,256,128]{3,2,1,0:T(8,128)(2,1)}), bf16[8,2,256,128]{3,2,1,0:T(8,128)(2,1)}, u32[]{:S(2)}, u32[]{:S(2)}) %all-to-all-start) | async-done | bytes 1048608 | tf_op jit(solution)/shard_map/all_to_all | solution.py:178
  31.1 0.0 collective-permute-start
  31.1 0.0 copy-done.2
  31.1 0.1 copy.45
  31.2 0.1 eq.67
  31.3 0.1 copy.48
  31.4 0.2 fusion.30
  31.6 1.0 copy.43.qpos_ref
  32.6 1.0 copy.44.qstart_ref
  33.7 0.4 collective-permute-done.other_ref
  34.1 8.8 %shard_map.145 = bf16[256,2048]{1,0:T(8,128)(2,1)} custom-call(s32[5]{0:T(128)} %stack.30.bounds_ref, f32[256,512]{1,0:T(8,128)} %fusion.49.q_ref, f32[256,128]{1,0:T(8,128)} %get-tuple-element.17.cos_ref, f32[256,128]{1,0:T(8,128)} %get-tuple-element.18.sin_ref, f32[1,128]{1,0:T(1,128)} %bitcast.74, bf16[8,2,256,128]{3,2,1,0:T(8,128)(2,1)} %all-to-all-done.own_ref, ...), custom_call_target="tpu_custom_call" | custom-call | tf_op jit(solution)/shard_map/pallas_call | solution.py:120
  42.9 0.0 copy-start.1
  42.9 5.5 %all-to-all-start.1 = ((bf16[8,32,2048]{2,1,0:T(8,128)(2,1)}), bf16[8,32,2048]{2,1,0:T(8,128)(2,1)}, u32[]{:S(2)}, u32[]{:S(2)}) async-start(bf16[8,32,2048]{2,1,0:T(8,128)(2,1)} %bitcast.67), calls=%async_computation.1 | async-start | bytes 2097152 | tf_op jit(solution)/shard_map/all_to_all | solution.py:199
  48.4 0.1 eq.63
  48.6 0.2 fusion.34
  48.8 0.1 reduce_sum.80
  48.9 0.3 compare_reduce_fusion
  49.2 14.8 %all-to-all-done.1 = bf16[8,32,2048]{2,1,0:T(8,128)(2,1)} async-done(((bf16[8,32,2048]{2,1,0:T(8,128)(2,1)}), bf16[8,32,2048]{2,1,0:T(8,128)(2,1)}, u32[]{:S(2)}, u32[]{:S(2)}) %all-to-all-start.1) | async-done | bytes 1048608 | tf_op jit(solution)/shard_map/all_to_all | solution.py:199
  63.9 1.4 convert_reduce_fusion
  65.3 1.1 multiply_reduce_fusion
  66.4 0.0 copy-done.1
  66.4 1.7 %convolution_convert_fusion = bf16[128,4,2048]{2,0,1:T(8,128)(2,1)S(1)} fusion(f32[2048]{0:T(1024)S(1)} %copy-done.1, f32[32]{0:T(128)S(1)} %add_rsqrt_fusion.2, f32[32,2048]{1,0:T(8,128)S(1)} %convert_reduce_fusion, bf16[256,2048]{1,0:T(8,128)(2,1)} %param.15, s32[]{:T(128)S(6)} %select_n.38, pred[32,128,4]{1,2,0:T(4,128)(4,1)S(1)} %compare_reduce_fusion), kind=kOutput, calls=%fused_computation.7 | convolution fusion | flops 68485120 | bytes 2515076 | tf_op jit(solution)/shard_map/dot_general | solution.py:213
  68.1 1.6 copy.52
  69.7 0.0 copy-start.5
  69.7 43.6 %all_to_all.20 = bf16[128,4,2048]{2,1,0:T(4,128)(2,1)S(1)} all-to-all(bf16[128,4,2048]{2,1,0:T(4,128)(2,1)S(1)} %copy.52), channel_id=1, replica_groups=mesh['seq'=16,'head'=8] {'seq','head'}, dimensions={0} | all-to-all | bytes 4194304 | tf_op jit(solution)/shard_map/all_to_all | solution.py:216
  113.3 0.0 copy-done.5
  113.3 3.6 %fusion.2 = f32[128,4,768]{2,0,1:T(8,128)S(1)} fusion(bf16[1,2048,768]{2,1,0:T(8,128)(2,1)S(1)} %copy-done.5, bf16[128,4,2048]{2,1,0:T(4,128)(2,1)S(1)} %all_to_all.20), kind=kOutput, calls=%fused_computation.2 | convolution fusion | flops 1610612736 | bytes 6815744 | tf_op jit(solution)/shard_map/scd,df->scf/dot_general | solution.py:218
  116.9 0.0 copy-done.6
  116.9 3.6 %fusion.4 = f32[128,4,768]{2,0,1:T(8,128)S(1)} fusion(bf16[1,2048,768]{2,1,0:T(8,128)(2,1)S(1)} %copy-done.6, bf16[128,4,2048]{2,1,0:T(4,128)(2,1)S(1)} %all_to_all.20), kind=kOutput, calls=%fused_computation.4 | convolution fusion | flops 1610612736 | bytes 6815744 | tf_op jit(solution)/shard_map/scd,df->scf/dot_general | solution.py:217
  120.5 0.0 copy-done
  120.5 1.8 %fusion.6 = bf16[128,4,2048]{2,0,1:T(8,128)(2,1)S(1)} fusion(bf16[1,768,2048]{2,1,0:T(8,128)(2,1)S(1)} %copy-done, f32[128,4,768]{2,0,1:T(8,128)S(1)} %fusion.2, f32[128,4,768]{2,0,1:T(8,128)S(1)} %fusion.4), kind=kOutput, calls=%fused_computation.6 | convolution fusion | flops 1614020608 | bytes 8388608 | tf_op jit(solution)/shard_map/scf,fd->scd/dot_general | solution.py:221
  122.4 2.9 %copy.55 = bf16[128,4,2048]{2,1,0:T(4,128)(2,1)} copy(bf16[128,4,2048]{2,0,1:T(8,128)(2,1)S(1)} %fusion.6) | data formatting | bytes 4194304 | tf_op jit(solution)/shard_map/convert_element_type | solution.py:223
  125.3 0.0 copy-start.3
  125.3 6.1 %all-to-all-start.3 = ((bf16[128,4,2048]{2,1,0:T(4,128)(2,1)}), bf16[128,4,2048]{2,1,0:T(4,128)(2,1)}, u32[]{:S(2)}, u32[]{:S(2)}) async-start(bf16[128,4,2048]{2,1,0:T(4,128)(2,1)} %copy.55), calls=%async_computation.3 | async-start | bytes 4194304 | tf_op jit(solution)/shard_map/all_to_all | solution.py:222
  131.4 0.0 copy-done.3
  131.5 0.1 copy.50
  131.5 0.3 fusion.19
  131.8 29.3 %all-to-all-done.3 = bf16[128,4,2048]{2,1,0:T(4,128)(2,1)} async-done(((bf16[128,4,2048]{2,1,0:T(4,128)(2,1)}), bf16[128,4,2048]{2,1,0:T(4,128)(2,1)}, u32[]{:S(2)}, u32[]{:S(2)}) %all-to-all-start.3) | async-done | bytes 2097184 | tf_op jit(solution)/shard_map/all_to_all | solution.py:222
  161.1 5.3 %fusion.10 = bf16[32,2048]{1,0:T(8,128)(2,1)} fusion(bf16[128,4,2048]{2,1,0:T(4,128)(2,1)} %all-to-all-done.3, f32[32,2048]{1,0:T(8,128)S(1)} %convert_reduce_fusion, bf16[256,2048]{1,0:T(8,128)(2,1)} %param.15, s32[]{:T(128)S(6)} %select_n.38, f32[32,128,4]{1,2,0:T(4,128)S(1)} %fusion.19), kind=kOutput, calls=%fused_computation.12 | convolution fusion | flops 402915328 | bytes 2686980 | tf_op jit(solution)/shard_map/dot_general | solution.py:226
  (20 shorter events, 0.2 us)
Async XLA Ops:
  0.0 120.5 %copy-start = (bf16[1,768,2048]{2,1,0:T(8,128)(2,1)S(1)}, bf16[1,768,2048]{2,1,0:T(8,128)(2,1)}, u32[]{:S(2)}) copy-start(bf16[1,768,2048]{2,1,0:T(8,128)(2,1)} %param.29) | copy-start | bytes 9437188
  0.0 4.2 %copy-start.7 = (f32[2048]{0:T(1024)S(1)}, f32[2048]{0:T(1024)}, u32[]{:S(2)}) copy-start(f32[2048]{0:T(1024)} %param.16) | copy-start | bytes 24580
  0.0 3.8 %copy-start.8 = (s32[6]{0:T(128)S(1)}, s32[6]{0:T(128)}, u32[]{:S(2)}) copy-start(s32[6]{0:T(128)} %param.24) | copy-start | bytes 76
  1.7 4.4 %copy-start.4 = (f32[128]{0:T(128)S(1)}, f32[128]{0:T(128)}, u32[]{:S(2)}) copy-start(f32[128]{0:T(128)} %param.21) | copy-start | bytes 1540
  8.1 23.0 %all-to-all-start = ((bf16[8,2,256,128]{3,2,1,0:T(8,128)(2,1)}), bf16[8,2,256,128]{3,2,1,0:T(8,128)(2,1)}, u32[]{:S(2)}, u32[]{:S(2)}) async-start(bf16[8,2,256,128]{3,2,1,0:T(8,128)(2,1)} %broadcast_in_dim.27), calls=%async_computation | async-start | bytes 2097152 | tf_op jit(solution)/shard_map/all_to_all | solution.py:178
  24.8 6.3 %copy-start.2 = (s32[32,8]{0,1:T(8,128)S(1)}, s32[32,8]{0,1:T(8,128)}, u32[]{:S(2)}) copy-start(s32[32,8]{0,1:T(8,128)} %param.25) | copy-start | bytes 3076
  31.1 3.0 %collective-permute-start = (bf16[8,2,256,128]{3,2,1,0:T(8,128)(2,1)}, bf16[8,2,256,128]{3,2,1,0:T(8,128)(2,1)}, u32[]{:S(2)}, u32[]{:S(2)}) collective-permute-start(bf16[8,2,256,128]{3,2,1,0:T(8,128)(2,1)} %all-to-all-done.own_ref), channel_id=1, source_target_pairs={{0,8},{8,0},{16,24},{24,16},{32,40},{40,32},{48,56},{56,48},{64,72... | collective-permute-start | bytes 3145736 | tf_op jit(solution)/shard_map/ppermute | solution.py:195
  42.9 23.5 %copy-start.1 = (f32[2048]{0:T(1024)S(1)}, f32[2048]{0:T(1024)}, u32[]{:S(2)}) copy-start(f32[2048]{0:T(1024)} %param.23) | copy-start | bytes 24580
  42.9 21.0 %all-to-all-start.1 = ((bf16[8,32,2048]{2,1,0:T(8,128)(2,1)}), bf16[8,32,2048]{2,1,0:T(8,128)(2,1)}, u32[]{:S(2)}, u32[]{:S(2)}) async-start(bf16[8,32,2048]{2,1,0:T(8,128)(2,1)} %bitcast.67), calls=%async_computation.1 | async-start | bytes 2097152 | tf_op jit(solution)/shard_map/all_to_all | solution.py:199
  69.7 43.6 %copy-start.5 = (bf16[1,2048,768]{2,1,0:T(8,128)(2,1)S(1)}, bf16[1,2048,768]{2,1,0:T(8,128)(2,1)}, u32[]{:S(2)}) copy-start(bf16[1,2048,768]{2,1,0:T(8,128)(2,1)} %param.28) | copy-start | bytes 9437188
  113.3 3.6 %copy-start.6 = (bf16[1,2048,768]{2,1,0:T(8,128)(2,1)S(1)}, bf16[1,2048,768]{2,1,0:T(8,128)(2,1)}, u32[]{:S(2)}) copy-start(bf16[1,2048,768]{2,1,0:T(8,128)(2,1)} %param.27) | copy-start | bytes 9437188
  125.3 6.1 %copy-start.3 = (f32[32,8]{0,1:T(8,128)S(1)}, f32[32,8]{0,1:T(8,128)}, u32[]{:S(2)}) copy-start(f32[32,8]{0,1:T(8,128)} %param.26) | copy-start | bytes 3076
  125.3 35.7 %all-to-all-start.3 = ((bf16[128,4,2048]{2,1,0:T(4,128)(2,1)}), bf16[128,4,2048]{2,1,0:T(4,128)(2,1)}, u32[]{:S(2)}, u32[]{:S(2)}) async-start(bf16[128,4,2048]{2,1,0:T(4,128)(2,1)} %copy.55), calls=%async_computation.3 | async-start | bytes 4194304 | tf_op jit(solution)/shard_map/all_to_all | solution.py:222

commit v14 on v12

--- a/solution.py
+++ b/solution.py
@@ -120,6 +120,54 @@
     return pl.pallas_call(
         kernel, grid_spec=spec, out_shape=jax.ShapeDtypeStruct((tok, w_out.shape[1]), jnp.bfloat16)
     )(bounds, queries, cosine, sine, gain, own, other, qpos, qstart, w_out)
+
+
+def _project_kernel(
+    index_ref, x_ref, ngain_ref, wk_ref, wv_ref, kgain_ref, cos_ref, sin_ref, normed_ref, spread_ref
+):
+    x = x_ref[...].astype(jnp.float32)
+    normed = (x * lax.rsqrt(jnp.mean(x * x, axis=1, keepdims=True) + EPSILON) * ngain_ref[...]).astype(
+        jnp.bfloat16
+    )
+    normed_ref[...] = normed
+    keys = jnp.dot(normed, wk_ref[...], preferred_element_type=jnp.float32)
+    keys = keys * lax.rsqrt(jnp.mean(keys * keys, axis=1, keepdims=True) + EPSILON) * kgain_ref[...]
+    keys = keys * cos_ref[...] + pltpu.roll(keys, keys.shape[1] // 2, 1) * sin_ref[...]
+    keys = keys.astype(jnp.bfloat16)
+    values = jnp.dot(normed, wv_ref[...], preferred_element_type=jnp.float32).astype(jnp.bfloat16)
+    for i in range(spread_ref.shape[0]):
+        spread_ref[i, 0] = keys
+        spread_ref[i, 1] = values
+
+
+def project(index, tokens, norm_gain, w_key, w_value, key_gain, cosine, sine, copies):
+    tok, width = tokens.shape
+    dim = key_gain.shape[0]
+    spec = pltpu.PrefetchScalarGridSpec(
+        num_scalar_prefetch=1,
+        grid=(1,),
+        in_specs=[
+            pl.BlockSpec((tok, width), lambda i, b: (0, 0)),
+            pl.BlockSpec((1, width), lambda i, b: (0, 0)),
+            pl.BlockSpec((width, dim), lambda i, b: (0, b[0])),
+            pl.BlockSpec((width, dim), lambda i, b: (0, b[0])),
+            pl.BlockSpec((1, dim), lambda i, b: (0, 0)),
+            pl.BlockSpec((tok, dim), lambda i, b: (0, 0)),
+            pl.BlockSpec((tok, dim), lambda i, b: (0, 0)),
+        ],
+        out_specs=[
+            pl.BlockSpec((tok, width), lambda i, b: (0, 0)),
+            pl.BlockSpec((copies, 2, tok, dim), lambda i, b: (0, 0, 0, 0)),
+        ],
+    )
+    return pl.pallas_call(
+        _project_kernel,
+        grid_spec=spec,
+        out_shape=[
+            jax.ShapeDtypeStruct((tok, width), jnp.bfloat16),
+            jax.ShapeDtypeStruct((copies, 2, tok, dim), jnp.bfloat16),
+        ],
+    )(index, tokens, norm_gain[None, :], w_key, w_value, key_gain[None, :], cosine, sine)
 
 
 def local(
@@ -159,22 +207,13 @@
     angles = offset[:, None] * inverse[None, :]
     cosine = jnp.cos(angles)
     sine = jnp.sin(angles)
-    inputs = tokens.astype(jnp.float32)
-    normed = rms_scale(inputs, norm_gain).astype(jnp.bfloat16)
-    queries = jnp.dot(normed, w_query, preferred_element_type=jnp.float32)
-    column = head_index * per_dev // (HEADS // KV_HEADS) * head_dim
-    key_cols = lax.dynamic_slice_in_dim(w_key, column, head_dim, 1)
-    value_cols = lax.dynamic_slice_in_dim(w_value, column, head_dim, 1)
-    keys = rotate(
-        rms_scale(jnp.dot(normed, key_cols, preferred_element_type=jnp.float32), key_gain),
-        cosine,
-        sine,
-    ).astype(jnp.bfloat16)
-    values = jnp.dot(normed, value_cols, preferred_element_type=jnp.float32).astype(jnp.bfloat16)
-    stacked = jnp.stack([keys, values])
+    cosine2 = jnp.concatenate([cosine, cosine], axis=-1)
+    sine2 = jnp.concatenate([-sine, sine], axis=-1)
     pairs = n_seq // 2
     groups = [[2 * i + c for i in range(pairs)] for c in range(2)]
-    spread = jnp.broadcast_to(stacked[None], (pairs,) + stacked.shape)
+    kv_head = jnp.reshape(head_index * per_dev // (HEADS // KV_HEADS), (1,)).astype(jnp.int32)
+    normed, spread = project(kv_head, tokens, norm_gain, w_key, w_value, key_gain, cosine2, sine2, pairs)
+    queries = jnp.dot(normed, w_query, preferred_element_type=jnp.float32)
     same_core = lax.all_to_all(spread, "seq", 0, 0, tiled=True, axis_index_groups=groups)
     block = 2 * tok_dev
     low = own_start[0] // block
@@ -185,8 +224,8 @@
     operands = (
         bounds,
         queries,
-        jnp.concatenate([cosine, cosine], axis=-1),
-        jnp.concatenate([-sine, sine], axis=-1),
+        cosine2,
+        sine2,
         query_gain[None, :],
         jnp.tile(positions[:, None], (per_dev, 1)),
         jnp.tile(own_start[:, None], (per_dev, 1)),

time: 165 us -> 162 us (0.982); the launches traced: 165 us -> 161 us
  matrix products: 17.1 us -> 13.2 us
  Pallas kernels: 8.82 us -> 12.4 us
  blocking collectives: 44.2 us -> 40.7 us
    dot_general x2 -> x0, matrix products: 3.82 us -> none  [the longest x1 1.96 us: local(): jnp.dot(normed, key_cols, preferred_element_type=jnp.float32)]
    pallas_call x0 -> x1, Pallas kernels: none -> 3.59 us  [project(): pl.pallas_call(_project_kernel, grid_spec=spec, out_shape=[jax.ShapeDtype...]
    all_to_all x1, blocking collectives: 44.2 us -> 40.7 us  [local(): lax.all_to_all(outgoing, ('seq', 'head'), split_axis=1, concat_axis=1, ti...]
    reduce_sum x2 -> x1, other arithmetic: 2.71 us -> 1.05 us  [rms_scale(): jnp.mean(values * values, axis=-1, keepdims=True) + EPSILON]
  transfers between devices with their start and end apart: 4 -> 4, of which waited for: 4 -> 4; matrix products, arithmetic and copies ran while one was open for 6% -> 5% of each run, Pallas kernels for 0% -> 0%
where the time goes in v14:
time: 162 us; the launch traced here: 161 us
  waiting for transfers between devices  48.7 us (30%)
  blocking collectives  40.7 us (25%)
  starting transfers between devices  18.4 us (11%)
  local copies, waits for them, and re-layouts  13.7 us (8%)
  matrix products  13.2 us (8%)
  Pallas kernels  12.4 us (8%)
  between operations  6.92 us (4%)
  other arithmetic  6.57 us (4%)
    all_to_all x1, blocking collectives, local(): lax.all_to_all(outgoing, ('seq', 'head'), split_axis=1, concat_axis=1, ti...  40.7 us
    all_to_all x1, waiting for transfers between devices, local(): lax.all_to_all(jnp.dot(hidden, w_down[0], preferred_element_type=jnp.floa...  29.5 us
    all_to_all x1, waiting for transfers between devices, local(): lax.all_to_all(terms.reshape(n_head, rows, width), 'head', 0, 0, tiled=True)  14.9 us
    pallas_call x1, Pallas kernels, attend(): pl.pallas_call(kernel, grid_spec=spec, out_shape=jax.ShapeDtypeStruct((to...  8.83 us
    all_to_all x1, starting transfers between devices, local(): lax.all_to_all(spread, 'seq', 0, 0, tiled=True, axis_index_groups=groups)  7.02 us
    all_to_all x1, starting transfers between devices, local(): lax.all_to_all(jnp.dot(hidden, w_down[0], preferred_element_type=jnp.floa...  5.91 us
    all_to_all x1, starting transfers between devices, local(): lax.all_to_all(terms.reshape(n_head, rows, width), 'head', 0, 0, tiled=True)  5.47 us
    all_to_all x1, waiting for transfers between devices, local(): lax.all_to_all(spread, 'seq', 0, 0, tiled=True, axis_index_groups=groups)  3.95 us
  transfers between devices with their start and end apart: 4, of which 4 were waited for; matrix products, arithmetic and copies ran while one was open for 5% of the time, Pallas kernels for 0%

profile of v14, /device:TPU:0, one launch (start us, length us, event | category | flops | bytes accessed | tf_op | source)
XLA Modules:
  0.0 160.7 jit_solution(7603017122105923354)
XLA Ops:
  0.0 0.0 copy-start
  0.0 1.0 reduce-window.18
  1.0 0.7 bitcast_subtract_fusion.1
  1.7 0.1 convert_reduce_fusion.1
  1.8 0.1 select_reduce_fusion.1
  1.9 0.5 fusion.19
  2.4 0.8 pad_maximum_fusion
  3.2 3.6 %shard_map.145 = (bf16[256,2048]{1,0:T(8,128)(2,1)}, bf16[8,2,256,128]{3,2,1,0:T(8,128)(2,1)}) custom-call(s32[1]{0:T(128)} %bitcast.11.index_ref, bf16[256,2048]{1,0:T(8,128)(2,1)} %x_ref.1, f32[1,2048]{1,0:T(1,128)} %bitcast.73, bf16[2048,512]{1,0:T(8,128)(2,1)} %wk_ref.1, bf16[2048,512]{1,0:T(8,128)(2,1)} %wv_ref.1, f32[1,128]{1,0:T(1,128)} %bitcast.74, ...), custom_call_target="tpu_custom_call" | custom-call | tf_op jit(solution)/shard_map/pallas_call | solution.py:163
  6.8 7.0 %all-to-all-start = ((bf16[8,2,256,128]{3,2,1,0:T(8,128)(2,1)}), bf16[8,2,256,128]{3,2,1,0:T(8,128)(2,1)}, u32[]{:S(2)}, u32[]{:S(2)}) async-start(bf16[8,2,256,128]{3,2,1,0:T(8,128)(2,1)} %get-tuple-element.18), calls=%async_computation | async-start | bytes 2097152 | tf_op jit(solution)/shard_map/all_to_all | solution.py:217
  13.9 0.0 copy-start.2
  13.9 0.6 fusion.23
  18.0 0.6 fusion.22
  21.8 0.7 stack.23.bounds_ref
  22.4 3.4 %fusion.24.q_ref = f32[256,512]{1,0:T(8,128)} fusion(bf16[256,2048]{1,0:T(8,128)(2,1)} %get-tuple-element.17, bf16[2048,512]{1,0:T(8,128)(2,1)} %param.17), kind=kOutput, calls=%fused_computation.51 | convolution fusion | flops 536870912 | bytes 3670016 | tf_op jit(solution)/shard_map/dot_general | solution.py:216
  25.8 4.0 %all-to-all-done.own_ref = bf16[8,2,256,128]{3,2,1,0:T(8,128)(2,1)} async-done(((bf16[8,2,256,128]{3,2,1,0:T(8,128)(2,1)}), bf16[8,2,256,128]{3,2,1,0:T(8,128)(2,1)}, u32[]{:S(2)}, u32[]{:S(2)}) %all-to-all-start) | async-done | bytes 1048608 | tf_op jit(solution)/shard_map/all_to_all | solution.py:217
  29.8 0.0 collective-permute-start
  29.8 0.0 copy-done.2
  29.8 0.1 copy.50
  29.9 0.1 eq.61
  30.0 0.1 eq.57
  30.1 0.1 copy.52
  30.2 0.2 fusion.12
  30.4 1.0 copy.48.qpos_ref
  31.4 1.0 copy.49.qstart_ref
  32.5 0.3 collective-permute-done.other_ref
  32.8 8.8 %shard_map.146 = bf16[256,2048]{1,0:T(8,128)(2,1)} custom-call(s32[5]{0:T(128)} %stack.23.bounds_ref, f32[256,512]{1,0:T(8,128)} %fusion.24.q_ref, f32[256,128]{1,0:T(8,128)} %get-tuple-element.21.cos_ref, f32[256,128]{1,0:T(8,128)} %get-tuple-element.22.sin_ref, f32[1,128]{1,0:T(1,128)} %bitcast.76, bf16[8,2,256,128]{3,2,1,0:T(8,128)(2,1)} %all-to-all-done.own_ref, ...), custom_call_target="tpu_custom_call" | custom-call | tf_op jit(solution)/shard_map/pallas_call | solution.py:120
  41.6 0.0 copy-start.1
  41.6 5.5 %all-to-all-start.1 = ((bf16[8,32,2048]{2,1,0:T(8,128)(2,1)}), bf16[8,32,2048]{2,1,0:T(8,128)(2,1)}, u32[]{:S(2)}, u32[]{:S(2)}) async-start(bf16[8,32,2048]{2,1,0:T(8,128)(2,1)} %bitcast.64), calls=%async_computation.1 | async-start | bytes 2097152 | tf_op jit(solution)/shard_map/all_to_all | solution.py:238
  47.2 0.2 fusion.14
  47.4 0.1 mul.76
  47.5 0.2 fusion.11
  47.7 14.9 %all-to-all-done.1 = bf16[8,32,2048]{2,1,0:T(8,128)(2,1)} async-done(((bf16[8,32,2048]{2,1,0:T(8,128)(2,1)}), bf16[8,32,2048]{2,1,0:T(8,128)(2,1)}, u32[]{:S(2)}, u32[]{:S(2)}) %all-to-all-start.1) | async-done | bytes 1048608 | tf_op jit(solution)/shard_map/all_to_all | solution.py:238
  62.6 1.4 convert_reduce_fusion
  64.0 1.1 multiply_reduce_fusion
  65.1 0.0 copy-done.1
  65.1 1.7 %convolution_convert_fusion = bf16[512,2048]{1,0:T(8,128)(2,1)S(1)} fusion(pred[32,512]{1,0:T(8,128)(4,1)S(1)} %fusion.11, f32[2048]{0:T(1024)S(1)} %copy-done.1, f32[32]{0:T(128)S(1)} %add_rsqrt_fusion, f32[32,2048]{1,0:T(8,128)S(1)} %convert_reduce_fusion, bf16[256,2048]{1,0:T(8,128)(2,1)} %x_ref.1, s32[]{:T(128)S(6)} %select_n.34), kind=kOutput, calls=%fused_computation.7 | convolution fusion | flops 68485120 | bytes 2515076 | tf_op jit(solution)/shard_map/dot_general | solution.py:252
  66.8 1.6 %copy.56 = bf16[4,128,2048]{2,0,1:T(4,128)(2,1)S(1)} copy(bf16[4,128,2048]{2,1,0:T(8,128)(2,1)S(1)} %bitcast.63) | data formatting | bytes 4194304 | tf_op jit(solution)/shard_map/reshape | solution.py:253
  68.4 40.7 %all_to_all.20 = bf16[4,128,2048]{2,0,1:T(4,128)(2,1)S(1)} all-to-all(bf16[4,128,2048]{2,0,1:T(4,128)(2,1)S(1)} %copy.56), channel_id=1, replica_groups=mesh['seq'=16,'head'=8] {'seq','head'}, dimensions={1} | all-to-all | bytes 4194304 | tf_op jit(solution)/shard_map/all_to_all | solution.py:254
  109.1 0.0 copy-start.4
  109.1 1.2 copy.57
  110.3 0.7 copy-done.4
  111.0 0.0 copy-start.5
  111.0 1.8 %fusion.2 = f32[512,768]{1,0:T(8,128)S(1)} fusion(bf16[512,2048]{1,0:T(8,128)(2,1)S(1)} %bitcast.65, bf16[1,2048,768]{2,1,0:T(8,128)(2,1)S(1)} %copy-done.4), kind=kOutput, calls=%fused_computation.2 | convolution fusion | flops 1610612736 | bytes 6815744 | tf_op jit(solution)/shard_map/dot_general | solution.py:257
  112.8 0.1 copy-done.5
  112.9 1.8 %fusion.4 = f32[512,768]{1,0:T(8,128)S(1)} fusion(bf16[512,2048]{1,0:T(8,128)(2,1)S(1)} %bitcast.66, bf16[1,2048,768]{2,1,0:T(8,128)(2,1)S(1)} %copy-done.5), kind=kOutput, calls=%fused_computation.4 | convolution fusion | flops 1610612736 | bytes 6815744 | tf_op jit(solution)/shard_map/dot_general | solution.py:256
  114.7 0.0 copy-done
  114.7 1.9 %fusion.6 = bf16[512,2048]{1,0:T(8,128)(2,1)S(1)} fusion(bf16[1,768,2048]{2,1,0:T(8,128)(2,1)S(1)} %copy-done, f32[512,768]{1,0:T(8,128)S(1)} %fusion.2, f32[512,768]{1,0:T(8,128)S(1)} %fusion.4), kind=kOutput, calls=%fused_computation.6 | convolution fusion | flops 1614020608 | bytes 8388608 | tf_op jit(solution)/shard_map/dot_general | solution.py:261
  116.6 2.9 %copy.58 = bf16[4,128,2048]{2,0,1:T(4,128)(2,1)} copy(bf16[4,128,2048]{2,1,0:T(8,128)(2,1)S(1)} %bitcast.67) | data formatting | bytes 4194304 | tf_op jit(solution)/shard_map/reshape | solution.py:263
  119.5 0.0 copy-start.3
  119.5 5.9 %all-to-all-start.3 = ((bf16[4,128,2048]{2,0,1:T(4,128)(2,1)}), bf16[4,128,2048]{2,0,1:T(4,128)(2,1)}, u32[]{:S(2)}, u32[]{:S(2)}) async-start(bf16[4,128,2048]{2,0,1:T(4,128)(2,1)} %copy.58), calls=%async_computation.3 | async-start | bytes 4194304 | tf_op jit(solution)/shard_map/all_to_all | solution.py:260
  125.4 0.0 copy-done.3
  125.4 0.1 copy.55
  125.5 0.2 select_reduce_fusion
  125.7 29.5 %all-to-all-done.3 = bf16[4,128,2048]{2,0,1:T(4,128)(2,1)} async-done(((bf16[4,128,2048]{2,0,1:T(4,128)(2,1)}), bf16[4,128,2048]{2,0,1:T(4,128)(2,1)}, u32[]{:S(2)}, u32[]{:S(2)}) %all-to-all-start.3) | async-done | bytes 2097184 | tf_op jit(solution)/shard_map/all_to_all | solution.py:260
  155.3 2.7 %copy.59 = bf16[4,128,2048]{2,1,0:T(8,128)(2,1)S(1)} copy(bf16[4,128,2048]{2,0,1:T(4,128)(2,1)} %all-to-all-done.3) | data formatting | bytes 4194304 | tf_op jit(solution)/shard_map/all_to_all | solution.py:260
  158.0 2.7 %fusion.9 = bf16[32,2048]{1,0:T(8,128)(2,1)} fusion(f32[32,512]{1,0:T(8,128)S(1)} %select_reduce_fusion, bf16[512,2048]{1,0:T(8,128)(2,1)S(1)} %bitcast.62, f32[32,2048]{1,0:T(8,128)S(1)} %convert_reduce_fusion, bf16[256,2048]{1,0:T(8,128)(2,1)} %x_ref.1, s32[]{:T(128)S(6)} %select_n.34), kind=kOutput, calls=%fused_computation.9 | convolution fusion | flops 402915328 | bytes 2686980 | tf_op jit(solution)/shard_map/dot_general | solution.py:270
  (16 shorter events, 0.1 us)
Async XLA Ops:
  0.0 114.7 %copy-start = (bf16[1,768,2048]{2,1,0:T(8,128)(2,1)S(1)}, bf16[1,768,2048]{2,1,0:T(8,128)(2,1)}, u32[]{:S(2)}) copy-start(bf16[1,768,2048]{2,1,0:T(8,128)(2,1)} %param.29) | copy-start | bytes 9437188
  6.8 23.0 %all-to-all-start = ((bf16[8,2,256,128]{3,2,1,0:T(8,128)(2,1)}), bf16[8,2,256,128]{3,2,1,0:T(8,128)(2,1)}, u32[]{:S(2)}, u32[]{:S(2)}) async-start(bf16[8,2,256,128]{3,2,1,0:T(8,128)(2,1)} %get-tuple-element.18), calls=%async_computation | async-start | bytes 2097152 | tf_op jit(solution)/shard_map/all_to_all | solution.py:217
  13.9 15.9 %copy-start.2 = (s32[32,8]{0,1:T(8,128)S(1)}, s32[32,8]{0,1:T(8,128)}, u32[]{:S(2)}) copy-start(s32[32,8]{0,1:T(8,128)} %param.25) | copy-start | bytes 3076
  29.8 3.0 %collective-permute-start = (bf16[8,2,256,128]{3,2,1,0:T(8,128)(2,1)}, bf16[8,2,256,128]{3,2,1,0:T(8,128)(2,1)}, u32[]{:S(2)}, u32[]{:S(2)}) collective-permute-start(bf16[8,2,256,128]{3,2,1,0:T(8,128)(2,1)} %all-to-all-done.own_ref), channel_id=1, source_target_pairs={{0,8},{8,0},{16,24},{24,16},{32,40},{40,32},{48,56},{56,48},{64,72... | collective-permute-start | bytes 3145736 | tf_op jit(solution)/shard_map/ppermute | solution.py:234
  41.6 23.5 %copy-start.1 = (f32[2048]{0:T(1024)S(1)}, f32[2048]{0:T(1024)}, u32[]{:S(2)}) copy-start(f32[2048]{0:T(1024)} %param.23) | copy-start | bytes 24580
  41.6 21.0 %all-to-all-start.1 = ((bf16[8,32,2048]{2,1,0:T(8,128)(2,1)}), bf16[8,32,2048]{2,1,0:T(8,128)(2,1)}, u32[]{:S(2)}, u32[]{:S(2)}) async-start(bf16[8,32,2048]{2,1,0:T(8,128)(2,1)} %bitcast.64), calls=%async_computation.1 | async-start | bytes 2097152 | tf_op jit(solution)/shard_map/all_to_all | solution.py:238
  109.1 1.9 %copy-start.4 = (bf16[1,2048,768]{2,1,0:T(8,128)(2,1)S(1)}, bf16[1,2048,768]{2,1,0:T(8,128)(2,1)}, u32[]{:S(2)}) copy-start(bf16[1,2048,768]{2,1,0:T(8,128)(2,1)} %param.28) | copy-start | bytes 9437188
  111.0 1.9 %copy-start.5 = (bf16[1,2048,768]{2,1,0:T(8,128)(2,1)S(1)}, bf16[1,2048,768]{2,1,0:T(8,128)(2,1)}, u32[]{:S(2)}) copy-start(bf16[1,2048,768]{2,1,0:T(8,128)(2,1)} %param.27) | copy-start | bytes 9437188
  119.5 5.9 %copy-start.3 = (f32[32,8]{0,1:T(8,128)S(1)}, f32[32,8]{0,1:T(8,128)}, u32[]{:S(2)}) copy-start(f32[32,8]{0,1:T(8,128)} %param.26) | copy-start | bytes 3076
  119.5 35.7 %all-to-all-start.3 = ((bf16[4,128,2048]{2,0,1:T(4,128)(2,1)}), bf16[4,128,2048]{2,0,1:T(4,128)(2,1)}, u32[]{:S(2)}, u32[]{:S(2)}) async-start(bf16[4,128,2048]{2,0,1:T(4,128)(2,1)} %copy.58), calls=%async_computation.3 | async-start | bytes 4194304 | tf_op jit(solution)/shard_map/all_to_all | solution.py:260

commit v15 on v14

--- a/solution.py
+++ b/solution.py
@@ -36,8 +36,11 @@
 
 
 def _attend_kernel(
-    bounds_ref, q_ref, cos_ref, sin_ref, gain_ref, own_ref, other_ref, qpos_ref, qstart_ref, w_ref, o_ref, *, dim
+    bounds_ref, q_ref, cos_ref, sin_ref, gain_ref, own_ref, other_ref, qpos_ref, qstart_ref, w_hbm, o_ref,
+    w_ref, w_sem, *, dim
 ):
+    w_copy = pltpu.make_async_copy(w_hbm, w_ref, w_sem)
+    w_copy.start()
     heads = q_ref.shape[1] // dim
     tok = q_ref.shape[0]
     block = 2 * own_ref.shape[2]
@@ -89,6 +92,7 @@
     carry = lax.fori_loop(bounds_ref[2], bounds_ref[3], lambda j, c: step(j, c, True), carry)
     high, total, accum = carry
     out = (accum / total).astype(jnp.bfloat16)
+    w_copy.wait()
     terms = jnp.dot(out[:tok], w_ref[:dim, :], preferred_element_type=jnp.float32)
     for h in range(1, heads):
         terms = terms + jnp.dot(
@@ -113,9 +117,10 @@
             pl.BlockSpec(other.shape, lambda i, b: (0, 0, 0, 0)),
             pl.BlockSpec(qpos.shape, lambda i, b: (0, 0)),
             pl.BlockSpec(qstart.shape, lambda i, b: (0, 0)),
-            pl.BlockSpec(w_out.shape, lambda i, b: (0, 0)),
+            pl.BlockSpec(memory_space=pl.ANY),
         ],
         out_specs=pl.BlockSpec((tok, w_out.shape[1]), lambda i, b: (0, 0)),
+        scratch_shapes=[pltpu.VMEM(w_out.shape, w_out.dtype), pltpu.SemaphoreType.DMA],
     )
     return pl.pallas_call(
         kernel, grid_spec=spec, out_shape=jax.ShapeDtypeStruct((tok, w_out.shape[1]), jnp.bfloat16)

time: 162 us -> 163 us (level)
  blocking collectives: 40.7 us -> 43.6 us
    all_to_all x1, blocking collectives: 40.7 us -> 43.6 us  [local(): lax.all_to_all(outgoing, ('seq', 'head'), split_axis=1, concat_axis=1, ti...]
where the time goes in v15:
time: 163 us
  waiting for transfers between devices  48.8 us (30%)
  blocking collectives  43.6 us (27%)
  starting transfers between devices  18.3 us (11%)
  local copies, waits for them, and re-layouts  13.7 us (8%)
  matrix products  13.2 us (8%)
  Pallas kernels  11.8 us (7%)
  between operations  6.94 us (4%)
  other arithmetic  6.57 us (4%)
    all_to_all x1, blocking collectives, local(): lax.all_to_all(outgoing, ('seq', 'head'), split_axis=1, concat_axis=1, ti...  43.6 us
    all_to_all x1, waiting for transfers between devices, local(): lax.all_to_all(jnp.dot(hidden, w_down[0], preferred_element_type=jnp.floa...  29.5 us
    all_to_all x1, waiting for transfers between devices, local(): lax.all_to_all(terms.reshape(n_head, rows, width), 'head', 0, 0, tiled=True)  14.9 us
    pallas_call x1, Pallas kernels, attend(): pl.pallas_call(kernel, grid_spec=spec, out_shape=jax.ShapeDtypeStruct((to...  8.2 us
    all_to_all x1, starting transfers between devices, local(): lax.all_to_all(spread, 'seq', 0, 0, tiled=True, axis_index_groups=groups)  7.02 us
    all_to_all x1, starting transfers between devices, local(): lax.all_to_all(jnp.dot(hidden, w_down[0], preferred_element_type=jnp.floa...  5.91 us
    all_to_all x1, starting transfers between devices, local(): lax.all_to_all(terms.reshape(n_head, rows, width), 'head', 0, 0, tiled=True)  5.35 us
    all_to_all x1, waiting for transfers between devices, local(): lax.all_to_all(spread, 'seq', 0, 0, tiled=True, axis_index_groups=groups)  3.95 us
  transfers between devices with their start and end apart: 4, of which 4 were waited for; matrix products, arithmetic and copies ran while one was open for 5% of the time, Pallas kernels for 0%

profile of v15, /device:TPU:0, one launch (start us, length us, event | category | flops | bytes accessed | tf_op | source)
XLA Modules:
  0.0 162.9 jit_solution(6427796646572707773)
XLA Ops:
  0.0 0.0 copy-start
  0.0 1.0 reduce-window.18
  1.0 0.7 bitcast_subtract_fusion.1
  1.7 0.1 convert_reduce_fusion.1
  1.8 0.1 select_reduce_fusion.1
  1.9 0.5 fusion.19
  2.4 0.8 pad_maximum_fusion
  3.2 3.6 %shard_map.145 = (bf16[256,2048]{1,0:T(8,128)(2,1)}, bf16[8,2,256,128]{3,2,1,0:T(8,128)(2,1)}) custom-call(s32[1]{0:T(128)} %bitcast.11.index_ref, bf16[256,2048]{1,0:T(8,128)(2,1)} %x_ref.1, f32[1,2048]{1,0:T(1,128)} %bitcast.73, bf16[2048,512]{1,0:T(8,128)(2,1)} %wk_ref.1, bf16[2048,512]{1,0:T(8,128)(2,1)} %wv_ref.1, f32[1,128]{1,0:T(1,128)} %bitcast.74, ...), custom_call_target="tpu_custom_call" | custom-call | tf_op jit(solution)/shard_map/pallas_call | solution.py:168
  6.8 7.0 %all-to-all-start = ((bf16[8,2,256,128]{3,2,1,0:T(8,128)(2,1)}), bf16[8,2,256,128]{3,2,1,0:T(8,128)(2,1)}, u32[]{:S(2)}, u32[]{:S(2)}) async-start(bf16[8,2,256,128]{3,2,1,0:T(8,128)(2,1)} %get-tuple-element.18), calls=%async_computation | async-start | bytes 2097152 | tf_op jit(solution)/shard_map/all_to_all | solution.py:222
  13.9 0.0 copy-start.2
  13.9 0.6 fusion.23
  18.0 0.6 fusion.22
  21.8 0.7 stack.23.bounds_ref
  22.4 3.4 %fusion.24.q_ref = f32[256,512]{1,0:T(8,128)} fusion(bf16[256,2048]{1,0:T(8,128)(2,1)} %get-tuple-element.17, bf16[2048,512]{1,0:T(8,128)(2,1)} %param.17), kind=kOutput, calls=%fused_computation.51 | convolution fusion | flops 536870912 | bytes 3670016 | tf_op jit(solution)/shard_map/dot_general | solution.py:221
  25.8 4.0 %all-to-all-done.own_ref = bf16[8,2,256,128]{3,2,1,0:T(8,128)(2,1)} async-done(((bf16[8,2,256,128]{3,2,1,0:T(8,128)(2,1)}), bf16[8,2,256,128]{3,2,1,0:T(8,128)(2,1)}, u32[]{:S(2)}, u32[]{:S(2)}) %all-to-all-start) | async-done | bytes 1048608 | tf_op jit(solution)/shard_map/all_to_all | solution.py:222
  29.8 0.0 collective-permute-start
  29.8 0.0 copy-done.2
  29.8 0.1 copy.50
  29.9 0.1 eq.61
  30.0 0.1 eq.57
  30.1 0.1 copy.52
  30.2 0.2 fusion.12
  30.4 1.0 copy.48.qpos_ref
  31.4 1.0 copy.49.qstart_ref
  32.5 0.3 collective-permute-done.other_ref
  32.8 8.2 %shard_map.146 = bf16[256,2048]{1,0:T(8,128)(2,1)} custom-call(s32[5]{0:T(128)} %stack.23.bounds_ref, f32[256,512]{1,0:T(8,128)} %fusion.24.q_ref, f32[256,128]{1,0:T(8,128)} %get-tuple-element.21.cos_ref, f32[256,128]{1,0:T(8,128)} %get-tuple-element.22.sin_ref, f32[1,128]{1,0:T(1,128)} %bitcast.76, bf16[8,2,256,128]{3,2,1,0:T(8,128)(2,1)} %all-to-all-done.own_ref, ...), custom_call_target="tpu_custom_call" | custom-call | tf_op jit(solution)/shard_map/pallas_call | solution.py:125
  41.0 0.0 copy-start.1
  41.0 5.3 %all-to-all-start.1 = ((bf16[8,32,2048]{2,1,0:T(8,128)(2,1)}), bf16[8,32,2048]{2,1,0:T(8,128)(2,1)}, u32[]{:S(2)}, u32[]{:S(2)}) async-start(bf16[8,32,2048]{2,1,0:T(8,128)(2,1)} %bitcast.64), calls=%async_computation.1 | async-start | bytes 2097152 | tf_op jit(solution)/shard_map/all_to_all | solution.py:243
  46.5 0.2 fusion.14
  46.6 0.1 mul.76
  46.7 0.2 fusion.11
  47.0 14.9 %all-to-all-done.1 = bf16[8,32,2048]{2,1,0:T(8,128)(2,1)} async-done(((bf16[8,32,2048]{2,1,0:T(8,128)(2,1)}), bf16[8,32,2048]{2,1,0:T(8,128)(2,1)}, u32[]{:S(2)}, u32[]{:S(2)}) %all-to-all-start.1) | async-done | bytes 1048608 | tf_op jit(solution)/shard_map/all_to_all | solution.py:243
  61.9 1.4 convert_reduce_fusion
  63.3 1.1 multiply_reduce_fusion
  64.4 0.0 copy-done.1
  64.4 1.7 %convolution_convert_fusion = bf16[512,2048]{1,0:T(8,128)(2,1)S(1)} fusion(pred[32,512]{1,0:T(8,128)(4,1)S(1)} %fusion.11, f32[2048]{0:T(1024)S(1)} %copy-done.1, f32[32]{0:T(128)S(1)} %add_rsqrt_fusion, f32[32,2048]{1,0:T(8,128)S(1)} %convert_reduce_fusion, bf16[256,2048]{1,0:T(8,128)(2,1)} %x_ref.1, s32[]{:T(128)S(6)} %select_n.34), kind=kOutput, calls=%fused_computation.7 | convolution fusion | flops 68485120 | bytes 2515076 | tf_op jit(solution)/shard_map/dot_general | solution.py:257
  66.1 1.6 copy.56
  67.7 43.6 %all_to_all.20 = bf16[4,128,2048]{2,0,1:T(4,128)(2,1)S(1)} all-to-all(bf16[4,128,2048]{2,0,1:T(4,128)(2,1)S(1)} %copy.56), channel_id=1, replica_groups=mesh['seq'=16,'head'=8] {'seq','head'}, dimensions={1} | all-to-all | bytes 4194304 | tf_op jit(solution)/shard_map/all_to_all | solution.py:259
  111.3 0.0 copy-start.4
  111.3 1.2 copy.57
  112.5 0.7 copy-done.4
  113.2 0.0 copy-start.5
  113.2 1.8 %fusion.2 = f32[512,768]{1,0:T(8,128)S(1)} fusion(bf16[512,2048]{1,0:T(8,128)(2,1)S(1)} %bitcast.65, bf16[1,2048,768]{2,1,0:T(8,128)(2,1)S(1)} %copy-done.4), kind=kOutput, calls=%fused_computation.2 | convolution fusion | flops 1610612736 | bytes 6815744 | tf_op jit(solution)/shard_map/dot_general | solution.py:262
  115.0 0.1 copy-done.5
  115.1 1.8 %fusion.4 = f32[512,768]{1,0:T(8,128)S(1)} fusion(bf16[512,2048]{1,0:T(8,128)(2,1)S(1)} %bitcast.66, bf16[1,2048,768]{2,1,0:T(8,128)(2,1)S(1)} %copy-done.5), kind=kOutput, calls=%fused_computation.4 | convolution fusion | flops 1610612736 | bytes 6815744 | tf_op jit(solution)/shard_map/dot_general | solution.py:261
  116.9 0.0 copy-done
  116.9 1.8 %fusion.6 = bf16[512,2048]{1,0:T(8,128)(2,1)S(1)} fusion(bf16[1,768,2048]{2,1,0:T(8,128)(2,1)S(1)} %copy-done, f32[512,768]{1,0:T(8,128)S(1)} %fusion.2, f32[512,768]{1,0:T(8,128)S(1)} %fusion.4), kind=kOutput, calls=%fused_computation.6 | convolution fusion | flops 1614020608 | bytes 8388608 | tf_op jit(solution)/shard_map/dot_general | solution.py:266
  118.8 2.9 %copy.58 = bf16[4,128,2048]{2,0,1:T(4,128)(2,1)} copy(bf16[4,128,2048]{2,1,0:T(8,128)(2,1)S(1)} %bitcast.67) | data formatting | bytes 4194304 | tf_op jit(solution)/shard_map/reshape | solution.py:268
  121.7 0.0 copy-start.3
  121.7 5.9 %all-to-all-start.3 = ((bf16[4,128,2048]{2,0,1:T(4,128)(2,1)}), bf16[4,128,2048]{2,0,1:T(4,128)(2,1)}, u32[]{:S(2)}, u32[]{:S(2)}) async-start(bf16[4,128,2048]{2,0,1:T(4,128)(2,1)} %copy.58), calls=%async_computation.3 | async-start | bytes 4194304 | tf_op jit(solution)/shard_map/all_to_all | solution.py:265
  127.6 0.0 copy-done.3
  127.6 0.1 copy.55
  127.7 0.2 select_reduce_fusion
  127.9 29.5 %all-to-all-done.3 = bf16[4,128,2048]{2,0,1:T(4,128)(2,1)} async-done(((bf16[4,128,2048]{2,0,1:T(4,128)(2,1)}), bf16[4,128,2048]{2,0,1:T(4,128)(2,1)}, u32[]{:S(2)}, u32[]{:S(2)}) %all-to-all-start.3) | async-done | bytes 2097184 | tf_op jit(solution)/shard_map/all_to_all | solution.py:265
  157.4 2.7 %copy.59 = bf16[4,128,2048]{2,1,0:T(8,128)(2,1)S(1)} copy(bf16[4,128,2048]{2,0,1:T(4,128)(2,1)} %all-to-all-done.3) | data formatting | bytes 4194304 | tf_op jit(solution)/shard_map/all_to_all | solution.py:265
  160.2 2.7 %fusion.9 = bf16[32,2048]{1,0:T(8,128)(2,1)} fusion(f32[32,512]{1,0:T(8,128)S(1)} %select_reduce_fusion, bf16[512,2048]{1,0:T(8,128)(2,1)S(1)} %bitcast.62, f32[32,2048]{1,0:T(8,128)S(1)} %convert_reduce_fusion, bf16[256,2048]{1,0:T(8,128)(2,1)} %x_ref.1, s32[]{:T(128)S(6)} %select_n.34), kind=kOutput, calls=%fused_computation.9 | convolution fusion | flops 402915328 | bytes 2686980 | tf_op jit(solution)/shard_map/dot_general | solution.py:275
  (16 shorter events, 0.1 us)
Async XLA Ops:
  0.0 116.9 %copy-start = (bf16[1,768,2048]{2,1,0:T(8,128)(2,1)S(1)}, bf16[1,768,2048]{2,1,0:T(8,128)(2,1)}, u32[]{:S(2)}) copy-start(bf16[1,768,2048]{2,1,0:T(8,128)(2,1)} %param.29) | copy-start | bytes 9437188
  6.8 23.0 %all-to-all-start = ((bf16[8,2,256,128]{3,2,1,0:T(8,128)(2,1)}), bf16[8,2,256,128]{3,2,1,0:T(8,128)(2,1)}, u32[]{:S(2)}, u32[]{:S(2)}) async-start(bf16[8,2,256,128]{3,2,1,0:T(8,128)(2,1)} %get-tuple-element.18), calls=%async_computation | async-start | bytes 2097152 | tf_op jit(solution)/shard_map/all_to_all | solution.py:222
  13.9 15.9 %copy-start.2 = (s32[32,8]{0,1:T(8,128)S(1)}, s32[32,8]{0,1:T(8,128)}, u32[]{:S(2)}) copy-start(s32[32,8]{0,1:T(8,128)} %param.25) | copy-start | bytes 3076
  29.8 3.0 %collective-permute-start = (bf16[8,2,256,128]{3,2,1,0:T(8,128)(2,1)}, bf16[8,2,256,128]{3,2,1,0:T(8,128)(2,1)}, u32[]{:S(2)}, u32[]{:S(2)}) collective-permute-start(bf16[8,2,256,128]{3,2,1,0:T(8,128)(2,1)} %all-to-all-done.own_ref), channel_id=1, source_target_pairs={{0,8},{8,0},{16,24},{24,16},{32,40},{40,32},{48,56},{56,48},{64,72... | collective-permute-start | bytes 3145736 | tf_op jit(solution)/shard_map/ppermute | solution.py:239
  41.0 23.4 %copy-start.1 = (f32[2048]{0:T(1024)S(1)}, f32[2048]{0:T(1024)}, u32[]{:S(2)}) copy-start(f32[2048]{0:T(1024)} %param.23) | copy-start | bytes 24580
  41.0 20.9 %all-to-all-start.1 = ((bf16[8,32,2048]{2,1,0:T(8,128)(2,1)}), bf16[8,32,2048]{2,1,0:T(8,128)(2,1)}, u32[]{:S(2)}, u32[]{:S(2)}) async-start(bf16[8,32,2048]{2,1,0:T(8,128)(2,1)} %bitcast.64), calls=%async_computation.1 | async-start | bytes 2097152 | tf_op jit(solution)/shard_map/all_to_all | solution.py:243
  111.3 1.9 %copy-start.4 = (bf16[1,2048,768]{2,1,0:T(8,128)(2,1)S(1)}, bf16[1,2048,768]{2,1,0:T(8,128)(2,1)}, u32[]{:S(2)}) copy-start(bf16[1,2048,768]{2,1,0:T(8,128)(2,1)} %param.28) | copy-start | bytes 9437188
  113.2 1.9 %copy-start.5 = (bf16[1,2048,768]{2,1,0:T(8,128)(2,1)S(1)}, bf16[1,2048,768]{2,1,0:T(8,128)(2,1)}, u32[]{:S(2)}) copy-start(bf16[1,2048,768]{2,1,0:T(8,128)(2,1)} %param.27) | copy-start | bytes 9437188
  121.7 5.9 %copy-start.3 = (f32[32,8]{0,1:T(8,128)S(1)}, f32[32,8]{0,1:T(8,128)}, u32[]{:S(2)}) copy-start(f32[32,8]{0,1:T(8,128)} %param.26) | copy-start | bytes 3076
  121.7 35.7 %all-to-all-start.3 = ((bf16[4,128,2048]{2,0,1:T(4,128)(2,1)}), bf16[4,128,2048]{2,0,1:T(4,128)(2,1)}, u32[]{:S(2)}, u32[]{:S(2)}) async-start(bf16[4,128,2048]{2,0,1:T(4,128)(2,1)} %copy.58), calls=%async_computation.3 | async-start | bytes 4194304 | tf_op jit(solution)/shard_map/all_to_all | solution.py:265

commit v16 on v14

--- a/solution.py
+++ b/solution.py
@@ -195,7 +195,8 @@
     seq_index = lax.axis_index("seq")
     head_index = lax.axis_index("head")
     ndocs = doc_lengths.shape[0]
-    ends = jnp.cumsum(doc_lengths)
+    order = jnp.arange(ndocs, dtype=jnp.int32)
+    ends = jnp.sum(jnp.where(order[None, :] <= order[:, None], doc_lengths[None, :], 0), axis=1)
     starts = ends - doc_lengths
     positions = seq_index * tok_dev + jnp.arange(tok_dev, dtype=jnp.int32)
     query_doc = doc_index(positions, ends)
@@ -204,11 +205,10 @@
     offset = (positions - own_start).astype(jnp.float32)
     half = head_dim // 2
     inverse = THETA ** (-2.0 * jnp.arange(half, dtype=jnp.float32) / head_dim)
-    angles = offset[:, None] * inverse[None, :]
-    cosine = jnp.cos(angles)
-    sine = jnp.sin(angles)
-    cosine2 = jnp.concatenate([cosine, cosine], axis=-1)
-    sine2 = jnp.concatenate([-sine, sine], axis=-1)
+    angles = offset[:, None] * jnp.concatenate([inverse, inverse])[None, :]
+    cosine2 = jnp.cos(angles)
+    sign = jnp.where(jnp.arange(head_dim) < half, -1.0, 1.0).astype(jnp.float32)
+    sine2 = jnp.sin(angles) * sign[None, :]
     pairs = n_seq // 2
     groups = [[2 * i + c for i in range(pairs)] for c in range(2)]
     kv_head = jnp.reshape(head_index * per_dev // (HEADS // KV_HEADS), (1,)).astype(jnp.int32)

time: 162 us -> 162 us (level)
  no operation moved by 1% of the time
where the time goes in v16:
time: 162 us; the launch traced here: 161 us
  waiting for transfers between devices  48.7 us (30%)
  blocking collectives  40.7 us (25%)
  starting transfers between devices  18.4 us (11%)
  local copies, waits for them, and re-layouts  13.7 us (8%)
  matrix products  13.2 us (8%)
  Pallas kernels  12.4 us (8%)
  between operations  6.91 us (4%)
  other arithmetic  6.46 us (4%)
    all_to_all x1, blocking collectives, local(): lax.all_to_all(outgoing, ('seq', 'head'), split_axis=1, concat_axis=1, ti...  40.7 us
    all_to_all x1, waiting for transfers between devices, local(): lax.all_to_all(jnp.dot(hidden, w_down[0], preferred_element_type=jnp.floa...  29.5 us
    all_to_all x1, waiting for transfers between devices, local(): lax.all_to_all(terms.reshape(n_head, rows, width), 'head', 0, 0, tiled=True)  14.9 us
    pallas_call x1, Pallas kernels, attend(): pl.pallas_call(kernel, grid_spec=spec, out_shape=jax.ShapeDtypeStruct((to...  8.82 us
    all_to_all x1, starting transfers between devices, local(): lax.all_to_all(spread, 'seq', 0, 0, tiled=True, axis_index_groups=groups)  7.01 us
    all_to_all x1, starting transfers between devices, local(): lax.all_to_all(jnp.dot(hidden, w_down[0], preferred_element_type=jnp.floa...  5.91 us
    all_to_all x1, starting transfers between devices, local(): lax.all_to_all(terms.reshape(n_head, rows, width), 'head', 0, 0, tiled=True)  5.48 us
    all_to_all x1, waiting for transfers between devices, local(): lax.all_to_all(spread, 'seq', 0, 0, tiled=True, axis_index_groups=groups)  3.95 us
  transfers between devices with their start and end apart: 4, of which 4 were waited for; matrix products, arithmetic and copies ran while one was open for 5% of the time, Pallas kernels for 0%

profile of v16, /device:TPU:0, one launch (start us, length us, event | category | flops | bytes accessed | tf_op | source)
XLA Modules:
  0.0 160.6 jit_solution(16584462431498154502)
XLA Ops:
  0.0 0.0 copy-start
  0.0 0.9 select_reduce_fusion.2
  1.0 0.7 sub.29
  1.6 0.1 convert_reduce_fusion.1
  1.7 0.1 select_reduce_fusion.1
  1.8 0.1 compare_select_fusion
  1.9 1.2 fusion.12
  3.1 3.6 %shard_map.145 = (bf16[256,2048]{1,0:T(8,128)(2,1)}, bf16[8,2,256,128]{3,2,1,0:T(8,128)(2,1)}) custom-call(s32[1]{0:T(128)} %bitcast.9.index_ref, bf16[256,2048]{1,0:T(8,128)(2,1)} %x_ref.1, f32[1,2048]{1,0:T(1,128)} %bitcast.70, bf16[2048,512]{1,0:T(8,128)(2,1)} %wk_ref.1, bf16[2048,512]{1,0:T(8,128)(2,1)} %wv_ref.1, f32[1,128]{1,0:T(1,128)} %bitcast.71, ...), custom_call_target="tpu_custom_call" | custom-call | tf_op jit(solution)/shard_map/pallas_call | solution.py:163
  6.7 7.0 %all-to-all-start = ((bf16[8,2,256,128]{3,2,1,0:T(8,128)(2,1)}), bf16[8,2,256,128]{3,2,1,0:T(8,128)(2,1)}, u32[]{:S(2)}, u32[]{:S(2)}) async-start(bf16[8,2,256,128]{3,2,1,0:T(8,128)(2,1)} %get-tuple-element.18), calls=%async_computation | async-start | bytes 2097152 | tf_op jit(solution)/shard_map/all_to_all | solution.py:217
  13.7 0.0 copy-start.2
  13.7 0.6 fusion.23
  17.9 0.6 fusion.22
  21.6 0.7 stack.23.bounds_ref
  22.3 3.4 %fusion.24.q_ref = f32[256,512]{1,0:T(8,128)} fusion(bf16[256,2048]{1,0:T(8,128)(2,1)} %get-tuple-element.17, bf16[2048,512]{1,0:T(8,128)(2,1)} %param.17), kind=kOutput, calls=%fused_computation.52 | convolution fusion | flops 536870912 | bytes 3670016 | tf_op jit(solution)/shard_map/dot_general | solution.py:216
  25.7 4.0 %all-to-all-done.own_ref = bf16[8,2,256,128]{3,2,1,0:T(8,128)(2,1)} async-done(((bf16[8,2,256,128]{3,2,1,0:T(8,128)(2,1)}), bf16[8,2,256,128]{3,2,1,0:T(8,128)(2,1)}, u32[]{:S(2)}, u32[]{:S(2)}) %all-to-all-start) | async-done | bytes 1048608 | tf_op jit(solution)/shard_map/all_to_all | solution.py:217
  29.7 0.0 collective-permute-start
  29.7 0.0 copy-done.2
  29.7 0.1 copy.50
  29.8 0.1 eq.61
  29.8 0.1 eq.57
  29.9 0.1 copy.52
  30.0 0.2 fusion.13
  30.3 1.0 copy.48.qpos_ref
  31.3 1.0 copy.49.qstart_ref
  32.3 0.3 collective-permute-done.other_ref
  32.7 8.8 %shard_map.146 = bf16[256,2048]{1,0:T(8,128)(2,1)} custom-call(s32[5]{0:T(128)} %stack.23.bounds_ref, f32[256,512]{1,0:T(8,128)} %fusion.24.q_ref, f32[256,128]{1,0:T(8,128)} %get-tuple-element.21.cos_ref, f32[256,128]{1,0:T(8,128)} %get-tuple-element.22.sin_ref, f32[1,128]{1,0:T(1,128)} %bitcast.72, bf16[8,2,256,128]{3,2,1,0:T(8,128)(2,1)} %all-to-all-done.own_ref, ...), custom_call_target="tpu_custom_call" | custom-call | tf_op jit(solution)/shard_map/pallas_call | solution.py:120
  41.5 0.0 copy-start.1
  41.5 5.5 %all-to-all-start.1 = ((bf16[8,32,2048]{2,1,0:T(8,128)(2,1)}), bf16[8,32,2048]{2,1,0:T(8,128)(2,1)}, u32[]{:S(2)}, u32[]{:S(2)}) async-start(bf16[8,32,2048]{2,1,0:T(8,128)(2,1)} %bitcast.61), calls=%async_computation.1 | async-start | bytes 2097152 | tf_op jit(solution)/shard_map/all_to_all | solution.py:238
  47.1 0.2 fusion.15
  47.3 0.1 mul.85
  47.4 0.2 fusion.11
  47.6 14.9 %all-to-all-done.1 = bf16[8,32,2048]{2,1,0:T(8,128)(2,1)} async-done(((bf16[8,32,2048]{2,1,0:T(8,128)(2,1)}), bf16[8,32,2048]{2,1,0:T(8,128)(2,1)}, u32[]{:S(2)}, u32[]{:S(2)}) %all-to-all-start.1) | async-done | bytes 1048608 | tf_op jit(solution)/shard_map/all_to_all | solution.py:238
  62.5 1.4 convert_reduce_fusion
  63.9 1.1 multiply_reduce_fusion
  65.0 0.0 copy-done.1
  65.0 1.7 %convolution_convert_fusion = bf16[512,2048]{1,0:T(8,128)(2,1)S(1)} fusion(pred[32,512]{1,0:T(8,128)(4,1)S(1)} %fusion.11, f32[2048]{0:T(1024)S(1)} %copy-done.1, f32[32]{0:T(128)S(1)} %add_rsqrt_fusion, f32[32,2048]{1,0:T(8,128)S(1)} %convert_reduce_fusion, bf16[256,2048]{1,0:T(8,128)(2,1)} %x_ref.1, s32[]{:T(128)S(6)} %select_n.46), kind=kOutput, calls=%fused_computation.7 | convolution fusion | flops 68485120 | bytes 2515076 | tf_op jit(solution)/shard_map/dot_general | solution.py:252
  66.7 1.6 %copy.56 = bf16[4,128,2048]{2,0,1:T(4,128)(2,1)S(1)} copy(bf16[4,128,2048]{2,1,0:T(8,128)(2,1)S(1)} %bitcast.60) | data formatting | bytes 4194304 | tf_op jit(solution)/shard_map/reshape | solution.py:253
  68.3 40.7 %all_to_all.20 = bf16[4,128,2048]{2,0,1:T(4,128)(2,1)S(1)} all-to-all(bf16[4,128,2048]{2,0,1:T(4,128)(2,1)S(1)} %copy.56), channel_id=1, replica_groups=mesh['seq'=16,'head'=8] {'seq','head'}, dimensions={1} | all-to-all | bytes 4194304 | tf_op jit(solution)/shard_map/all_to_all | solution.py:254
  109.0 0.0 copy-start.4
  109.0 1.2 copy.57
  110.2 0.7 copy-done.4
  110.9 0.0 copy-start.5
  110.9 1.8 %fusion.2 = f32[512,768]{1,0:T(8,128)S(1)} fusion(bf16[512,2048]{1,0:T(8,128)(2,1)S(1)} %bitcast.62, bf16[1,2048,768]{2,1,0:T(8,128)(2,1)S(1)} %copy-done.4), kind=kOutput, calls=%fused_computation.2 | convolution fusion | flops 1610612736 | bytes 6815744 | tf_op jit(solution)/shard_map/dot_general | solution.py:257
  112.7 0.1 copy-done.5
  112.8 1.8 %fusion.4 = f32[512,768]{1,0:T(8,128)S(1)} fusion(bf16[512,2048]{1,0:T(8,128)(2,1)S(1)} %bitcast.63, bf16[1,2048,768]{2,1,0:T(8,128)(2,1)S(1)} %copy-done.5), kind=kOutput, calls=%fused_computation.4 | convolution fusion | flops 1610612736 | bytes 6815744 | tf_op jit(solution)/shard_map/dot_general | solution.py:256
  114.6 0.0 copy-done
  114.6 1.9 %fusion.6 = bf16[512,2048]{1,0:T(8,128)(2,1)S(1)} fusion(bf16[1,768,2048]{2,1,0:T(8,128)(2,1)S(1)} %copy-done, f32[512,768]{1,0:T(8,128)S(1)} %fusion.2, f32[512,768]{1,0:T(8,128)S(1)} %fusion.4), kind=kOutput, calls=%fused_computation.6 | convolution fusion | flops 1614020608 | bytes 8388608 | tf_op jit(solution)/shard_map/dot_general | solution.py:261
  116.5 2.9 %copy.58 = bf16[4,128,2048]{2,0,1:T(4,128)(2,1)} copy(bf16[4,128,2048]{2,1,0:T(8,128)(2,1)S(1)} %bitcast.64) | data formatting | bytes 4194304 | tf_op jit(solution)/shard_map/reshape | solution.py:263
  119.4 0.0 copy-start.3
  119.4 5.9 %all-to-all-start.3 = ((bf16[4,128,2048]{2,0,1:T(4,128)(2,1)}), bf16[4,128,2048]{2,0,1:T(4,128)(2,1)}, u32[]{:S(2)}, u32[]{:S(2)}) async-start(bf16[4,128,2048]{2,0,1:T(4,128)(2,1)} %copy.58), calls=%async_computation.3 | async-start | bytes 4194304 | tf_op jit(solution)/shard_map/all_to_all | solution.py:260
  125.3 0.0 copy-done.3
  125.3 0.1 copy.55
  125.4 0.2 select_reduce_fusion
  125.6 29.5 %all-to-all-done.3 = bf16[4,128,2048]{2,0,1:T(4,128)(2,1)} async-done(((bf16[4,128,2048]{2,0,1:T(4,128)(2,1)}), bf16[4,128,2048]{2,0,1:T(4,128)(2,1)}, u32[]{:S(2)}, u32[]{:S(2)}) %all-to-all-start.3) | async-done | bytes 2097184 | tf_op jit(solution)/shard_map/all_to_all | solution.py:260
  155.1 2.7 %copy.59 = bf16[4,128,2048]{2,1,0:T(8,128)(2,1)S(1)} copy(bf16[4,128,2048]{2,0,1:T(4,128)(2,1)} %all-to-all-done.3) | data formatting | bytes 4194304 | tf_op jit(solution)/shard_map/all_to_all | solution.py:260
  157.9 2.7 %fusion.9 = bf16[32,2048]{1,0:T(8,128)(2,1)} fusion(f32[32,512]{1,0:T(8,128)S(1)} %select_reduce_fusion, bf16[512,2048]{1,0:T(8,128)(2,1)S(1)} %bitcast.59, f32[32,2048]{1,0:T(8,128)S(1)} %convert_reduce_fusion, bf16[256,2048]{1,0:T(8,128)(2,1)} %x_ref.1, s32[]{:T(128)S(6)} %select_n.46), kind=kOutput, calls=%fused_computation.9 | convolution fusion | flops 402915328 | bytes 2686980 | tf_op jit(solution)/shard_map/dot_general | solution.py:270
  (16 shorter events, 0.1 us)
Async XLA Ops:
  0.0 114.6 %copy-start = (bf16[1,768,2048]{2,1,0:T(8,128)(2,1)S(1)}, bf16[1,768,2048]{2,1,0:T(8,128)(2,1)}, u32[]{:S(2)}) copy-start(bf16[1,768,2048]{2,1,0:T(8,128)(2,1)} %param.29) | copy-start | bytes 9437188
  6.7 23.0 %all-to-all-start = ((bf16[8,2,256,128]{3,2,1,0:T(8,128)(2,1)}), bf16[8,2,256,128]{3,2,1,0:T(8,128)(2,1)}, u32[]{:S(2)}, u32[]{:S(2)}) async-start(bf16[8,2,256,128]{3,2,1,0:T(8,128)(2,1)} %get-tuple-element.18), calls=%async_computation | async-start | bytes 2097152 | tf_op jit(solution)/shard_map/all_to_all | solution.py:217
  13.7 16.0 %copy-start.2 = (s32[32,8]{0,1:T(8,128)S(1)}, s32[32,8]{0,1:T(8,128)}, u32[]{:S(2)}) copy-start(s32[32,8]{0,1:T(8,128)} %param.25) | copy-start | bytes 3076
  29.7 3.0 %collective-permute-start = (bf16[8,2,256,128]{3,2,1,0:T(8,128)(2,1)}, bf16[8,2,256,128]{3,2,1,0:T(8,128)(2,1)}, u32[]{:S(2)}, u32[]{:S(2)}) collective-permute-start(bf16[8,2,256,128]{3,2,1,0:T(8,128)(2,1)} %all-to-all-done.own_ref), channel_id=1, source_target_pairs={{0,8},{8,0},{16,24},{24,16},{32,40},{40,32},{48,56},{56,48},{64,72... | collective-permute-start | bytes 3145736 | tf_op jit(solution)/shard_map/ppermute | solution.py:234
  41.5 23.5 %copy-start.1 = (f32[2048]{0:T(1024)S(1)}, f32[2048]{0:T(1024)}, u32[]{:S(2)}) copy-start(f32[2048]{0:T(1024)} %param.23) | copy-start | bytes 24580
  41.5 21.0 %all-to-all-start.1 = ((bf16[8,32,2048]{2,1,0:T(8,128)(2,1)}), bf16[8,32,2048]{2,1,0:T(8,128)(2,1)}, u32[]{:S(2)}, u32[]{:S(2)}) async-start(bf16[8,32,2048]{2,1,0:T(8,128)(2,1)} %bitcast.61), calls=%async_computation.1 | async-start | bytes 2097152 | tf_op jit(solution)/shard_map/all_to_all | solution.py:238
  109.0 1.9 %copy-start.4 = (bf16[1,2048,768]{2,1,0:T(8,128)(2,1)S(1)}, bf16[1,2048,768]{2,1,0:T(8,128)(2,1)}, u32[]{:S(2)}) copy-start(bf16[1,2048,768]{2,1,0:T(8,128)(2,1)} %param.28) | copy-start | bytes 9437188
  110.9 1.9 %copy-start.5 = (bf16[1,2048,768]{2,1,0:T(8,128)(2,1)S(1)}, bf16[1,2048,768]{2,1,0:T(8,128)(2,1)}, u32[]{:S(2)}) copy-start(bf16[1,2048,768]{2,1,0:T(8,128)(2,1)} %param.27) | copy-start | bytes 9437188
  119.4 5.9 %copy-start.3 = (f32[32,8]{0,1:T(8,128)S(1)}, f32[32,8]{0,1:T(8,128)}, u32[]{:S(2)}) copy-start(f32[32,8]{0,1:T(8,128)} %param.26) | copy-start | bytes 3076
  119.4 35.7 %all-to-all-start.3 = ((bf16[4,128,2048]{2,0,1:T(4,128)(2,1)}), bf16[4,128,2048]{2,0,1:T(4,128)(2,1)}, u32[]{:S(2)}, u32[]{:S(2)}) async-start(bf16[4,128,2048]{2,0,1:T(4,128)(2,1)} %copy.58), calls=%async_computation.3 | async-start | bytes 4194304 | tf_op jit(solution)/shard_map/all_to_all | solution.py:260

commit v17 on v14

--- a/solution.py
+++ b/solution.py
@@ -168,6 +168,45 @@
             jax.ShapeDtypeStruct((copies, 2, tok, dim), jnp.bfloat16),
         ],
     )(index, tokens, norm_gain[None, :], w_key, w_value, key_gain[None, :], cosine, sine)
+
+
+def _route_kernel(index_ref, terms_ref, tok_ref, gain_ref, src_ref, resid_ref, out_ref):
+    attn = terms_ref[0].astype(jnp.float32)
+    for i in range(1, terms_ref.shape[0]):
+        attn = attn + terms_ref[i].astype(jnp.float32)
+    resid = tok_ref[...].astype(jnp.float32) + attn
+    resid_ref[...] = resid
+    routed = (
+        resid * lax.rsqrt(jnp.mean(resid * resid, axis=1, keepdims=True) + EPSILON) * gain_ref[...]
+    ).astype(jnp.bfloat16)
+    out_ref[...] = jnp.dot(src_ref[...], routed, preferred_element_type=jnp.float32).astype(out_ref.dtype)
+
+
+def route(index, terms, tokens, gain, sources):
+    parts, rows, width = terms.shape
+    slots = sources.shape[0]
+    spec = pltpu.PrefetchScalarGridSpec(
+        num_scalar_prefetch=1,
+        grid=(1,),
+        in_specs=[
+            pl.BlockSpec((parts, rows, width), lambda i, b: (0, 0, 0)),
+            pl.BlockSpec((rows, width), lambda i, b: (b[0], 0)),
+            pl.BlockSpec((1, width), lambda i, b: (0, 0)),
+            pl.BlockSpec((slots, rows), lambda i, b: (0, 0)),
+        ],
+        out_specs=[
+            pl.BlockSpec((rows, width), lambda i, b: (0, 0)),
+            pl.BlockSpec((slots, width), lambda i, b: (0, 0)),
+        ],
+    )
+    return pl.pallas_call(
+        _route_kernel,
+        grid_spec=spec,
+        out_shape=[
+            jax.ShapeDtypeStruct((rows, width), jnp.float32),
+            jax.ShapeDtypeStruct((slots, width), jnp.bfloat16),
+        ],
+    )(index, terms, tokens, gain[None, :], sources)
 
 
 def local(
@@ -236,9 +275,6 @@
     terms = attend(bounds, queries, cosine2, sine2, gain, same_core, other_core, qpos, qstart, w_out)
     rows = tok_dev // n_head
     terms = lax.all_to_all(terms.reshape(n_head, rows, width), "head", 0, 0, tiled=True)
-    attn_rows = jnp.sum(terms.astype(jnp.float32), axis=0)
-    resid = lax.dynamic_slice_in_dim(tokens, head_index * rows, rows, 0).astype(jnp.float32) + attn_rows
-    routed = rms_scale(resid, post_gain).astype(jnp.bfloat16)
     experts = n_seq * n_head * w_gate.shape[0]
     capacity = 2 * TOP * rows // experts
     chosen = expert_ids.reshape(-1)
@@ -249,7 +285,7 @@
         rows, TOP, capacity * experts
     )
     sources = jnp.transpose(jnp.any(select, axis=1)).astype(jnp.bfloat16)
-    outgoing = jnp.dot(sources, routed, preferred_element_type=jnp.float32).astype(jnp.bfloat16)
+    resid, outgoing = route(jnp.reshape(head_index, (1,)).astype(jnp.int32), terms, tokens, post_gain, sources)
     outgoing = outgoing.reshape(capacity, experts, width)
     block = lax.all_to_all(outgoing, ("seq", "head"), split_axis=1, concat_axis=1, tiled=True)
     flat = block.reshape(-1, width)

time: 162 us -> 163 us (level)
  Pallas kernels: 12.4 us -> 16 us
  matrix products: 13.2 us -> 9.99 us
  local copies, waits for them, and re-layouts: 13.7 us -> 16.2 us
  other arithmetic: 6.57 us -> 4.8 us
    pallas_call x0 -> x1, Pallas kernels: none -> 3.59 us  [route(): pl.pallas_call(_route_kernel, grid_spec=spec, out_shape=[jax.ShapeDtypeSt...]
    reduce_sum x2 -> x0, other arithmetic: 2.44 us -> none  [the longest x1 1.39 us: local(): attn_rows = jnp.sum(terms.astype(jnp.float32), axis=0)]
    dot_general x1 -> x0, matrix products: 1.68 us -> none  [local(): jnp.dot(sources, routed, preferred_element_type=jnp.float32)]
  transfers between devices with their start and end apart: 4 -> 4, of which waited for: 4 -> 4; matrix products, arithmetic and copies ran while one was open for 5% -> 6% of each run, Pallas kernels for 0% -> 0%
where the time goes in v17:
time: 163 us; the launch traced here: 162 us
  waiting for transfers between devices  47.9 us (29%)
  blocking collectives  41.6 us (26%)
  starting transfers between devices  18.3 us (11%)
  local copies, waits for them, and re-layouts  16.2 us (10%)
  Pallas kernels  16 us (10%)
  matrix products  9.99 us (6%)
  between operations  6.87 us (4%)
  other arithmetic  4.8 us (3%)
    all_to_all x1, blocking collectives, local(): lax.all_to_all(outgoing, ('seq', 'head'), split_axis=1, concat_axis=1, ti...  41.6 us
    all_to_all x1, waiting for transfers between devices, local(): lax.all_to_all(jnp.dot(hidden, w_down[0], preferred_element_type=jnp.floa...  29.5 us
    all_to_all x1, waiting for transfers between devices, local(): lax.all_to_all(terms.reshape(n_head, rows, width), 'head', 0, 0, tiled=True)  14.2 us
    pallas_call x1, Pallas kernels, attend(): pl.pallas_call(kernel, grid_spec=spec, out_shape=jax.ShapeDtypeStruct((to...  8.83 us
    all_to_all x1, starting transfers between devices, local(): lax.all_to_all(spread, 'seq', 0, 0, tiled=True, axis_index_groups=groups)  7.02 us
    all_to_all x1, starting transfers between devices, local(): lax.all_to_all(jnp.dot(hidden, w_down[0], preferred_element_type=jnp.floa...  5.91 us
    all_to_all x1, starting transfers between devices, local(): lax.all_to_all(terms.reshape(n_head, rows, width), 'head', 0, 0, tiled=True)  5.34 us
    all_to_all x1, waiting for transfers between devices, local(): lax.all_to_all(spread, 'seq', 0, 0, tiled=True, axis_index_groups=groups)  3.88 us
  transfers between devices with their start and end apart: 4, of which 4 were waited for; matrix products, arithmetic and copies ran while one was open for 6% of the time, Pallas kernels for 0%

profile of v17, /device:TPU:0, one launch (start us, length us, event | category | flops | bytes accessed | tf_op | source)
XLA Modules:
  0.0 161.6 jit_solution(9247379322466187075)
XLA Ops:
  0.0 0.0 copy-start
  0.0 1.0 reduce-window.18
  1.0 0.7 bitcast_subtract_fusion.1
  1.7 0.1 convert_reduce_fusion
  1.8 0.1 select_reduce_fusion.1
  1.9 0.5 fusion.16
  2.4 0.8 pad_maximum_fusion
  3.2 3.6 %shard_map.145 = (bf16[256,2048]{1,0:T(8,128)(2,1)}, bf16[8,2,256,128]{3,2,1,0:T(8,128)(2,1)}) custom-call(s32[1]{0:T(128)} %bitcast.12.index_ref, bf16[256,2048]{1,0:T(8,128)(2,1)} %tok_ref.1, f32[1,2048]{1,0:T(1,128)} %bitcast.76, bf16[2048,512]{1,0:T(8,128)(2,1)} %wk_ref.1, bf16[2048,512]{1,0:T(8,128)(2,1)} %wv_ref.1, f32[1,128]{1,0:T(1,128)} %bitcast.78, ...), custom_call_target="tpu_custom_call" | custom-call | tf_op jit(solution)/shard_map/pallas_call | solution.py:163
  6.8 7.0 %all-to-all-start = ((bf16[8,2,256,128]{3,2,1,0:T(8,128)(2,1)}), bf16[8,2,256,128]{3,2,1,0:T(8,128)(2,1)}, u32[]{:S(2)}, u32[]{:S(2)}) async-start(bf16[8,2,256,128]{3,2,1,0:T(8,128)(2,1)} %get-tuple-element.20), calls=%async_computation | async-start | bytes 2097152 | tf_op jit(solution)/shard_map/all_to_all | solution.py:256
  13.9 0.0 copy-start.2
  13.9 0.6 fusion.18
  15.2 0.7 fusion.19
  21.8 0.7 stack.23.bounds_ref
  22.5 3.4 %fusion.20.q_ref = f32[256,512]{1,0:T(8,128)} fusion(bf16[256,2048]{1,0:T(8,128)(2,1)} %get-tuple-element.19, bf16[2048,512]{1,0:T(8,128)(2,1)} %param.17), kind=kOutput, calls=%fused_computation.41 | convolution fusion | flops 536870912 | bytes 3670016 | tf_op jit(solution)/shard_map/dot_general | solution.py:255
  25.9 3.9 %all-to-all-done.own_ref = bf16[8,2,256,128]{3,2,1,0:T(8,128)(2,1)} async-done(((bf16[8,2,256,128]{3,2,1,0:T(8,128)(2,1)}), bf16[8,2,256,128]{3,2,1,0:T(8,128)(2,1)}, u32[]{:S(2)}, u32[]{:S(2)}) %all-to-all-start) | async-done | bytes 1048608 | tf_op jit(solution)/shard_map/all_to_all | solution.py:256
  29.8 0.0 collective-permute-start
  29.8 0.0 copy-done.2
  29.8 0.1 copy.63
  29.9 0.1 eq.61
  30.0 0.1 eq.57
  30.1 0.1 copy.65
  30.2 0.2 fusion.11
  30.4 1.0 copy.61.qpos_ref
  31.4 1.0 copy.62.qstart_ref
  32.5 0.3 collective-permute-done.other_ref
  32.8 8.8 %shard_map.146 = bf16[256,2048]{1,0:T(8,128)(2,1)} custom-call(s32[5]{0:T(128)} %stack.23.bounds_ref, f32[256,512]{1,0:T(8,128)} %fusion.20.q_ref, f32[256,128]{1,0:T(8,128)} %get-tuple-element.23.cos_ref, f32[256,128]{1,0:T(8,128)} %get-tuple-element.24.sin_ref, f32[1,128]{1,0:T(1,128)} %bitcast.80, bf16[8,2,256,128]{3,2,1,0:T(8,128)(2,1)} %all-to-all-done.own_ref, ...), custom_call_target="tpu_custom_call" | custom-call | tf_op jit(solution)/shard_map/pallas_call | solution.py:120
  41.6 5.3 %all-to-all-start.1 = ((bf16[8,32,2048]{2,1,0:T(8,128)(2,1)}), bf16[8,32,2048]{2,1,0:T(8,128)(2,1)}, u32[]{:S(2)}, u32[]{:S(2)}) async-start(bf16[8,32,2048]{2,1,0:T(8,128)(2,1)} %bitcast.65), calls=%async_computation.1 | async-start | bytes 2097152 | tf_op jit(solution)/shard_map/all_to_all | solution.py:277
  47.1 0.2 fusion.13
  47.2 0.1 mul.53
  47.3 0.2 fusion.10
  47.6 0.8 copy.68
  48.4 14.2 %all-to-all-done.1.terms_ref = bf16[8,32,2048]{2,1,0:T(8,128)(2,1)} async-done(((bf16[8,32,2048]{2,1,0:T(8,128)(2,1)}), bf16[8,32,2048]{2,1,0:T(8,128)(2,1)}, u32[]{:S(2)}, u32[]{:S(2)}) %all-to-all-start.1) | async-done | bytes 1048608 | tf_op jit(solution)/shard_map/all_to_all | solution.py:277
  62.5 3.6 %shard_map.147 = (f32[32,2048]{1,0:T(8,128)}, bf16[512,2048]{1,0:T(8,128)(2,1)}) custom-call(s32[1]{0:T(128)} %bitcast.index_ref, bf16[8,32,2048]{2,1,0:T(8,128)(2,1)} %all-to-all-done.1.terms_ref, bf16[256,2048]{1,0:T(8,128)(2,1)} %tok_ref.1, f32[1,2048]{1,0:T(1,128)} %bitcast.77, bf16[512,32]{1,0:T(8,128)(2,1)} %bitcast.71), custom_call_target="tpu_custom_call" | custom-call | tf_op jit(solution)/shard_map/pallas_call | solution.py:202
  66.1 3.2 %copy.70 = bf16[4,128,2048]{2,0,1:T(4,128)(2,1)S(1)} copy(bf16[4,128,2048]{2,1,0:T(8,128)(2,1)} %bitcast.66) | data formatting | bytes 4194304 | tf_op jit(solution)/shard_map/reshape | solution.py:289
  69.3 41.6 %all_to_all.20 = bf16[4,128,2048]{2,0,1:T(4,128)(2,1)S(1)} all-to-all(bf16[4,128,2048]{2,0,1:T(4,128)(2,1)S(1)} %copy.70), channel_id=1, replica_groups=mesh['seq'=16,'head'=8] {'seq','head'}, dimensions={1} | all-to-all | bytes 4194304 | tf_op jit(solution)/shard_map/all_to_all | solution.py:290
  110.9 0.0 copy-start.4
  110.9 1.2 copy.71
  112.1 0.7 copy-done.4
  112.8 0.0 copy-start.5
  112.8 1.8 %fusion.2 = f32[512,768]{1,0:T(8,128)S(1)} fusion(bf16[512,2048]{1,0:T(8,128)(2,1)S(1)} %bitcast.67, bf16[1,2048,768]{2,1,0:T(8,128)(2,1)S(1)} %copy-done.4), kind=kOutput, calls=%fused_computation.2 | convolution fusion | flops 1610612736 | bytes 6815744 | tf_op jit(solution)/shard_map/dot_general | solution.py:293
  114.6 0.1 copy-done.5
  114.7 1.8 %fusion.4 = f32[512,768]{1,0:T(8,128)S(1)} fusion(bf16[512,2048]{1,0:T(8,128)(2,1)S(1)} %bitcast.68, bf16[1,2048,768]{2,1,0:T(8,128)(2,1)S(1)} %copy-done.5), kind=kOutput, calls=%fused_computation.4 | convolution fusion | flops 1610612736 | bytes 6815744 | tf_op jit(solution)/shard_map/dot_general | solution.py:292
  116.5 0.0 copy-done
  116.5 1.9 %fusion.6 = bf16[512,2048]{1,0:T(8,128)(2,1)S(1)} fusion(bf16[1,768,2048]{2,1,0:T(8,128)(2,1)S(1)} %copy-done, f32[512,768]{1,0:T(8,128)S(1)} %fusion.2, f32[512,768]{1,0:T(8,128)S(1)} %fusion.4), kind=kOutput, calls=%fused_computation.6 | convolution fusion | flops 1614020608 | bytes 8388608 | tf_op jit(solution)/shard_map/dot_general | solution.py:297
  118.4 2.9 %copy.72 = bf16[4,128,2048]{2,0,1:T(4,128)(2,1)} copy(bf16[4,128,2048]{2,1,0:T(8,128)(2,1)S(1)} %bitcast.69) | data formatting | bytes 4194304 | tf_op jit(solution)/shard_map/reshape | solution.py:299
  121.3 0.0 copy-start.3
  121.3 5.9 %all-to-all-start.3 = ((bf16[4,128,2048]{2,0,1:T(4,128)(2,1)}), bf16[4,128,2048]{2,0,1:T(4,128)(2,1)}, u32[]{:S(2)}, u32[]{:S(2)}) async-start(bf16[4,128,2048]{2,0,1:T(4,128)(2,1)} %copy.72), calls=%async_computation.3 | async-start | bytes 4194304 | tf_op jit(solution)/shard_map/all_to_all | solution.py:296
  127.2 0.0 copy-done.3
  127.2 0.1 copy.69
  127.3 0.2 select_reduce_fusion
  127.5 29.5 %all-to-all-done.3 = bf16[4,128,2048]{2,0,1:T(4,128)(2,1)} async-done(((bf16[4,128,2048]{2,0,1:T(4,128)(2,1)}), bf16[4,128,2048]{2,0,1:T(4,128)(2,1)}, u32[]{:S(2)}, u32[]{:S(2)}) %all-to-all-start.3) | async-done | bytes 2097184 | tf_op jit(solution)/shard_map/all_to_all | solution.py:296
  157.0 2.7 %copy.73 = bf16[4,128,2048]{2,1,0:T(8,128)(2,1)S(1)} copy(bf16[4,128,2048]{2,0,1:T(4,128)(2,1)} %all-to-all-done.3) | data formatting | bytes 4194304 | tf_op jit(solution)/shard_map/all_to_all | solution.py:296
  159.8 0.0 copy-start.1
  159.8 1.1 fusion.21
  160.9 0.0 copy-done.1
  160.9 0.7 add_convert_fusion
  (16 shorter events, 0.1 us)
Async XLA Ops:
  0.0 116.5 %copy-start = (bf16[1,768,2048]{2,1,0:T(8,128)(2,1)S(1)}, bf16[1,768,2048]{2,1,0:T(8,128)(2,1)}, u32[]{:S(2)}) copy-start(bf16[1,768,2048]{2,1,0:T(8,128)(2,1)} %param.29) | copy-start | bytes 9437188
  6.8 23.0 %all-to-all-start = ((bf16[8,2,256,128]{3,2,1,0:T(8,128)(2,1)}), bf16[8,2,256,128]{3,2,1,0:T(8,128)(2,1)}, u32[]{:S(2)}, u32[]{:S(2)}) async-start(bf16[8,2,256,128]{3,2,1,0:T(8,128)(2,1)} %get-tuple-element.20), calls=%async_computation | async-start | bytes 2097152 | tf_op jit(solution)/shard_map/all_to_all | solution.py:256
  13.9 15.9 %copy-start.2 = (s32[32,8]{0,1:T(8,128)S(1)}, s32[32,8]{0,1:T(8,128)}, u32[]{:S(2)}) copy-start(s32[32,8]{0,1:T(8,128)} %param.25) | copy-start | bytes 3076
  29.8 3.0 %collective-permute-start = (bf16[8,2,256,128]{3,2,1,0:T(8,128)(2,1)}, bf16[8,2,256,128]{3,2,1,0:T(8,128)(2,1)}, u32[]{:S(2)}, u32[]{:S(2)}) collective-permute-start(bf16[8,2,256,128]{3,2,1,0:T(8,128)(2,1)} %all-to-all-done.own_ref), channel_id=1, source_target_pairs={{0,8},{8,0},{16,24},{24,16},{32,40},{40,32},{48,56},{56,48},{64,72... | collective-permute-start | bytes 3145736 | tf_op jit(solution)/shard_map/ppermute | solution.py:273
  41.6 20.9 %all-to-all-start.1 = ((bf16[8,32,2048]{2,1,0:T(8,128)(2,1)}), bf16[8,32,2048]{2,1,0:T(8,128)(2,1)}, u32[]{:S(2)}, u32[]{:S(2)}) async-start(bf16[8,32,2048]{2,1,0:T(8,128)(2,1)} %bitcast.65), calls=%async_computation.1 | async-start | bytes 2097152 | tf_op jit(solution)/shard_map/all_to_all | solution.py:277
  110.9 1.9 %copy-start.4 = (bf16[1,2048,768]{2,1,0:T(8,128)(2,1)S(1)}, bf16[1,2048,768]{2,1,0:T(8,128)(2,1)}, u32[]{:S(2)}) copy-start(bf16[1,2048,768]{2,1,0:T(8,128)(2,1)} %param.28) | copy-start | bytes 9437188
  112.8 1.9 %copy-start.5 = (bf16[1,2048,768]{2,1,0:T(8,128)(2,1)S(1)}, bf16[1,2048,768]{2,1,0:T(8,128)(2,1)}, u32[]{:S(2)}) copy-start(bf16[1,2048,768]{2,1,0:T(8,128)(2,1)} %param.27) | copy-start | bytes 9437188
  121.3 5.9 %copy-start.3 = (f32[32,8]{0,1:T(8,128)S(1)}, f32[32,8]{0,1:T(8,128)}, u32[]{:S(2)}) copy-start(f32[32,8]{0,1:T(8,128)} %param.26) | copy-start | bytes 3076
  121.3 35.7 %all-to-all-start.3 = ((bf16[4,128,2048]{2,0,1:T(4,128)(2,1)}), bf16[4,128,2048]{2,0,1:T(4,128)(2,1)}, u32[]{:S(2)}, u32[]{:S(2)}) async-start(bf16[4,128,2048]{2,0,1:T(4,128)(2,1)} %copy.72), calls=%async_computation.3 | async-start | bytes 4194304 | tf_op jit(solution)/shard_map/all_to_all | solution.py:296
  159.8 1.1 copy-start.1

commit v18 on v14

--- a/solution.py
+++ b/solution.py
@@ -36,7 +36,7 @@
 
 
 def _attend_kernel(
-    bounds_ref, q_ref, cos_ref, sin_ref, gain_ref, own_ref, other_ref, qpos_ref, qstart_ref, w_ref, o_ref, *, dim
+    bounds_ref, q_ref, cos_ref, sin_ref, gain_ref, own_ref, other_ref, w_ref, o_ref, *, dim
 ):
     heads = q_ref.shape[1] // dim
     tok = q_ref.shape[0]
@@ -48,8 +48,11 @@
         part = part * cos_ref[...] + pltpu.roll(part, dim // 2, 1) * sin_ref[...]
         parts.append(part.astype(jnp.bfloat16))
     q = jnp.concatenate(parts, axis=0)
-    qpos = qpos_ref[...]
-    qstart = qstart_ref[...]
+    row = lax.broadcasted_iota(jnp.int32, (heads * tok, 1), 0)
+    qpos = bounds_ref[5] + row % tok
+    qstart = jnp.zeros_like(qpos)
+    for d in range(6, bounds_ref.shape[0]):
+        qstart = jnp.maximum(qstart, jnp.where(bounds_ref[d] <= qpos, bounds_ref[d], 0))
     scale = dim ** (-0.5)
 
     def step(j, carry, masked):
@@ -97,7 +100,7 @@
     o_ref[...] = terms.astype(o_ref.dtype)
 
 
-def attend(bounds, queries, cosine, sine, gain, own, other, qpos, qstart, w_out):
+def attend(bounds, queries, cosine, sine, gain, own, other, w_out):
     tok, width = queries.shape
     dim = own.shape[-1]
     kernel = functools.partial(_attend_kernel, dim=dim)
@@ -111,15 +114,13 @@
             pl.BlockSpec(gain.shape, lambda i, b: (0, 0)),
             pl.BlockSpec(own.shape, lambda i, b: (0, 0, 0, 0)),
             pl.BlockSpec(other.shape, lambda i, b: (0, 0, 0, 0)),
-            pl.BlockSpec(qpos.shape, lambda i, b: (0, 0)),
-            pl.BlockSpec(qstart.shape, lambda i, b: (0, 0)),
             pl.BlockSpec(w_out.shape, lambda i, b: (0, 0)),
         ],
         out_specs=pl.BlockSpec((tok, w_out.shape[1]), lambda i, b: (0, 0)),
     )
     return pl.pallas_call(
         kernel, grid_spec=spec, out_shape=jax.ShapeDtypeStruct((tok, w_out.shape[1]), jnp.bfloat16)
-    )(bounds, queries, cosine, sine, gain, own, other, qpos, qstart, w_out)
+    )(bounds, queries, cosine, sine, gain, own, other, w_out)
 
 
 def _project_kernel(
@@ -220,20 +221,20 @@
     high = positions[-1] // block + 1
     inner_low = jnp.clip(-(-own_start[-1] // block), low, high)
     inner_high = jnp.clip((positions[0] + 1) // block, inner_low, high)
-    bounds = jnp.stack([low, inner_low, inner_high, high, seq_index % 2]).astype(jnp.int32)
+    bounds = jnp.concatenate(
+        [jnp.stack([low, inner_low, inner_high, high, seq_index % 2, positions[0]]), starts]
+    ).astype(jnp.int32)
     operands = (
         bounds,
         queries,
         cosine2,
         sine2,
         query_gain[None, :],
-        jnp.tile(positions[:, None], (per_dev, 1)),
-        jnp.tile(own_start[:, None], (per_dev, 1)),
     )
     operands, same_core = lax.optimization_barrier((operands, same_core))
     other_core = lax.ppermute(same_core, "seq", [(i, i ^ 1) for i in range(n_seq)])
-    bounds, queries, cosine2, sine2, gain, qpos, qstart = operands
-    terms = attend(bounds, queries, cosine2, sine2, gain, same_core, other_core, qpos, qstart, w_out)
+    bounds, queries, cosine2, sine2, gain = operands
+    terms = attend(bounds, queries, cosine2, sine2, gain, same_core, other_core, w_out)
     rows = tok_dev // n_head
     terms = lax.all_to_all(terms.reshape(n_head, rows, width), "head", 0, 0, tiled=True)
     attn_rows = jnp.sum(terms.astype(jnp.float32), axis=0)

time: 162 us -> 164 us (1.012); the launches traced: 161 us -> 164 us
  blocking collectives: 40.7 us -> 44.5 us
    all_to_all x1, blocking collectives: 40.7 us -> 44.5 us  [local(): lax.all_to_all(outgoing, ('seq', 'head'), split_axis=1, concat_axis=1, ti...]
    ppermute x1, waiting for transfers between devices: 0.34 us -> 2.41 us  [local(): lax.ppermute(same_core, 'seq', [(i, i ^ 1) for i in range(n_seq)])]
    optimization_barrier x2 -> x0, local copies, waits for them, and re-layouts: 2.07 us -> none  [local(): operands, same_core = lax.optimization_barrier((operands, same_core))]
  transfers between devices with their start and end apart: 4 -> 4, of which waited for: 4 -> 4; matrix products, arithmetic and copies ran while one was open for 5% -> 4% of each run, Pallas kernels for 0% -> 0%
where the time goes in v18:
time: 164 us
  waiting for transfers between devices  50.3 us (31%)
  blocking collectives  44.5 us (27%)
  starting transfers between devices  18.4 us (11%)
  matrix products  13.2 us (8%)
  Pallas kernels  12.4 us (8%)
  local copies, waits for them, and re-layouts  12.1 us (7%)
  between operations  6.88 us (4%)
  other arithmetic  6.55 us (4%)
    all_to_all x1, blocking collectives, local(): lax.all_to_all(outgoing, ('seq', 'head'), split_axis=1, concat_axis=1, ti...  44.5 us
    all_to_all x1, waiting for transfers between devices, local(): lax.all_to_all(jnp.dot(hidden, w_down[0], preferred_element_type=jnp.floa...  29.5 us
    all_to_all x1, waiting for transfers between devices, local(): lax.all_to_all(terms.reshape(n_head, rows, width), 'head', 0, 0, tiled=True)  14.9 us
    pallas_call x1, Pallas kernels, attend(): pl.pallas_call(kernel, grid_spec=spec, out_shape=jax.ShapeDtypeStruct((to...  8.81 us
    all_to_all x1, starting transfers between devices, local(): lax.all_to_all(spread, 'seq', 0, 0, tiled=True, axis_index_groups=groups)  7.02 us
    all_to_all x1, starting transfers between devices, local(): lax.all_to_all(jnp.dot(hidden, w_down[0], preferred_element_type=jnp.floa...  5.91 us
    all_to_all x1, starting transfers between devices, local(): lax.all_to_all(terms.reshape(n_head, rows, width), 'head', 0, 0, tiled=True)  5.48 us
    pallas_call x1, Pallas kernels, project(): pl.pallas_call(_project_kernel, grid_spec=spec, out_shape=[jax.ShapeDtype...  3.59 us
  transfers between devices with their start and end apart: 4, of which 4 were waited for; matrix products, arithmetic and copies ran while one was open for 4% of the time, Pallas kernels for 0%

profile of v18, /device:TPU:0, one launch (start us, length us, event | category | flops | bytes accessed | tf_op | source)
XLA Modules:
  0.0 164.4 jit_solution(12294358263704066613)
XLA Ops:
  0.0 0.0 copy-start
  0.0 1.0 reduce-window.18
  1.0 0.7 bitcast_subtract_fusion.1
  1.7 0.1 convert_reduce_fusion.1
  1.8 0.1 select_reduce_fusion.1
  1.9 0.5 fusion.19
  2.4 0.8 pad_maximum_fusion
  3.2 3.6 %shard_map.145 = (bf16[256,2048]{1,0:T(8,128)(2,1)}, bf16[8,2,256,128]{3,2,1,0:T(8,128)(2,1)}) custom-call(s32[1]{0:T(128)} %bitcast.11.index_ref, bf16[256,2048]{1,0:T(8,128)(2,1)} %x_ref.1, f32[1,2048]{1,0:T(1,128)} %bitcast.61, bf16[2048,512]{1,0:T(8,128)(2,1)} %wk_ref.1, bf16[2048,512]{1,0:T(8,128)(2,1)} %wv_ref.1, f32[1,128]{1,0:T(1,128)} %bitcast.62, ...), custom_call_target="tpu_custom_call" | custom-call | tf_op jit(solution)/shard_map/pallas_call | solution.py:164
  6.8 7.0 %all-to-all-start = ((bf16[8,2,256,128]{3,2,1,0:T(8,128)(2,1)}), bf16[8,2,256,128]{3,2,1,0:T(8,128)(2,1)}, u32[]{:S(2)}, u32[]{:S(2)}) async-start(bf16[8,2,256,128]{3,2,1,0:T(8,128)(2,1)} %get-tuple-element.16), calls=%async_computation | async-start | bytes 2097152 | tf_op jit(solution)/shard_map/all_to_all | solution.py:218
  13.8 0.0 copy-start.2
  13.8 0.6 fusion.23
  18.0 0.6 fusion.22
  21.7 1.2 concatenate.9.bounds_ref
  22.9 3.4 %fusion.24.q_ref = f32[256,512]{1,0:T(8,128)} fusion(bf16[256,2048]{1,0:T(8,128)(2,1)} %get-tuple-element.15, bf16[2048,512]{1,0:T(8,128)(2,1)} %param.17), kind=kOutput, calls=%fused_computation.49 | convolution fusion | flops 536870912 | bytes 3670016 | tf_op jit(solution)/shard_map/dot_general | solution.py:217
  26.3 3.5 %all-to-all-done.own_ref = bf16[8,2,256,128]{3,2,1,0:T(8,128)(2,1)} async-done(((bf16[8,2,256,128]{3,2,1,0:T(8,128)(2,1)}), bf16[8,2,256,128]{3,2,1,0:T(8,128)(2,1)}, u32[]{:S(2)}, u32[]{:S(2)}) %all-to-all-start) | async-done | bytes 1048608 | tf_op jit(solution)/shard_map/all_to_all | solution.py:218
  29.8 0.0 collective-permute-start
  29.8 0.0 copy-done.2
  29.8 0.1 copy.42
  29.9 0.1 eq.61
  29.9 0.1 eq.57
  30.0 0.1 copy.44
  30.1 0.2 fusion.12
  30.4 2.4 %collective-permute-done.other_ref = bf16[8,2,256,128]{3,2,1,0:T(8,128)(2,1)} collective-permute-done((bf16[8,2,256,128]{3,2,1,0:T(8,128)(2,1)}, bf16[8,2,256,128]{3,2,1,0:T(8,128)(2,1)}, u32[]{:S(2)}, u32[]{:S(2)}) %collective-permute-start) | collective-permute-done | bytes 1048608 | tf_op jit(solution)/shard_map/ppermute | solution.py:235
  32.8 8.8 %shard_map.146 = bf16[256,2048]{1,0:T(8,128)(2,1)} custom-call(s32[12]{0:T(128)} %concatenate.9.bounds_ref, f32[256,512]{1,0:T(8,128)} %fusion.24.q_ref, f32[256,128]{1,0:T(8,128)} %get-tuple-element.19.cos_ref, f32[256,128]{1,0:T(8,128)} %get-tuple-element.20.sin_ref, f32[1,128]{1,0:T(1,128)} %bitcast.63, bf16[8,2,256,128]{3,2,1,0:T(8,128)(2,1)} %all-to-all-done.own_ref, ...), custom_call_target="tpu_custom_call" | custom-call | tf_op jit(solution)/shard_map/pallas_call | solution.py:121
  41.6 0.0 copy-start.1
  41.6 5.5 %all-to-all-start.1 = ((bf16[8,32,2048]{2,1,0:T(8,128)(2,1)}), bf16[8,32,2048]{2,1,0:T(8,128)(2,1)}, u32[]{:S(2)}, u32[]{:S(2)}) async-start(bf16[8,32,2048]{2,1,0:T(8,128)(2,1)} %bitcast.54), calls=%async_computation.1 | async-start | bytes 2097152 | tf_op jit(solution)/shard_map/all_to_all | solution.py:239
  47.2 0.2 fusion.14
  47.4 0.1 mul.76
  47.5 0.2 fusion.11
  47.7 14.9 %all-to-all-done.1 = bf16[8,32,2048]{2,1,0:T(8,128)(2,1)} async-done(((bf16[8,32,2048]{2,1,0:T(8,128)(2,1)}), bf16[8,32,2048]{2,1,0:T(8,128)(2,1)}, u32[]{:S(2)}, u32[]{:S(2)}) %all-to-all-start.1) | async-done | bytes 1048608 | tf_op jit(solution)/shard_map/all_to_all | solution.py:239
  62.6 1.4 convert_reduce_fusion
  64.0 1.1 multiply_reduce_fusion
  65.1 0.0 copy-done.1
  65.1 1.7 %convolution_convert_fusion = bf16[512,2048]{1,0:T(8,128)(2,1)S(1)} fusion(pred[32,512]{1,0:T(8,128)(4,1)S(1)} %fusion.11, f32[2048]{0:T(1024)S(1)} %copy-done.1, f32[32]{0:T(128)S(1)} %add_rsqrt_fusion, f32[32,2048]{1,0:T(8,128)S(1)} %convert_reduce_fusion, bf16[256,2048]{1,0:T(8,128)(2,1)} %x_ref.1, s32[]{:T(128)S(6)} %select_n.34), kind=kOutput, calls=%fused_computation.7 | convolution fusion | flops 68485120 | bytes 2515076 | tf_op jit(solution)/shard_map/dot_general | solution.py:253
  66.7 1.6 copy.48
  68.4 44.5 %all_to_all.20 = bf16[4,128,2048]{2,0,1:T(4,128)(2,1)S(1)} all-to-all(bf16[4,128,2048]{2,0,1:T(4,128)(2,1)S(1)} %copy.48), channel_id=1, replica_groups=mesh['seq'=16,'head'=8] {'seq','head'}, dimensions={1} | all-to-all | bytes 4194304 | tf_op jit(solution)/shard_map/all_to_all | solution.py:255
  112.9 0.0 copy-start.4
  112.9 1.2 copy.49
  114.0 0.7 copy-done.4
  114.8 0.0 copy-start.5
  114.8 1.8 %fusion.2 = f32[512,768]{1,0:T(8,128)S(1)} fusion(bf16[512,2048]{1,0:T(8,128)(2,1)S(1)} %bitcast.55, bf16[1,2048,768]{2,1,0:T(8,128)(2,1)S(1)} %copy-done.4), kind=kOutput, calls=%fused_computation.2 | convolution fusion | flops 1610612736 | bytes 6815744 | tf_op jit(solution)/shard_map/dot_general | solution.py:258
  116.6 0.1 copy-done.5
  116.7 1.8 %fusion.4 = f32[512,768]{1,0:T(8,128)S(1)} fusion(bf16[512,2048]{1,0:T(8,128)(2,1)S(1)} %bitcast.56, bf16[1,2048,768]{2,1,0:T(8,128)(2,1)S(1)} %copy-done.5), kind=kOutput, calls=%fused_computation.4 | convolution fusion | flops 1610612736 | bytes 6815744 | tf_op jit(solution)/shard_map/dot_general | solution.py:257
  118.5 0.0 copy-done
  118.5 1.8 %fusion.6 = bf16[512,2048]{1,0:T(8,128)(2,1)S(1)} fusion(bf16[1,768,2048]{2,1,0:T(8,128)(2,1)S(1)} %copy-done, f32[512,768]{1,0:T(8,128)S(1)} %fusion.2, f32[512,768]{1,0:T(8,128)S(1)} %fusion.4), kind=kOutput, calls=%fused_computation.6 | convolution fusion | flops 1614020608 | bytes 8388608 | tf_op jit(solution)/shard_map/dot_general | solution.py:262
  120.3 2.9 %copy.50 = bf16[4,128,2048]{2,0,1:T(4,128)(2,1)} copy(bf16[4,128,2048]{2,1,0:T(8,128)(2,1)S(1)} %bitcast.57) | data formatting | bytes 4194304 | tf_op jit(solution)/shard_map/reshape | solution.py:264
  123.3 0.0 copy-start.3
  123.3 5.9 %all-to-all-start.3 = ((bf16[4,128,2048]{2,0,1:T(4,128)(2,1)}), bf16[4,128,2048]{2,0,1:T(4,128)(2,1)}, u32[]{:S(2)}, u32[]{:S(2)}) async-start(bf16[4,128,2048]{2,0,1:T(4,128)(2,1)} %copy.50), calls=%async_computation.3 | async-start | bytes 4194304 | tf_op jit(solution)/shard_map/all_to_all | solution.py:261
  129.2 0.0 copy-done.3
  129.2 0.1 copy.47
  129.3 0.2 select_reduce_fusion
  129.5 29.5 %all-to-all-done.3 = bf16[4,128,2048]{2,0,1:T(4,128)(2,1)} async-done(((bf16[4,128,2048]{2,0,1:T(4,128)(2,1)}), bf16[4,128,2048]{2,0,1:T(4,128)(2,1)}, u32[]{:S(2)}, u32[]{:S(2)}) %all-to-all-start.3) | async-done | bytes 2097184 | tf_op jit(solution)/shard_map/all_to_all | solution.py:261
  159.0 2.7 %copy.51 = bf16[4,128,2048]{2,1,0:T(8,128)(2,1)S(1)} copy(bf16[4,128,2048]{2,0,1:T(4,128)(2,1)} %all-to-all-done.3) | data formatting | bytes 4194304 | tf_op jit(solution)/shard_map/all_to_all | solution.py:261
  161.8 2.7 %fusion.9 = bf16[32,2048]{1,0:T(8,128)(2,1)} fusion(f32[32,512]{1,0:T(8,128)S(1)} %select_reduce_fusion, bf16[512,2048]{1,0:T(8,128)(2,1)S(1)} %bitcast.52, f32[32,2048]{1,0:T(8,128)S(1)} %convert_reduce_fusion, bf16[256,2048]{1,0:T(8,128)(2,1)} %x_ref.1, s32[]{:T(128)S(6)} %select_n.34), kind=kOutput, calls=%fused_computation.9 | convolution fusion | flops 402915328 | bytes 2686980 | tf_op jit(solution)/shard_map/dot_general | solution.py:271
  (12 shorter events, 0.1 us)
Async XLA Ops:
  0.0 118.5 %copy-start = (bf16[1,768,2048]{2,1,0:T(8,128)(2,1)S(1)}, bf16[1,768,2048]{2,1,0:T(8,128)(2,1)}, u32[]{:S(2)}) copy-start(bf16[1,768,2048]{2,1,0:T(8,128)(2,1)} %param.29) | copy-start | bytes 9437188
  6.8 23.0 %all-to-all-start = ((bf16[8,2,256,128]{3,2,1,0:T(8,128)(2,1)}), bf16[8,2,256,128]{3,2,1,0:T(8,128)(2,1)}, u32[]{:S(2)}, u32[]{:S(2)}) async-start(bf16[8,2,256,128]{3,2,1,0:T(8,128)(2,1)} %get-tuple-element.16), calls=%async_computation | async-start | bytes 2097152 | tf_op jit(solution)/shard_map/all_to_all | solution.py:218
  13.8 15.9 %copy-start.2 = (s32[32,8]{0,1:T(8,128)S(1)}, s32[32,8]{0,1:T(8,128)}, u32[]{:S(2)}) copy-start(s32[32,8]{0,1:T(8,128)} %param.25) | copy-start | bytes 3076
  29.8 3.0 %collective-permute-start = (bf16[8,2,256,128]{3,2,1,0:T(8,128)(2,1)}, bf16[8,2,256,128]{3,2,1,0:T(8,128)(2,1)}, u32[]{:S(2)}, u32[]{:S(2)}) collective-permute-start(bf16[8,2,256,128]{3,2,1,0:T(8,128)(2,1)} %all-to-all-done.own_ref), channel_id=1, source_target_pairs={{0,8},{8,0},{16,24},{24,16},{32,40},{40,32},{48,56},{56,48},{64,72... | collective-permute-start | bytes 3145736 | tf_op jit(solution)/shard_map/ppermute | solution.py:235
  41.6 23.5 %copy-start.1 = (f32[2048]{0:T(1024)S(1)}, f32[2048]{0:T(1024)}, u32[]{:S(2)}) copy-start(f32[2048]{0:T(1024)} %param.23) | copy-start | bytes 24580
  41.6 21.0 %all-to-all-start.1 = ((bf16[8,32,2048]{2,1,0:T(8,128)(2,1)}), bf16[8,32,2048]{2,1,0:T(8,128)(2,1)}, u32[]{:S(2)}, u32[]{:S(2)}) async-start(bf16[8,32,2048]{2,1,0:T(8,128)(2,1)} %bitcast.54), calls=%async_computation.1 | async-start | bytes 2097152 | tf_op jit(solution)/shard_map/all_to_all | solution.py:239
  112.9 1.9 %copy-start.4 = (bf16[1,2048,768]{2,1,0:T(8,128)(2,1)S(1)}, bf16[1,2048,768]{2,1,0:T(8,128)(2,1)}, u32[]{:S(2)}) copy-start(bf16[1,2048,768]{2,1,0:T(8,128)(2,1)} %param.28) | copy-start | bytes 9437188
  114.8 1.9 %copy-start.5 = (bf16[1,2048,768]{2,1,0:T(8,128)(2,1)S(1)}, bf16[1,2048,768]{2,1,0:T(8,128)(2,1)}, u32[]{:S(2)}) copy-start(bf16[1,2048,768]{2,1,0:T(8,128)(2,1)} %param.27) | copy-start | bytes 9437188
  123.3 5.9 %copy-start.3 = (f32[32,8]{0,1:T(8,128)S(1)}, f32[32,8]{0,1:T(8,128)}, u32[]{:S(2)}) copy-start(f32[32,8]{0,1:T(8,128)} %param.26) | copy-start | bytes 3076
  123.3 35.7 %all-to-all-start.3 = ((bf16[4,128,2048]{2,0,1:T(4,128)(2,1)}), bf16[4,128,2048]{2,0,1:T(4,128)(2,1)}, u32[]{:S(2)}, u32[]{:S(2)}) async-start(bf16[4,128,2048]{2,0,1:T(4,128)(2,1)} %copy.50), calls=%async_computation.3 | async-start | bytes 4194304 | tf_op jit(solution)/shard_map/all_to_all | solution.py:261
